TPU v7x, 256 devices: a whole 4x4x8 slice. The times are simulated.
256 devices in a mesh: req: 8 (over x, z_hi), blk: 32 (over y, z_lo, core).
Axes of the slice: x: 4, y: 4, z: 8 (z_hi: 2, z_lo: 4; z = z_hi * 4 + z_lo), core: 2. Of those that a mesh axis runs over, the one named last changes fastest.
Arguments:
- tokens: bfloat16 [256, 128, 1536], P(('req', 'blk')), may hold values from -6 to 6
- cache_kv: bfloat16 [256, 2, 256, 384], P(('req', 'blk')), may hold values from -200 to 200
- cache_len: int32 [256], P(('req', 'blk')), may hold values from 2 to 256, as said below
- holder: int32 [256], P(('req', 'blk')), may hold values from 0 to 7, as said below
- accept: int32 [256, 128], P(('req', 'blk')), may hold values from 0 to 1, as said below
- attn_gain: float32 [1536], replicated, may hold values from 0.1 to 1.9
- q_weight: bfloat16 [1536, 768], replicated, may hold values from -0.15625 to 0.15625
- k_weight: bfloat16 [1536, 384], replicated, may hold values from -0.15625 to 0.15625
- v_weight: bfloat16 [1536, 384], replicated, may hold values from -0.15625 to 0.15625
- o_weight: bfloat16 [768, 1536], replicated, may hold values from -0.21875 to 0.21875
- ffn_gain: float32 [1536], replicated, may hold values from 0.4 to 2.5
- w_gate: bfloat16 [1536, 4096], P(None, 'blk'), may hold values from -0.15625 to 0.15625
- w_up: bfloat16 [1536, 4096], P(None, 'blk'), may hold values from -0.15625 to 0.15625
- w_down: bfloat16 [4096, 1536], P('blk'), may hold values from -0.09375 to 0.09375
Outputs:
- refined: float32 [256, 128, 1536], P(('req', 'blk'))
Inputs may be any that keep to these rules, and one draw needn't show every extreme that they name: `holder`: requests whose numbers agree modulo 32 have distinct holders. `cache_len`: some request has exactly 256 cached positions. `accept`: each request accepts exactly 64 positions.
All inputs are finite; a program needn't handle non-finite values.
Results may differ from a plain program's by a relative error of at most 0.04.
Values may be sent and summed in bfloat16 or wider, within the bound.
No kernel may reach another device: no remote copies, remote signals or barrier semaphores. Data moves between devices by JAX's collectives and lax.ppermute only.
A program may use at most 128 MiB of HBM per device.

v0:
```python
import jax
import jax.numpy as jnp
from jax import lax
from jax.sharding import PartitionSpec as P

HEAD = 96


norm_eps = 1e-05
rope_base = 100000.0


def rms_scale(values, gain_row):
    return (
        values * lax.rsqrt(jnp.mean(values * values, axis=-1, keepdims=True) + norm_eps) * gain_row
    )


def rotate_heads(flat, positions, head_count):
    half_dim = HEAD // 2
    shaped = flat.reshape(flat.shape[0], head_count, HEAD)
    freqs = jnp.exp(-jnp.log(rope_base) * 2.0 * jnp.arange(half_dim, dtype=jnp.float32) / HEAD)
    angles = positions[:, None] * freqs[None, :]
    cosine = jnp.cos(angles)[:, None, :]
    sine = jnp.sin(angles)[:, None, :]
    first_half = shaped[..., :half_dim]
    second_half = shaped[..., half_dim:]
    turned = jnp.concatenate(
        [first_half * cosine - second_half * sine, second_half * cosine + first_half * sine],
        axis=-1,
    )
    return turned.reshape(flat.shape[0], head_count * HEAD)


def attend_block(
    tok_rows,
    cache_keys,
    cache_vals,
    cache_length,
    attn_gain,
    q_weight,
    k_weight,
    v_weight,
    o_weight,
):
    block_len = tok_rows.shape[0]
    slot_len = cache_keys.shape[0]
    kv_count = k_weight.shape[1] // HEAD
    q_count = q_weight.shape[1] // HEAD
    widened = tok_rows.astype(jnp.float32)
    normed = rms_scale(widened, attn_gain).astype(jnp.bfloat16)
    positions = (cache_length + jnp.arange(block_len, dtype=jnp.int32)).astype(jnp.float32)
    queries = rotate_heads(
        jnp.dot(normed, q_weight, preferred_element_type=jnp.float32), positions, q_count
    ).astype(jnp.bfloat16)
    new_keys = rotate_heads(
        jnp.dot(normed, k_weight, preferred_element_type=jnp.float32), positions, kv_count
    ).astype(jnp.bfloat16)
    new_vals = jnp.dot(normed, v_weight, preferred_element_type=jnp.float32).astype(jnp.bfloat16)
    all_keys = jnp.concatenate([cache_keys, new_keys], axis=0).reshape(
        slot_len + block_len, kv_count, HEAD
    )
    all_vals = jnp.concatenate([cache_vals, new_vals], axis=0).reshape(
        slot_len + block_len, kv_count, HEAD
    )
    grouped = queries.reshape(block_len, kv_count, q_count // kv_count, HEAD)
    scores = jnp.einsum(
        "bgid,kgd->gibk", grouped, all_keys, preferred_element_type=jnp.float32
    ) * HEAD ** (-0.5)
    valid = jnp.concatenate(
        [
            jnp.arange(slot_len, dtype=jnp.int32) < cache_length,
            jnp.ones((block_len,), dtype=jnp.bool_),
        ]
    )
    scores = jnp.where(valid, scores, -jnp.inf)
    peaks = jnp.max(scores, axis=-1, keepdims=True)
    expd = jnp.exp(scores - peaks)
    probs = (expd / jnp.sum(expd, axis=-1, keepdims=True)).astype(jnp.bfloat16)
    context = jnp.einsum("gibk,kgd->bgid", probs, all_vals, preferred_element_type=jnp.float32)
    context = context.astype(jnp.bfloat16).reshape(block_len, q_count * HEAD)
    return widened + jnp.dot(context, o_weight, preferred_element_type=jnp.float32)


def run_ffn(normed_rows, w_gate, w_up, w_down):
    part_rows = lax.all_gather(normed_rows, "blk", axis=0, tiled=True)
    gate_vals = jnp.dot(part_rows, w_gate, preferred_element_type=jnp.float32)
    up_vals = jnp.dot(part_rows, w_up, preferred_element_type=jnp.float32)
    hidden_all = (jax.nn.silu(gate_vals) * up_vals).astype(jnp.bfloat16)
    return lax.psum_scatter(
        jnp.dot(hidden_all, w_down, preferred_element_type=jnp.float32).astype(jnp.bfloat16),
        "blk",
        scatter_dimension=0,
        tiled=True,
    ).astype(jnp.float32)


def local(
    tokens,
    cache_kv,
    cache_len,
    holder,
    accept,
    attn_gain,
    q_weight,
    k_weight,
    v_weight,
    o_weight,
    ffn_gain,
    w_gate,
    w_up,
    w_down,
):
    own_holder = holder[0]
    part_rows = lax.all_gather(cache_kv, "req", axis=0, tiled=True)
    matches = jnp.arange(part_rows.shape[0], dtype=jnp.int32) == own_holder
    fetched = jnp.sum(
        jnp.where(matches[:, None, None, None], part_rows, jnp.zeros_like(part_rows)), axis=0
    )
    cache_keys = fetched[0]
    cache_vals = fetched[1]
    cache_length = cache_len[0]
    block_rows = tokens[0]
    first_pass = attend_block(
        block_rows,
        cache_keys,
        cache_vals,
        cache_length,
        attn_gain,
        q_weight,
        k_weight,
        v_weight,
        o_weight,
    )
    chosen_mask = accept[0] == 1
    ffn_sum = run_ffn(rms_scale(first_pass, ffn_gain).astype(jnp.bfloat16), w_gate, w_up, w_down)
    placed = first_pass + ffn_sum
    second_in = jnp.where(chosen_mask[:, None], placed, block_rows.astype(jnp.float32))
    refined = attend_block(
        second_in,
        cache_keys,
        cache_vals,
        cache_length,
        attn_gain,
        q_weight,
        k_weight,
        v_weight,
        o_weight,
    )
    return refined[None]


def solution(mesh):
    return jax.shard_map(
        local,
        mesh=mesh,
        in_specs=(
            P(("req", "blk"), None, None),
            P(("req", "blk"), None, None, None),
            P(("req", "blk")),
            P(("req", "blk")),
            P(("req", "blk"), None),
            P(),
            P(),
            P(),
            P(),
            P(),
            P(),
            P(None, "blk"),
            P(None, "blk"),
            P("blk", None),
        ),
        out_specs=P(("req", "blk"), None, None),
        check_vma=False,
    )
```

profile of v0, /device:TPU:1, one launch (start us, length us, event | category | flops | bytes accessed | tf_op | source)
XLA Modules:
  0.0 408.1 jit_solution(16125476862326176305)
XLA Ops:
  6.5 0.7 all-gather.3.cloned.1.call-update
  7.3 0.0 all-gather.5.cloned.1.call-start
  8.0 4.3 %copy.35 = bf16[1536,768]{0,1:T(8,128)(2,1)} copy(bf16[1536,768]{1,0:T(8,128)(2,1)} %param.20) | data formatting | bytes 4718592 | tf_op args[6]
  12.3 2.5 copy.34
  15.4 0.2 fusion.23
  15.6 1.7 convolution_convert_fusion.4
  17.3 0.8 copy.32
  18.1 0.2 multiply_cosine_fusion
  18.3 2.6 fusion.56
  20.9 0.1 subtract_convert_fusion.1
  21.0 0.5 fusion.58
  21.6 0.7 subtract_convert_fusion.3
  22.2 83.0 %all-gather.3.cloned.1.call-done = bf16[8,2,256,384]{3,2,1,0:T(8,128)(2,1)} async-done(((bf16[1,2,256,384]{3,2,1,0:T(8,128)(2,1)}), bf16[8,2,256,384]{3,2,1,0:T(8,128)(2,1)}) %all-gather.3.cloned.1.call-update) | async-done | bytes 3145744 | tf_op jit(solution)/shard_map/all_gather | solution.py:115
  105.2 3.0 select_reduce_fusion
  108.2 0.1 copy.33
  108.4 0.1 copy.31
  108.6 0.0 copy-start.16
  108.6 2.7 fusion.79
  111.3 1.7 convolution_convert_fusion.2
  113.0 0.0 copy-start.18
  113.1 0.6 multiply_reduce_fusion.1
  113.7 0.9 copy-done.3
  114.5 0.9 multiply_convert_fusion.1
  115.4 0.0 all-gather.5.cloned.1.call-update
  115.5 0.0 copy-start.6
  115.5 0.0 copy-start.12
  115.5 0.2 reduce-scatter.2.cloned.1.call-start
  115.7 75.2 %all-gather.5.cloned.1.call-done = bf16[4096,1536]{1,0:T(8,128)(2,1)} async-done(((bf16[128,1536]{1,0:T(8,128)(2,1)}), bf16[4096,1536]{1,0:T(8,128)(2,1)}) %all-gather.5.cloned.1.call-update) | async-done | bytes 12582928 | tf_op jit(solution)/shard_map/all_gather | solution.py:86
  190.9 9.4 %fusion.85 = f32[4096,128]{1,0:T(8,128)} fusion(bf16[4096,1536]{1,0:T(8,128)(2,1)} %all-gather.5.cloned.1.call-done, bf16[1536,128]{1,0:T(8,128)(2,1)} %param.25), kind=kOutput, calls=%fused_computation.100 | convolution fusion | flops 1610612736 | bytes 15073280 | tf_op jit(solution)/shard_map/dot_general | solution.py:87
  200.3 18.2 %convolution_convert_fusion = bf16[4096,1536]{1,0:T(8,128)(2,1)} fusion(bf16[128,1536]{1,0:T(8,128)(2,1)S(1)} %copy-done.12, bf16[4096,1536]{1,0:T(8,128)(2,1)} %all-gather.5.cloned.1.call-done, bf16[1536,128]{1,0:T(8,128)(2,1)S(1)} %copy-done.6, f32[4096,128]{1,0:T(8,128)} %fusion.85), kind=kOutput, calls=%fused_computation.2 | convolution fusion | flops 3230662656 | bytes 28049408 | tf_op jit(solution)/shard_map/dot_general | solution.py:91
  218.5 0.0 reduce-scatter.2.cloned.1.call-update
  218.5 0.6 copy-done.19
  219.2 169.8 %reduce-scatter.2.cloned.1.call-done = bf16[128,1536]{1,0:T(8,128)(2,1)} async-done(((bf16[4096,1536]{1,0:T(8,128)(2,1)}), bf16[128,1536]{1,0:T(8,128)(2,1)}) %reduce-scatter.2.cloned.1.call-update) | async-done | bytes 393232 | tf_op jit(solution)/shard_map/reduce_scatter | solution.py:90
  389.0 1.6 multiply_reduce_fusion
  390.6 0.1 multiply_convert_fusion
  390.8 0.2 copy-done.2
  391.0 1.0 fusion.87
  392.1 0.2 copy-done.4
  392.3 0.6 fusion.86
  392.9 0.7 copy-done.7
  393.5 0.4 convolution_convert_fusion.3
  394.0 0.1 subtract_convert_fusion
  394.0 0.7 subtract_convert_fusion.2
  394.7 0.1 copy.37
  394.8 0.7 pad_maximum_fusion.5
  395.5 2.9 fusion.82
  398.4 1.7 convolution_convert_fusion.1
  400.1 1.4 fusion.3
  (43 shorter events, 0.2 us)
Async XLA Ops:
  6.5 106.5 %copy-start = (bf16[768,1536]{1,0:T(8,128)(2,1)S(1)}, bf16[768,1536]{1,0:T(8,128)(2,1)}, u32[]{:S(2)}) copy-start(bf16[768,1536]{1,0:T(8,128)(2,1)} %param.23) | copy-start | bytes 7077892
  6.5 98.6 %all-gather.3.cloned.1.call-start = ((), (), s32[]{:S(2)}) async-start(), calls=%async_computation.1 | async-start | bytes 3538944 | tf_op jit(solution)/shard_map/all_gather | solution.py:115
  7.3 183.7 %all-gather.5.cloned.1.call-start = ((), (), s32[]{:S(2)}) async-start(), calls=%async_computation.2 | async-start | bytes 12976128 | tf_op jit(solution)/shard_map/all_gather | solution.py:86
  12.3 3.1 copy-start.1
  12.3 3.3 copy-start.17
  18.3 3.3 copy-start.8
  18.3 3.3 copy-start.10
  18.3 2.7 copy-start.5
  108.4 2.9 copy-start.15
  108.5 2.8 copy-start.13
  108.6 2.8 copy-start.16
  113.0 1.5 copy-start.18
  113.6 0.9 copy-start.3
  115.5 84.9 %copy-start.6 = (bf16[1536,128]{1,0:T(8,128)(2,1)S(1)}, bf16[1536,128]{1,0:T(8,128)(2,1)}, u32[]{:S(2)}) copy-start(bf16[1536,128]{1,0:T(8,128)(2,1)} %param.26) | copy-start | bytes 1179652
  115.5 84.9 %copy-start.12 = (bf16[128,1536]{1,0:T(8,128)(2,1)S(1)}, bf16[128,1536]{1,0:T(8,128)(2,1)}, u32[]{:S(2)}) copy-start(bf16[128,1536]{1,0:T(8,128)(2,1)} %param.27) | copy-start | bytes 1179652
  115.5 273.5 %reduce-scatter.2.cloned.1.call-start = ((), (), s32[]{:S(2)}) async-start(), calls=%async_computation.3 | async-start | bytes 12976128 | tf_op jit(solution)/shard_map/reduce_scatter | solution.py:90
  218.5 0.7 copy-start.19
  389.0 2.0 copy-start.2
  391.0 1.3 copy-start.4
  392.3 1.3 copy-start.7
  392.3 1.7 copy-start.9
  392.3 1.7 copy-start.11
  395.5 2.9 copy-start.14
Sparse Core Ops, SparseCore 0:
  10.0 95.1 all-gather.2
  115.6 75.3 all-gather.4
  218.7 170.2 reduce-scatter.1
where the time goes:
time: 412 us; the launch traced here: 408 us
  waiting for transfers between devices  329 us (80%)
  matrix products  45.5 us (11%)
  between operations  14.7 us (4%)
  local copies, waits for them, and re-layouts  10.7 us (3%)
  other arithmetic  8.23 us (2%)
    reduce_scatter x1, waiting for transfers between devices, run_ffn(): lax.psum_scatter(jnp.dot(hidden_all, w_down, preferred_element_type=jnp.f...  170 us
    all_gather x1, waiting for transfers between devices, local(): part_rows = lax.all_gather(cache_kv, 'req', axis=0, tiled=True)  83 us
    all_gather x1, waiting for transfers between devices, run_ffn(): part_rows = lax.all_gather(normed_rows, 'blk', axis=0, tiled=True)  75.2 us
    dot_general x1, matrix products, run_ffn(): jnp.dot(hidden_all, w_down, preferred_element_type=jnp.float32)  18.2 us
    unnamed x42, local copies, waits for them, and re-layouts  9.46 us
    dot_general x1, matrix products, run_ffn(): gate_vals = jnp.dot(part_rows, w_gate, preferred_element_type=jnp.float32)  9.38 us
  transfers between devices with their start and end apart: 3, of which 3 were waited for; matrix products, arithmetic and copies ran while one was open for 3% of the time, Pallas kernels for 0%

commit v1 on v0

--- a/solution.py
+++ b/solution.py
@@ -82,17 +82,52 @@
     return widened + jnp.dot(context, o_weight, preferred_element_type=jnp.float32)
 
 
-def run_ffn(normed_rows, w_gate, w_up, w_down):
+def run_ffn(normed_rows, w_gate, w_up, w_down, down_all):
     part_rows = lax.all_gather(normed_rows, "blk", axis=0, tiled=True)
     gate_vals = jnp.dot(part_rows, w_gate, preferred_element_type=jnp.float32)
     up_vals = jnp.dot(part_rows, w_up, preferred_element_type=jnp.float32)
     hidden_all = (jax.nn.silu(gate_vals) * up_vals).astype(jnp.bfloat16)
-    return lax.psum_scatter(
-        jnp.dot(hidden_all, w_down, preferred_element_type=jnp.float32).astype(jnp.bfloat16),
-        "blk",
-        scatter_dimension=0,
-        tiled=True,
-    ).astype(jnp.float32)
+    hidden_own = lax.all_to_all(hidden_all, "blk", 0, 1, tiled=True)
+    groups = w_down.shape[0]
+    group_count = down_all.shape[0] // groups
+    terms = jnp.einsum(
+        "rgk,gkd->grd",
+        hidden_own.reshape(hidden_own.shape[0], group_count, groups),
+        down_all.reshape(group_count, groups, down_all.shape[1]),
+        preferred_element_type=jnp.float32,
+    ).astype(jnp.bfloat16)
+    return jnp.sum(terms.astype(jnp.float32), axis=0)
+
+
+def fetch_slot(cache_kv, holder):
+    count = lax.axis_size("req")
+    own = cache_kv[0]
+    holders = lax.all_gather(holder, "req", axis=0, tiled=True)
+    if count != 8:
+        slots = lax.all_gather(own, "req", axis=0, tiled=False)
+        return slots[holder[0]]
+    me = lax.axis_index("req")
+
+    def swap(values, mask):
+        return lax.ppermute(values, "req", perm=[(i, i ^ mask) for i in range(count)])
+
+    def pick(cond, a, b):
+        return jnp.where(cond, a, b)
+
+    got1 = swap(own, 4)
+    target = me ^ 2
+    send_a = pick(holders[target] == (me ^ 4), got1, own)
+    send_b = pick(holders[target ^ 1] == (me ^ 4), got1, own)
+    got2 = swap(jnp.stack([send_a, send_b]), 2)
+    want = holders[me ^ 1]
+    send_c = pick(want == me, own, pick(want == (me ^ 4), got1, got2[1]))
+    got3 = swap(send_c, 1)
+    need = holders[me]
+    return pick(
+        need == me,
+        own,
+        pick(need == (me ^ 4), got1, pick((need ^ me) == 2, got2[0], pick((need ^ me) == 6, got2[0], got3))),
+    )
 
 
 def local(
@@ -111,12 +146,9 @@
     w_up,
     w_down,
 ):
-    own_holder = holder[0]
-    part_rows = lax.all_gather(cache_kv, "req", axis=0, tiled=True)
-    matches = jnp.arange(part_rows.shape[0], dtype=jnp.int32) == own_holder
-    fetched = jnp.sum(
-        jnp.where(matches[:, None, None, None], part_rows, jnp.zeros_like(part_rows)), axis=0
-    )
+    fetched = fetch_slot(cache_kv, holder)
+    down_all = lax.all_gather(w_down, "blk", axis=0, tiled=True)
+    fetched, down_all = lax.optimization_barrier((fetched, down_all))
     cache_keys = fetched[0]
     cache_vals = fetched[1]
     cache_length = cache_len[0]
@@ -133,7 +165,7 @@
         o_weight,
     )
     chosen_mask = accept[0] == 1
-    ffn_sum = run_ffn(rms_scale(first_pass, ffn_gain).astype(jnp.bfloat16), w_gate, w_up, w_down)
+    ffn_sum = run_ffn(rms_scale(first_pass, ffn_gain).astype(jnp.bfloat16), w_gate, w_up, w_down, down_all)
     placed = first_pass + ffn_sum
     second_in = jnp.where(chosen_mask[:, None], placed, block_rows.astype(jnp.float32))
     refined = attend_block(

time: 412 us -> 275 us (0.67)
  waiting for transfers between devices: 329 us -> 153 us
  starting transfers between devices: 0.26 us -> 16.5 us
  blocking collectives: 0 us -> 13 us
  local copies, waits for them, and re-layouts: 10.7 us -> 17.2 us
  other arithmetic: 8.23 us -> 13.7 us
  between operations: 14.7 us -> 19.3 us
    reduce_scatter x1 -> x0, waiting for transfers between devices: 170 us -> none  [run_ffn(): lax.psum_scatter(jnp.dot(hidden_all, w_down, preferred_element_type=jnp.f...]
    all_gather x1, waiting for transfers between devices: 83 us -> 23 us  [local(): down_all = lax.all_gather(w_down, 'blk', axis=0, tiled=True)]
    all_to_all x0 -> x1, waiting for transfers between devices: none -> 27.9 us  [run_ffn(): hidden_own = lax.all_to_all(hidden_all, 'blk', 0, 1, tiled=True)]
    ppermute x0 -> x3, waiting for transfers between devices: none -> 22 us  [swap(): lax.ppermute(values, 'req', perm=[(i, i ^ mask) for i in range(count)])]
    unnamed x0 -> x1, blocking collectives: none -> 13 us
    ppermute x0 -> x3, starting transfers between devices: none -> 9.55 us  [swap(): lax.ppermute(values, 'req', perm=[(i, i ^ mask) for i in range(count)])]
    all_to_all x0 -> x1, starting transfers between devices: none -> 6.88 us  [run_ffn(): hidden_own = lax.all_to_all(hidden_all, 'blk', 0, 1, tiled=True)]
    dot_general x1 -> x2, matrix products: 18.2 us -> 12.9 us  [the longest x1 8.39 us: run_ffn(): jnp.einsum('rgk,gkd->grd', hidden_own.reshape(hidden_own.shape[0], group_...]
  transfers between devices with their start and end apart: 3 -> 6, of which waited for: 3 -> 5; matrix products, arithmetic and copies ran while one was open for 3% -> 11% of each run, Pallas kernels for 0% -> 0%
where the time goes in v1:
time: 275 us; the launch traced here: 274 us
  waiting for transfers between devices  153 us (56%)
  matrix products  41.8 us (15%)
  between operations  19.3 us (7%)
  local copies, waits for them, and re-layouts  17.2 us (6%)
  starting transfers between devices  16.5 us (6%)
  other arithmetic  13.7 us (5%)
  blocking collectives  13 us (5%)
    all_gather x1, waiting for transfers between devices, run_ffn(): part_rows = lax.all_gather(normed_rows, 'blk', axis=0, tiled=True)  79 us
    all_to_all x1, waiting for transfers between devices, run_ffn(): hidden_own = lax.all_to_all(hidden_all, 'blk', 0, 1, tiled=True)  27.9 us
    all_gather x1, waiting for transfers between devices, local(): down_all = lax.all_gather(w_down, 'blk', axis=0, tiled=True)  23 us
    ppermute x3, waiting for transfers between devices, swap(): lax.ppermute(values, 'req', perm=[(i, i ^ mask) for i in range(count)])  22 us
    unnamed x1, blocking collectives  13 us
    unnamed x51, local copies, waits for them, and re-layouts  11.9 us
    ppermute x3, starting transfers between devices, swap(): lax.ppermute(values, 'req', perm=[(i, i ^ mask) for i in range(count)])  9.55 us
    dot_general x1, matrix products, run_ffn(): jnp.einsum('rgk,gkd->grd', hidden_own.reshape(hidden_own.shape[0], group_...  8.39 us
  transfers between devices with their start and end apart: 6, of which 5 were waited for; matrix products, arithmetic and copies ran while one was open for 11% of the time, Pallas kernels for 0%

profile of v1, /device:TPU:1, one launch (start us, length us, event | category | flops | bytes accessed | tf_op | source)
XLA Modules:
  0.0 274.1 jit_solution(2990724950177425223)
XLA Ops:
  6.5 0.7 all-gather.3.cloned.1.call-update
  8.0 1.3 dynamic-slice
  9.2 0.8 dynamic-update-slice
  10.0 3.6 %collective-permute-start = (bf16[2,256,384]{2,1,0:T(8,128)(2,1)}, bf16[2,256,384]{2,1,0:T(8,128)(2,1)S(1)}, u32[]{:S(2)}, u32[]{:S(2)}) collective-permute-start(bf16[2,256,384]{2,1,0:T(8,128)(2,1)} %bitcast.154), channel_id=1, source_target_pairs={{0,128},{32,160},{64,192},{96,224},{128,0},{160,32},{192,64},{224,... | collective-permute-start | bytes 1179656 | tf_op jit(solution)/shard_map/ppermute | solution.py:112
  13.6 13.0 %all-reduce.1 = s32[8]{0:T(128)S(1)} all-reduce(s32[8]{0:T(128)S(1)} %dynamic-update-slice), channel_id=1, replica_groups=mesh['req'=8,'blk'=32] {'req'}, use_global_device_ids=true, to_apply=%add.1 | all-reduce | flops 8 | bytes 64
  26.6 4.3 %copy.29 = bf16[1536,768]{0,1:T(8,128)(2,1)} copy(bf16[1536,768]{1,0:T(8,128)(2,1)} %param.20) | data formatting | bytes 4718592 | tf_op args[6]
  31.6 0.6 fusion.77
  33.7 3.4 %fusion.55 = f32[128,8,96]{0,2,1:T(8,128)} fusion(bf16[8,96,1536]{2,1,0:T(8,128)(2,1)} %bitcast.152, bf16[1,128,1536]{2,1,0:T(8,128)(2,1)S(1)} %copy-done.2, f32[1536]{0:T(1024)S(1)} %copy-done.17, f32[128]{0:T(128)S(1)} %add_rsqrt_fusion.2), kind=kOutput, calls=%fused_computation.75 | convolution fusion | flops 302776320 | bytes 3152384 | tf_op jit(solution)/shard_map/dot_general | solution.py:54
  37.2 1.0 pad_maximum_fusion
  38.1 0.8 multiply_cosine_fusion
  40.1 2.4 copy.28
  42.5 1.9 subtract_convert_fusion.1
  44.4 2.4 convolution_convert_fusion.4
  46.7 1.2 fusion.57
  48.0 6.3 %collective-permute-done.1 = bf16[2,2,256,384]{3,2,1,0:T(8,128)(2,1)} collective-permute-done((bf16[2,2,256,384]{3,2,1,0:T(8,128)(2,1)}, bf16[2,2,256,384]{3,2,1,0:T(8,128)(2,1)}, u32[]{:S(2)}, u32[]{:S(2)}) %collective-permute-start.1) | collective-permute-done | bytes 786464 | tf_op jit(solution)/shard_map/ppermute | solution.py:112
  54.3 1.8 fusion.28
  56.1 6.0 %collective-permute-start.2 = (bf16[2,256,384]{2,1,0:T(8,128)(2,1)}, bf16[2,256,384]{2,1,0:T(8,128)(2,1)}, u32[]{:S(2)}, u32[]{:S(2)}) collective-permute-start(bf16[2,256,384]{2,1,0:T(8,128)(2,1)} %fusion.28), channel_id=1, source_target_pairs={{0,32},{32,0},{64,96},{96,64},{128,160},{160,128},{192,224},{224,1... | collective-permute-start | bytes 1179656 | tf_op jit(solution)/shard_map/ppermute | solution.py:112
  63.9 1.6 copy.26
  65.6 1.7 pad_maximum_fusion.5
  67.2 1.6 subtract_convert_fusion.3
  68.8 15.7 %collective-permute-done.2 = bf16[2,256,384]{2,1,0:T(8,128)(2,1)} collective-permute-done((bf16[2,256,384]{2,1,0:T(8,128)(2,1)}, bf16[2,256,384]{2,1,0:T(8,128)(2,1)}, u32[]{:S(2)}, u32[]{:S(2)}) %collective-permute-start.2) | collective-permute-done | bytes 393248 | tf_op jit(solution)/shard_map/ppermute | solution.py:112
  84.6 1.9 fusion.24
  86.5 23.0 %all-gather.3.cloned.1.call-done = bf16[4096,1536]{1,0:T(8,128)(2,1)} async-done(((bf16[128,1536]{1,0:T(8,128)(2,1)}), bf16[4096,1536]{1,0:T(8,128)(2,1)}) %all-gather.3.cloned.1.call-update) | async-done | bytes 12582928 | tf_op jit(solution)/shard_map/all_gather | solution.py:150
  109.5 1.1 fusion.76
  110.9 2.9 %fusion.78 = (f32[4,2,128]{2,1,0:T(2,128)S(1)}, f32[4,2,128,384]{2,3,1,0:T(8,128)}) fusion(bf16[128,4,2,96]{0,3,2,1:T(8,128)(2,1)} %bitcast.164, bf16[256,4,96]{0,2,1:T(8,128)(2,1)S(1)} %bitcast.162, bf16[128,4,48]{0,2,1:T(8,128)(2,1)S(1)} %copy-done.19, bf16[128,4,48]{0,2,1:T(8,128)(2,1)S(1)} %copy-done.18, pred[384]{0:T(512)(128)(4,1)S(1)} %concatenate.47), kind=kOutput, calls=%fused_computation.102 | convolution fusion | flops 77955456 | bytes 2068864 | tf_op jit(solution)/shard_map/sub | solution.py:78
  113.8 1.7 convolution_convert_fusion.2
  115.5 0.6 multiply_reduce_fusion.1
  116.1 0.9 copy-done.4
  117.0 0.9 multiply_convert_fusion.1
  117.9 79.0 %all-gather.5.cloned.1.call-done = bf16[4096,1536]{1,0:T(8,128)(2,1)} async-done(((bf16[128,1536]{1,0:T(8,128)(2,1)}), bf16[4096,1536]{1,0:T(8,128)(2,1)}) %all-gather.5.cloned.1.call-update) | async-done | bytes 12582928 | tf_op jit(solution)/shard_map/all_gather | solution.py:86
  196.9 8.0 %fusion.84 = f32[4096,128]{1,0:T(8,128)S(1)} fusion(bf16[4096,1536]{1,0:T(8,128)(2,1)} %all-gather.5.cloned.1.call-done, bf16[1536,128]{1,0:T(8,128)(2,1)S(1)} %copy-done.12), kind=kOutput, calls=%fused_computation.104 | convolution fusion | flops 1610612736 | bytes 15073280 | tf_op jit(solution)/shard_map/dot_general | solution.py:87
  205.1 4.6 %fusion.2 = bf16[4096,128]{1,0:T(8,128)(2,1)} fusion(bf16[4096,1536]{1,0:T(8,128)(2,1)S(1)} %copy-done.1, bf16[1536,128]{1,0:T(8,128)(2,1)S(1)} %copy-done.21, f32[4096,128]{1,0:T(8,128)S(1)} %fusion.84), kind=kOutput, calls=%fused_computation.5 | convolution fusion | flops 1613758464 | bytes 16121856 | tf_op jit(solution)/shard_map/dot_general | solution.py:88
  209.6 6.9 %all-to-all-start = ((bf16[32,128,128]{2,1,0:T(8,128)(2,1)}), bf16[32,128,128]{2,1,0:T(8,128)(2,1)}, u32[]{:S(2)}, u32[]{:S(2)}) async-start(bf16[32,128,128]{2,1,0:T(8,128)(2,1)} %bitcast.156), calls=%async_computation | async-start | bytes 2097152 | tf_op jit(solution)/shard_map/all_to_all | solution.py:90
  216.6 27.9 %all-to-all-done = bf16[32,128,128]{2,1,0:T(8,128)(2,1)} async-done(((bf16[32,128,128]{2,1,0:T(8,128)(2,1)}), bf16[32,128,128]{2,1,0:T(8,128)(2,1)}, u32[]{:S(2)}, u32[]{:S(2)}) %all-to-all-start) | async-done | bytes 1048608 | tf_op jit(solution)/shard_map/all_to_all | solution.py:90
  244.4 8.4 %convert_reduce_fusion = f32[128,1536]{1,0:T(8,128)S(1)} fusion(bf16[32,128,1536]{2,1,0:T(8,128)(2,1)} %bitcast.151, bf16[32,128,128]{2,1,0:T(8,128)(2,1)} %all-to-all-done), kind=kOutput, calls=%fused_computation.2 | convolution fusion | flops 1629290496 | bytes 14417920 | tf_op jit(solution)/shard_map/rgk,gkd->grd/dot_general | solution.py:93
  252.9 0.3 multiply_reduce_fusion
  253.3 1.2 copy-done.3
  254.5 1.1 fusion.86
  255.6 0.2 copy-done.6
  255.8 0.6 fusion.85
  256.4 0.7 copy-done.9
  257.1 1.0 convolution_convert_fusion.3
  258.1 0.7 subtract_convert_fusion.2
  258.8 1.6 copy.31
  260.4 0.7 pad_maximum_fusion.6
  261.1 2.9 %fusion.81 = (f32[4,2,128]{2,1,0:T(2,128)S(1)}, f32[4,2,128,384]{2,3,1,0:T(8,128)}) fusion(bf16[128,4,2,96]{0,3,2,1:T(8,128)(2,1)} %bitcast.165, bf16[256,4,96]{0,2,1:T(8,128)(2,1)} %bitcast.163, bf16[128,4,48]{0,2,1:T(8,128)(2,1)} %get-tuple-element.20, bf16[128,4,48]{0,2,1:T(8,128)(2,1)} %get-tuple-element.19, pred[384]{0:T(512)(128)(4,1)S(1)} %concatenate.47), kind=kOutput, calls=%fused_computation.103 | convolution fusion | flops 77955456 | bytes 2068864 | tf_op jit(solution)/shard_map/sub | solution.py:78
  264.1 1.8 convolution_convert_fusion.1
  265.8 1.4 fusion.3
  (62 shorter events, 1.1 us)
Async XLA Ops:
  6.5 109.0 %copy-start = (bf16[768,1536]{1,0:T(8,128)(2,1)S(1)}, bf16[768,1536]{1,0:T(8,128)(2,1)}, u32[]{:S(2)}) copy-start(bf16[768,1536]{1,0:T(8,128)(2,1)} %param.23) | copy-start | bytes 7077892
  6.5 103.0 %all-gather.3.cloned.1.call-start = ((), (), s32[]{:S(2)}) async-start(), calls=%async_computation.1 | async-start | bytes 12976128 | tf_op jit(solution)/shard_map/all_gather | solution.py:150
  7.3 189.6 %all-gather.5.cloned.1.call-start = ((), (), s32[]{:S(2)}) async-start(), calls=%async_computation.2 | async-start | bytes 12976128 | tf_op jit(solution)/shard_map/all_gather | solution.py:86
  10.0 27.1 %collective-permute-start = (bf16[2,256,384]{2,1,0:T(8,128)(2,1)}, bf16[2,256,384]{2,1,0:T(8,128)(2,1)S(1)}, u32[]{:S(2)}, u32[]{:S(2)}) collective-permute-start(bf16[2,256,384]{2,1,0:T(8,128)(2,1)} %bitcast.154), channel_id=1, source_target_pairs={{0,128},{32,160},{64,192},{96,224},{128,0},{160,32},{192,64},{224,... | collective-permute-start | bytes 1179656 | tf_op jit(solution)/shard_map/ppermute | solution.py:112
  26.5 7.0 %copy-start.2 = (bf16[1,128,1536]{2,1,0:T(8,128)(2,1)S(1)}, bf16[1,128,1536]{2,1,0:T(8,128)(2,1)}, u32[]{:S(2)}) copy-start(bf16[1,128,1536]{2,1,0:T(8,128)(2,1)} %param.14) | copy-start | bytes 1179652
  26.5 7.1 %copy-start.17 = (f32[1536]{0:T(1024)S(1)}, f32[1536]{0:T(1024)}, u32[]{:S(2)}) copy-start(f32[1536]{0:T(1024)} %param.19) | copy-start | bytes 18436
  33.7 3.4 %copy-start.8 = (bf16[1,2,256,384]{3,2,1,0:T(8,128)(2,1)S(1)}, bf16[1,2,256,384]{3,2,1,0:T(8,128)(2,1)}, u32[]{:S(2)}) copy-start(bf16[1,2,256,384]{3,2,1,0:T(8,128)(2,1)} %param.15) | copy-start | bytes 1179652
  38.1 16.2 %collective-permute-start.1 = (bf16[2,2,256,384]{3,2,1,0:T(8,128)(2,1)}, bf16[2,2,256,384]{3,2,1,0:T(8,128)(2,1)}, u32[]{:S(2)}, u32[]{:S(2)}) collective-permute-start(bf16[2,2,256,384]{3,2,1,0:T(8,128)(2,1)} %pad_maximum_fusion), channel_id=1, source_target_pairs={{0,64},{32,96},{64,0},{96,32},{128,192},{160,224},{192,128},{224,1... | collective-permute-start | bytes 2359304 | tf_op jit(solution)/shard_map/ppermute | solution.py:112
  42.5 4.2 %copy-start.7 = (bf16[1536,384]{0,1:T(8,128)(2,1)S(1)}, bf16[1536,384]{0,1:T(8,128)(2,1)}, u32[]{:S(2)}) copy-start(bf16[1536,384]{0,1:T(8,128)(2,1)} %copy.28) | copy-start | bytes 3538948
  56.1 28.4 %collective-permute-start.2 = (bf16[2,256,384]{2,1,0:T(8,128)(2,1)}, bf16[2,256,384]{2,1,0:T(8,128)(2,1)}, u32[]{:S(2)}, u32[]{:S(2)}) collective-permute-start(bf16[2,256,384]{2,1,0:T(8,128)(2,1)} %fusion.28), channel_id=1, source_target_pairs={{0,32},{32,0},{64,96},{96,64},{128,160},{160,128},{192,224},{224,1... | collective-permute-start | bytes 1179656 | tf_op jit(solution)/shard_map/ppermute | solution.py:112
  86.5 24.4 %copy-start.18 = (bf16[128,4,48]{0,2,1:T(8,128)(2,1)S(1)}, bf16[128,4,48]{0,2,1:T(8,128)(2,1)}, u32[]{:S(2)}) copy-start(bf16[128,4,48]{0,2,1:T(8,128)(2,1)} %get-tuple-element.21) | copy-start | bytes 147460
  86.5 24.4 %copy-start.19 = (bf16[128,4,48]{0,2,1:T(8,128)(2,1)S(1)}, bf16[128,4,48]{0,2,1:T(8,128)(2,1)}, u32[]{:S(2)}) copy-start(bf16[128,4,48]{0,2,1:T(8,128)(2,1)} %get-tuple-element.22) | copy-start | bytes 147460
  110.7 3.1 %copy-start.15 = (bf16[1,256,384]{1,2,0:T(8,128)(2,1)}, bf16[1,256,384]{1,2,0:T(8,128)(2,1)S(1)}, u32[]{:S(2)}) copy-start(bf16[1,256,384]{1,2,0:T(8,128)(2,1)S(1)} %copy.27) | copy-start | bytes 589828
  110.9 2.9 %copy-start.13 = (bf16[1,256,384]{1,2,0:T(8,128)(2,1)}, bf16[1,256,384]{1,2,0:T(8,128)(2,1)S(1)}, u32[]{:S(2)}) copy-start(bf16[1,256,384]{1,2,0:T(8,128)(2,1)S(1)} %copy.25) | copy-start | bytes 589828
  110.9 2.9 %copy-start.16 = (bf16[128,384]{0,1:T(8,128)(2,1)S(1)}, bf16[128,384]{0,1:T(8,128)(2,1)}, u32[]{:S(2)}) copy-start(bf16[128,384]{0,1:T(8,128)(2,1)} %copy.26) | copy-start | bytes 294916
  115.5 1.5 copy-start.20
  116.1 0.9 copy-start.4
  116.1 80.8 %copy-start.12 = (bf16[1536,128]{1,0:T(8,128)(2,1)S(1)}, bf16[1536,128]{1,0:T(8,128)(2,1)}, u32[]{:S(2)}) copy-start(bf16[1536,128]{1,0:T(8,128)(2,1)} %param.25) | copy-start | bytes 1179652
  117.9 87.0 %copy-start.21 = (bf16[1536,128]{1,0:T(8,128)(2,1)S(1)}, bf16[1536,128]{1,0:T(8,128)(2,1)}, u32[]{:S(2)}) copy-start(bf16[1536,128]{1,0:T(8,128)(2,1)} %param.26) | copy-start | bytes 1179652
  196.9 8.2 %copy-start.1 = (bf16[4096,1536]{1,0:T(8,128)(2,1)S(1)}, bf16[4096,1536]{1,0:T(8,128)(2,1)}, u32[]{:S(2)}) copy-start(bf16[4096,1536]{1,0:T(8,128)(2,1)} %all-gather.5.cloned.1.call-done) | copy-start | bytes 37748740
  209.6 6.9 %copy-start.22 = (s32[1,128]{1,0:T(1,128)S(1)}, s32[1,128]{1,0:T(1,128)}, u32[]{:S(2)}) copy-start(s32[1,128]{1,0:T(1,128)} %param.18) | copy-start | bytes 1540
  209.6 34.8 %all-to-all-start = ((bf16[32,128,128]{2,1,0:T(8,128)(2,1)}), bf16[32,128,128]{2,1,0:T(8,128)(2,1)}, u32[]{:S(2)}, u32[]{:S(2)}) async-start(bf16[32,128,128]{2,1,0:T(8,128)(2,1)} %bitcast.156), calls=%async_computation | async-start | bytes 2097152 | tf_op jit(solution)/shard_map/all_to_all | solution.py:90
  244.4 8.4 %copy-start.5 = (f32[128,1536]{1,0:T(8,128)S(1)}, f32[128,1536]{1,0:T(8,128)}, u32[]{:S(2)}) copy-start(f32[128,1536]{1,0:T(8,128)} %copy-done.4) | copy-start | bytes 2359300
  252.9 1.7 copy-start.3
  254.5 1.3 copy-start.6
  255.8 1.3 copy-start.9
  255.8 2.3 copy-start.10
  255.8 2.3 copy-start.11
  261.1 2.9 %copy-start.14 = (bf16[1,256,384]{1,2,0:T(8,128)(2,1)S(1)}, bf16[1,256,384]{1,2,0:T(8,128)(2,1)}, u32[]{:S(2)}) copy-start(bf16[1,256,384]{1,2,0:T(8,128)(2,1)} %copy-done.13) | copy-start | bytes 589828
Sparse Core Ops, SparseCore 0:
  9.2 100.2 all-gather.2
  118.0 78.8 all-gather.4

commit v2 on v1

--- a/solution.py
+++ b/solution.py
@@ -102,7 +102,6 @@
 def fetch_slot(cache_kv, holder):
     count = lax.axis_size("req")
     own = cache_kv[0]
-    holders = lax.all_gather(holder, "req", axis=0, tiled=True)
     if count != 8:
         slots = lax.all_gather(own, "req", axis=0, tiled=False)
         return slots[holder[0]]
@@ -114,15 +113,18 @@
     def pick(cond, a, b):
         return jnp.where(cond, a, b)
 
+    near = swap(holder, 1)
+    quad = swap(jnp.concatenate([holder, near]), 2)
+    holders = {0: holder[0], 1: near[0], 2: quad[0], 3: quad[1]}
+
     got1 = swap(own, 4)
-    target = me ^ 2
-    send_a = pick(holders[target] == (me ^ 4), got1, own)
-    send_b = pick(holders[target ^ 1] == (me ^ 4), got1, own)
+    send_a = pick(holders[2] == (me ^ 4), got1, own)
+    send_b = pick(holders[3] == (me ^ 4), got1, own)
     got2 = swap(jnp.stack([send_a, send_b]), 2)
-    want = holders[me ^ 1]
+    want = holders[1]
     send_c = pick(want == me, own, pick(want == (me ^ 4), got1, got2[1]))
     got3 = swap(send_c, 1)
-    need = holders[me]
+    need = holders[0]
     return pick(
         need == me,
         own,
@@ -147,7 +149,8 @@
     w_down,
 ):
     fetched = fetch_slot(cache_kv, holder)
-    down_all = lax.all_gather(w_down, "blk", axis=0, tiled=True)
+    copies = jnp.broadcast_to(w_down[None], (lax.axis_size("blk"),) + w_down.shape)
+    down_all = lax.all_to_all(copies, "blk", 0, 0, tiled=True).reshape(-1, w_down.shape[1])
     fetched, down_all = lax.optimization_barrier((fetched, down_all))
     cache_keys = fetched[0]
     cache_vals = fetched[1]

time: 275 us -> 478 us (1.74)
  waiting for transfers between devices: 153 us -> 355 us
  blocking collectives: 13 us -> 0 us
  starting transfers between devices: 16.5 us -> 28 us
    ppermute x3 -> x5, waiting for transfers between devices: 22 us -> 214 us  [swap(): lax.ppermute(values, 'req', perm=[(i, i ^ mask) for i in range(count)])]
    all_to_all x0 -> x1, waiting for transfers between devices: none -> 34 us  [local(): lax.all_to_all(copies, 'blk', 0, 0, tiled=True).reshape(-1, w_down.shape[1])]
    all_gather x1 -> x0, waiting for transfers between devices: 23 us -> none  [local(): down_all = lax.all_gather(w_down, 'blk', axis=0, tiled=True)]
    unnamed x1 -> x0, blocking collectives: 13 us -> none
    all_to_all x0 -> x1, starting transfers between devices: none -> 10.4 us  [local(): lax.all_to_all(copies, 'blk', 0, 0, tiled=True).reshape(-1, w_down.shape[1])]
    broadcast_in_dim x0 -> x1, local copies, waits for them, and re-layouts: none -> 7.06 us  [local(): jnp.broadcast_to(w_down[None], (lax.axis_size('blk'),) + w_down.shape)]
    unnamed x51 -> x50, local copies, waits for them, and re-layouts: 11.9 us -> 9.99 us
    ppermute x3 -> x5, starting transfers between devices: 9.55 us -> 10.7 us  [swap(): lax.ppermute(values, 'req', perm=[(i, i ^ mask) for i in range(count)])]
  transfers between devices with their start and end apart: 6 -> 8, of which waited for: 5 -> 7; matrix products, arithmetic and copies ran while one was open for 11% -> 6% of each run, Pallas kernels for 0% -> 0%
where the time goes in v2:
time: 478 us; the launch traced here: 477 us
  waiting for transfers between devices  355 us (74%)
  matrix products  40.9 us (9%)
  starting transfers between devices  28 us (6%)
  local copies, waits for them, and re-layouts  20.8 us (4%)
  between operations  17.6 us (4%)
  other arithmetic  14.9 us (3%)
    ppermute x5, waiting for transfers between devices, swap(): lax.ppermute(values, 'req', perm=[(i, i ^ mask) for i in range(count)])  214 us
    all_gather x1, waiting for transfers between devices, run_ffn(): part_rows = lax.all_gather(normed_rows, 'blk', axis=0, tiled=True)  78.8 us
    all_to_all x1, waiting for transfers between devices, local(): lax.all_to_all(copies, 'blk', 0, 0, tiled=True).reshape(-1, w_down.shape[1])  34 us
    all_to_all x1, waiting for transfers between devices, run_ffn(): hidden_own = lax.all_to_all(hidden_all, 'blk', 0, 1, tiled=True)  27.9 us
    ppermute x5, starting transfers between devices, swap(): lax.ppermute(values, 'req', perm=[(i, i ^ mask) for i in range(count)])  10.7 us
    all_to_all x1, starting transfers between devices, local(): lax.all_to_all(copies, 'blk', 0, 0, tiled=True).reshape(-1, w_down.shape[1])  10.4 us
    unnamed x50, local copies, waits for them, and re-layouts  9.99 us
  transfers between devices with their start and end apart: 8, of which 7 were waited for; matrix products, arithmetic and copies ran while one was open for 6% of the time, Pallas kernels for 0%

profile of v2, /device:TPU:1, one launch (start us, length us, event | category | flops | bytes accessed | tf_op | source)
XLA Modules:
  0.0 477.4 jit_solution(10398602093591844268)
XLA Ops:
  6.5 7.1 %broadcast_in_dim.20 = bf16[32,128,1536]{2,1,0:T(8,128)(2,1)} broadcast(bf16[128,1536]{1,0:T(8,128)(2,1)} %param.27), dimensions={1,2} | broadcast | bytes 12976128 | tf_op jit(solution)/shard_map/broadcast_in_dim | solution.py:152
  13.6 10.4 %all-to-all-start = ((bf16[32,128,1536]{2,1,0:T(8,128)(2,1)}), bf16[32,128,1536]{2,1,0:T(8,128)(2,1)}, u32[]{:S(2)}, u32[]{:S(2)}) async-start(bf16[32,128,1536]{2,1,0:T(8,128)(2,1)} %broadcast_in_dim.20), calls=%async_computation | async-start | bytes 25165824 | tf_op jit(solution)/shard_map/all_to_all | solution.py:153
  24.0 2.8 collective-permute-start
  26.9 4.2 collective-permute-start.1
  31.8 4.4 copy.29
  37.0 3.3 fusion.55
  40.8 200.4 %collective-permute-done.1 = s32[1]{0:T(128)} collective-permute-done((s32[1]{0:T(128)}, s32[1]{0:T(128)}, u32[]{:S(2)}, u32[]{:S(2)}) %collective-permute-start.1) | collective-permute-done | bytes 36 | tf_op jit(solution)/shard_map/ppermute | solution.py:111
  241.3 0.7 pad_add_fusion
  242.0 1.2 collective-permute-start.2
  243.2 1.6 collective-permute-done.2
  244.8 0.6 fusion.77
  246.8 1.0 pad_maximum_fusion
  247.8 1.2 collective-permute-start.3
  249.0 0.8 multiply_cosine_fusion
  249.8 2.5 copy.28
  252.3 1.9 subtract_convert_fusion.1
  254.1 2.3 convolution_convert_fusion.4
  256.5 1.2 fusion.57
  259.0 6.3 %collective-permute-done.3 = bf16[2,2,256,384]{3,2,1,0:T(8,128)(2,1)} collective-permute-done((bf16[2,2,256,384]{3,2,1,0:T(8,128)(2,1)}, bf16[2,2,256,384]{3,2,1,0:T(8,128)(2,1)}, u32[]{:S(2)}, u32[]{:S(2)}) %collective-permute-start.3) | collective-permute-done | bytes 786464 | tf_op jit(solution)/shard_map/ppermute | solution.py:111
  265.3 1.8 fusion.28
  267.1 1.2 collective-permute-start.4
  268.3 1.6 copy.26
  269.9 1.6 pad_maximum_fusion.5
  271.5 1.6 subtract_convert_fusion.3
  273.1 6.1 %collective-permute-done.4 = bf16[2,256,384]{2,1,0:T(8,128)(2,1)} collective-permute-done((bf16[2,256,384]{2,1,0:T(8,128)(2,1)}, bf16[2,256,384]{2,1,0:T(8,128)(2,1)}, u32[]{:S(2)}, u32[]{:S(2)}) %collective-permute-start.4) | collective-permute-done | bytes 393248 | tf_op jit(solution)/shard_map/ppermute | solution.py:111
  279.2 1.9 fusion.24
  281.1 34.0 %all-to-all-done = bf16[32,128,1536]{2,1,0:T(8,128)(2,1)} async-done(((bf16[32,128,1536]{2,1,0:T(8,128)(2,1)}), bf16[32,128,1536]{2,1,0:T(8,128)(2,1)}, u32[]{:S(2)}, u32[]{:S(2)}) %all-to-all-start) | async-done | bytes 12582944 | tf_op jit(solution)/shard_map/all_to_all | solution.py:153
  315.1 1.1 fusion.76
  316.6 2.8 fusion.78
  319.4 1.7 convolution_convert_fusion.2
  321.1 0.6 multiply_reduce_fusion.1
  321.7 0.9 copy-done.4
  322.6 0.9 multiply_convert_fusion.1
  323.6 78.8 %all-gather.2.cloned.1.call-done = bf16[4096,1536]{1,0:T(8,128)(2,1)} async-done(((bf16[128,1536]{1,0:T(8,128)(2,1)}), bf16[4096,1536]{1,0:T(8,128)(2,1)}) %all-gather.2.cloned.1.call-update) | async-done | bytes 12582928 | tf_op jit(solution)/shard_map/all_gather | solution.py:86
  402.4 8.0 %fusion.84 = f32[4096,128]{1,0:T(8,128)S(1)} fusion(bf16[4096,1536]{1,0:T(8,128)(2,1)} %all-gather.2.cloned.1.call-done, bf16[1536,128]{1,0:T(8,128)(2,1)S(1)} %copy-done.12), kind=kOutput, calls=%fused_computation.105 | convolution fusion | flops 1610612736 | bytes 15073280 | tf_op jit(solution)/shard_map/dot_general | solution.py:87
  410.6 4.6 fusion.2
  415.2 6.9 %all-to-all-start.1 = ((bf16[32,128,128]{2,1,0:T(8,128)(2,1)}), bf16[32,128,128]{2,1,0:T(8,128)(2,1)}, u32[]{:S(2)}, u32[]{:S(2)}) async-start(bf16[32,128,128]{2,1,0:T(8,128)(2,1)} %bitcast.158), calls=%async_computation.1 | async-start | bytes 2097152 | tf_op jit(solution)/shard_map/all_to_all | solution.py:90
  422.1 27.9 %all-to-all-done.1 = bf16[32,128,128]{2,1,0:T(8,128)(2,1)} async-done(((bf16[32,128,128]{2,1,0:T(8,128)(2,1)}), bf16[32,128,128]{2,1,0:T(8,128)(2,1)}, u32[]{:S(2)}, u32[]{:S(2)}) %all-to-all-start.1) | async-done | bytes 1048608 | tf_op jit(solution)/shard_map/all_to_all | solution.py:90
  450.0 8.4 %convert_reduce_fusion = f32[128,1536]{1,0:T(8,128)S(1)} fusion(bf16[32,128,1536]{2,1,0:T(8,128)(2,1)} %bitcast.32, bf16[32,128,128]{2,1,0:T(8,128)(2,1)} %all-to-all-done.1), kind=kOutput, calls=%fused_computation.2 | convolution fusion | flops 1629290496 | bytes 14417920 | tf_op jit(solution)/shard_map/rgk,gkd->grd/dot_general | solution.py:93
  458.9 1.2 copy-done.3
  460.0 1.1 fusion.86
  461.3 0.6 fusion.85
  461.9 0.7 copy-done.9
  463.0 0.7 subtract_convert_fusion.2
  463.9 0.7 pad_maximum_fusion.6
  464.6 2.9 fusion.81
  467.5 1.7 convolution_convert_fusion.1
  469.2 1.4 fusion.3
  (65 shorter events, 2.7 us)
Async XLA Ops:
  6.5 314.6 %copy-start = (bf16[768,1536]{1,0:T(8,128)(2,1)S(1)}, bf16[768,1536]{1,0:T(8,128)(2,1)}, u32[]{:S(2)}) copy-start(bf16[768,1536]{1,0:T(8,128)(2,1)} %param.23) | copy-start | bytes 7077892
  13.6 10.4 %copy-start.8 = (bf16[1,2,256,384]{3,2,1,0:T(8,128)(2,1)S(1)}, bf16[1,2,256,384]{3,2,1,0:T(8,128)(2,1)}, u32[]{:S(2)}) copy-start(bf16[1,2,256,384]{3,2,1,0:T(8,128)(2,1)} %param.15) | copy-start | bytes 1179652
  13.6 301.5 %all-to-all-start = ((bf16[32,128,1536]{2,1,0:T(8,128)(2,1)}), bf16[32,128,1536]{2,1,0:T(8,128)(2,1)}, u32[]{:S(2)}, u32[]{:S(2)}) async-start(bf16[32,128,1536]{2,1,0:T(8,128)(2,1)} %broadcast_in_dim.20), calls=%async_computation | async-start | bytes 25165824 | tf_op jit(solution)/shard_map/all_to_all | solution.py:153
  24.0 378.4 %all-gather.2.cloned.1.call-start = ((), (), s32[]{:S(2)}) async-start(), calls=%async_computation.2 | async-start | bytes 12976128 | tf_op jit(solution)/shard_map/all_gather | solution.py:86
  24.0 222.7 %collective-permute-start = (bf16[2,256,384]{2,1,0:T(8,128)(2,1)S(1)}, bf16[2,256,384]{2,1,0:T(8,128)(2,1)S(1)}, u32[]{:S(2)}, u32[]{:S(2)}) collective-permute-start(bf16[2,256,384]{2,1,0:T(8,128)(2,1)S(1)} %bitcast.156), channel_id=1, source_target_pairs={{0,128},{32,160},{64,192},{96,224},{128,0},{160,32},{192,64},{224,... | collective-permute-start | bytes 1179656 | tf_op jit(solution)/shard_map/ppermute | solution.py:111
  26.9 214.4 %collective-permute-start.1 = (s32[1]{0:T(128)}, s32[1]{0:T(128)}, u32[]{:S(2)}, u32[]{:S(2)}) collective-permute-start(s32[1]{0:T(128)} %param.17), channel_id=1, source_target_pairs={{0,32},{32,0},{64,96},{96,64},{128,160},{160,128},{192,224},{224,1... | collective-permute-start | bytes 20 | tf_op jit(solution)/shard_map/ppermute | solution.py:111
  31.8 5.0 %copy-start.2 = (bf16[1,128,1536]{2,1,0:T(8,128)(2,1)S(1)}, bf16[1,128,1536]{2,1,0:T(8,128)(2,1)}, u32[]{:S(2)}) copy-start(bf16[1,128,1536]{2,1,0:T(8,128)(2,1)} %param.14) | copy-start | bytes 1179652
  31.8 5.2 %copy-start.17 = (f32[1536]{0:T(1024)S(1)}, f32[1536]{0:T(1024)}, u32[]{:S(2)}) copy-start(f32[1536]{0:T(1024)} %param.19) | copy-start | bytes 18436
  242.0 2.8 collective-permute-start.2
  246.7 2.3 copy-start.21
  247.8 17.5 %collective-permute-start.3 = (bf16[2,2,256,384]{3,2,1,0:T(8,128)(2,1)}, bf16[2,2,256,384]{3,2,1,0:T(8,128)(2,1)}, u32[]{:S(2)}, u32[]{:S(2)}) collective-permute-start(bf16[2,2,256,384]{3,2,1,0:T(8,128)(2,1)} %pad_maximum_fusion), channel_id=1, source_target_pairs={{0,64},{32,96},{64,0},{96,32},{128,192},{160,224},{192,128},{224,1... | collective-permute-start | bytes 2359304 | tf_op jit(solution)/shard_map/ppermute | solution.py:111
  252.3 4.2 copy-start.7
  267.1 12.1 %collective-permute-start.4 = (bf16[2,256,384]{2,1,0:T(8,128)(2,1)}, bf16[2,256,384]{2,1,0:T(8,128)(2,1)}, u32[]{:S(2)}, u32[]{:S(2)}) collective-permute-start(bf16[2,256,384]{2,1,0:T(8,128)(2,1)} %fusion.28), channel_id=1, source_target_pairs={{0,32},{32,0},{64,96},{96,64},{128,160},{160,128},{192,224},{224,1... | collective-permute-start | bytes 1179656 | tf_op jit(solution)/shard_map/ppermute | solution.py:111
  281.1 35.4 %copy-start.18 = (bf16[128,4,48]{0,2,1:T(8,128)(2,1)S(1)}, bf16[128,4,48]{0,2,1:T(8,128)(2,1)}, u32[]{:S(2)}) copy-start(bf16[128,4,48]{0,2,1:T(8,128)(2,1)} %get-tuple-element.21) | copy-start | bytes 147460
  281.1 35.4 %copy-start.19 = (bf16[128,4,48]{0,2,1:T(8,128)(2,1)S(1)}, bf16[128,4,48]{0,2,1:T(8,128)(2,1)}, u32[]{:S(2)}) copy-start(bf16[128,4,48]{0,2,1:T(8,128)(2,1)} %get-tuple-element.22) | copy-start | bytes 147460
  316.4 3.0 copy-start.15
  316.5 2.9 copy-start.13
  316.5 2.9 copy-start.16
  321.1 1.5 copy-start.20
  321.7 0.9 copy-start.4
  321.7 80.7 %copy-start.12 = (bf16[1536,128]{1,0:T(8,128)(2,1)S(1)}, bf16[1536,128]{1,0:T(8,128)(2,1)}, u32[]{:S(2)}) copy-start(bf16[1536,128]{1,0:T(8,128)(2,1)} %param.25) | copy-start | bytes 1179652
  323.5 86.8 %copy-start.22 = (bf16[1536,128]{1,0:T(8,128)(2,1)S(1)}, bf16[1536,128]{1,0:T(8,128)(2,1)}, u32[]{:S(2)}) copy-start(bf16[1536,128]{1,0:T(8,128)(2,1)} %param.26) | copy-start | bytes 1179652
  402.4 8.2 %copy-start.1 = (bf16[4096,1536]{1,0:T(8,128)(2,1)S(1)}, bf16[4096,1536]{1,0:T(8,128)(2,1)}, u32[]{:S(2)}) copy-start(bf16[4096,1536]{1,0:T(8,128)(2,1)} %all-gather.2.cloned.1.call-done) | copy-start | bytes 37748740
  415.2 6.9 %copy-start.23 = (s32[1,128]{1,0:T(1,128)S(1)}, s32[1,128]{1,0:T(1,128)}, u32[]{:S(2)}) copy-start(s32[1,128]{1,0:T(1,128)} %param.18) | copy-start | bytes 1540
  415.2 34.8 %all-to-all-start.1 = ((bf16[32,128,128]{2,1,0:T(8,128)(2,1)}), bf16[32,128,128]{2,1,0:T(8,128)(2,1)}, u32[]{:S(2)}, u32[]{:S(2)}) async-start(bf16[32,128,128]{2,1,0:T(8,128)(2,1)} %bitcast.158), calls=%async_computation.1 | async-start | bytes 2097152 | tf_op jit(solution)/shard_map/all_to_all | solution.py:90
  449.9 8.4 %copy-start.5 = (f32[128,1536]{1,0:T(8,128)S(1)}, f32[128,1536]{1,0:T(8,128)}, u32[]{:S(2)}) copy-start(f32[128,1536]{1,0:T(8,128)} %copy-done.4) | copy-start | bytes 2359300
  458.4 1.7 copy-start.3
  460.0 1.3 copy-start.6
  461.3 1.3 copy-start.9
  461.3 1.7 copy-start.10
  461.3 1.7 copy-start.11
  464.5 2.9 copy-start.14
Sparse Core Ops, SparseCore 0:
  323.7 78.6 all-gather.1

commit v3 on v2

--- a/solution.py
+++ b/solution.py
@@ -82,21 +82,29 @@
     return widened + jnp.dot(context, o_weight, preferred_element_type=jnp.float32)
 
 
-def run_ffn(normed_rows, w_gate, w_up, w_down, down_all):
+def run_ffn(normed_rows, w_gate, w_up, w_down, down_head):
     part_rows = lax.all_gather(normed_rows, "blk", axis=0, tiled=True)
+    split = down_head.shape[1]
+    tail_cols, part_rows = lax.optimization_barrier((w_down[:, split:], part_rows))
+    down_tail = lax.all_gather(tail_cols, "blk", axis=0, tiled=True)
     gate_vals = jnp.dot(part_rows, w_gate, preferred_element_type=jnp.float32)
     up_vals = jnp.dot(part_rows, w_up, preferred_element_type=jnp.float32)
     hidden_all = (jax.nn.silu(gate_vals) * up_vals).astype(jnp.bfloat16)
     hidden_own = lax.all_to_all(hidden_all, "blk", 0, 1, tiled=True)
     groups = w_down.shape[0]
-    group_count = down_all.shape[0] // groups
-    terms = jnp.einsum(
-        "rgk,gkd->grd",
-        hidden_own.reshape(hidden_own.shape[0], group_count, groups),
-        down_all.reshape(group_count, groups, down_all.shape[1]),
-        preferred_element_type=jnp.float32,
-    ).astype(jnp.bfloat16)
-    return jnp.sum(terms.astype(jnp.float32), axis=0)
+    group_count = down_head.shape[0] // groups
+    shaped = hidden_own.reshape(hidden_own.shape[0], group_count, groups)
+
+    def down(cols):
+        terms = jnp.einsum(
+            "rgk,gkd->grd",
+            shaped,
+            cols.reshape(group_count, groups, cols.shape[1]),
+            preferred_element_type=jnp.float32,
+        ).astype(jnp.bfloat16)
+        return jnp.sum(terms.astype(jnp.float32), axis=0)
+
+    return jnp.concatenate([down(down_head), down(down_tail)], axis=1)
 
 
 def fetch_slot(cache_kv, holder):
@@ -149,9 +157,9 @@
     w_down,
 ):
     fetched = fetch_slot(cache_kv, holder)
-    copies = jnp.broadcast_to(w_down[None], (lax.axis_size("blk"),) + w_down.shape)
-    down_all = lax.all_to_all(copies, "blk", 0, 0, tiled=True).reshape(-1, w_down.shape[1])
-    fetched, down_all = lax.optimization_barrier((fetched, down_all))
+    split = min(w_down.shape[1], 128 * ((w_down.shape[1] * 7 // 12 + 127) // 128))
+    down_head = lax.all_gather(w_down[:, :split], "blk", axis=0, tiled=True)
+    fetched, down_head = lax.optimization_barrier((fetched, down_head))
     cache_keys = fetched[0]
     cache_vals = fetched[1]
     cache_length = cache_len[0]
@@ -168,7 +176,7 @@
         o_weight,
     )
     chosen_mask = accept[0] == 1
-    ffn_sum = run_ffn(rms_scale(first_pass, ffn_gain).astype(jnp.bfloat16), w_gate, w_up, w_down, down_all)
+    ffn_sum = run_ffn(rms_scale(first_pass, ffn_gain).astype(jnp.bfloat16), w_gate, w_up, w_down, down_head)
     placed = first_pass + ffn_sum
     second_in = jnp.where(chosen_mask[:, None], placed, block_rows.astype(jnp.float32))
     refined = attend_block(

time: 478 us -> 286 us (0.60)
  waiting for transfers between devices: 355 us -> 175 us
  starting transfers between devices: 28 us -> 18.9 us
    ppermute x5, waiting for transfers between devices: 214 us -> 34.1 us  [swap(): lax.ppermute(values, 'req', perm=[(i, i ^ mask) for i in range(count)])]
    all_to_all x1 -> x0, waiting for transfers between devices: 34 us -> none  [local(): lax.all_to_all(copies, 'blk', 0, 0, tiled=True).reshape(-1, w_down.shape[1])]
    all_gather x0 -> x2, waiting for transfers between devices: none -> 23.9 us  [the longest x1 15.8 us: run_ffn(): down_tail = lax.all_gather(tail_cols, 'blk', axis=0, tiled=True)]
    all_to_all x1 -> x0, starting transfers between devices: 10.4 us -> none  [local(): lax.all_to_all(copies, 'blk', 0, 0, tiled=True).reshape(-1, w_down.shape[1])]
    all_to_all x1, waiting for transfers between devices: 27.9 us -> 37.9 us  [run_ffn(): hidden_own = lax.all_to_all(hidden_all, 'blk', 0, 1, tiled=True)]
    broadcast_in_dim x1 -> x0, local copies, waits for them, and re-layouts: 7.06 us -> none  [local(): jnp.broadcast_to(w_down[None], (lax.axis_size('blk'),) + w_down.shape)]
    dot_general x1 -> x2, matrix products: 8.39 us -> 10.1 us  [down(): jnp.einsum('rgk,gkd->grd', shaped, cols.reshape(group_count, groups, cols...]
  transfers between devices with their start and end apart: 8 -> 9, of which waited for: 7 -> 7; matrix products, arithmetic and copies ran while one was open for 6% -> 17% of each run, Pallas kernels for 0% -> 0%
where the time goes in v3:
time: 286 us; the launch traced here: 285 us
  waiting for transfers between devices  175 us (61%)
  matrix products  42.5 us (15%)
  starting transfers between devices  18.9 us (7%)
  between operations  17.2 us (6%)
  local copies, waits for them, and re-layouts  16.4 us (6%)
  other arithmetic  14.9 us (5%)
    all_gather x1, waiting for transfers between devices, run_ffn(): part_rows = lax.all_gather(normed_rows, 'blk', axis=0, tiled=True)  78.9 us
    all_to_all x1, waiting for transfers between devices, run_ffn(): hidden_own = lax.all_to_all(hidden_all, 'blk', 0, 1, tiled=True)  37.9 us
    ppermute x5, waiting for transfers between devices, swap(): lax.ppermute(values, 'req', perm=[(i, i ^ mask) for i in range(count)])  34.1 us
    all_gather x1, waiting for transfers between devices, run_ffn(): down_tail = lax.all_gather(tail_cols, 'blk', axis=0, tiled=True)  15.8 us
    ppermute x5, starting transfers between devices, swap(): lax.ppermute(values, 'req', perm=[(i, i ^ mask) for i in range(count)])  11.9 us
    dot_general x2, matrix products, down(): jnp.einsum('rgk,gkd->grd', shaped, cols.reshape(group_count, groups, cols...  10.1 us
    unnamed x50, local copies, waits for them, and re-layouts  9.26 us
    all_gather x1, waiting for transfers between devices, local(): down_head = lax.all_gather(w_down[:, :split], 'blk', axis=0, tiled=True)  8.15 us
  transfers between devices with their start and end apart: 9, of which 7 were waited for; matrix products, arithmetic and copies ran while one was open for 17% of the time, Pallas kernels for 0%

profile of v3, /device:TPU:1, one launch (start us, length us, event | category | flops | bytes accessed | tf_op | source)
XLA Modules:
  0.0 284.9 jit_solution(10005721595860434899)
XLA Ops:
  6.5 1.8 slice.53
  8.4 7.8 %collective-permute-start.1 = (s32[1]{0:T(128)}, s32[1]{0:T(128)}, u32[]{:S(2)}, u32[]{:S(2)}) collective-permute-start(s32[1]{0:T(128)} %param.17), channel_id=1, source_target_pairs={{0,32},{32,0},{64,96},{96,64},{128,160},{160,128},{192,224},{224,1... | collective-permute-start | bytes 20 | tf_op jit(solution)/shard_map/ppermute | solution.py:119
  16.2 2.7 collective-permute-start
  20.3 4.3 %copy.29 = bf16[1536,768]{0,1:T(8,128)(2,1)} copy(bf16[1536,768]{1,0:T(8,128)(2,1)} %param.20) | data formatting | bytes 4718592 | tf_op args[6]
  24.8 3.3 %fusion.56 = f32[128,8,96]{0,2,1:T(8,128)} fusion(bf16[8,96,1536]{2,1,0:T(8,128)(2,1)} %bitcast.159, bf16[1,128,1536]{2,1,0:T(8,128)(2,1)S(1)} %copy-done.2, f32[1536]{0:T(1024)S(1)} %copy-done.19, f32[128]{0:T(128)S(1)} %add_rsqrt_fusion.2), kind=kOutput, calls=%fused_computation.77 | convolution fusion | flops 302776320 | bytes 3152384 | tf_op jit(solution)/shard_map/dot_general | solution.py:54
  28.1 0.6 add_convert_fusion.4
  28.7 0.7 pad_add_fusion
  29.4 0.5 collective-permute-start.2
  29.9 2.4 collective-permute-done.2
  32.2 0.6 fusion.78
  34.1 1.0 pad_maximum_fusion
  35.1 0.4 collective-permute-start.3
  35.5 0.8 multiply_cosine_fusion
  36.3 2.4 copy.28
  38.7 1.9 subtract_convert_fusion.1
  40.6 2.3 convolution_convert_fusion.3
  42.9 1.2 fusion.58
  45.4 7.1 %collective-permute-done.3 = bf16[2,2,256,384]{3,2,1,0:T(8,128)(2,1)} collective-permute-done((bf16[2,2,256,384]{3,2,1,0:T(8,128)(2,1)}, bf16[2,2,256,384]{3,2,1,0:T(8,128)(2,1)}, u32[]{:S(2)}, u32[]{:S(2)}) %collective-permute-start.3) | collective-permute-done | bytes 786464 | tf_op jit(solution)/shard_map/ppermute | solution.py:119
  52.5 1.8 fusion.29
  54.7 1.6 copy.26
  56.3 1.6 pad_maximum_fusion.5
  57.9 1.6 subtract_convert_fusion.3
  59.6 24.7 %collective-permute-done.4 = bf16[2,256,384]{2,1,0:T(8,128)(2,1)} collective-permute-done((bf16[2,256,384]{2,1,0:T(8,128)(2,1)}, bf16[2,256,384]{2,1,0:T(8,128)(2,1)}, u32[]{:S(2)}, u32[]{:S(2)}) %collective-permute-start.4) | collective-permute-done | bytes 393248 | tf_op jit(solution)/shard_map/ppermute | solution.py:119
  84.3 1.9 fusion.25
  86.2 8.2 %all-gather.4.cloned.1.call-done = bf16[4096,896]{1,0:T(8,128)(2,1)} async-done(((bf16[128,896]{1,0:T(8,128)(2,1)}), bf16[4096,896]{1,0:T(8,128)(2,1)}) %all-gather.4.cloned.1.call-update) | async-done | bytes 7340048 | tf_op jit(solution)/shard_map/all_gather | solution.py:161
  94.4 1.1 fusion.77
  95.8 2.9 %fusion.79 = (f32[4,2,128]{2,1,0:T(2,128)S(1)}, f32[4,2,128,384]{2,3,1,0:T(8,128)}) fusion(bf16[128,4,2,96]{0,3,2,1:T(8,128)(2,1)} %bitcast.171, bf16[256,4,96]{0,2,1:T(8,128)(2,1)S(1)} %bitcast.169, bf16[128,4,48]{0,2,1:T(8,128)(2,1)} %get-tuple-element.26, bf16[128,4,48]{0,2,1:T(8,128)(2,1)} %get-tuple-element.25, pred[384]{0:T(512)(128)(4,1)S(1)} %concatenate.54), kind=kOutput, calls=%fused_computation.105 | convolution fusion | flops 77955456 | bytes 2068864 | tf_op jit(solution)/shard_map/sub | solution.py:78
  98.6 1.7 convolution_convert_fusion.1
  100.4 0.6 multiply_reduce_fusion.1
  101.0 0.9 copy-done.5
  101.9 0.9 multiply_convert_fusion.1
  103.0 1.6 slice.60
  104.6 78.9 %all-gather.6.cloned.1.call-done = bf16[4096,1536]{1,0:T(8,128)(2,1)} async-done(((bf16[128,1536]{1,0:T(8,128)(2,1)}), bf16[4096,1536]{1,0:T(8,128)(2,1)}) %all-gather.6.cloned.1.call-update) | async-done | bytes 12582928 | tf_op jit(solution)/shard_map/all_gather | solution.py:86
  183.6 7.8 %fusion.85 = f32[4096,128]{1,0:T(8,128)S(1)} fusion(bf16[4096,1536]{1,0:T(8,128)(2,1)} %all-gather.6.cloned.1.call-done, bf16[1536,128]{1,0:T(8,128)(2,1)S(1)} %copy-done.14), kind=kOutput, calls=%fused_computation.107 | convolution fusion | flops 1610612736 | bytes 15073280 | tf_op jit(solution)/shard_map/dot_general | solution.py:90
  191.7 4.6 %fusion.2 = bf16[4096,128]{1,0:T(8,128)(2,1)} fusion(bf16[4096,1536]{1,0:T(8,128)(2,1)S(1)} %copy-done.1, bf16[1536,128]{1,0:T(8,128)(2,1)S(1)} %copy-done.22, f32[4096,128]{1,0:T(8,128)S(1)} %fusion.85), kind=kOutput, calls=%fused_computation.5 | convolution fusion | flops 1613758464 | bytes 16121856 | tf_op jit(solution)/shard_map/dot_general | solution.py:91
  196.3 6.8 %all-to-all-start = ((bf16[32,128,128]{2,1,0:T(8,128)(2,1)}), bf16[32,128,128]{2,1,0:T(8,128)(2,1)S(1)}, u32[]{:S(2)}, u32[]{:S(2)}) async-start(bf16[32,128,128]{2,1,0:T(8,128)(2,1)} %bitcast.163), calls=%async_computation | async-start | bytes 2097152 | tf_op jit(solution)/shard_map/all_to_all | solution.py:93
  203.2 37.9 %all-to-all-done = bf16[32,128,128]{2,1,0:T(8,128)(2,1)S(1)} async-done(((bf16[32,128,128]{2,1,0:T(8,128)(2,1)}), bf16[32,128,128]{2,1,0:T(8,128)(2,1)S(1)}, u32[]{:S(2)}, u32[]{:S(2)}) %all-to-all-start) | async-done | bytes 1048608 | tf_op jit(solution)/shard_map/all_to_all | solution.py:93
  241.1 6.0 %convert_reduce_fusion = f32[128,896]{1,0:T(8,128)} fusion(bf16[32,128,896]{2,1,0:T(8,128)(2,1)} %bitcast.157, bf16[32,128,128]{2,1,0:T(8,128)(2,1)S(1)} %all-to-all-done), kind=kOutput, calls=%fused_computation.2 | convolution fusion | flops 950419456 | bytes 8847360 | tf_op jit(solution)/shard_map/rgk,gkd->grd/dot_general | solution.py:99
  247.1 15.8 %all-gather.8.cloned.1.call-done = bf16[4096,640]{1,0:T(8,128)(2,1)} async-done(((bf16[128,640]{1,0:T(8,128)(2,1)}), bf16[4096,640]{1,0:T(8,128)(2,1)}) %all-gather.8.cloned.1.call-update) | async-done | bytes 5242896 | tf_op jit(solution)/shard_map/all_gather | solution.py:89
  262.9 4.1 %convert_reduce_fusion.1 = f32[128,640]{1,0:T(8,128)S(1)} fusion(bf16[32,128,640]{2,1,0:T(8,128)(2,1)} %bitcast.158, bf16[32,128,128]{2,1,0:T(8,128)(2,1)S(1)} %all-to-all-done), kind=kOutput, calls=%fused_computation.3 | convolution fusion | flops 678871040 | bytes 6619136 | tf_op jit(solution)/shard_map/rgk,gkd->grd/dot_general | solution.py:99
  267.5 1.2 copy-done.4
  268.7 1.0 fusion.87
  269.8 0.6 fusion.86
  270.9 0.7 subtract_convert_fusion.2
  271.7 0.7 pad_maximum_fusion.6
  272.4 2.9 %fusion.82 = (f32[4,2,128]{2,1,0:T(2,128)S(1)}, f32[4,2,128,384]{2,3,1,0:T(8,128)}) fusion(bf16[128,4,2,96]{0,3,2,1:T(8,128)(2,1)} %bitcast.172, bf16[256,4,96]{0,2,1:T(8,128)(2,1)} %bitcast.170, bf16[128,4,48]{0,2,1:T(8,128)(2,1)} %get-tuple-element.24, bf16[128,4,48]{0,2,1:T(8,128)(2,1)} %get-tuple-element.23, pred[384]{0:T(512)(128)(4,1)S(1)} %concatenate.54), kind=kOutput, calls=%fused_computation.106 | convolution fusion | flops 77955456 | bytes 2068864 | tf_op jit(solution)/shard_map/sub | solution.py:78
  275.3 1.7 convolution_convert_fusion
  277.0 1.4 fusion.3
  (71 shorter events, 2.7 us)
Async XLA Ops:
  6.5 93.8 %copy-start = (bf16[768,1536]{1,0:T(8,128)(2,1)S(1)}, bf16[768,1536]{1,0:T(8,128)(2,1)}, u32[]{:S(2)}) copy-start(bf16[768,1536]{1,0:T(8,128)(2,1)} %param.23) | copy-start | bytes 7077892
  6.5 87.8 %all-gather.4.cloned.1.call-start = ((), (), s32[]{:S(2)}) async-start(), calls=%async_computation.1 | async-start | bytes 7569408 | tf_op jit(solution)/shard_map/all_gather | solution.py:161
  8.4 175.1 %all-gather.6.cloned.1.call-start = ((), (), s32[]{:S(2)}) async-start(), calls=%async_computation.2 | async-start | bytes 12976128 | tf_op jit(solution)/shard_map/all_gather | solution.py:86
  8.4 20.3 %collective-permute-start.1 = (s32[1]{0:T(128)}, s32[1]{0:T(128)}, u32[]{:S(2)}, u32[]{:S(2)}) collective-permute-start(s32[1]{0:T(128)} %param.17), channel_id=1, source_target_pairs={{0,32},{32,0},{64,96},{96,64},{128,160},{160,128},{192,224},{224,1... | collective-permute-start | bytes 20 | tf_op jit(solution)/shard_map/ppermute | solution.py:119
  16.2 17.8 %collective-permute-start = (bf16[2,256,384]{2,1,0:T(8,128)(2,1)}, bf16[2,256,384]{2,1,0:T(8,128)(2,1)S(1)}, u32[]{:S(2)}, u32[]{:S(2)}) collective-permute-start(bf16[2,256,384]{2,1,0:T(8,128)(2,1)} %bitcast.161), channel_id=1, source_target_pairs={{0,128},{32,160},{64,192},{96,224},{128,0},{160,32},{192,64},{224,... | collective-permute-start | bytes 1179656 | tf_op jit(solution)/shard_map/ppermute | solution.py:119
  20.3 4.4 %copy-start.2 = (bf16[1,128,1536]{2,1,0:T(8,128)(2,1)S(1)}, bf16[1,128,1536]{2,1,0:T(8,128)(2,1)}, u32[]{:S(2)}) copy-start(bf16[1,128,1536]{2,1,0:T(8,128)(2,1)} %param.14) | copy-start | bytes 1179652
  20.3 4.5 %copy-start.19 = (f32[1536]{0:T(1024)S(1)}, f32[1536]{0:T(1024)}, u32[]{:S(2)}) copy-start(f32[1536]{0:T(1024)} %param.19) | copy-start | bytes 18436
  24.6 9.4 %copy-start.9 = (bf16[1,2,256,384]{3,2,1,0:T(8,128)(2,1)S(1)}, bf16[1,2,256,384]{3,2,1,0:T(8,128)(2,1)}, u32[]{:S(2)}) copy-start(bf16[1,2,256,384]{3,2,1,0:T(8,128)(2,1)} %param.15) | copy-start | bytes 1179652
  29.4 2.8 collective-permute-start.2
  34.0 1.5 copy-start.21
  35.1 17.4 %collective-permute-start.3 = (bf16[2,2,256,384]{3,2,1,0:T(8,128)(2,1)}, bf16[2,2,256,384]{3,2,1,0:T(8,128)(2,1)}, u32[]{:S(2)}, u32[]{:S(2)}) collective-permute-start(bf16[2,2,256,384]{3,2,1,0:T(8,128)(2,1)} %pad_maximum_fusion), channel_id=1, source_target_pairs={{0,64},{32,96},{64,0},{96,32},{128,192},{160,224},{192,128},{224,1... | collective-permute-start | bytes 2359304 | tf_op jit(solution)/shard_map/ppermute | solution.py:119
  38.7 4.2 %copy-start.8 = (bf16[1536,384]{0,1:T(8,128)(2,1)S(1)}, bf16[1536,384]{0,1:T(8,128)(2,1)}, u32[]{:S(2)}) copy-start(bf16[1536,384]{0,1:T(8,128)(2,1)} %copy.28) | copy-start | bytes 3538948
  54.3 30.0 %collective-permute-start.4 = (bf16[2,256,384]{2,1,0:T(8,128)(2,1)}, bf16[2,256,384]{2,1,0:T(8,128)(2,1)}, u32[]{:S(2)}, u32[]{:S(2)}) collective-permute-start(bf16[2,256,384]{2,1,0:T(8,128)(2,1)} %fusion.29), channel_id=1, source_target_pairs={{0,32},{32,0},{64,96},{96,64},{128,160},{160,128},{192,224},{224,1... | collective-permute-start | bytes 1179656 | tf_op jit(solution)/shard_map/ppermute | solution.py:119
  95.4 3.2 %copy-start.18 = (bf16[128,384]{0,1:T(8,128)(2,1)S(1)}, bf16[128,384]{0,1:T(8,128)(2,1)}, u32[]{:S(2)}) copy-start(bf16[128,384]{0,1:T(8,128)(2,1)} %copy.26) | copy-start | bytes 294916
  95.6 4.7 %copy-start.17 = (bf16[1,256,384]{1,2,0:T(8,128)(2,1)}, bf16[1,256,384]{1,2,0:T(8,128)(2,1)S(1)}, u32[]{:S(2)}) copy-start(bf16[1,256,384]{1,2,0:T(8,128)(2,1)S(1)} %copy.27) | copy-start | bytes 589828
  95.8 4.6 %copy-start.15 = (bf16[1,256,384]{1,2,0:T(8,128)(2,1)}, bf16[1,256,384]{1,2,0:T(8,128)(2,1)S(1)}, u32[]{:S(2)}) copy-start(bf16[1,256,384]{1,2,0:T(8,128)(2,1)S(1)} %copy.25) | copy-start | bytes 589828
  100.4 1.5 copy-start.20
  100.4 83.2 %copy-start.14 = (bf16[1536,128]{1,0:T(8,128)(2,1)S(1)}, bf16[1536,128]{1,0:T(8,128)(2,1)}, u32[]{:S(2)}) copy-start(bf16[1536,128]{1,0:T(8,128)(2,1)} %param.25) | copy-start | bytes 1179652
  101.0 0.9 copy-start.5
  102.8 160.1 %all-gather.8.cloned.1.call-start = ((), (), s32[]{:S(2)}) async-start(), calls=%async_computation.3 | async-start | bytes 5406720 | tf_op jit(solution)/shard_map/all_gather | solution.py:89
  183.5 8.2 %copy-start.1 = (bf16[4096,1536]{1,0:T(8,128)(2,1)S(1)}, bf16[4096,1536]{1,0:T(8,128)(2,1)}, u32[]{:S(2)}) copy-start(bf16[4096,1536]{1,0:T(8,128)(2,1)} %all-gather.6.cloned.1.call-done) | copy-start | bytes 37748740
  183.6 8.2 %copy-start.22 = (bf16[1536,128]{1,0:T(8,128)(2,1)S(1)}, bf16[1536,128]{1,0:T(8,128)(2,1)}, u32[]{:S(2)}) copy-start(bf16[1536,128]{1,0:T(8,128)(2,1)} %param.26) | copy-start | bytes 1179652
  196.3 6.8 %copy-start.23 = (s32[1,128]{1,0:T(1,128)S(1)}, s32[1,128]{1,0:T(1,128)}, u32[]{:S(2)}) copy-start(s32[1,128]{1,0:T(1,128)} %param.18) | copy-start | bytes 1540
  196.3 44.8 %all-to-all-start = ((bf16[32,128,128]{2,1,0:T(8,128)(2,1)}), bf16[32,128,128]{2,1,0:T(8,128)(2,1)S(1)}, u32[]{:S(2)}, u32[]{:S(2)}) async-start(bf16[32,128,128]{2,1,0:T(8,128)(2,1)} %bitcast.163), calls=%async_computation | async-start | bytes 2097152 | tf_op jit(solution)/shard_map/all_to_all | solution.py:93
  262.9 4.1 %copy-start.3 = (bf16[1,128,1536]{2,1,0:T(8,128)(2,1)S(1)}, bf16[1,128,1536]{2,1,0:T(8,128)(2,1)}, u32[]{:S(2)}) copy-start(bf16[1,128,1536]{2,1,0:T(8,128)(2,1)} %param.14) | copy-start | bytes 1179652
  262.9 4.2 %copy-start.6 = (f32[128,1536]{1,0:T(8,128)S(1)}, f32[128,1536]{1,0:T(8,128)}, u32[]{:S(2)}) copy-start(f32[128,1536]{1,0:T(8,128)} %copy-done.5) | copy-start | bytes 2359300
  262.9 4.2 %copy-start.10 = (f32[128,896]{1,0:T(8,128)S(1)}, f32[128,896]{1,0:T(8,128)}, u32[]{:S(2)}) copy-start(f32[128,896]{1,0:T(8,128)} %convert_reduce_fusion) | copy-start | bytes 1376260
  267.0 1.7 copy-start.4
  267.4 2.4 copy-start.7
  268.7 1.7 copy-start.11
  269.8 1.0 copy-start.12
  269.8 1.0 copy-start.13
  272.4 2.9 %copy-start.16 = (bf16[1,256,384]{1,2,0:T(8,128)(2,1)S(1)}, bf16[1,256,384]{1,2,0:T(8,128)(2,1)}, u32[]{:S(2)}) copy-start(bf16[1,256,384]{1,2,0:T(8,128)(2,1)} %copy-done.15) | copy-start | bytes 589828
Sparse Core Ops, SparseCore 0:
  9.2 85.1 all-gather.3
  102.9 80.5 all-gather.5
  185.4 77.4 all-gather.7

commit v4 on v2

--- a/solution.py
+++ b/solution.py
@@ -82,17 +82,22 @@
     return widened + jnp.dot(context, o_weight, preferred_element_type=jnp.float32)
 
 
-def run_ffn(normed_rows, w_gate, w_up, w_down, down_all):
-    part_rows = lax.all_gather(normed_rows, "blk", axis=0, tiled=True)
-    gate_vals = jnp.dot(part_rows, w_gate, preferred_element_type=jnp.float32)
-    up_vals = jnp.dot(part_rows, w_up, preferred_element_type=jnp.float32)
-    hidden_all = (jax.nn.silu(gate_vals) * up_vals).astype(jnp.bfloat16)
-    hidden_own = lax.all_to_all(hidden_all, "blk", 0, 1, tiled=True)
-    groups = w_down.shape[0]
+def gather_ffn_weights(w_gate, w_up, w_down):
+    width = w_down.shape[1]
+    packed = jnp.concatenate([w_gate.T, w_up.T, w_down], axis=1)
+    full = lax.all_gather(packed, "blk", axis=0, tiled=True)
+    return full[:, :width], full[:, width : 2 * width], full[:, 2 * width :]
+
+
+def run_ffn(normed_rows, gate_t, up_t, down_all, groups):
+    contract = (((1,), (1,)), ((), ()))
+    gate_vals = lax.dot_general(normed_rows, gate_t, contract, preferred_element_type=jnp.float32)
+    up_vals = lax.dot_general(normed_rows, up_t, contract, preferred_element_type=jnp.float32)
+    hidden = (jax.nn.silu(gate_vals) * up_vals).astype(jnp.bfloat16)
     group_count = down_all.shape[0] // groups
     terms = jnp.einsum(
         "rgk,gkd->grd",
-        hidden_own.reshape(hidden_own.shape[0], group_count, groups),
+        hidden.reshape(hidden.shape[0], group_count, groups),
         down_all.reshape(group_count, groups, down_all.shape[1]),
         preferred_element_type=jnp.float32,
     ).astype(jnp.bfloat16)
@@ -149,9 +154,7 @@
     w_down,
 ):
     fetched = fetch_slot(cache_kv, holder)
-    copies = jnp.broadcast_to(w_down[None], (lax.axis_size("blk"),) + w_down.shape)
-    down_all = lax.all_to_all(copies, "blk", 0, 0, tiled=True).reshape(-1, w_down.shape[1])
-    fetched, down_all = lax.optimization_barrier((fetched, down_all))
+    gate_t, up_t, down_all = gather_ffn_weights(w_gate, w_up, w_down)
     cache_keys = fetched[0]
     cache_vals = fetched[1]
     cache_length = cache_len[0]
@@ -168,7 +171,7 @@
         o_weight,
     )
     chosen_mask = accept[0] == 1
-    ffn_sum = run_ffn(rms_scale(first_pass, ffn_gain).astype(jnp.bfloat16), w_gate, w_up, w_down, down_all)
+    ffn_sum = run_ffn(rms_scale(first_pass, ffn_gain).astype(jnp.bfloat16), gate_t, up_t, down_all, w_down.shape[0])
     placed = first_pass + ffn_sum
     second_in = jnp.where(chosen_mask[:, None], placed, block_rows.astype(jnp.float32))
     refined = attend_block(

time: 478 us -> 292 us (0.61)
  waiting for transfers between devices: 355 us -> 176 us
  starting transfers between devices: 28 us -> 12.5 us
  local copies, waits for them, and re-layouts: 20.8 us -> 25.7 us
    ppermute x5, waiting for transfers between devices: 214 us -> 33.5 us  [swap(): lax.ppermute(values, 'req', perm=[(i, i ^ mask) for i in range(count)])]
    all_gather x1, waiting for transfers between devices: 78.8 us -> 142 us  [gather_ffn_weights(): full = lax.all_gather(packed, 'blk', axis=0, tiled=True)]
    all_to_all x2 -> x0, waiting for transfers between devices: 61.9 us -> none  [the longest x1 34 us: local(): lax.all_to_all(copies, 'blk', 0, 0, tiled=True).reshape(-1, w_down.shape[1])]
    all_to_all x2 -> x0, starting transfers between devices: 17.2 us -> none  [the longest x1 10.4 us: local(): lax.all_to_all(copies, 'blk', 0, 0, tiled=True).reshape(-1, w_down.shape[1])]
    slice x0 -> x1, local copies, waits for them, and re-layouts: none -> 10.5 us  [gather_ffn_weights(): return (full[:, :width], full[:, width:2 * width], full[:, 2 * width:])]
    broadcast_in_dim x1 -> x0, local copies, waits for them, and re-layouts: 7.06 us -> none  [local(): jnp.broadcast_to(w_down[None], (lax.axis_size('blk'),) + w_down.shape)]
  transfers between devices with their start and end apart: 8 -> 6, of which waited for: 7 -> 4; matrix products, arithmetic and copies ran while one was open for 6% -> 12% of each run, Pallas kernels for 0% -> 0%
where the time goes in v4:
time: 292 us; the launch traced here: 291 us
  waiting for transfers between devices  176 us (60%)
  matrix products  44.1 us (15%)
  local copies, waits for them, and re-layouts  25.7 us (9%)
  between operations  17.6 us (6%)
  other arithmetic  16 us (5%)
  starting transfers between devices  12.5 us (4%)
    all_gather x1, waiting for transfers between devices, gather_ffn_weights(): full = lax.all_gather(packed, 'blk', axis=0, tiled=True)  142 us
    ppermute x5, waiting for transfers between devices, swap(): lax.ppermute(values, 'req', perm=[(i, i ^ mask) for i in range(count)])  33.5 us
    ppermute x5, starting transfers between devices, swap(): lax.ppermute(values, 'req', perm=[(i, i ^ mask) for i in range(count)])  12.5 us
    unnamed x50, local copies, waits for them, and re-layouts  11.9 us
    slice x1, local copies, waits for them, and re-layouts, gather_ffn_weights(): return (full[:, :width], full[:, width:2 * width], full[:, 2 * width:])  10.5 us
    dot_general x1, matrix products, run_ffn(): lax.dot_general(normed_rows, up_t, contract, preferred_element_type=jnp.f...  8.86 us
    dot_general x1, matrix products, run_ffn(): jnp.einsum('rgk,gkd->grd', hidden.reshape(hidden.shape[0], group_count, g...  8.09 us
    dot_general x1, matrix products, run_ffn(): lax.dot_general(normed_rows, gate_t, contract, preferred_element_type=jnp...  7.15 us
  transfers between devices with their start and end apart: 6, of which 4 were waited for; matrix products, arithmetic and copies ran while one was open for 12% of the time, Pallas kernels for 0%

profile of v4, /device:TPU:1, one launch (start us, length us, event | category | flops | bytes accessed | tf_op | source)
XLA Modules:
  0.0 291.4 jit_solution(16204560022342222627)
XLA Ops:
  6.5 1.3 copy.34
  7.9 1.2 copy.35
  9.0 2.1 pad_maximum_fusion
  11.2 7.8 %collective-permute-start.1 = (s32[1]{0:T(128)}, s32[1]{0:T(128)}, u32[]{:S(2)}, u32[]{:S(2)}) collective-permute-start(s32[1]{0:T(128)} %param.17), channel_id=1, source_target_pairs={{0,32},{32,0},{64,96},{96,64},{128,160},{160,128},{192,224},{224,1... | collective-permute-start | bytes 20 | tf_op jit(solution)/shard_map/ppermute | solution.py:116
  19.0 2.7 collective-permute-start
  23.1 4.3 %copy.32 = bf16[1536,768]{0,1:T(8,128)(2,1)} copy(bf16[1536,768]{1,0:T(8,128)(2,1)} %param.20) | data formatting | bytes 4718592 | tf_op args[6]
  27.6 3.3 %fusion.68 = f32[128,8,96]{0,2,1:T(8,128)} fusion(bf16[8,96,1536]{2,1,0:T(8,128)(2,1)} %bitcast.153, bf16[1,128,1536]{2,1,0:T(8,128)(2,1)S(1)} %copy-done.1, f32[1536]{0:T(1024)S(1)} %copy-done.15, f32[128]{0:T(128)S(1)} %add_rsqrt_fusion.2), kind=kOutput, calls=%fused_computation.82 | convolution fusion | flops 302776320 | bytes 3152384 | tf_op jit(solution)/shard_map/dot_general | solution.py:54
  31.0 0.8 multiply_cosine_fusion
  31.8 0.8 pad_add_fusion
  32.5 0.8 collective-permute-start.2
  33.4 2.0 collective-permute-done.2
  35.4 0.6 fusion.90
  37.4 1.0 pad_maximum_fusion.1
  38.4 0.8 collective-permute-start.3
  39.2 2.5 copy.31
  41.6 1.9 subtract_convert_fusion.1
  43.5 2.3 convolution_convert_fusion.4
  45.8 1.2 fusion.70
  48.4 7.4 %collective-permute-done.3 = bf16[2,2,256,384]{3,2,1,0:T(8,128)(2,1)} collective-permute-done((bf16[2,2,256,384]{3,2,1,0:T(8,128)(2,1)}, bf16[2,2,256,384]{3,2,1,0:T(8,128)(2,1)}, u32[]{:S(2)}, u32[]{:S(2)}) %collective-permute-start.3) | collective-permute-done | bytes 786464 | tf_op jit(solution)/shard_map/ppermute | solution.py:116
  55.8 1.8 fusion.41
  57.9 0.5 iota_compare_fusion
  58.4 1.6 copy.29
  60.0 0.6 concatenate.54
  60.6 1.6 pad_maximum_fusion.6
  62.2 1.6 subtract_convert_fusion.3
  63.9 24.1 %collective-permute-done.4 = bf16[2,256,384]{2,1,0:T(8,128)(2,1)} collective-permute-done((bf16[2,256,384]{2,1,0:T(8,128)(2,1)}, bf16[2,256,384]{2,1,0:T(8,128)(2,1)}, u32[]{:S(2)}, u32[]{:S(2)}) %collective-permute-start.4) | collective-permute-done | bytes 393248 | tf_op jit(solution)/shard_map/ppermute | solution.py:116
  88.0 1.2 fusion.37
  89.6 0.4 copy-done.16
  90.0 2.7 fusion.91
  92.8 1.7 convolution_convert_fusion.2
  94.5 0.6 multiply_reduce_fusion.1
  95.1 0.6 add_rsqrt_fusion.1
  95.7 142.0 %all-gather.2.cloned.1.call-done = bf16[4096,4608]{1,0:T(8,128)(2,1)} async-done(((bf16[128,4608]{1,0:T(8,128)(2,1)}), bf16[4096,4608]{1,0:T(8,128)(2,1)}) %all-gather.2.cloned.1.call-update) | async-done | bytes 37748752 | tf_op jit(solution)/shard_map/all_gather | solution.py:88
  237.7 10.5 %slice.79 = bf16[4096,1536]{1,0:T(8,128)(2,1)} slice(bf16[4096,4608]{1,0:T(8,128)(2,1)} %all-gather.2.cloned.1.call-done), slice={[0:4096], [3072:4608]} | slice | bytes 25165824 | tf_op jit(solution)/shard_map/slice | solution.py:89
  248.2 7.2 %fusion.4 = f32[128,4096]{1,0:T(8,128)S(1)} fusion(bf16[4096,4608]{1,0:T(8,128)(2,1)} %all-gather.2.cloned.1.call-done, f32[128,1536]{1,0:T(8,128)S(1)} %get-tuple-element.26, f32[1536]{0:T(1024)S(1)} %copy-done.18, f32[128]{0:T(128)S(1)} %copy-done.22), kind=kOutput, calls=%fused_computation.6 | convolution fusion | flops 1611202560 | bytes 15473152 | tf_op jit(solution)/shard_map/dot_general | solution.py:94
  255.4 8.9 %fusion.23 = bf16[16,32,8,128]{3,2,1,0:T(8,128)(2,1)S(1)} fusion(bf16[4096,4608]{1,0:T(8,128)(2,1)} %all-gather.2.cloned.1.call-done, f32[128,4096]{1,0:T(8,128)S(1)} %fusion.4, f32[128,1536]{1,0:T(8,128)S(1)} %get-tuple-element.26, f32[1536]{0:T(1024)S(1)} %copy-done.18, f32[128]{0:T(128)S(1)} %copy-done.22), kind=kOutput, calls=%fused_computation.25 | convolution fusion | flops 1614348288 | bytes 16521728 | tf_op jit(solution)/shard_map/dot_general | solution.py:95
  264.3 8.1 %convert_reduce_fusion = f32[128,1536]{1,0:T(8,128)S(1)} fusion(bf16[32,128,1536]{2,1,0:T(8,128)(2,1)} %bitcast.152, bf16[16,32,8,128]{3,2,1,0:T(8,128)(2,1)S(1)} %fusion.23), kind=kOutput, calls=%fused_computation.2 | convolution fusion | flops 1629290496 | bytes 14417920 | tf_op jit(solution)/shard_map/rgk,gkd->grd/dot_general | solution.py:98
  272.4 0.3 multiply_reduce_fusion
  272.9 1.2 copy-done.2
  274.0 1.0 fusion.98
  275.3 0.6 fusion.97
  275.9 0.7 copy-done.8
  276.6 0.4 convolution_convert_fusion.3
  277.1 0.7 subtract_convert_fusion.2
  277.9 0.7 pad_maximum_fusion.7
  278.6 2.9 %fusion.94 = (f32[4,2,128]{2,1,0:T(2,128)S(1)}, f32[4,2,128,384]{2,3,1,0:T(8,128)}) fusion(bf16[128,4,2,96]{0,3,2,1:T(8,128)(2,1)} %bitcast.167, bf16[256,4,96]{0,2,1:T(8,128)(2,1)} %bitcast.165, bf16[128,4,48]{0,2,1:T(8,128)(2,1)} %get-tuple-element.16, bf16[128,4,48]{0,2,1:T(8,128)(2,1)} %get-tuple-element.15, pred[384]{0:T(512)(128)(4,1)S(1)} %copy-done.21), kind=kOutput, calls=%fused_computation.111 | convolution fusion | flops 77955456 | bytes 2068864 | tf_op jit(solution)/shard_map/sub | solution.py:78
  281.5 1.7 convolution_convert_fusion.1
  283.2 1.4 fusion.12
  (61 shorter events, 1.5 us)
Async XLA Ops:
  6.5 88.0 %copy-start = (bf16[768,1536]{1,0:T(8,128)(2,1)S(1)}, bf16[768,1536]{1,0:T(8,128)(2,1)}, u32[]{:S(2)}) copy-start(bf16[768,1536]{1,0:T(8,128)(2,1)} %param.23) | copy-start | bytes 7077892
  6.5 231.2 %all-gather.2.cloned.1.call-start = ((), (), s32[]{:S(2)}) async-start(), calls=%async_computation | async-start | bytes 38928384 | tf_op jit(solution)/shard_map/all_gather | solution.py:88
  9.0 10.0 %copy-start.5 = (bf16[1,2,256,384]{3,2,1,0:T(8,128)(2,1)S(1)}, bf16[1,2,256,384]{3,2,1,0:T(8,128)(2,1)}, u32[]{:S(2)}) copy-start(bf16[1,2,256,384]{3,2,1,0:T(8,128)(2,1)} %param.15) | copy-start | bytes 1179652
  11.2 20.6 %collective-permute-start.1 = (s32[1]{0:T(128)}, s32[1]{0:T(128)}, u32[]{:S(2)}, u32[]{:S(2)}) collective-permute-start(s32[1]{0:T(128)} %param.17), channel_id=1, source_target_pairs={{0,32},{32,0},{64,96},{96,64},{128,160},{160,128},{192,224},{224,1... | collective-permute-start | bytes 20 | tf_op jit(solution)/shard_map/ppermute | solution.py:116
  19.0 18.3 %collective-permute-start = (bf16[2,256,384]{2,1,0:T(8,128)(2,1)S(1)}, bf16[2,256,384]{2,1,0:T(8,128)(2,1)S(1)}, u32[]{:S(2)}, u32[]{:S(2)}) collective-permute-start(bf16[2,256,384]{2,1,0:T(8,128)(2,1)S(1)} %bitcast.155), channel_id=1, source_target_pairs={{0,128},{32,160},{64,192},{96,224},{128,0},{160,32},{192,64},{224,... | collective-permute-start | bytes 1179656 | tf_op jit(solution)/shard_map/ppermute | solution.py:116
  23.1 4.4 %copy-start.1 = (bf16[1,128,1536]{2,1,0:T(8,128)(2,1)S(1)}, bf16[1,128,1536]{2,1,0:T(8,128)(2,1)}, u32[]{:S(2)}) copy-start(bf16[1,128,1536]{2,1,0:T(8,128)(2,1)} %param.14) | copy-start | bytes 1179652
  23.1 4.6 %copy-start.15 = (f32[1536]{0:T(1024)S(1)}, f32[1536]{0:T(1024)}, u32[]{:S(2)}) copy-start(f32[1536]{0:T(1024)} %param.19) | copy-start | bytes 18436
  32.5 2.8 collective-permute-start.2
  37.3 1.9 copy-start.19
  38.4 17.4 %collective-permute-start.3 = (bf16[2,2,256,384]{3,2,1,0:T(8,128)(2,1)}, bf16[2,2,256,384]{3,2,1,0:T(8,128)(2,1)}, u32[]{:S(2)}, u32[]{:S(2)}) collective-permute-start(bf16[2,2,256,384]{3,2,1,0:T(8,128)(2,1)} %pad_maximum_fusion.1), channel_id=1, source_target_pairs={{0,64},{32,96},{64,0},{96,32},{128,192},{160,224},{192,128},{224,1... | collective-permute-start | bytes 2359304 | tf_op jit(solution)/shard_map/ppermute | solution.py:116
  41.6 4.2 %copy-start.4 = (bf16[1536,384]{0,1:T(8,128)(2,1)S(1)}, bf16[1536,384]{0,1:T(8,128)(2,1)}, u32[]{:S(2)}) copy-start(bf16[1536,384]{0,1:T(8,128)(2,1)} %copy.31) | copy-start | bytes 3538948
  57.6 30.4 %collective-permute-start.4 = (bf16[2,256,384]{2,1,0:T(8,128)(2,1)}, bf16[2,256,384]{2,1,0:T(8,128)(2,1)}, u32[]{:S(2)}, u32[]{:S(2)}) collective-permute-start(bf16[2,256,384]{2,1,0:T(8,128)(2,1)} %fusion.41), channel_id=1, source_target_pairs={{0,32},{32,0},{64,96},{96,64},{128,160},{160,128},{192,224},{224,1... | collective-permute-start | bytes 1179656 | tf_op jit(solution)/shard_map/ppermute | solution.py:116
  60.6 29.0 %copy-start.20 = (pred[384]{0:T(512)(128)(4,1)}, pred[384]{0:T(512)(128)(4,1)S(1)}, u32[]{:S(2)}) copy-start(pred[384]{0:T(512)(128)(4,1)S(1)} %concatenate.54) | copy-start | bytes 1156
  89.2 0.8 copy-start.16
  89.2 0.8 copy-start.17
  89.4 3.4 %copy-start.13 = (bf16[1,256,384]{1,2,0:T(8,128)(2,1)}, bf16[1,256,384]{1,2,0:T(8,128)(2,1)S(1)}, u32[]{:S(2)}) copy-start(bf16[1,256,384]{1,2,0:T(8,128)(2,1)S(1)} %copy.30) | copy-start | bytes 589828
  89.6 3.2 %copy-start.11 = (bf16[1,256,384]{1,2,0:T(8,128)(2,1)}, bf16[1,256,384]{1,2,0:T(8,128)(2,1)S(1)}, u32[]{:S(2)}) copy-start(bf16[1,256,384]{1,2,0:T(8,128)(2,1)S(1)} %copy.28) | copy-start | bytes 589828
  90.0 2.8 copy-start.14
  95.1 160.3 %copy-start.6 = (f32[128,1536]{1,0:T(8,128)}, f32[128,1536]{1,0:T(8,128)S(1)}, u32[]{:S(2)}) copy-start(f32[128,1536]{1,0:T(8,128)S(1)} %get-tuple-element.26) | copy-start | bytes 2359300
  95.7 152.5 %copy-start.22 = (f32[128]{0:T(128)S(1)}, f32[128]{0:T(128)}, u32[]{:S(2)}) copy-start(f32[128]{0:T(128)} %add_rsqrt_fusion.1) | copy-start | bytes 1540
  237.7 10.5 %copy-start.18 = (f32[1536]{0:T(1024)S(1)}, f32[1536]{0:T(1024)}, u32[]{:S(2)}) copy-start(f32[1536]{0:T(1024)} %param.24) | copy-start | bytes 18436
  264.3 8.1 %copy-start.7 = (f32[128,1536]{1,0:T(8,128)S(1)}, f32[128,1536]{1,0:T(8,128)}, u32[]{:S(2)}) copy-start(f32[128,1536]{1,0:T(8,128)} %copy-done.6) | copy-start | bytes 2359300
  272.4 1.7 copy-start.2
  274.0 1.3 copy-start.3
  275.3 1.3 copy-start.8
  275.3 1.7 copy-start.9
  275.3 1.7 copy-start.10
  276.6 2.0 copy-start.21
  278.5 2.9 %copy-start.12 = (bf16[1,256,384]{1,2,0:T(8,128)(2,1)S(1)}, bf16[1,256,384]{1,2,0:T(8,128)(2,1)}, u32[]{:S(2)}) copy-start(bf16[1,256,384]{1,2,0:T(8,128)(2,1)} %copy-done.11) | copy-start | bytes 589828
Sparse Core Ops, SparseCore 0:
  11.3 226.3 all-gather.1

commit v5 on v2

--- a/solution.py
+++ b/solution.py
@@ -82,13 +82,12 @@
     return widened + jnp.dot(context, o_weight, preferred_element_type=jnp.float32)
 
 
-def run_ffn(normed_rows, w_gate, w_up, w_down, down_all):
+def run_ffn(normed_rows, w_gate, w_up, down_all, groups):
     part_rows = lax.all_gather(normed_rows, "blk", axis=0, tiled=True)
     gate_vals = jnp.dot(part_rows, w_gate, preferred_element_type=jnp.float32)
     up_vals = jnp.dot(part_rows, w_up, preferred_element_type=jnp.float32)
     hidden_all = (jax.nn.silu(gate_vals) * up_vals).astype(jnp.bfloat16)
     hidden_own = lax.all_to_all(hidden_all, "blk", 0, 1, tiled=True)
-    groups = w_down.shape[0]
     group_count = down_all.shape[0] // groups
     terms = jnp.einsum(
         "rgk,gkd->grd",
@@ -149,9 +148,7 @@
     w_down,
 ):
     fetched = fetch_slot(cache_kv, holder)
-    copies = jnp.broadcast_to(w_down[None], (lax.axis_size("blk"),) + w_down.shape)
-    down_all = lax.all_to_all(copies, "blk", 0, 0, tiled=True).reshape(-1, w_down.shape[1])
-    fetched, down_all = lax.optimization_barrier((fetched, down_all))
+    down_all = lax.all_gather(w_down, "blk", axis=0, tiled=True)
     cache_keys = fetched[0]
     cache_vals = fetched[1]
     cache_length = cache_len[0]
@@ -168,7 +165,10 @@
         o_weight,
     )
     chosen_mask = accept[0] == 1
-    ffn_sum = run_ffn(rms_scale(first_pass, ffn_gain).astype(jnp.bfloat16), w_gate, w_up, w_down, down_all)
+    ffn_rows, down_all = lax.optimization_barrier(
+        (rms_scale(first_pass, ffn_gain).astype(jnp.bfloat16), down_all)
+    )
+    ffn_sum = run_ffn(ffn_rows, w_gate, w_up, down_all, w_down.shape[0])
     placed = first_pass + ffn_sum
     second_in = jnp.where(chosen_mask[:, None], placed, block_rows.astype(jnp.float32))
     refined = attend_block(

time: 478 us -> 268 us (0.56)
  waiting for transfers between devices: 355 us -> 162 us
  starting transfers between devices: 28 us -> 17.8 us
  local copies, waits for them, and re-layouts: 20.8 us -> 14.6 us
    ppermute x5, waiting for transfers between devices: 214 us -> 35.5 us  [swap(): lax.ppermute(values, 'req', perm=[(i, i ^ mask) for i in range(count)])]
    all_to_all x1 -> x0, waiting for transfers between devices: 34 us -> none  [local(): lax.all_to_all(copies, 'blk', 0, 0, tiled=True).reshape(-1, w_down.shape[1])]
    all_gather x0 -> x1, waiting for transfers between devices: none -> 17 us  [local(): down_all = lax.all_gather(w_down, 'blk', axis=0, tiled=True)]
    all_to_all x1 -> x0, starting transfers between devices: 10.4 us -> none  [local(): lax.all_to_all(copies, 'blk', 0, 0, tiled=True).reshape(-1, w_down.shape[1])]
    broadcast_in_dim x1 -> x0, local copies, waits for them, and re-layouts: 7.06 us -> none  [local(): jnp.broadcast_to(w_down[None], (lax.axis_size('blk'),) + w_down.shape)]
  transfers between devices with their start and end apart: 8 -> 8, of which waited for: 7 -> 6; matrix products, arithmetic and copies ran while one was open for 6% -> 13% of each run, Pallas kernels for 0% -> 0%
where the time goes in v5:
time: 268 us
  waiting for transfers between devices  162 us (60%)
  matrix products  41.9 us (16%)
  starting transfers between devices  17.8 us (7%)
  between operations  17.6 us (7%)
  local copies, waits for them, and re-layouts  14.6 us (5%)
  other arithmetic  14 us (5%)
    all_gather x1, waiting for transfers between devices, run_ffn(): part_rows = lax.all_gather(normed_rows, 'blk', axis=0, tiled=True)  80.5 us
    ppermute x5, waiting for transfers between devices, swap(): lax.ppermute(values, 'req', perm=[(i, i ^ mask) for i in range(count)])  35.5 us
    all_to_all x1, waiting for transfers between devices, run_ffn(): hidden_own = lax.all_to_all(hidden_all, 'blk', 0, 1, tiled=True)  27.9 us
    all_gather x1, waiting for transfers between devices, local(): down_all = lax.all_gather(w_down, 'blk', axis=0, tiled=True)  17 us
    ppermute x5, starting transfers between devices, swap(): lax.ppermute(values, 'req', perm=[(i, i ^ mask) for i in range(count)])  10.7 us
    unnamed x50, local copies, waits for them, and re-layouts  10.4 us
    dot_general x1, matrix products, run_ffn(): jnp.einsum('rgk,gkd->grd', hidden_own.reshape(hidden_own.shape[0], group_...  8.39 us
    dot_general x1, matrix products, run_ffn(): gate_vals = jnp.dot(part_rows, w_gate, preferred_element_type=jnp.float32)  7.95 us
  transfers between devices with their start and end apart: 8, of which 6 were waited for; matrix products, arithmetic and copies ran while one was open for 13% of the time, Pallas kernels for 0%

profile of v5, /device:TPU:1, one launch (start us, length us, event | category | flops | bytes accessed | tf_op | source)
XLA Modules:
  0.0 267.6 jit_solution(13072522321120384567)
XLA Ops:
  6.5 0.7 all-gather.3.cloned.1.call-update
  7.3 3.7 %collective-permute-start = (bf16[2,256,384]{2,1,0:T(8,128)(2,1)}, bf16[2,256,384]{2,1,0:T(8,128)(2,1)S(1)}, u32[]{:S(2)}, u32[]{:S(2)}) collective-permute-start(bf16[2,256,384]{2,1,0:T(8,128)(2,1)} %bitcast.156), channel_id=1, source_target_pairs={{0,128},{32,160},{64,192},{96,224},{128,0},{160,32},{192,64},{224,... | collective-permute-start | bytes 1179656 | tf_op jit(solution)/shard_map/ppermute | solution.py:110
  11.0 6.9 %collective-permute-start.1 = (s32[1]{0:T(128)}, s32[1]{0:T(128)}, u32[]{:S(2)}, u32[]{:S(2)}) collective-permute-start(s32[1]{0:T(128)} %param.17), channel_id=1, source_target_pairs={{0,32},{32,0},{64,96},{96,64},{128,160},{160,128},{192,224},{224,1... | collective-permute-start | bytes 20 | tf_op jit(solution)/shard_map/ppermute | solution.py:110
  18.6 4.3 %copy.29 = bf16[1536,768]{0,1:T(8,128)(2,1)} copy(bf16[1536,768]{1,0:T(8,128)(2,1)} %param.20) | data formatting | bytes 4718592 | tf_op args[6]
  23.8 3.6 %fusion.55 = f32[128,8,96]{0,2,1:T(8,128)} fusion(bf16[8,96,1536]{2,1,0:T(8,128)(2,1)} %bitcast.154, bf16[1,128,1536]{2,1,0:T(8,128)(2,1)S(1)} %copy-done.2, f32[1536]{0:T(1024)S(1)} %copy-done.17, f32[128]{0:T(128)S(1)} %add_rsqrt_fusion.2), kind=kOutput, calls=%fused_computation.75 | convolution fusion | flops 302776320 | bytes 3152384 | tf_op jit(solution)/shard_map/dot_general | solution.py:54
  27.3 0.5 add_convert_fusion.4
  27.8 0.7 pad_add_fusion
  28.6 2.7 %collective-permute-done.2 = s32[2]{0:T(128)S(1)} collective-permute-done((s32[2]{0:T(128)S(1)}, s32[2]{0:T(128)S(1)}, u32[]{:S(2)}, u32[]{:S(2)}) %collective-permute-start.2) | collective-permute-done | bytes 40 | tf_op jit(solution)/shard_map/ppermute | solution.py:110
  31.4 0.6 fusion.77
  33.3 1.0 pad_maximum_fusion
  34.4 0.8 multiply_cosine_fusion
  35.2 2.4 copy.28
  37.6 1.9 subtract_convert_fusion.1
  39.5 2.4 convolution_convert_fusion.4
  41.8 1.2 fusion.57
  44.3 7.3 %collective-permute-done.3 = bf16[2,2,256,384]{3,2,1,0:T(8,128)(2,1)} collective-permute-done((bf16[2,2,256,384]{3,2,1,0:T(8,128)(2,1)}, bf16[2,2,256,384]{3,2,1,0:T(8,128)(2,1)}, u32[]{:S(2)}, u32[]{:S(2)}) %collective-permute-start.3) | collective-permute-done | bytes 786464 | tf_op jit(solution)/shard_map/ppermute | solution.py:110
  51.7 1.8 fusion.28
  53.5 1.6 copy.26
  55.1 1.6 pad_maximum_fusion.5
  56.8 1.6 subtract_convert_fusion.3
  58.4 25.4 %collective-permute-done.4 = bf16[2,256,384]{2,1,0:T(8,128)(2,1)} collective-permute-done((bf16[2,256,384]{2,1,0:T(8,128)(2,1)}, bf16[2,256,384]{2,1,0:T(8,128)(2,1)}, u32[]{:S(2)}, u32[]{:S(2)}) %collective-permute-start.4) | collective-permute-done | bytes 393248 | tf_op jit(solution)/shard_map/ppermute | solution.py:110
  83.8 1.1 fusion.24
  85.3 0.4 copy-done.18
  85.7 2.8 %fusion.78 = (f32[4,2,128]{2,1,0:T(2,128)S(1)}, f32[4,2,128,384]{2,3,1,0:T(8,128)}) fusion(bf16[128,4,2,96]{0,3,2,1:T(8,128)(2,1)} %bitcast.166, bf16[256,4,96]{0,2,1:T(8,128)(2,1)S(1)} %bitcast.164, bf16[128,4,48]{0,2,1:T(8,128)(2,1)S(1)} %copy-done.19, bf16[128,4,48]{0,2,1:T(8,128)(2,1)S(1)} %copy-done.18, pred[384]{0:T(512)(128)(4,1)S(1)} %concatenate.51), kind=kOutput, calls=%fused_computation.103 | convolution fusion | flops 77955456 | bytes 2068864 | tf_op jit(solution)/shard_map/sub | solution.py:78
  88.5 1.7 convolution_convert_fusion.2
  90.3 0.6 multiply_reduce_fusion.1
  90.9 0.9 copy-done.4
  91.7 0.9 multiply_convert_fusion.1
  92.7 17.0 %all-gather.3.cloned.1.call-done = bf16[4096,1536]{1,0:T(8,128)(2,1)} async-done(((bf16[128,1536]{1,0:T(8,128)(2,1)}), bf16[4096,1536]{1,0:T(8,128)(2,1)}) %all-gather.3.cloned.1.call-update) | async-done | bytes 12582928 | tf_op jit(solution)/shard_map/all_gather | solution.py:151
  109.7 80.5 %all-gather.5.cloned.1.call-done = bf16[4096,1536]{1,0:T(8,128)(2,1)} async-done(((bf16[128,1536]{1,0:T(8,128)(2,1)}), bf16[4096,1536]{1,0:T(8,128)(2,1)}) %all-gather.5.cloned.1.call-update) | async-done | bytes 12582928 | tf_op jit(solution)/shard_map/all_gather | solution.py:86
  190.2 7.9 %fusion.84 = f32[4096,128]{1,0:T(8,128)S(1)} fusion(bf16[4096,1536]{1,0:T(8,128)(2,1)} %all-gather.5.cloned.1.call-done, bf16[1536,128]{1,0:T(8,128)(2,1)S(1)} %copy-done.12), kind=kOutput, calls=%fused_computation.105 | convolution fusion | flops 1610612736 | bytes 15073280 | tf_op jit(solution)/shard_map/dot_general | solution.py:87
  198.2 0.2 copy-done.1
  198.4 4.6 %fusion.2 = bf16[4096,128]{1,0:T(8,128)(2,1)} fusion(bf16[4096,1536]{1,0:T(8,128)(2,1)S(1)} %copy-done.1, bf16[1536,128]{1,0:T(8,128)(2,1)S(1)} %copy-done.22, f32[4096,128]{1,0:T(8,128)S(1)} %fusion.84), kind=kOutput, calls=%fused_computation.5 | convolution fusion | flops 1613758464 | bytes 16121856 | tf_op jit(solution)/shard_map/dot_general | solution.py:88
  203.0 7.0 %all-to-all-start = ((bf16[32,128,128]{2,1,0:T(8,128)(2,1)}), bf16[32,128,128]{2,1,0:T(8,128)(2,1)}, u32[]{:S(2)}, u32[]{:S(2)}) async-start(bf16[32,128,128]{2,1,0:T(8,128)(2,1)} %bitcast.158), calls=%async_computation | async-start | bytes 2097152 | tf_op jit(solution)/shard_map/all_to_all | solution.py:90
  210.0 27.9 %all-to-all-done = bf16[32,128,128]{2,1,0:T(8,128)(2,1)} async-done(((bf16[32,128,128]{2,1,0:T(8,128)(2,1)}), bf16[32,128,128]{2,1,0:T(8,128)(2,1)}, u32[]{:S(2)}, u32[]{:S(2)}) %all-to-all-start) | async-done | bytes 1048608 | tf_op jit(solution)/shard_map/all_to_all | solution.py:90
  237.9 8.4 %convert_reduce_fusion = f32[128,1536]{1,0:T(8,128)S(1)} fusion(bf16[32,128,1536]{2,1,0:T(8,128)(2,1)} %bitcast.153, bf16[32,128,128]{2,1,0:T(8,128)(2,1)} %all-to-all-done), kind=kOutput, calls=%fused_computation.2 | convolution fusion | flops 1629290496 | bytes 14417920 | tf_op jit(solution)/shard_map/rgk,gkd->grd/dot_general | solution.py:92
  246.4 0.3 multiply_reduce_fusion
  246.8 1.2 copy-done.3
  248.0 1.1 fusion.86
  249.3 0.6 fusion.85
  249.9 0.7 copy-done.9
  250.5 1.0 convolution_convert_fusion.3
  251.6 0.7 subtract_convert_fusion.2
  252.3 1.6 copy.31
  253.9 0.7 pad_maximum_fusion.6
  254.6 2.9 %fusion.81 = (f32[4,2,128]{2,1,0:T(2,128)S(1)}, f32[4,2,128,384]{2,3,1,0:T(8,128)}) fusion(bf16[128,4,2,96]{0,3,2,1:T(8,128)(2,1)} %bitcast.167, bf16[256,4,96]{0,2,1:T(8,128)(2,1)} %bitcast.165, bf16[128,4,48]{0,2,1:T(8,128)(2,1)} %get-tuple-element.20, bf16[128,4,48]{0,2,1:T(8,128)(2,1)} %get-tuple-element.19, pred[384]{0:T(512)(128)(4,1)S(1)} %concatenate.51), kind=kOutput, calls=%fused_computation.104 | convolution fusion | flops 77955456 | bytes 2068864 | tf_op jit(solution)/shard_map/sub | solution.py:78
  257.6 1.8 convolution_convert_fusion.1
  259.3 1.4 fusion.3
  (65 shorter events, 1.4 us)
Async XLA Ops:
  6.5 83.7 %copy-start = (bf16[768,1536]{1,0:T(8,128)(2,1)S(1)}, bf16[768,1536]{1,0:T(8,128)(2,1)}, u32[]{:S(2)}) copy-start(bf16[768,1536]{1,0:T(8,128)(2,1)} %param.23) | copy-start | bytes 7077892
  6.5 103.1 %all-gather.3.cloned.1.call-start = ((), (), s32[]{:S(2)}) async-start(), calls=%async_computation.1 | async-start | bytes 12976128 | tf_op jit(solution)/shard_map/all_gather | solution.py:151
  7.3 182.9 %all-gather.5.cloned.1.call-start = ((), (), s32[]{:S(2)}) async-start(), calls=%async_computation.2 | async-start | bytes 12976128 | tf_op jit(solution)/shard_map/all_gather | solution.py:86
  7.3 25.9 %collective-permute-start = (bf16[2,256,384]{2,1,0:T(8,128)(2,1)}, bf16[2,256,384]{2,1,0:T(8,128)(2,1)S(1)}, u32[]{:S(2)}, u32[]{:S(2)}) collective-permute-start(bf16[2,256,384]{2,1,0:T(8,128)(2,1)} %bitcast.156), channel_id=1, source_target_pairs={{0,128},{32,160},{64,192},{96,224},{128,0},{160,32},{192,64},{224,... | collective-permute-start | bytes 1179656 | tf_op jit(solution)/shard_map/ppermute | solution.py:110
  11.0 16.9 %collective-permute-start.1 = (s32[1]{0:T(128)}, s32[1]{0:T(128)}, u32[]{:S(2)}, u32[]{:S(2)}) collective-permute-start(s32[1]{0:T(128)} %param.17), channel_id=1, source_target_pairs={{0,32},{32,0},{64,96},{96,64},{128,160},{160,128},{192,224},{224,1... | collective-permute-start | bytes 20 | tf_op jit(solution)/shard_map/ppermute | solution.py:110
  18.6 5.0 %copy-start.2 = (bf16[1,128,1536]{2,1,0:T(8,128)(2,1)S(1)}, bf16[1,128,1536]{2,1,0:T(8,128)(2,1)}, u32[]{:S(2)}) copy-start(bf16[1,128,1536]{2,1,0:T(8,128)(2,1)} %param.14) | copy-start | bytes 1179652
  18.6 5.2 %copy-start.17 = (f32[1536]{0:T(1024)S(1)}, f32[1536]{0:T(1024)}, u32[]{:S(2)}) copy-start(f32[1536]{0:T(1024)} %param.19) | copy-start | bytes 18436
  23.8 9.5 %copy-start.8 = (bf16[1,2,256,384]{3,2,1,0:T(8,128)(2,1)S(1)}, bf16[1,2,256,384]{3,2,1,0:T(8,128)(2,1)}, u32[]{:S(2)}) copy-start(bf16[1,2,256,384]{3,2,1,0:T(8,128)(2,1)} %param.15) | copy-start | bytes 1179652
  28.5 2.8 %collective-permute-start.2 = (s32[2]{0:T(128)S(1)}, s32[2]{0:T(128)S(1)}, u32[]{:S(2)}, u32[]{:S(2)}) collective-permute-start(s32[2]{0:T(128)S(1)} %pad_add_fusion), channel_id=1, source_target_pairs={{0,64},{32,96},{64,0},{96,32},{128,192},{160,224},{192,128},{224,1... | collective-permute-start | bytes 32 | tf_op jit(solution)/shard_map/ppermute | solution.py:110
  33.2 1.2 copy-start.21
  34.3 17.4 %collective-permute-start.3 = (bf16[2,2,256,384]{3,2,1,0:T(8,128)(2,1)}, bf16[2,2,256,384]{3,2,1,0:T(8,128)(2,1)}, u32[]{:S(2)}, u32[]{:S(2)}) collective-permute-start(bf16[2,2,256,384]{3,2,1,0:T(8,128)(2,1)} %pad_maximum_fusion), channel_id=1, source_target_pairs={{0,64},{32,96},{64,0},{96,32},{128,192},{160,224},{192,128},{224,1... | collective-permute-start | bytes 2359304 | tf_op jit(solution)/shard_map/ppermute | solution.py:110
  37.6 4.2 %copy-start.7 = (bf16[1536,384]{0,1:T(8,128)(2,1)S(1)}, bf16[1536,384]{0,1:T(8,128)(2,1)}, u32[]{:S(2)}) copy-start(bf16[1536,384]{0,1:T(8,128)(2,1)} %copy.28) | copy-start | bytes 3538948
  53.5 30.3 %collective-permute-start.4 = (bf16[2,256,384]{2,1,0:T(8,128)(2,1)}, bf16[2,256,384]{2,1,0:T(8,128)(2,1)}, u32[]{:S(2)}, u32[]{:S(2)}) collective-permute-start(bf16[2,256,384]{2,1,0:T(8,128)(2,1)} %fusion.28), channel_id=1, source_target_pairs={{0,32},{32,0},{64,96},{96,64},{128,160},{160,128},{192,224},{224,1... | collective-permute-start | bytes 1179656 | tf_op jit(solution)/shard_map/ppermute | solution.py:110
  84.9 0.8 copy-start.18
  84.9 0.8 copy-start.19
  85.1 3.4 %copy-start.15 = (bf16[1,256,384]{1,2,0:T(8,128)(2,1)}, bf16[1,256,384]{1,2,0:T(8,128)(2,1)S(1)}, u32[]{:S(2)}) copy-start(bf16[1,256,384]{1,2,0:T(8,128)(2,1)S(1)} %copy.27) | copy-start | bytes 589828
  85.3 3.2 %copy-start.13 = (bf16[1,256,384]{1,2,0:T(8,128)(2,1)}, bf16[1,256,384]{1,2,0:T(8,128)(2,1)S(1)}, u32[]{:S(2)}) copy-start(bf16[1,256,384]{1,2,0:T(8,128)(2,1)S(1)} %copy.25) | copy-start | bytes 589828
  85.7 2.8 %copy-start.16 = (bf16[128,384]{0,1:T(8,128)(2,1)S(1)}, bf16[128,384]{0,1:T(8,128)(2,1)}, u32[]{:S(2)}) copy-start(bf16[128,384]{0,1:T(8,128)(2,1)} %copy.26) | copy-start | bytes 294916
  90.3 1.5 copy-start.20
  90.8 0.9 copy-start.4
  90.9 99.3 %copy-start.12 = (bf16[1536,128]{1,0:T(8,128)(2,1)S(1)}, bf16[1536,128]{1,0:T(8,128)(2,1)}, u32[]{:S(2)}) copy-start(bf16[1536,128]{1,0:T(8,128)(2,1)} %param.25) | copy-start | bytes 1179652
  109.6 88.5 %copy-start.22 = (bf16[1536,128]{1,0:T(8,128)(2,1)S(1)}, bf16[1536,128]{1,0:T(8,128)(2,1)}, u32[]{:S(2)}) copy-start(bf16[1536,128]{1,0:T(8,128)(2,1)} %param.26) | copy-start | bytes 1179652
  190.2 8.2 %copy-start.1 = (bf16[4096,1536]{1,0:T(8,128)(2,1)S(1)}, bf16[4096,1536]{1,0:T(8,128)(2,1)}, u32[]{:S(2)}) copy-start(bf16[4096,1536]{1,0:T(8,128)(2,1)} %all-gather.5.cloned.1.call-done) | copy-start | bytes 37748740
  203.0 7.1 %copy-start.23 = (s32[1,128]{1,0:T(1,128)S(1)}, s32[1,128]{1,0:T(1,128)}, u32[]{:S(2)}) copy-start(s32[1,128]{1,0:T(1,128)} %param.18) | copy-start | bytes 1540
  203.0 35.0 %all-to-all-start = ((bf16[32,128,128]{2,1,0:T(8,128)(2,1)}), bf16[32,128,128]{2,1,0:T(8,128)(2,1)}, u32[]{:S(2)}, u32[]{:S(2)}) async-start(bf16[32,128,128]{2,1,0:T(8,128)(2,1)} %bitcast.158), calls=%async_computation | async-start | bytes 2097152 | tf_op jit(solution)/shard_map/all_to_all | solution.py:90
  237.9 8.4 %copy-start.5 = (f32[128,1536]{1,0:T(8,128)S(1)}, f32[128,1536]{1,0:T(8,128)}, u32[]{:S(2)}) copy-start(f32[128,1536]{1,0:T(8,128)} %copy-done.4) | copy-start | bytes 2359300
  246.3 1.7 copy-start.3
  248.0 1.3 copy-start.6
  249.3 1.3 copy-start.9
  249.3 2.3 copy-start.10
  249.3 2.3 copy-start.11
  254.6 2.9 %copy-start.14 = (bf16[1,256,384]{1,2,0:T(8,128)(2,1)S(1)}, bf16[1,256,384]{1,2,0:T(8,128)(2,1)}, u32[]{:S(2)}) copy-start(bf16[1,256,384]{1,2,0:T(8,128)(2,1)} %copy-done.13) | copy-start | bytes 589828
Sparse Core Ops, SparseCore 0:
  9.2 100.3 all-gather.2
  111.5 78.6 all-gather.4

commit v6 on v5

--- a/solution.py
+++ b/solution.py
@@ -82,28 +82,40 @@
     return widened + jnp.dot(context, o_weight, preferred_element_type=jnp.float32)
 
 
-def run_ffn(normed_rows, w_gate, w_up, down_all, groups):
+def run_ffn(normed_rows, w_gate, w_up, down_held, held_groups):
     part_rows = lax.all_gather(normed_rows, "blk", axis=0, tiled=True)
     gate_vals = jnp.dot(part_rows, w_gate, preferred_element_type=jnp.float32)
     up_vals = jnp.dot(part_rows, w_up, preferred_element_type=jnp.float32)
     hidden_all = (jax.nn.silu(gate_vals) * up_vals).astype(jnp.bfloat16)
     hidden_own = lax.all_to_all(hidden_all, "blk", 0, 1, tiled=True)
-    group_count = down_all.shape[0] // groups
+    group_count, groups = down_held.shape[0], down_held.shape[1]
+    grouped = hidden_own.reshape(hidden_own.shape[0], group_count, groups)
+    grouped = jnp.take(grouped, held_groups, axis=1)
     terms = jnp.einsum(
-        "rgk,gkd->grd",
-        hidden_own.reshape(hidden_own.shape[0], group_count, groups),
-        down_all.reshape(group_count, groups, down_all.shape[1]),
-        preferred_element_type=jnp.float32,
+        "rgk,gkd->grd", grouped, down_held, preferred_element_type=jnp.float32
     ).astype(jnp.bfloat16)
     return jnp.sum(terms.astype(jnp.float32), axis=0)
 
 
-def fetch_slot(cache_kv, holder):
+def held_order(masks, count):
+    offsets = []
+    for j in range(count):
+        offset = 0
+        for bit, mask in enumerate(masks):
+            if (j >> bit) & 1:
+                offset ^= mask
+        offsets.append(offset)
+    return jnp.bitwise_xor(lax.axis_index("blk"), jnp.array(offsets, dtype=jnp.int32))
+
+
+def fetch_and_gather(cache_kv, holder, w_down):
     count = lax.axis_size("req")
+    blocks = lax.axis_size("blk")
     own = cache_kv[0]
-    if count != 8:
+    if count != 8 or blocks != 32:
         slots = lax.all_gather(own, "req", axis=0, tiled=False)
-        return slots[holder[0]]
+        down = lax.all_gather(w_down, "blk", axis=0, tiled=False)
+        return slots[holder[0]], down, jnp.arange(blocks, dtype=jnp.int32)
     me = lax.axis_index("req")
 
     def swap(values, mask):
@@ -112,23 +124,46 @@
     def pick(cond, a, b):
         return jnp.where(cond, a, b)
 
+    masks = (16, 4, 8, 2, 1)
+    held = [w_down[None]]
+
+    def grow(mask):
+        got = lax.ppermute(held[0], "blk", perm=[(i, i ^ mask) for i in range(blocks)])
+        return got
+
+    def keep(got):
+        held[0] = jnp.concatenate([held[0], got], axis=0)
+
     near = swap(holder, 1)
+    got1 = swap(own, 4)
+    w_got = grow(masks[0])
+    near, got1, w_got = lax.optimization_barrier((near, got1, w_got))
+    keep(w_got)
     quad = swap(jnp.concatenate([holder, near]), 2)
+    w_got = grow(masks[1])
+    quad, w_got = lax.optimization_barrier((quad, w_got))
+    keep(w_got)
     holders = {0: holder[0], 1: near[0], 2: quad[0], 3: quad[1]}
-
-    got1 = swap(own, 4)
     send_a = pick(holders[2] == (me ^ 4), got1, own)
     send_b = pick(holders[3] == (me ^ 4), got1, own)
     got2 = swap(jnp.stack([send_a, send_b]), 2)
+    w_got = grow(masks[2])
+    got2, w_got = lax.optimization_barrier((got2, w_got))
+    keep(w_got)
     want = holders[1]
     send_c = pick(want == me, own, pick(want == (me ^ 4), got1, got2[1]))
     got3 = swap(send_c, 1)
+    w_got = grow(masks[3])
+    got3, w_got = lax.optimization_barrier((got3, w_got))
+    keep(w_got)
     need = holders[0]
-    return pick(
+    slot = pick(
         need == me,
         own,
         pick(need == (me ^ 4), got1, pick((need ^ me) == 2, got2[0], pick((need ^ me) == 6, got2[0], got3))),
     )
+    keep(grow(masks[4]))
+    return slot, held[0], held_order(masks, blocks)
 
 
 def local(
@@ -147,8 +182,7 @@
     w_up,
     w_down,
 ):
-    fetched = fetch_slot(cache_kv, holder)
-    down_all = lax.all_gather(w_down, "blk", axis=0, tiled=True)
+    fetched, down_held, held_groups = fetch_and_gather(cache_kv, holder, w_down)
     cache_keys = fetched[0]
     cache_vals = fetched[1]
     cache_length = cache_len[0]
@@ -165,10 +199,10 @@
         o_weight,
     )
     chosen_mask = accept[0] == 1
-    ffn_rows, down_all = lax.optimization_barrier(
-        (rms_scale(first_pass, ffn_gain).astype(jnp.bfloat16), down_all)
-    )
-    ffn_sum = run_ffn(ffn_rows, w_gate, w_up, down_all, w_down.shape[0])
+    ffn_rows, down_held = lax.optimization_barrier(
+        (rms_scale(first_pass, ffn_gain).astype(jnp.bfloat16), down_held)
+    )
+    ffn_sum = run_ffn(ffn_rows, w_gate, w_up, down_held, held_groups)
     placed = first_pass + ffn_sum
     second_in = jnp.where(chosen_mask[:, None], placed, block_rows.astype(jnp.float32))
     refined = attend_block(

time: 268 us -> 378 us (1.41)
  waiting for transfers between devices: 162 us -> 236 us
  starting transfers between devices: 17.8 us -> 37 us
  local copies, waits for them, and re-layouts: 14.6 us -> 33.1 us
  matrix products: 41.9 us -> 38 us
    ppermute x5, waiting for transfers between devices: 35.5 us -> 85 us  [swap(): lax.ppermute(values, 'req', perm=[(i, i ^ mask) for i in range(count)])]
    ppermute x0 -> x5, waiting for transfers between devices: none -> 42.3 us  [grow(): lax.ppermute(held[0], 'blk', perm=[(i, i ^ mask) for i in range(blocks)])]
    all_gather x1 -> x0, waiting for transfers between devices: 17 us -> none  [local(): down_all = lax.all_gather(w_down, 'blk', axis=0, tiled=True)]
    ppermute x0 -> x5, starting transfers between devices: none -> 13.2 us  [grow(): lax.ppermute(held[0], 'blk', perm=[(i, i ^ mask) for i in range(blocks)])]
    concatenate x0 -> x2, local copies, waits for them, and re-layouts: none -> 11.2 us  [keep(): held[0] = jnp.concatenate([held[0], got], axis=0)]
    unnamed x50 -> x68, local copies, waits for them, and re-layouts: 10.4 us -> 17.1 us
    concatenate x1 -> x4, other arithmetic: 0.71 us -> 7.07 us  [the longest x3 6.4 us: keep(): held[0] = jnp.concatenate([held[0], got], axis=0)]
    ppermute x5, starting transfers between devices: 10.7 us -> 17 us  [swap(): lax.ppermute(values, 'req', perm=[(i, i ^ mask) for i in range(count)])]
  transfers between devices with their start and end apart: 8 -> 12, of which waited for: 6 -> 9; matrix products, arithmetic and copies ran while one was open for 13% -> 9% of each run, Pallas kernels for 0% -> 0%
where the time goes in v6:
time: 378 us; the launch traced here: 377 us
  waiting for transfers between devices  236 us (62%)
  matrix products  38 us (10%)
  starting transfers between devices  37 us (10%)
  local copies, waits for them, and re-layouts  33.1 us (9%)
  between operations  17.7 us (5%)
  other arithmetic  15.1 us (4%)
    ppermute x5, waiting for transfers between devices, swap(): lax.ppermute(values, 'req', perm=[(i, i ^ mask) for i in range(count)])  85 us
    all_gather x1, waiting for transfers between devices, run_ffn(): part_rows = lax.all_gather(normed_rows, 'blk', axis=0, tiled=True)  82.3 us
    ppermute x5, waiting for transfers between devices, grow(): lax.ppermute(held[0], 'blk', perm=[(i, i ^ mask) for i in range(blocks)])  42.3 us
    all_to_all x1, waiting for transfers between devices, run_ffn(): hidden_own = lax.all_to_all(hidden_all, 'blk', 0, 1, tiled=True)  26.7 us
    unnamed x68, local copies, waits for them, and re-layouts  17.1 us
    ppermute x5, starting transfers between devices, swap(): lax.ppermute(values, 'req', perm=[(i, i ^ mask) for i in range(count)])  17 us
    ppermute x5, starting transfers between devices, grow(): lax.ppermute(held[0], 'blk', perm=[(i, i ^ mask) for i in range(blocks)])  13.2 us
    concatenate x2, local copies, waits for them, and re-layouts, keep(): held[0] = jnp.concatenate([held[0], got], axis=0)  11.2 us
  transfers between devices with their start and end apart: 12, of which 9 were waited for; matrix products, arithmetic and copies ran while one was open for 9% of the time, Pallas kernels for 0%

profile of v6, /device:TPU:1, one launch (start us, length us, event | category | flops | bytes accessed | tf_op | source)
XLA Modules:
  0.0 377.3 jit_solution(490652434953971692)
XLA Ops:
  6.5 3.7 collective-permute-start.2
  10.3 2.7 collective-permute-start.1
  13.0 6.9 %collective-permute-start = (s32[1]{0:T(128)}, s32[1]{0:T(128)}, u32[]{:S(2)}, u32[]{:S(2)}) collective-permute-start(s32[1]{0:T(128)} %param.18), channel_id=1, source_target_pairs={{0,32},{32,0},{64,96},{96,64},{128,160},{160,128},{192,224},{224,1... | collective-permute-start | bytes 20 | tf_op jit(solution)/shard_map/ppermute | solution.py:122
  19.9 1.2 collective-permute-done
  21.8 1.1 pad_maximum_fusion.2
  22.8 3.1 collective-permute-start.4
  27.2 1.2 collective-permute-start.3
  28.5 1.2 collective-permute-done.3
  29.7 29.7 %collective-permute-done.4 = bf16[2,128,1536]{2,1,0:T(8,128)(2,1)S(1)} collective-permute-done((bf16[2,128,1536]{2,1,0:T(8,128)(2,1)S(1)}, bf16[2,128,1536]{2,1,0:T(8,128)(2,1)S(1)}, u32[]{:S(2)}, u32[]{:S(2)}) %collective-permute-start.4) | collective-permute-done | bytes 786464 | tf_op jit(solution)/shard_map/ppermute | solution.py:131
  59.4 2.3 pad_maximum_fusion.1
  64.1 1.2 select_bitcast_fusion.1
  65.4 1.3 collective-permute-start.5
  66.7 15.7 %collective-permute-done.5 = bf16[2,2,256,384]{3,2,1,0:T(8,128)(2,1)S(1)} collective-permute-done((bf16[2,2,256,384]{3,2,1,0:T(8,128)(2,1)S(1)}, bf16[2,2,256,384]{3,2,1,0:T(8,128)(2,1)S(1)}, u32[]{:S(2)}, u32[]{:S(2)}) %collective-permute-start.5) | collective-permute-done | bytes 786464 | tf_op jit(solution)/shard_map/ppermute | solution.py:122
  82.5 0.9 copy-done.13
  83.3 12.6 %collective-permute-done.6 = bf16[4,128,1536]{2,1,0:T(8,128)(2,1)} collective-permute-done((bf16[4,128,1536]{2,1,0:T(8,128)(2,1)}, bf16[4,128,1536]{2,1,0:T(8,128)(2,1)}, u32[]{:S(2)}, u32[]{:S(2)}) %collective-permute-start.6) | collective-permute-done | bytes 1572896 | tf_op jit(solution)/shard_map/ppermute | solution.py:131
  96.0 3.0 pad_maximum_fusion
  99.0 3.4 collective-permute-start.8
  102.3 0.9 constant_dynamic-update-slice_fusion.4
  104.5 1.9 constant_dynamic-update-slice_fusion.3
  106.4 1.2 fusion.30
  107.6 4.8 %collective-permute-start.7 = (bf16[2,256,384]{2,1,0:T(8,128)(2,1)S(1)}, bf16[2,256,384]{2,1,0:T(8,128)(2,1)S(1)}, u32[]{:S(2)}, u32[]{:S(2)}) collective-permute-start(bf16[2,256,384]{2,1,0:T(8,128)(2,1)S(1)} %fusion.30), channel_id=1, source_target_pairs={{0,32},{32,0},{64,96},{96,64},{128,160},{160,128},{192,224},{224,1... | collective-permute-start | bytes 1179656 | tf_op jit(solution)/shard_map/ppermute | solution.py:122
  112.4 1.3 constant_dynamic-update-slice_fusion.2
  113.7 3.4 constant_dynamic-update-slice_fusion.1
  117.1 66.3 %collective-permute-done.7 = bf16[2,256,384]{2,1,0:T(8,128)(2,1)S(1)} collective-permute-done((bf16[2,256,384]{2,1,0:T(8,128)(2,1)S(1)}, bf16[2,256,384]{2,1,0:T(8,128)(2,1)S(1)}, u32[]{:S(2)}, u32[]{:S(2)}) %collective-permute-start.7) | collective-permute-done | bytes 393248 | tf_op jit(solution)/shard_map/ppermute | solution.py:122
  183.4 5.2 %constant_dynamic-update-slice_fusion = (bf16[16,128,1536]{2,1,0:T(8,128)(2,1)}, bf16[32,128,1536]{2,1,0:T(8,128)(2,1)}) fusion(bf16[16,128,1536]{2,1,0:T(8,128)(2,1)} %get-tuple-element.33, bf16[8,128,1536]{2,1,0:T(8,128)(2,1)} %collective-permute-done.8, bf16[32,128,1536]{2,1,0:T(8,128)(2,1)} %get-tuple-element.34), kind=kLoop, calls=%fused_computation.88 | loop fusion | bytes 9437184 | tf_op jit(solution)/shard_map/concatenate | solution.py:135
  188.6 2.7 collective-permute-start.9
  191.9 4.3 %copy.30 = bf16[1536,768]{0,1:T(8,128)(2,1)} copy(bf16[1536,768]{1,0:T(8,128)(2,1)} %param.21) | data formatting | bytes 4718592 | tf_op args[6]
  196.2 2.4 copy.29
  198.8 1.7 convolution_convert_fusion.4
  201.5 2.6 fusion.57
  206.2 1.1 fusion.27
  207.6 2.9 fusion.81
  210.5 1.7 convolution_convert_fusion.2
  212.9 0.9 multiply_convert_fusion.1
  213.8 6.0 %constant_dynamic-update-slice_fusion.5 = bf16[32,128,1536]{2,1,0:T(8,128)(2,1)} fusion(bf16[32,128,1536]{2,1,0:T(8,128)(2,1)} %get-tuple-element.32, bf16[16,128,1536]{2,1,0:T(8,128)(2,1)} %collective-permute-done.9), kind=kLoop, calls=%fused_computation.93 | loop fusion | bytes 12582912 | tf_op jit(solution)/shard_map/concatenate | solution.py:135
  219.8 82.3 %all-gather.2.cloned.1.call-done = bf16[4096,1536]{1,0:T(8,128)(2,1)} async-done(((bf16[128,1536]{1,0:T(8,128)(2,1)}), bf16[4096,1536]{1,0:T(8,128)(2,1)}) %all-gather.2.cloned.1.call-update) | async-done | bytes 12582928 | tf_op jit(solution)/shard_map/all_gather | solution.py:86
  302.2 7.9 %fusion.87 = f32[4096,128]{1,0:T(8,128)S(1)} fusion(bf16[4096,1536]{1,0:T(8,128)(2,1)} %all-gather.2.cloned.1.call-done, bf16[1536,128]{1,0:T(8,128)(2,1)} %param.26), kind=kOutput, calls=%fused_computation.125 | convolution fusion | flops 1610612736 | bytes 15073280 | tf_op jit(solution)/shard_map/dot_general | solution.py:87
  310.5 4.6 %fusion.2 = bf16[4096,128]{1,0:T(8,128)(2,1)} fusion(bf16[4096,1536]{1,0:T(8,128)(2,1)S(1)} %copy-done.1, bf16[1536,128]{1,0:T(8,128)(2,1)S(1)} %copy-done.28, f32[4096,128]{1,0:T(8,128)S(1)} %fusion.87), kind=kOutput, calls=%fused_computation.6 | convolution fusion | flops 1613758464 | bytes 16121856 | tf_op jit(solution)/shard_map/dot_general | solution.py:88
  315.1 6.7 %all-to-all-start = ((bf16[32,128,128]{2,1,0:T(8,128)(2,1)}), bf16[32,128,128]{2,1,0:T(8,128)(2,1)}, u32[]{:S(2)}, u32[]{:S(2)}) async-start(bf16[32,128,128]{2,1,0:T(8,128)(2,1)} %bitcast.160), calls=%async_computation | async-start | bytes 2097152 | tf_op jit(solution)/shard_map/all_to_all | solution.py:90
  321.9 1.2 compare_bitcast_fusion
  323.0 26.7 %all-to-all-done = bf16[32,128,128]{2,1,0:T(8,128)(2,1)} async-done(((bf16[32,128,128]{2,1,0:T(8,128)(2,1)}), bf16[32,128,128]{2,1,0:T(8,128)(2,1)}, u32[]{:S(2)}, u32[]{:S(2)}) %all-to-all-start) | async-done | bytes 1048608 | tf_op jit(solution)/shard_map/all_to_all | solution.py:90
  349.7 2.9 gather_fusion
  352.6 8.4 %convert_reduce_fusion = f32[128,1536]{1,0:T(8,128)S(1)} fusion(bf16[32,128,1536]{2,1,0:T(8,128)(2,1)} %constant_dynamic-update-slice_fusion.5, bf16[32,128,128]{2,1,0:T(8,128)(2,1)} %gather_fusion, pred[32]{0:T(512)(128)(4,1)S(1)} %get-tuple-element.29), kind=kOutput, calls=%fused_computation.3 | convolution fusion | flops 1629814784 | bytes 14417952 | tf_op jit(solution)/shard_map/rgk,gkd->grd/dot_general | solution.py:94
  361.4 0.9 copy-done.4
  363.0 1.1 fusion.89
  365.4 1.8 fusion.84
  367.3 1.8 convolution_convert_fusion.1
  369.0 1.4 fusion.3
  (98 shorter events, 9.3 us)
Async XLA Ops:
  6.5 205.7 %copy-start = (bf16[768,1536]{1,0:T(8,128)(2,1)S(1)}, bf16[768,1536]{1,0:T(8,128)(2,1)}, u32[]{:S(2)}) copy-start(bf16[768,1536]{1,0:T(8,128)(2,1)} %param.24) | copy-start | bytes 7077892
  6.5 295.6 %all-gather.2.cloned.1.call-start = ((), (), s32[]{:S(2)}) async-start(), calls=%async_computation.1 | async-start | bytes 12976128 | tf_op jit(solution)/shard_map/all_gather | solution.py:86
  6.5 14.6 %collective-permute-start.2 = (bf16[1,128,1536]{2,1,0:T(8,128)(2,1)}, bf16[1,128,1536]{2,1,0:T(8,128)(2,1)S(1)}, u32[]{:S(2)}, u32[]{:S(2)}) collective-permute-start(bf16[1,128,1536]{2,1,0:T(8,128)(2,1)} %bitcast.153), channel_id=1, source_target_pairs={{0,16},{1,17},{2,18},{3,19},{4,20},{5,21},{6,22},{7,23},{8,24},{9,... | collective-permute-start | bytes 1179656 | tf_op jit(solution)/shard_map/ppermute | solution.py:131
  10.3 11.5 %collective-permute-start.1 = (bf16[2,256,384]{2,1,0:T(8,128)(2,1)}, bf16[2,256,384]{2,1,0:T(8,128)(2,1)}, u32[]{:S(2)}, u32[]{:S(2)}) collective-permute-start(bf16[2,256,384]{2,1,0:T(8,128)(2,1)} %bitcast.158), channel_id=1, source_target_pairs={{0,128},{32,160},{64,192},{96,224},{128,0},{160,32},{192,64},{224,... | collective-permute-start | bytes 1179656 | tf_op jit(solution)/shard_map/ppermute | solution.py:122
  13.0 8.1 %collective-permute-start = (s32[1]{0:T(128)}, s32[1]{0:T(128)}, u32[]{:S(2)}, u32[]{:S(2)}) collective-permute-start(s32[1]{0:T(128)} %param.18), channel_id=1, source_target_pairs={{0,32},{32,0},{64,96},{96,64},{128,160},{160,128},{192,224},{224,1... | collective-permute-start | bytes 20 | tf_op jit(solution)/shard_map/ppermute | solution.py:122
  21.1 40.6 %copy-start.7 = (bf16[1,128,1536]{2,1,0:T(8,128)(2,1)}, bf16[1,128,1536]{2,1,0:T(8,128)(2,1)S(1)}, u32[]{:S(2)}) copy-start(bf16[1,128,1536]{2,1,0:T(8,128)(2,1)S(1)} %collective-permute-done.2) | copy-start | bytes 1179652
  22.8 36.5 %collective-permute-start.4 = (bf16[2,128,1536]{2,1,0:T(8,128)(2,1)S(1)}, bf16[2,128,1536]{2,1,0:T(8,128)(2,1)S(1)}, u32[]{:S(2)}, u32[]{:S(2)}) collective-permute-start(bf16[2,128,1536]{2,1,0:T(8,128)(2,1)S(1)} %pad_maximum_fusion.2), channel_id=1, source_target_pairs={{0,4},{1,5},{2,6},{3,7},{4,0},{5,1},{6,2},{7,3},{8,12},{9,13},{10,... | collective-permute-start | bytes 2359304 | tf_op jit(solution)/shard_map/ppermute | solution.py:131
  27.2 2.4 collective-permute-start.3
  61.7 34.3 %copy-start.6 = (bf16[128,1536]{1,0:T(8,128)(2,1)S(1)}, bf16[128,1536]{1,0:T(8,128)(2,1)}, u32[]{:S(2)}) copy-start(bf16[128,1536]{1,0:T(8,128)(2,1)} %param.28) | copy-start | bytes 1179652
  61.7 34.3 %collective-permute-start.6 = (bf16[4,128,1536]{2,1,0:T(8,128)(2,1)}, bf16[4,128,1536]{2,1,0:T(8,128)(2,1)}, u32[]{:S(2)}, u32[]{:S(2)}) collective-permute-start(bf16[4,128,1536]{2,1,0:T(8,128)(2,1)} %pad_maximum_fusion.1), channel_id=1, source_target_pairs={{0,8},{1,9},{2,10},{3,11},{4,12},{5,13},{6,14},{7,15},{8,0},{9,1},... | collective-permute-start | bytes 4718600 | tf_op jit(solution)/shard_map/ppermute | solution.py:131
  64.1 31.9 %copy-start.8 = (bf16[1,128,1536]{2,1,0:T(8,128)(2,1)S(1)}, bf16[1,128,1536]{2,1,0:T(8,128)(2,1)}, u32[]{:S(2)}) copy-start(bf16[1,128,1536]{2,1,0:T(8,128)(2,1)} %copy-done.7) | copy-start | bytes 1179652
  65.4 17.0 %collective-permute-start.5 = (bf16[2,2,256,384]{3,2,1,0:T(8,128)(2,1)S(1)}, bf16[2,2,256,384]{3,2,1,0:T(8,128)(2,1)S(1)}, u32[]{:S(2)}, u32[]{:S(2)}) collective-permute-start(bf16[2,2,256,384]{3,2,1,0:T(8,128)(2,1)S(1)} %pad_maximum_fusion.3), channel_id=1, source_target_pairs={{0,64},{32,96},{64,0},{96,32},{128,192},{160,224},{192,128},{224,1... | collective-permute-start | bytes 2359304 | tf_op jit(solution)/shard_map/ppermute | solution.py:122
  82.5 0.9 copy-start.13
  99.0 84.4 %collective-permute-start.8 = (bf16[8,128,1536]{2,1,0:T(8,128)(2,1)}, bf16[8,128,1536]{2,1,0:T(8,128)(2,1)}, u32[]{:S(2)}, u32[]{:S(2)}) collective-permute-start(bf16[8,128,1536]{2,1,0:T(8,128)(2,1)} %pad_maximum_fusion), channel_id=1, source_target_pairs={{0,2},{1,3},{2,0},{3,1},{4,6},{5,7},{6,4},{7,5},{8,10},{9,11},{10,... | collective-permute-start | bytes 9437192 | tf_op jit(solution)/shard_map/ppermute | solution.py:131
  107.6 75.7 %collective-permute-start.7 = (bf16[2,256,384]{2,1,0:T(8,128)(2,1)S(1)}, bf16[2,256,384]{2,1,0:T(8,128)(2,1)S(1)}, u32[]{:S(2)}, u32[]{:S(2)}) collective-permute-start(bf16[2,256,384]{2,1,0:T(8,128)(2,1)S(1)} %fusion.30), channel_id=1, source_target_pairs={{0,32},{32,0},{64,96},{96,64},{128,160},{160,128},{192,224},{224,1... | collective-permute-start | bytes 1179656 | tf_op jit(solution)/shard_map/ppermute | solution.py:122
  188.6 25.2 %collective-permute-start.9 = (bf16[16,128,1536]{2,1,0:T(8,128)(2,1)}, bf16[16,128,1536]{2,1,0:T(8,128)(2,1)}, u32[]{:S(2)}, u32[]{:S(2)}) collective-permute-start(bf16[16,128,1536]{2,1,0:T(8,128)(2,1)} %get-tuple-element.31), channel_id=1, source_target_pairs={{0,1},{1,0},{2,3},{3,2},{4,5},{5,4},{6,7},{7,6},{8,9},{9,8},{10,11... | collective-permute-start | bytes 18874376 | tf_op jit(solution)/shard_map/ppermute | solution.py:131
  196.2 2.4 copy-start.2
  196.2 2.6 copy-start.24
  201.3 3.7 copy-start.10
  201.3 6.4 %copy-start.29 = (pred[384]{0:T(512)(128)(4,1)}, pred[384]{0:T(512)(128)(4,1)S(1)}, u32[]{:S(2)}) copy-start(pred[384]{0:T(512)(128)(4,1)S(1)} %concatenate.73) | copy-start | bytes 1156
  201.5 4.0 %copy-start.15 = (f32[128,48]{0,1:T(8,128)}, f32[128,48]{0,1:T(8,128)S(1)}, u32[]{:S(2)}) copy-start(f32[128,48]{0,1:T(8,128)S(1)} %get-tuple-element.53) | copy-start | bytes 73732
  201.5 4.0 %copy-start.17 = (f32[128,48]{0,1:T(8,128)}, f32[128,48]{0,1:T(8,128)S(1)}, u32[]{:S(2)}) copy-start(f32[128,48]{0,1:T(8,128)S(1)} %get-tuple-element.54) | copy-start | bytes 73732
  204.1 2.0 copy-start.11
  204.2 2.0 copy-start.14
  207.3 3.2 copy-start.23
  207.5 4.8 %copy-start.21 = (bf16[1,256,384]{1,2,0:T(8,128)(2,1)}, bf16[1,256,384]{1,2,0:T(8,128)(2,1)S(1)}, u32[]{:S(2)}) copy-start(bf16[1,256,384]{1,2,0:T(8,128)(2,1)S(1)} %copy.28) | copy-start | bytes 589828
  207.6 4.6 %copy-start.19 = (bf16[1,256,384]{1,2,0:T(8,128)(2,1)}, bf16[1,256,384]{1,2,0:T(8,128)(2,1)S(1)}, u32[]{:S(2)}) copy-start(bf16[1,256,384]{1,2,0:T(8,128)(2,1)S(1)} %copy.26) | copy-start | bytes 589828
  212.2 0.7 copy-start.25
  302.2 8.3 %copy-start.1 = (bf16[4096,1536]{1,0:T(8,128)(2,1)S(1)}, bf16[4096,1536]{1,0:T(8,128)(2,1)}, u32[]{:S(2)}) copy-start(bf16[4096,1536]{1,0:T(8,128)(2,1)} %all-gather.2.cloned.1.call-done) | copy-start | bytes 37748740
  302.2 8.3 %copy-start.28 = (bf16[1536,128]{1,0:T(8,128)(2,1)S(1)}, bf16[1536,128]{1,0:T(8,128)(2,1)}, u32[]{:S(2)}) copy-start(bf16[1536,128]{1,0:T(8,128)(2,1)} %param.27) | copy-start | bytes 1179652
  310.5 11.4 %copy-start.27 = (s32[32]{0:T(128)S(1)}, s32[32]{0:T(128)}, u32[]{:S(2)}) copy-start(s32[32]{0:T(128)} %constant.58.clone) | copy-start | bytes 388
  315.1 34.7 %all-to-all-start = ((bf16[32,128,128]{2,1,0:T(8,128)(2,1)}), bf16[32,128,128]{2,1,0:T(8,128)(2,1)}, u32[]{:S(2)}, u32[]{:S(2)}) async-start(bf16[32,128,128]{2,1,0:T(8,128)(2,1)} %bitcast.160), calls=%async_computation | async-start | bytes 2097152 | tf_op jit(solution)/shard_map/all_to_all | solution.py:90
  352.6 8.4 %copy-start.26 = (pred[128]{0:T(512)(128)(4,1)S(1)}, pred[128]{0:T(512)(128)(4,1)}, u32[]{:S(2)}) copy-start(pred[128]{0:T(512)(128)(4,1)} %compare_bitcast_fusion) | copy-start | bytes 388
  361.1 2.0 copy-start.3
  361.4 0.9 copy-start.4
  361.4 2.7 copy-start.9
  363.0 1.7 copy-start.12
  364.1 1.0 copy-start.16
  364.1 1.0 copy-start.18
  364.1 1.3 copy-start.22
  364.1 1.3 copy-start.30
  365.2 2.1 copy-start.20
  367.3 1.8 copy-start.5
Sparse Core Ops, SparseCore 0:
  220.0 82.1 all-gather.1

commit v7 on v5

--- a/solution.py
+++ b/solution.py
@@ -1,10 +1,14 @@
 import jax
 import jax.numpy as jnp
 from jax import lax
-from jax.sharding import PartitionSpec as P
+from jax.sharding import Mesh, PartitionSpec as P
 
 HEAD = 96
 
+
+REQ = "req"
+BLK = "blk"
+BLK_PARTS = None
 
 norm_eps = 1e-05
 rope_base = 100000.0
@@ -82,12 +86,23 @@
     return widened + jnp.dot(context, o_weight, preferred_element_type=jnp.float32)
 
 
+def return_hidden(hidden_all):
+    if BLK_PARTS is None:
+        return lax.all_to_all(hidden_all, BLK, 0, 1, tiled=True)
+    sizes = [lax.psum(1, name) for name in BLK_PARTS]
+    rows, units = hidden_all.shape[0] // (sizes[0] * sizes[1] * sizes[2]), hidden_all.shape[1]
+    parts = hidden_all.reshape(sizes[0], sizes[1], sizes[2], rows, units)
+    for axis in (2, 1, 0):
+        parts = lax.all_to_all(parts, BLK_PARTS[axis], axis, axis, tiled=True)
+    return parts.reshape(-1, rows, units).transpose(1, 0, 2).reshape(rows, -1)
+
+
 def run_ffn(normed_rows, w_gate, w_up, down_all, groups):
-    part_rows = lax.all_gather(normed_rows, "blk", axis=0, tiled=True)
+    part_rows = lax.all_gather(normed_rows, BLK, axis=0, tiled=True)
     gate_vals = jnp.dot(part_rows, w_gate, preferred_element_type=jnp.float32)
     up_vals = jnp.dot(part_rows, w_up, preferred_element_type=jnp.float32)
     hidden_all = (jax.nn.silu(gate_vals) * up_vals).astype(jnp.bfloat16)
-    hidden_own = lax.all_to_all(hidden_all, "blk", 0, 1, tiled=True)
+    hidden_own = return_hidden(hidden_all)
     group_count = down_all.shape[0] // groups
     terms = jnp.einsum(
         "rgk,gkd->grd",
@@ -99,15 +114,15 @@
 
 
 def fetch_slot(cache_kv, holder):
-    count = lax.axis_size("req")
+    count = lax.psum(1, REQ)
     own = cache_kv[0]
     if count != 8:
-        slots = lax.all_gather(own, "req", axis=0, tiled=False)
+        slots = lax.all_gather(own, REQ, axis=0, tiled=False)
         return slots[holder[0]]
-    me = lax.axis_index("req")
+    me = lax.axis_index(REQ)
 
     def swap(values, mask):
-        return lax.ppermute(values, "req", perm=[(i, i ^ mask) for i in range(count)])
+        return lax.ppermute(values, REQ, perm=[(i, i ^ mask) for i in range(count)])
 
     def pick(cond, a, b):
         return jnp.where(cond, a, b)
@@ -148,7 +163,7 @@
     w_down,
 ):
     fetched = fetch_slot(cache_kv, holder)
-    down_all = lax.all_gather(w_down, "blk", axis=0, tiled=True)
+    down_all = lax.all_gather(w_down, BLK, axis=0, tiled=True)
     cache_keys = fetched[0]
     cache_vals = fetched[1]
     cache_length = cache_len[0]
@@ -186,25 +201,30 @@
 
 
 def solution(mesh):
+    global REQ, BLK, BLK_PARTS
+    if dict(mesh.shape) == {"req": 8, "blk": 32}:
+        mesh = Mesh(mesh.devices.reshape(4, 2, 4, 4, 2), ("x", "zh", "y", "zl", "c"))
+        REQ, BLK, BLK_PARTS = ("x", "zh"), ("y", "zl", "c"), ("y", "zl", "c")
+    rows = REQ + BLK if isinstance(REQ, tuple) else (REQ, BLK)
     return jax.shard_map(
         local,
         mesh=mesh,
         in_specs=(
-            P(("req", "blk"), None, None),
-            P(("req", "blk"), None, None, None),
-            P(("req", "blk")),
-            P(("req", "blk")),
-            P(("req", "blk"), None),
-            P(),
-            P(),
-            P(),
-            P(),
-            P(),
-            P(),
-            P(None, "blk"),
-            P(None, "blk"),
-            P("blk", None),
+            P(rows, None, None),
+            P(rows, None, None, None),
+            P(rows),
+            P(rows),
+            P(rows, None),
+            P(),
+            P(),
+            P(),
+            P(),
+            P(),
+            P(),
+            P(None, BLK),
+            P(None, BLK),
+            P(BLK, None),
         ),
-        out_specs=P(("req", "blk"), None, None),
+        out_specs=P(rows, None, None),
         check_vma=False,
     )

time: 268 us -> 282 us (1.052)
  blocking collectives: 0 us -> 33.4 us
  waiting for transfers between devices: 162 us -> 148 us
    all_to_all x0 -> x2, blocking collectives: none -> 33.4 us  [return_hidden(): parts = lax.all_to_all(parts, BLK_PARTS[axis], axis, axis, tiled=True)]
    all_to_all x1, waiting for transfers between devices: 27.9 us -> 13.5 us  [return_hidden(): parts = lax.all_to_all(parts, BLK_PARTS[axis], axis, axis, tiled=True)]
    unnamed x50 -> x54, local copies, waits for them, and re-layouts: 10.4 us -> 10.3 us
  transfers between devices with their start and end apart: 8 -> 8, of which waited for: 6 -> 6; matrix products, arithmetic and copies ran while one was open for 13% -> 12% of each run, Pallas kernels for 0% -> 0%
where the time goes in v7:
time: 282 us; the launch traced here: 281 us
  waiting for transfers between devices  148 us (52%)
  matrix products  39.2 us (14%)
  blocking collectives  33.4 us (12%)
  between operations  17.6 us (6%)
  starting transfers between devices  15.5 us (5%)
  local copies, waits for them, and re-layouts  14.3 us (5%)
  other arithmetic  12.9 us (5%)
    all_gather x1, waiting for transfers between devices, run_ffn(): part_rows = lax.all_gather(normed_rows, BLK, axis=0, tiled=True)  80.7 us
    ppermute x5, waiting for transfers between devices, swap(): return lax.ppermute(values, REQ, perm=[(i, i ^ mask) for i in range(count)])  35.1 us
    all_to_all x2, blocking collectives, return_hidden(): parts = lax.all_to_all(parts, BLK_PARTS[axis], axis, axis, tiled=True)  33.4 us
    all_gather x1, waiting for transfers between devices, local(): down_all = lax.all_gather(w_down, BLK, axis=0, tiled=True)  17.8 us
    all_to_all x1, waiting for transfers between devices, return_hidden(): parts = lax.all_to_all(parts, BLK_PARTS[axis], axis, axis, tiled=True)  13.5 us
    ppermute x5, starting transfers between devices, swap(): return lax.ppermute(values, REQ, perm=[(i, i ^ mask) for i in range(count)])  10.8 us
    unnamed x54, local copies, waits for them, and re-layouts  10.3 us
    dot_general x1, matrix products, run_ffn(): jnp.einsum('rgk,gkd->grd', hidden_own.reshape(hidden_own.shape[0], group_...  8.34 us
  transfers between devices with their start and end apart: 8, of which 6 were waited for; matrix products, arithmetic and copies ran while one was open for 12% of the time, Pallas kernels for 0%

profile of v7, /device:TPU:1, one launch (start us, length us, event | category | flops | bytes accessed | tf_op | source)
XLA Modules:
  0.0 280.6 jit_solution(3372209594726545814)
XLA Ops:
  6.5 0.7 all-gather.3.cloned.1.call-update
  7.3 7.8 %collective-permute-start.1 = (s32[1]{0:T(128)}, s32[1]{0:T(128)}, u32[]{:S(2)}, u32[]{:S(2)}) collective-permute-start(s32[1]{0:T(128)} %param.17), channel_id=1, source_target_pairs={{0,32},{32,0},{64,96},{96,64},{128,160},{160,128},{192,224},{224,1... | collective-permute-start | bytes 20 | tf_op jit(solution)/shard_map/ppermute | solution.py:125
  15.1 2.7 collective-permute-start
  19.2 4.3 %copy.52 = bf16[1536,768]{0,1:T(8,128)(2,1)} copy(bf16[1536,768]{1,0:T(8,128)(2,1)} %param.20) | data formatting | bytes 4718592 | tf_op args[6]
  23.7 3.5 %fusion.54 = f32[128,8,96]{0,2,1:T(8,128)} fusion(bf16[8,96,1536]{2,1,0:T(8,128)(2,1)} %bitcast.155, bf16[1,128,1536]{2,1,0:T(8,128)(2,1)S(1)} %copy-done.2, f32[1536]{0:T(1024)S(1)} %copy-done.17, f32[128]{0:T(128)S(1)} %add_rsqrt_fusion.2), kind=kOutput, calls=%fused_computation.74 | convolution fusion | flops 302776320 | bytes 3152384 | tf_op jit(solution)/shard_map/dot_general | solution.py:58
  27.2 0.6 add_convert_fusion.4
  27.8 0.7 pad_add_fusion
  28.7 2.7 collective-permute-done.2
  31.4 0.6 fusion.76
  33.4 1.0 pad_maximum_fusion
  34.5 0.8 multiply_cosine_fusion
  35.3 2.5 copy.51
  37.8 1.9 subtract_convert_fusion.1
  39.6 2.4 convolution_convert_fusion.4
  42.0 1.2 fusion.56
  44.4 7.3 %collective-permute-done.3 = bf16[2,2,256,384]{3,2,1,0:T(8,128)(2,1)} collective-permute-done((bf16[2,2,256,384]{3,2,1,0:T(8,128)(2,1)}, bf16[2,2,256,384]{3,2,1,0:T(8,128)(2,1)}, u32[]{:S(2)}, u32[]{:S(2)}) %collective-permute-start.3) | collective-permute-done | bytes 786464 | tf_op jit(solution)/shard_map/ppermute | solution.py:125
  51.7 1.8 fusion.27
  53.5 1.6 copy.49
  55.2 1.6 pad_maximum_fusion.5
  56.8 1.6 subtract_convert_fusion.3
  58.4 25.2 %collective-permute-done.4 = bf16[2,256,384]{2,1,0:T(8,128)(2,1)} collective-permute-done((bf16[2,256,384]{2,1,0:T(8,128)(2,1)}, bf16[2,256,384]{2,1,0:T(8,128)(2,1)}, u32[]{:S(2)}, u32[]{:S(2)}) %collective-permute-start.4) | collective-permute-done | bytes 393248 | tf_op jit(solution)/shard_map/ppermute | solution.py:125
  83.6 1.2 fusion.23
  85.2 0.4 copy-done.18
  85.6 2.8 fusion.77
  88.4 1.7 convolution_convert_fusion.2
  90.2 0.6 multiply_reduce_fusion.1
  90.9 0.9 multiply_convert_fusion.1
  91.7 17.8 %all-gather.3.cloned.1.call-done = bf16[4096,1536]{1,0:T(8,128)(2,1)} async-done(((bf16[128,1536]{1,0:T(8,128)(2,1)}), bf16[4096,1536]{1,0:T(8,128)(2,1)}) %all-gather.3.cloned.1.call-update) | async-done | bytes 12582928 | tf_op jit(solution)/shard_map/all_gather | solution.py:166
  109.5 80.7 %all-gather.5.cloned.1.call-done = bf16[4096,1536]{1,0:T(8,128)(2,1)} async-done(((bf16[128,1536]{1,0:T(8,128)(2,1)}), bf16[4096,1536]{1,0:T(8,128)(2,1)}) %all-gather.5.cloned.1.call-update) | async-done | bytes 12582928 | tf_op jit(solution)/shard_map/all_gather | solution.py:101
  190.2 8.0 %fusion.83 = f32[4096,128]{1,0:T(8,128)S(1)} fusion(bf16[4096,1536]{1,0:T(8,128)(2,1)} %all-gather.5.cloned.1.call-done, bf16[1536,128]{1,0:T(8,128)(2,1)} %param.25), kind=kOutput, calls=%fused_computation.104 | convolution fusion | flops 1610612736 | bytes 15073280 | tf_op jit(solution)/shard_map/dot_general | solution.py:102
  198.2 0.3 copy-done.1
  198.5 3.7 %fusion.2 = bf16[4096,128]{1,0:T(8,128)(2,1)S(1)} fusion(bf16[4096,1536]{1,0:T(8,128)(2,1)S(1)} %copy-done.1, bf16[1536,128]{1,0:T(8,128)(2,1)S(1)} %copy-done.22, f32[4096,128]{1,0:T(8,128)S(1)} %fusion.83), kind=kOutput, calls=%fused_computation.5 | convolution fusion | flops 1613758464 | bytes 16121856 | tf_op jit(solution)/shard_map/dot_general | solution.py:103
  202.2 4.5 %all_to_all.15 = bf16[4,4,2,128,128]{4,3,1,0,2:T(8,128)(2,1)S(1)} all-to-all(bf16[4,4,2,128,128]{4,3,1,0,2:T(8,128)(2,1)S(1)} %copy.54), channel_id=1, replica_groups=mesh['x'=4,'zh'=2,'y'=4,'zl'=4,'c'=2] {'c'}, dimensions={2} | all-to-all | bytes 2097152 | tf_op jit(solution)/shard_map/all_to_all | solution.py:96
  206.8 28.9 %all_to_all.16 = bf16[4,4,2,128,128]{4,3,2,0,1:T(8,128)(2,1)S(1)} all-to-all(bf16[4,4,2,128,128]{4,3,2,0,1:T(8,128)(2,1)S(1)} %copy.55), channel_id=1, replica_groups=mesh['x'=4,'zh'=2,'y'=4,'zl'=4,'c'=2] {'zl'}, dimensions={1} | all-to-all | bytes 2097152 | tf_op jit(solution)/shard_map/all_to_all | solution.py:96
  235.7 1.0 copy.56
  236.8 4.6 %all-to-all-start.2 = ((bf16[4,4,2,128,128]{4,3,2,1,0:T(8,128)(2,1)}), bf16[4,4,2,128,128]{4,3,2,1,0:T(8,128)(2,1)}, u32[]{:S(2)}, u32[]{:S(2)}) async-start(bf16[4,4,2,128,128]{4,3,2,1,0:T(8,128)(2,1)} %copy.56), calls=%async_computation.2 | async-start | bytes 2097152 | tf_op jit(solution)/shard_map/all_to_all | solution.py:96
  241.4 13.5 %all-to-all-done.2 = bf16[4,4,2,128,128]{4,3,2,1,0:T(8,128)(2,1)} async-done(((bf16[4,4,2,128,128]{4,3,2,1,0:T(8,128)(2,1)}), bf16[4,4,2,128,128]{4,3,2,1,0:T(8,128)(2,1)}, u32[]{:S(2)}, u32[]{:S(2)}) %all-to-all-start.2) | async-done | bytes 1048608 | tf_op jit(solution)/shard_map/all_to_all | solution.py:96
  254.9 8.3 %convert_reduce_fusion = f32[128,1536]{1,0:T(8,128)S(1)} fusion(bf16[128,32,128]{2,0,1:T(8,128)(2,1)} %bitcast.31, bf16[32,128,1536]{2,1,0:T(8,128)(2,1)} %bitcast.154), kind=kOutput, calls=%fused_computation.2 | convolution fusion | flops 1629290496 | bytes 14417920 | tf_op jit(solution)/shard_map/rgk,gkd->grd/dot_general | solution.py:107
  263.3 0.3 multiply_reduce_fusion
  263.6 0.9 copy-done.4
  264.7 0.6 copy-done.3
  265.2 1.0 fusion.85
  266.5 0.6 fusion.84
  267.1 0.7 copy-done.9
  267.8 0.4 convolution_convert_fusion.3
  268.7 1.8 fusion.80
  270.6 1.8 convolution_convert_fusion.1
  272.3 1.4 fusion.3
  (74 shorter events, 2.1 us)
Async XLA Ops:
  6.5 83.6 %copy-start = (bf16[768,1536]{1,0:T(8,128)(2,1)S(1)}, bf16[768,1536]{1,0:T(8,128)(2,1)}, u32[]{:S(2)}) copy-start(bf16[768,1536]{1,0:T(8,128)(2,1)} %param.23) | copy-start | bytes 7077892
  6.5 103.0 %all-gather.3.cloned.1.call-start = ((), (), s32[]{:S(2)}) async-start(), calls=%async_computation.3 | async-start | bytes 12976128 | tf_op jit(solution)/shard_map/all_gather | solution.py:166
  7.3 182.9 %all-gather.5.cloned.1.call-start = ((), (), s32[]{:S(2)}) async-start(), calls=%async_computation.4 | async-start | bytes 12976128 | tf_op jit(solution)/shard_map/all_gather | solution.py:101
  7.3 20.5 %collective-permute-start.1 = (s32[1]{0:T(128)}, s32[1]{0:T(128)}, u32[]{:S(2)}, u32[]{:S(2)}) collective-permute-start(s32[1]{0:T(128)} %param.17), channel_id=1, source_target_pairs={{0,32},{32,0},{64,96},{96,64},{128,160},{160,128},{192,224},{224,1... | collective-permute-start | bytes 20 | tf_op jit(solution)/shard_map/ppermute | solution.py:125
  15.1 18.2 %collective-permute-start = (bf16[2,256,384]{2,1,0:T(8,128)(2,1)}, bf16[2,256,384]{2,1,0:T(8,128)(2,1)S(1)}, u32[]{:S(2)}, u32[]{:S(2)}) collective-permute-start(bf16[2,256,384]{2,1,0:T(8,128)(2,1)} %bitcast.157), channel_id=1, source_target_pairs={{0,128},{32,160},{64,192},{96,224},{128,0},{160,32},{192,64},{224,... | collective-permute-start | bytes 1179656 | tf_op jit(solution)/shard_map/ppermute | solution.py:125
  19.2 4.4 %copy-start.2 = (bf16[1,128,1536]{2,1,0:T(8,128)(2,1)S(1)}, bf16[1,128,1536]{2,1,0:T(8,128)(2,1)}, u32[]{:S(2)}) copy-start(bf16[1,128,1536]{2,1,0:T(8,128)(2,1)} %param.14) | copy-start | bytes 1179652
  19.2 4.5 %copy-start.17 = (f32[1536]{0:T(1024)S(1)}, f32[1536]{0:T(1024)}, u32[]{:S(2)}) copy-start(f32[1536]{0:T(1024)} %param.19) | copy-start | bytes 18436
  23.7 9.6 %copy-start.8 = (bf16[1,2,256,384]{3,2,1,0:T(8,128)(2,1)S(1)}, bf16[1,2,256,384]{3,2,1,0:T(8,128)(2,1)}, u32[]{:S(2)}) copy-start(bf16[1,2,256,384]{3,2,1,0:T(8,128)(2,1)} %param.15) | copy-start | bytes 1179652
  28.5 2.8 %collective-permute-start.2 = (s32[2]{0:T(128)S(1)}, s32[2]{0:T(128)S(1)}, u32[]{:S(2)}, u32[]{:S(2)}) collective-permute-start(s32[2]{0:T(128)S(1)} %pad_add_fusion), channel_id=1, source_target_pairs={{0,64},{32,96},{64,0},{96,32},{128,192},{160,224},{192,128},{224,1... | collective-permute-start | bytes 32 | tf_op jit(solution)/shard_map/ppermute | solution.py:125
  33.3 1.2 copy-start.21
  34.4 17.3 %collective-permute-start.3 = (bf16[2,2,256,384]{3,2,1,0:T(8,128)(2,1)}, bf16[2,2,256,384]{3,2,1,0:T(8,128)(2,1)}, u32[]{:S(2)}, u32[]{:S(2)}) collective-permute-start(bf16[2,2,256,384]{3,2,1,0:T(8,128)(2,1)} %pad_maximum_fusion), channel_id=1, source_target_pairs={{0,64},{32,96},{64,0},{96,32},{128,192},{160,224},{192,128},{224,1... | collective-permute-start | bytes 2359304 | tf_op jit(solution)/shard_map/ppermute | solution.py:125
  37.8 4.2 %copy-start.7 = (bf16[1536,384]{0,1:T(8,128)(2,1)S(1)}, bf16[1536,384]{0,1:T(8,128)(2,1)}, u32[]{:S(2)}) copy-start(bf16[1536,384]{0,1:T(8,128)(2,1)} %copy.51) | copy-start | bytes 3538948
  53.5 30.1 %collective-permute-start.4 = (bf16[2,256,384]{2,1,0:T(8,128)(2,1)}, bf16[2,256,384]{2,1,0:T(8,128)(2,1)}, u32[]{:S(2)}, u32[]{:S(2)}) collective-permute-start(bf16[2,256,384]{2,1,0:T(8,128)(2,1)} %fusion.27), channel_id=1, source_target_pairs={{0,32},{32,0},{64,96},{96,64},{128,160},{160,128},{192,224},{224,1... | collective-permute-start | bytes 1179656 | tf_op jit(solution)/shard_map/ppermute | solution.py:125
  55.2 30.0 %copy-start.24 = (pred[384]{0:T(512)(128)(4,1)}, pred[384]{0:T(512)(128)(4,1)S(1)}, u32[]{:S(2)}) copy-start(pred[384]{0:T(512)(128)(4,1)S(1)} %concatenate.51) | copy-start | bytes 1156
  84.8 0.8 copy-start.18
  84.8 0.8 copy-start.19
  85.0 3.4 %copy-start.14 = (bf16[1,256,384]{1,2,0:T(8,128)(2,1)}, bf16[1,256,384]{1,2,0:T(8,128)(2,1)S(1)}, u32[]{:S(2)}) copy-start(bf16[1,256,384]{1,2,0:T(8,128)(2,1)S(1)} %copy.50) | copy-start | bytes 589828
  85.2 3.2 %copy-start.12 = (bf16[1,256,384]{1,2,0:T(8,128)(2,1)}, bf16[1,256,384]{1,2,0:T(8,128)(2,1)S(1)}, u32[]{:S(2)}) copy-start(bf16[1,256,384]{1,2,0:T(8,128)(2,1)S(1)} %copy.48) | copy-start | bytes 589828
  85.6 2.8 copy-start.16
  90.2 0.7 copy-start.20
  190.2 8.3 %copy-start.1 = (bf16[4096,1536]{1,0:T(8,128)(2,1)S(1)}, bf16[4096,1536]{1,0:T(8,128)(2,1)}, u32[]{:S(2)}) copy-start(bf16[4096,1536]{1,0:T(8,128)(2,1)} %all-gather.5.cloned.1.call-done) | copy-start | bytes 37748740
  190.2 8.3 %copy-start.22 = (bf16[1536,128]{1,0:T(8,128)(2,1)S(1)}, bf16[1536,128]{1,0:T(8,128)(2,1)}, u32[]{:S(2)}) copy-start(bf16[1536,128]{1,0:T(8,128)(2,1)} %param.26) | copy-start | bytes 1179652
  236.8 4.6 %copy-start.23 = (s32[1,128]{1,0:T(1,128)S(1)}, s32[1,128]{1,0:T(1,128)}, u32[]{:S(2)}) copy-start(s32[1,128]{1,0:T(1,128)} %param.18) | copy-start | bytes 1540
  236.8 18.2 %all-to-all-start.2 = ((bf16[4,4,2,128,128]{4,3,2,1,0:T(8,128)(2,1)}), bf16[4,4,2,128,128]{4,3,2,1,0:T(8,128)(2,1)}, u32[]{:S(2)}, u32[]{:S(2)}) async-start(bf16[4,4,2,128,128]{4,3,2,1,0:T(8,128)(2,1)} %copy.56), calls=%async_computation.2 | async-start | bytes 2097152 | tf_op jit(solution)/shard_map/all_to_all | solution.py:96
  263.3 2.0 copy-start.3
  263.6 0.9 copy-start.4
  265.2 1.3 copy-start.6
  266.5 1.3 copy-start.9
  266.5 1.7 copy-start.10
  266.5 1.7 copy-start.11
  267.8 0.9 copy-start.15
  267.8 0.9 copy-start.25
  268.7 1.8 copy-start.13
  270.6 1.8 copy-start.5
Sparse Core Ops, SparseCore 0:
  9.2 100.2 all-gather.2
  111.4 78.7 all-gather.4

commit v8 on v5

--- a/solution.py
+++ b/solution.py
@@ -165,10 +165,15 @@
         o_weight,
     )
     chosen_mask = accept[0] == 1
-    ffn_rows, down_all = lax.optimization_barrier(
-        (rms_scale(first_pass, ffn_gain).astype(jnp.bfloat16), down_all)
-    )
-    ffn_sum = run_ffn(ffn_rows, w_gate, w_up, down_all, w_down.shape[0])
+    block_len = block_rows.shape[0]
+    kept = block_len // 2
+    slot_of = jnp.cumsum(chosen_mask.astype(jnp.int32)) - 1
+    hits = chosen_mask[None, :] & (slot_of[None, :] == jnp.arange(kept, dtype=jnp.int32)[:, None])
+    kept_rows = jnp.sum(jnp.where(hits, jnp.arange(block_len, dtype=jnp.int32)[None, :], 0), axis=1)
+    fnorm = rms_scale(first_pass, ffn_gain).astype(jnp.bfloat16)
+    ffn_rows, down_all = lax.optimization_barrier((fnorm[kept_rows], down_all))
+    ffn_kept = run_ffn(ffn_rows, w_gate, w_up, down_all, w_down.shape[0])
+    ffn_sum = ffn_kept[jnp.clip(slot_of, 0, kept - 1)]
     placed = first_pass + ffn_sum
     second_in = jnp.where(chosen_mask[:, None], placed, block_rows.astype(jnp.float32))
     refined = attend_block(

time: 268 us -> 239 us (0.89)
  waiting for transfers between devices: 162 us -> 133 us
  matrix products: 41.9 us -> 34.7 us
  local copies, waits for them, and re-layouts: 14.6 us -> 18.8 us
    all_gather x1, waiting for transfers between devices: 80.5 us -> 67.7 us  [run_ffn(): part_rows = lax.all_gather(normed_rows, 'blk', axis=0, tiled=True)]
    all_to_all x1, waiting for transfers between devices: 27.9 us -> 16.8 us  [run_ffn(): hidden_own = lax.all_to_all(hidden_all, 'blk', 0, 1, tiled=True)]
    dot_general x1, matrix products: 7.95 us -> 4.73 us  [run_ffn(): gate_vals = jnp.dot(part_rows, w_gate, preferred_element_type=jnp.float32)]
    gather x0 -> x2, local copies, waits for them, and re-layouts: none -> 3.14 us  [the longest x1 1.74 us: local(): ffn_sum = ffn_kept[jnp.clip(slot_of, 0, kept - 1)]]
    unnamed x50 -> x60, local copies, waits for them, and re-layouts: 10.4 us -> 10.1 us
  transfers between devices with their start and end apart: 8 -> 8, of which waited for: 6 -> 6; matrix products, arithmetic and copies ran while one was open for 13% -> 15% of each run, Pallas kernels for 0% -> 0%
where the time goes in v8:
time: 239 us; the launch traced here: 238 us
  waiting for transfers between devices  133 us (56%)
  matrix products  34.7 us (15%)
  local copies, waits for them, and re-layouts  18.8 us (8%)
  between operations  17.7 us (7%)
  starting transfers between devices  17.5 us (7%)
  other arithmetic  16 us (7%)
    all_gather x1, waiting for transfers between devices, run_ffn(): part_rows = lax.all_gather(normed_rows, 'blk', axis=0, tiled=True)  67.7 us
    ppermute x5, waiting for transfers between devices, swap(): lax.ppermute(values, 'req', perm=[(i, i ^ mask) for i in range(count)])  33 us
    all_to_all x1, waiting for transfers between devices, run_ffn(): hidden_own = lax.all_to_all(hidden_all, 'blk', 0, 1, tiled=True)  16.8 us
    all_gather x1, waiting for transfers between devices, local(): down_all = lax.all_gather(w_down, 'blk', axis=0, tiled=True)  15 us
    ppermute x5, starting transfers between devices, swap(): lax.ppermute(values, 'req', perm=[(i, i ^ mask) for i in range(count)])  12 us
    unnamed x60, local copies, waits for them, and re-layouts  10.1 us
    dot_general x1, matrix products, run_ffn(): jnp.einsum('rgk,gkd->grd', hidden_own.reshape(hidden_own.shape[0], group_...  6.58 us
    sub x2, matrix products, attend_block(): expd = jnp.exp(scores - peaks)  5.73 us
  transfers between devices with their start and end apart: 8, of which 6 were waited for; matrix products, arithmetic and copies ran while one was open for 15% of the time, Pallas kernels for 0%

profile of v8, /device:TPU:1, one launch (start us, length us, event | category | flops | bytes accessed | tf_op | source)
XLA Modules:
  0.0 237.9 jit_solution(3644035282979284593)
XLA Ops:
  6.5 0.7 all-gather.3.cloned.1.call-update
  7.3 3.7 %collective-permute-start = (bf16[2,256,384]{2,1,0:T(8,128)(2,1)}, bf16[2,256,384]{2,1,0:T(8,128)(2,1)S(1)}, u32[]{:S(2)}, u32[]{:S(2)}) collective-permute-start(bf16[2,256,384]{2,1,0:T(8,128)(2,1)} %bitcast.162), channel_id=1, source_target_pairs={{0,128},{32,160},{64,192},{96,224},{128,0},{160,32},{192,64},{224,... | collective-permute-start | bytes 1179656 | tf_op jit(solution)/shard_map/ppermute | solution.py:110
  11.0 6.9 %collective-permute-start.1 = (s32[1]{0:T(128)}, s32[1]{0:T(128)}, u32[]{:S(2)}, u32[]{:S(2)}) collective-permute-start(s32[1]{0:T(128)} %param.17), channel_id=1, source_target_pairs={{0,32},{32,0},{64,96},{96,64},{128,160},{160,128},{192,224},{224,1... | collective-permute-start | bytes 20 | tf_op jit(solution)/shard_map/ppermute | solution.py:110
  18.6 4.3 %copy.41 = bf16[1536,768]{0,1:T(8,128)(2,1)} copy(bf16[1536,768]{1,0:T(8,128)(2,1)} %param.20) | data formatting | bytes 4718592 | tf_op args[6]
  24.3 0.8 multiply_cosine_fusion
  25.1 3.3 %fusion.55 = f32[128,8,96]{0,2,1:T(8,128)} fusion(bf16[8,96,1536]{2,1,0:T(8,128)(2,1)} %bitcast.160, bf16[1,128,1536]{2,1,0:T(8,128)(2,1)S(1)} %copy-done.2, f32[1536]{0:T(1024)S(1)} %copy-done.17, f32[128]{0:T(128)S(1)} %add_rsqrt_fusion.2), kind=kOutput, calls=%fused_computation.77 | convolution fusion | flops 302776320 | bytes 3152384 | tf_op jit(solution)/shard_map/dot_general | solution.py:54
  29.0 0.7 pad_add_fusion
  29.7 0.6 collective-permute-start.2
  30.3 2.2 collective-permute-done.2
  32.6 0.6 fusion.81
  34.6 1.0 pad_maximum_fusion
  36.2 2.4 %copy.40 = bf16[1536,384]{0,1:T(8,128)(2,1)} copy(bf16[1536,384]{1,0:T(8,128)(2,1)} %param.21) | data formatting | bytes 2359296 | tf_op args[7]
  38.6 1.9 subtract_convert_fusion.1
  40.5 2.4 %convolution_convert_fusion.3 = bf16[128,384]{1,0:T(8,128)(2,1)} fusion(bf16[1536,384]{1,0:T(8,128)(2,1)} %param.22, bf16[1,128,1536]{2,1,0:T(8,128)(2,1)S(1)} %copy-done.2, f32[1536]{0:T(1024)S(1)} %copy-done.17, f32[128]{0:T(128)} %copy-done.21), kind=kOutput, calls=%fused_computation.25 | convolution fusion | flops 151830528 | bytes 1677824 | tf_op jit(solution)/shard_map/dot_general | solution.py:59
  42.9 1.2 fusion.57
  45.4 7.6 %collective-permute-done.3 = bf16[2,2,256,384]{3,2,1,0:T(8,128)(2,1)} collective-permute-done((bf16[2,2,256,384]{3,2,1,0:T(8,128)(2,1)}, bf16[2,2,256,384]{3,2,1,0:T(8,128)(2,1)}, u32[]{:S(2)}, u32[]{:S(2)}) %collective-permute-start.3) | collective-permute-done | bytes 786464 | tf_op jit(solution)/shard_map/ppermute | solution.py:110
  53.0 1.8 fusion.28
  55.1 0.6 iota_compare_fusion.1
  55.7 1.6 copy.38
  57.3 1.2 concatenate.51
  58.5 1.6 pad_maximum_fusion.5
  60.2 1.6 subtract_convert_fusion.3
  61.8 23.2 %collective-permute-done.4 = bf16[2,256,384]{2,1,0:T(8,128)(2,1)} collective-permute-done((bf16[2,256,384]{2,1,0:T(8,128)(2,1)}, bf16[2,256,384]{2,1,0:T(8,128)(2,1)}, u32[]{:S(2)}, u32[]{:S(2)}) %collective-permute-start.4) | collective-permute-done | bytes 393248 | tf_op jit(solution)/shard_map/ppermute | solution.py:110
  85.0 1.2 fusion.24
  87.0 2.8 %fusion.82 = (f32[4,2,128]{2,1,0:T(2,128)S(1)}, f32[4,2,128,384]{2,3,1,0:T(8,128)}) fusion(bf16[128,4,2,96]{0,3,2,1:T(8,128)(2,1)} %bitcast.172, bf16[256,4,96]{0,2,1:T(8,128)(2,1)S(1)} %bitcast.170, bf16[128,4,48]{0,2,1:T(8,128)(2,1)S(1)} %copy-done.19, bf16[128,4,48]{0,2,1:T(8,128)(2,1)S(1)} %copy-done.18, pred[384]{0:T(512)(128)(4,1)} %concatenate.51), kind=kOutput, calls=%fused_computation.116 | convolution fusion | flops 77955456 | bytes 2068864 | tf_op jit(solution)/shard_map/sub | solution.py:78
  89.9 1.7 convolution_convert_fusion.1
  92.2 0.9 copy-done.4
  93.2 1.4 gather_fusion
  94.6 15.0 %all-gather.3.cloned.1.call-done = bf16[4096,1536]{1,0:T(8,128)(2,1)} async-done(((bf16[128,1536]{1,0:T(8,128)(2,1)}), bf16[4096,1536]{1,0:T(8,128)(2,1)}) %all-gather.3.cloned.1.call-update) | async-done | bytes 12582928 | tf_op jit(solution)/shard_map/all_gather | solution.py:151
  109.6 67.7 %all-gather.5.cloned.1.call-done = bf16[2048,1536]{1,0:T(8,128)(2,1)} async-done(((bf16[64,1536]{1,0:T(8,128)(2,1)}), bf16[2048,1536]{1,0:T(8,128)(2,1)}) %all-gather.5.cloned.1.call-update) | async-done | bytes 6291472 | tf_op jit(solution)/shard_map/all_gather | solution.py:86
  177.3 4.7 %fusion.88 = f32[2048,128]{1,0:T(8,128)S(1)} fusion(bf16[2048,1536]{1,0:T(8,128)(2,1)} %all-gather.5.cloned.1.call-done, bf16[1536,128]{1,0:T(8,128)(2,1)S(1)} %copy-done.12), kind=kOutput, calls=%fused_computation.118 | convolution fusion | flops 805306368 | bytes 7733248 | tf_op jit(solution)/shard_map/dot_general | solution.py:87
  182.1 2.7 %fusion.3 = bf16[2048,128]{1,0:T(8,128)(2,1)} fusion(bf16[2048,1536]{1,0:T(8,128)(2,1)S(1)} %copy-done.1, bf16[1536,128]{1,0:T(8,128)(2,1)S(1)} %copy-done.26, f32[2048,128]{1,0:T(8,128)S(1)} %fusion.88), kind=kOutput, calls=%fused_computation.9 | convolution fusion | flops 806879232 | bytes 8257536 | tf_op jit(solution)/shard_map/dot_general | solution.py:88
  184.8 5.5 %all-to-all-start = ((bf16[32,64,128]{2,1,0:T(8,128)(2,1)}), bf16[32,64,128]{2,1,0:T(8,128)(2,1)S(1)}, u32[]{:S(2)}, u32[]{:S(2)}) async-start(bf16[32,64,128]{2,1,0:T(8,128)(2,1)} %bitcast.165), calls=%async_computation | async-start | bytes 1048576 | tf_op jit(solution)/shard_map/all_to_all | solution.py:90
  190.2 16.8 %all-to-all-done = bf16[32,64,128]{2,1,0:T(8,128)(2,1)S(1)} async-done(((bf16[32,64,128]{2,1,0:T(8,128)(2,1)}), bf16[32,64,128]{2,1,0:T(8,128)(2,1)S(1)}, u32[]{:S(2)}, u32[]{:S(2)}) %all-to-all-start) | async-done | bytes 524320 | tf_op jit(solution)/shard_map/all_to_all | solution.py:90
  207.0 0.8 copy-done.8
  207.9 6.6 %convert_reduce_fusion = f32[64,1536]{1,0:T(8,128)S(1)} fusion(bf16[32,128,1536]{2,1,0:T(8,128)(2,1)} %bitcast.159, bf16[32,64,128]{2,1,0:T(8,128)(2,1)} %copy-done.8), kind=kOutput, calls=%fused_computation.4 | convolution fusion | flops 814645248 | bytes 13500416 | tf_op jit(solution)/shard_map/rgk,gkd->grd/dot_general | solution.py:92
  214.4 1.7 gather_fusion.1
  216.2 1.8 multiply_reduce_fusion
  218.3 1.1 fusion.90
  219.6 0.6 fusion.89
  220.2 0.7 copy-done.9
  220.9 1.0 convolution_convert_fusion.2
  222.0 0.7 subtract_convert_fusion.2
  222.6 1.6 copy.44
  224.3 0.7 pad_maximum_fusion.6
  225.0 2.9 %fusion.85 = (f32[4,2,128]{2,1,0:T(2,128)S(1)}, f32[4,2,128,384]{2,3,1,0:T(8,128)}) fusion(bf16[128,4,2,96]{0,3,2,1:T(8,128)(2,1)} %bitcast.173, bf16[256,4,96]{0,2,1:T(8,128)(2,1)} %bitcast.171, bf16[128,4,48]{0,2,1:T(8,128)(2,1)} %get-tuple-element.22, bf16[128,4,48]{0,2,1:T(8,128)(2,1)} %get-tuple-element.21, pred[384]{0:T(512)(128)(4,1)S(1)} %copy-done.28), kind=kOutput, calls=%fused_computation.117 | convolution fusion | flops 77955456 | bytes 2068864 | tf_op jit(solution)/shard_map/sub | solution.py:78
  227.9 1.8 convolution_convert_fusion
  229.7 1.4 fusion.2
  (84 shorter events, 4.4 us)
Async XLA Ops:
  6.5 85.0 %copy-start = (bf16[768,1536]{1,0:T(8,128)(2,1)S(1)}, bf16[768,1536]{1,0:T(8,128)(2,1)}, u32[]{:S(2)}) copy-start(bf16[768,1536]{1,0:T(8,128)(2,1)} %param.23) | copy-start | bytes 7077892
  6.5 103.1 %all-gather.3.cloned.1.call-start = ((), (), s32[]{:S(2)}) async-start(), calls=%async_computation.1 | async-start | bytes 12976128 | tf_op jit(solution)/shard_map/all_gather | solution.py:151
  7.3 170.1 %all-gather.5.cloned.1.call-start = ((), (), s32[]{:S(2)}) async-start(), calls=%async_computation.2 | async-start | bytes 6488064 | tf_op jit(solution)/shard_map/all_gather | solution.py:86
  7.3 27.2 %collective-permute-start = (bf16[2,256,384]{2,1,0:T(8,128)(2,1)}, bf16[2,256,384]{2,1,0:T(8,128)(2,1)S(1)}, u32[]{:S(2)}, u32[]{:S(2)}) collective-permute-start(bf16[2,256,384]{2,1,0:T(8,128)(2,1)} %bitcast.162), channel_id=1, source_target_pairs={{0,128},{32,160},{64,192},{96,224},{128,0},{160,32},{192,64},{224,... | collective-permute-start | bytes 1179656 | tf_op jit(solution)/shard_map/ppermute | solution.py:110
  11.0 18.1 %collective-permute-start.1 = (s32[1]{0:T(128)}, s32[1]{0:T(128)}, u32[]{:S(2)}, u32[]{:S(2)}) collective-permute-start(s32[1]{0:T(128)} %param.17), channel_id=1, source_target_pairs={{0,32},{32,0},{64,96},{96,64},{128,160},{160,128},{192,224},{224,1... | collective-permute-start | bytes 20 | tf_op jit(solution)/shard_map/ppermute | solution.py:110
  18.6 5.0 %copy-start.27 = (s32[1,128]{1,0:T(1,128)S(1)}, s32[1,128]{1,0:T(1,128)}, u32[]{:S(2)}) copy-start(s32[1,128]{1,0:T(1,128)} %param.18) | copy-start | bytes 1540
  18.6 5.6 %copy-start.2 = (bf16[1,128,1536]{2,1,0:T(8,128)(2,1)S(1)}, bf16[1,128,1536]{2,1,0:T(8,128)(2,1)}, u32[]{:S(2)}) copy-start(bf16[1,128,1536]{2,1,0:T(8,128)(2,1)} %param.14) | copy-start | bytes 1179652
  18.6 6.6 %copy-start.17 = (f32[1536]{0:T(1024)S(1)}, f32[1536]{0:T(1024)}, u32[]{:S(2)}) copy-start(f32[1536]{0:T(1024)} %param.19) | copy-start | bytes 18436
  23.6 0.5 copy-start.23
  24.3 4.1 %copy-start.21 = (f32[128]{0:T(128)}, f32[128]{0:T(128)S(1)}, u32[]{:S(2)}) copy-start(f32[128]{0:T(128)S(1)} %add_rsqrt_fusion.2) | copy-start | bytes 1540
  25.1 9.4 %copy-start.7 = (bf16[1,2,256,384]{3,2,1,0:T(8,128)(2,1)S(1)}, bf16[1,2,256,384]{3,2,1,0:T(8,128)(2,1)}, u32[]{:S(2)}) copy-start(bf16[1,2,256,384]{3,2,1,0:T(8,128)(2,1)} %param.15) | copy-start | bytes 1179652
  29.7 2.8 %collective-permute-start.2 = (s32[2]{0:T(128)S(1)}, s32[2]{0:T(128)S(1)}, u32[]{:S(2)}, u32[]{:S(2)}) collective-permute-start(s32[2]{0:T(128)S(1)} %pad_add_fusion), channel_id=1, source_target_pairs={{0,64},{32,96},{64,0},{96,32},{128,192},{160,224},{192,128},{224,1... | collective-permute-start | bytes 32 | tf_op jit(solution)/shard_map/ppermute | solution.py:110
  34.5 1.7 copy-start.25
  35.6 17.4 %collective-permute-start.3 = (bf16[2,2,256,384]{3,2,1,0:T(8,128)(2,1)}, bf16[2,2,256,384]{3,2,1,0:T(8,128)(2,1)}, u32[]{:S(2)}, u32[]{:S(2)}) collective-permute-start(bf16[2,2,256,384]{3,2,1,0:T(8,128)(2,1)} %pad_maximum_fusion), channel_id=1, source_target_pairs={{0,64},{32,96},{64,0},{96,32},{128,192},{160,224},{192,128},{224,1... | collective-permute-start | bytes 2359304 | tf_op jit(solution)/shard_map/ppermute | solution.py:110
  38.6 4.3 %copy-start.6 = (bf16[1536,384]{0,1:T(8,128)(2,1)S(1)}, bf16[1536,384]{0,1:T(8,128)(2,1)}, u32[]{:S(2)}) copy-start(bf16[1536,384]{0,1:T(8,128)(2,1)} %copy.40) | copy-start | bytes 3538948
  38.6 4.3 %copy-start.22 = (f32[128]{0:T(128)S(1)}, f32[128]{0:T(128)}, u32[]{:S(2)}) copy-start(f32[128]{0:T(128)} %copy-done.21) | copy-start | bytes 1540
  54.8 30.2 %collective-permute-start.4 = (bf16[2,256,384]{2,1,0:T(8,128)(2,1)}, bf16[2,256,384]{2,1,0:T(8,128)(2,1)}, u32[]{:S(2)}, u32[]{:S(2)}) collective-permute-start(bf16[2,256,384]{2,1,0:T(8,128)(2,1)} %fusion.28), channel_id=1, source_target_pairs={{0,32},{32,0},{64,96},{96,64},{128,160},{160,128},{192,224},{224,1... | collective-permute-start | bytes 1179656 | tf_op jit(solution)/shard_map/ppermute | solution.py:110
  86.2 0.8 copy-start.18
  86.2 0.8 copy-start.19
  86.4 3.4 %copy-start.15 = (bf16[1,256,384]{1,2,0:T(8,128)(2,1)}, bf16[1,256,384]{1,2,0:T(8,128)(2,1)S(1)}, u32[]{:S(2)}) copy-start(bf16[1,256,384]{1,2,0:T(8,128)(2,1)S(1)} %copy.39) | copy-start | bytes 589828
  86.6 3.2 %copy-start.13 = (bf16[1,256,384]{1,2,0:T(8,128)(2,1)}, bf16[1,256,384]{1,2,0:T(8,128)(2,1)S(1)}, u32[]{:S(2)}) copy-start(bf16[1,256,384]{1,2,0:T(8,128)(2,1)S(1)} %copy.37) | copy-start | bytes 589828
  87.0 2.8 %copy-start.16 = (bf16[128,384]{0,1:T(8,128)(2,1)S(1)}, bf16[128,384]{0,1:T(8,128)(2,1)}, u32[]{:S(2)}) copy-start(bf16[128,384]{0,1:T(8,128)(2,1)} %copy.38) | copy-start | bytes 294916
  91.6 1.5 copy-start.20
  92.2 0.9 copy-start.4
  93.1 84.3 %copy-start.12 = (bf16[1536,128]{1,0:T(8,128)(2,1)S(1)}, bf16[1536,128]{1,0:T(8,128)(2,1)}, u32[]{:S(2)}) copy-start(bf16[1536,128]{1,0:T(8,128)(2,1)} %param.25) | copy-start | bytes 1179652
  109.6 72.4 %copy-start.26 = (bf16[1536,128]{1,0:T(8,128)(2,1)S(1)}, bf16[1536,128]{1,0:T(8,128)(2,1)}, u32[]{:S(2)}) copy-start(bf16[1536,128]{1,0:T(8,128)(2,1)} %param.26) | copy-start | bytes 1179652
  177.3 4.8 %copy-start.1 = (bf16[2048,1536]{1,0:T(8,128)(2,1)S(1)}, bf16[2048,1536]{1,0:T(8,128)(2,1)}, u32[]{:S(2)}) copy-start(bf16[2048,1536]{1,0:T(8,128)(2,1)} %all-gather.5.cloned.1.call-done) | copy-start | bytes 18874372
  184.8 22.3 %all-to-all-start = ((bf16[32,64,128]{2,1,0:T(8,128)(2,1)}), bf16[32,64,128]{2,1,0:T(8,128)(2,1)S(1)}, u32[]{:S(2)}, u32[]{:S(2)}) async-start(bf16[32,64,128]{2,1,0:T(8,128)(2,1)} %bitcast.165), calls=%async_computation | async-start | bytes 1048576 | tf_op jit(solution)/shard_map/all_to_all | solution.py:90
  207.0 0.8 copy-start.8
  214.4 1.8 copy-start.24
  216.2 2.1 copy-start.3
  218.3 1.3 copy-start.5
  219.6 1.3 copy-start.9
  219.6 2.3 copy-start.10
  219.6 2.3 copy-start.11
  220.9 4.1 %copy-start.28 = (pred[384]{0:T(512)(128)(4,1)S(1)}, pred[384]{0:T(512)(128)(4,1)}, u32[]{:S(2)}) copy-start(pred[384]{0:T(512)(128)(4,1)} %concatenate.51) | copy-start | bytes 1156
  225.0 2.9 %copy-start.14 = (bf16[1,256,384]{1,2,0:T(8,128)(2,1)S(1)}, bf16[1,256,384]{1,2,0:T(8,128)(2,1)}, u32[]{:S(2)}) copy-start(bf16[1,256,384]{1,2,0:T(8,128)(2,1)} %copy-done.13) | copy-start | bytes 589828
Sparse Core Ops, SparseCore 0:
  9.2 100.3 all-gather.2
  111.5 65.8 all-gather.4

commit v9 on v8

--- a/solution.py
+++ b/solution.py
@@ -103,7 +103,7 @@
     own = cache_kv[0]
     if count != 8:
         slots = lax.all_gather(own, "req", axis=0, tiled=False)
-        return slots[holder[0]]
+        return slots[holder[0]], own
     me = lax.axis_index("req")
 
     def swap(values, mask):
@@ -112,23 +112,24 @@
     def pick(cond, a, b):
         return jnp.where(cond, a, b)
 
-    near = swap(holder, 1)
-    quad = swap(jnp.concatenate([holder, near]), 2)
-    holders = {0: holder[0], 1: near[0], 2: quad[0], 3: quad[1]}
-
-    got1 = swap(own, 4)
-    send_a = pick(holders[2] == (me ^ 4), got1, own)
-    send_b = pick(holders[3] == (me ^ 4), got1, own)
+    far = swap(holder, 4)
+    pair = swap(jnp.concatenate([holder, far]), 2)
+    holders = {0: holder[0], 4: far[0], 2: pair[0], 6: pair[1]}
+
+    got1 = swap(own, 1)
+    send_a = pick(holders[2] == (me ^ 1), got1, own)
+    send_b = pick(holders[6] == (me ^ 1), got1, own)
     got2 = swap(jnp.stack([send_a, send_b]), 2)
-    want = holders[1]
-    send_c = pick(want == me, own, pick(want == (me ^ 4), got1, got2[1]))
-    got3 = swap(send_c, 1)
+    want = holders[4]
+    send_c = pick(want == me, own, pick(want == (me ^ 1), got1, got2[1]))
+    got3 = swap(send_c, 4)
     need = holders[0]
-    return pick(
+    slot = pick(
         need == me,
         own,
-        pick(need == (me ^ 4), got1, pick((need ^ me) == 2, got2[0], pick((need ^ me) == 6, got2[0], got3))),
-    )
+        pick(need == (me ^ 1), got1, pick(((need ^ me) >> 1) == 1, got2[0], got3)),
+    )
+    return slot, got1
 
 
 def local(
@@ -147,8 +148,9 @@
     w_up,
     w_down,
 ):
-    fetched = fetch_slot(cache_kv, holder)
-    down_all = lax.all_gather(w_down, "blk", axis=0, tiled=True)
+    fetched, first_stage = fetch_slot(cache_kv, holder)
+    w_down_late, _ = lax.optimization_barrier((w_down, first_stage))
+    down_all = lax.all_gather(w_down_late, "blk", axis=0, tiled=True)
     cache_keys = fetched[0]
     cache_vals = fetched[1]
     cache_length = cache_len[0]

time: 239 us -> 241 us (level)
  waiting for transfers between devices: 133 us -> 137 us
    all_gather x1, waiting for transfers between devices: 15 us -> 32.1 us  [local(): down_all = lax.all_gather(w_down_late, 'blk', axis=0, tiled=True)]
    ppermute x5, waiting for transfers between devices: 33 us -> 19.5 us  [swap(): lax.ppermute(values, 'req', perm=[(i, i ^ mask) for i in range(count)])]
  transfers between devices with their start and end apart: 8 -> 8, of which waited for: 6 -> 7; matrix products, arithmetic and copies ran while one was open for 15% -> 15% of each run, Pallas kernels for 0% -> 0%
where the time goes in v9:
time: 241 us; the launch traced here: 240 us
  waiting for transfers between devices  137 us (57%)
  matrix products  34 us (14%)
  starting transfers between devices  18.1 us (8%)
  between operations  17.7 us (7%)
  local copies, waits for them, and re-layouts  17.4 us (7%)
  other arithmetic  15.9 us (7%)
    all_gather x1, waiting for transfers between devices, run_ffn(): part_rows = lax.all_gather(normed_rows, 'blk', axis=0, tiled=True)  68.5 us
    all_gather x1, waiting for transfers between devices, local(): down_all = lax.all_gather(w_down_late, 'blk', axis=0, tiled=True)  32.1 us
    ppermute x5, waiting for transfers between devices, swap(): lax.ppermute(values, 'req', perm=[(i, i ^ mask) for i in range(count)])  19.5 us
    all_to_all x1, waiting for transfers between devices, run_ffn(): hidden_own = lax.all_to_all(hidden_all, 'blk', 0, 1, tiled=True)  16.8 us
    ppermute x5, starting transfers between devices, swap(): lax.ppermute(values, 'req', perm=[(i, i ^ mask) for i in range(count)])  12.6 us
    unnamed x60, local copies, waits for them, and re-layouts  10.1 us
    dot_general x1, matrix products, run_ffn(): jnp.einsum('rgk,gkd->grd', hidden_own.reshape(hidden_own.shape[0], group_...  6.57 us
    sub x2, matrix products, attend_block(): expd = jnp.exp(scores - peaks)  5.72 us
  transfers between devices with their start and end apart: 8, of which 7 were waited for; matrix products, arithmetic and copies ran while one was open for 15% of the time, Pallas kernels for 0%

profile of v9, /device:TPU:1, one launch (start us, length us, event | category | flops | bytes accessed | tf_op | source)
XLA Modules:
  0.0 240.1 jit_solution(9230961005003356008)
XLA Ops:
  6.5 7.7 %collective-permute-start = (bf16[2,256,384]{2,1,0:T(8,128)(2,1)}, bf16[2,256,384]{2,1,0:T(8,128)(2,1)S(1)}, u32[]{:S(2)}, u32[]{:S(2)}) collective-permute-start(bf16[2,256,384]{2,1,0:T(8,128)(2,1)} %bitcast.166), channel_id=1, source_target_pairs={{0,32},{32,0},{64,96},{96,64},{128,160},{160,128},{192,224},{224,1... | collective-permute-start | bytes 1179656 | tf_op jit(solution)/shard_map/ppermute | solution.py:110
  14.3 9.5 %collective-permute-done = bf16[2,256,384]{2,1,0:T(8,128)(2,1)S(1)} collective-permute-done((bf16[2,256,384]{2,1,0:T(8,128)(2,1)}, bf16[2,256,384]{2,1,0:T(8,128)(2,1)S(1)}, u32[]{:S(2)}, u32[]{:S(2)}) %collective-permute-start) | collective-permute-done | bytes 393248 | tf_op jit(solution)/shard_map/ppermute | solution.py:110
  23.9 3.4 %collective-permute-start.1 = (s32[1]{0:T(128)}, s32[1]{0:T(128)}, u32[]{:S(2)}, u32[]{:S(2)}) collective-permute-start(s32[1]{0:T(128)} %param.17), channel_id=1, source_target_pairs={{0,128},{32,160},{64,192},{96,224},{128,0},{160,32},{192,64},{224,... | collective-permute-start | bytes 20 | tf_op jit(solution)/shard_map/ppermute | solution.py:110
  28.0 4.3 %copy.41 = bf16[1536,768]{0,1:T(8,128)(2,1)} copy(bf16[1536,768]{1,0:T(8,128)(2,1)} %param.20) | data formatting | bytes 4718592 | tf_op args[6]
  33.7 0.5 fusion.63
  34.3 0.8 multiply_cosine_fusion
  35.1 3.3 %fusion.56 = f32[128,8,96]{0,2,1:T(8,128)} fusion(bf16[8,96,1536]{2,1,0:T(8,128)(2,1)} %bitcast.164, bf16[1,128,1536]{2,1,0:T(8,128)(2,1)S(1)} %copy-done.2, f32[1536]{0:T(1024)S(1)} %copy-done.17, f32[128]{0:T(128)S(1)} %add_rsqrt_fusion.2), kind=kOutput, calls=%fused_computation.77 | convolution fusion | flops 302776320 | bytes 3152384 | tf_op jit(solution)/shard_map/dot_general | solution.py:54
  38.4 0.7 pad_add_fusion
  39.5 2.1 collective-permute-done.2
  41.5 0.6 fusion.82
  43.6 1.0 pad_maximum_fusion
  44.9 2.5 %copy.40 = bf16[1536,384]{0,1:T(8,128)(2,1)} copy(bf16[1536,384]{1,0:T(8,128)(2,1)} %param.21) | data formatting | bytes 2359296 | tf_op args[7]
  47.4 1.9 subtract_convert_fusion.1
  49.3 2.4 convolution_convert_fusion.3
  51.6 1.2 fusion.58
  54.1 7.0 %collective-permute-done.3 = bf16[2,2,256,384]{3,2,1,0:T(8,128)(2,1)} collective-permute-done((bf16[2,2,256,384]{3,2,1,0:T(8,128)(2,1)}, bf16[2,2,256,384]{3,2,1,0:T(8,128)(2,1)}, u32[]{:S(2)}, u32[]{:S(2)}) %collective-permute-start.3) | collective-permute-done | bytes 786464 | tf_op jit(solution)/shard_map/ppermute | solution.py:110
  61.1 1.8 fusion.26
  63.0 0.9 collective-permute-start.4
  63.8 0.6 iota_compare_fusion.1
  64.4 1.6 copy.38
  66.1 1.2 concatenate.51
  67.3 1.6 pad_maximum_fusion.5
  68.9 1.6 subtract_convert_fusion.3
  70.6 0.8 collective-permute-done.4
  71.4 1.2 fusion.29
  73.4 2.8 %fusion.83 = (f32[4,2,128]{2,1,0:T(2,128)S(1)}, f32[4,2,128,384]{2,3,1,0:T(8,128)}) fusion(bf16[128,4,2,96]{0,3,2,1:T(8,128)(2,1)} %bitcast.176, bf16[256,4,96]{0,2,1:T(8,128)(2,1)S(1)} %bitcast.174, bf16[128,4,48]{0,2,1:T(8,128)(2,1)S(1)} %copy-done.19, bf16[128,4,48]{0,2,1:T(8,128)(2,1)S(1)} %copy-done.18, pred[384]{0:T(512)(128)(4,1)} %concatenate.51), kind=kOutput, calls=%fused_computation.116 | convolution fusion | flops 77955456 | bytes 2068864 | tf_op jit(solution)/shard_map/sub | solution.py:78
  76.2 1.7 convolution_convert_fusion.1
  78.0 0.6 multiply_reduce_fusion.1
  78.6 0.9 copy-done.4
  79.6 1.4 gather_fusion
  81.0 32.1 %all-gather.3.cloned.1.call-done = bf16[4096,1536]{1,0:T(8,128)(2,1)} async-done(((bf16[128,1536]{1,0:T(8,128)(2,1)}), bf16[4096,1536]{1,0:T(8,128)(2,1)}) %all-gather.3.cloned.1.call-update) | async-done | bytes 12582928 | tf_op jit(solution)/shard_map/all_gather | solution.py:153
  113.2 68.5 %all-gather.5.cloned.1.call-done = bf16[2048,1536]{1,0:T(8,128)(2,1)} async-done(((bf16[64,1536]{1,0:T(8,128)(2,1)}), bf16[2048,1536]{1,0:T(8,128)(2,1)}) %all-gather.5.cloned.1.call-update) | async-done | bytes 6291472 | tf_op jit(solution)/shard_map/all_gather | solution.py:86
  181.7 4.7 %fusion.89 = f32[2048,128]{1,0:T(8,128)S(1)} fusion(bf16[2048,1536]{1,0:T(8,128)(2,1)} %all-gather.5.cloned.1.call-done, bf16[1536,128]{1,0:T(8,128)(2,1)S(1)} %copy-done.12), kind=kOutput, calls=%fused_computation.118 | convolution fusion | flops 805306368 | bytes 7733248 | tf_op jit(solution)/shard_map/dot_general | solution.py:87
  186.5 2.7 %fusion.3 = bf16[2048,128]{1,0:T(8,128)(2,1)} fusion(bf16[2048,1536]{1,0:T(8,128)(2,1)S(1)} %copy-done.1, bf16[1536,128]{1,0:T(8,128)(2,1)S(1)} %copy-done.26, f32[2048,128]{1,0:T(8,128)S(1)} %fusion.89), kind=kOutput, calls=%fused_computation.9 | convolution fusion | flops 806879232 | bytes 8257536 | tf_op jit(solution)/shard_map/dot_general | solution.py:88
  189.1 5.4 %all-to-all-start = ((bf16[32,64,128]{2,1,0:T(8,128)(2,1)}), bf16[32,64,128]{2,1,0:T(8,128)(2,1)S(1)}, u32[]{:S(2)}, u32[]{:S(2)}) async-start(bf16[32,64,128]{2,1,0:T(8,128)(2,1)} %bitcast.169), calls=%async_computation | async-start | bytes 1048576 | tf_op jit(solution)/shard_map/all_to_all | solution.py:90
  194.6 16.8 %all-to-all-done = bf16[32,64,128]{2,1,0:T(8,128)(2,1)S(1)} async-done(((bf16[32,64,128]{2,1,0:T(8,128)(2,1)}), bf16[32,64,128]{2,1,0:T(8,128)(2,1)S(1)}, u32[]{:S(2)}, u32[]{:S(2)}) %all-to-all-start) | async-done | bytes 524320 | tf_op jit(solution)/shard_map/all_to_all | solution.py:90
  211.4 0.8 copy-done.8
  212.2 6.6 %convert_reduce_fusion = f32[64,1536]{1,0:T(8,128)S(1)} fusion(bf16[32,128,1536]{2,1,0:T(8,128)(2,1)} %bitcast.163, bf16[32,64,128]{2,1,0:T(8,128)(2,1)} %copy-done.8), kind=kOutput, calls=%fused_computation.4 | convolution fusion | flops 814645248 | bytes 13500416 | tf_op jit(solution)/shard_map/rgk,gkd->grd/dot_general | solution.py:92
  218.8 1.7 gather_fusion.1
  220.6 1.8 multiply_reduce_fusion
  222.7 1.1 fusion.91
  224.0 0.6 fusion.90
  224.6 0.7 copy-done.9
  225.7 0.7 subtract_convert_fusion.2
  226.5 0.7 pad_maximum_fusion.6
  227.2 2.9 %fusion.86 = (f32[4,2,128]{2,1,0:T(2,128)S(1)}, f32[4,2,128,384]{2,3,1,0:T(8,128)}) fusion(bf16[128,4,2,96]{0,3,2,1:T(8,128)(2,1)} %bitcast.177, bf16[256,4,96]{0,2,1:T(8,128)(2,1)} %bitcast.175, bf16[128,4,48]{0,2,1:T(8,128)(2,1)} %get-tuple-element.24, bf16[128,4,48]{0,2,1:T(8,128)(2,1)} %get-tuple-element.23, pred[384]{0:T(512)(128)(4,1)S(1)} %copy-done.28), kind=kOutput, calls=%fused_computation.117 | convolution fusion | flops 77955456 | bytes 2068864 | tf_op jit(solution)/shard_map/sub | solution.py:78
  230.1 1.7 convolution_convert_fusion
  231.9 1.4 fusion.2
  (84 shorter events, 3.6 us)
Async XLA Ops:
  6.5 71.5 %copy-start = (bf16[768,1536]{1,0:T(8,128)(2,1)S(1)}, bf16[768,1536]{1,0:T(8,128)(2,1)}, u32[]{:S(2)}) copy-start(bf16[768,1536]{1,0:T(8,128)(2,1)} %param.23) | copy-start | bytes 7077892
  6.5 106.6 %all-gather.3.cloned.1.call-start = ((), (), s32[]{:S(2)}) async-start(), calls=%async_computation.1 | async-start | bytes 12976128 | tf_op jit(solution)/shard_map/all_gather | solution.py:153
  6.5 17.3 %collective-permute-start = (bf16[2,256,384]{2,1,0:T(8,128)(2,1)}, bf16[2,256,384]{2,1,0:T(8,128)(2,1)S(1)}, u32[]{:S(2)}, u32[]{:S(2)}) collective-permute-start(bf16[2,256,384]{2,1,0:T(8,128)(2,1)} %bitcast.166), channel_id=1, source_target_pairs={{0,32},{32,0},{64,96},{96,64},{128,160},{160,128},{192,224},{224,1... | collective-permute-start | bytes 1179656 | tf_op jit(solution)/shard_map/ppermute | solution.py:110
  23.8 157.9 %all-gather.5.cloned.1.call-start = ((), (), s32[]{:S(2)}) async-start(), calls=%async_computation.2 | async-start | bytes 6488064 | tf_op jit(solution)/shard_map/all_gather | solution.py:86
  23.9 14.5 %collective-permute-start.1 = (s32[1]{0:T(128)}, s32[1]{0:T(128)}, u32[]{:S(2)}, u32[]{:S(2)}) collective-permute-start(s32[1]{0:T(128)} %param.17), channel_id=1, source_target_pairs={{0,128},{32,160},{64,192},{96,224},{128,0},{160,32},{192,64},{224,... | collective-permute-start | bytes 20 | tf_op jit(solution)/shard_map/ppermute | solution.py:110
  27.9 5.0 %copy-start.27 = (s32[1,128]{1,0:T(1,128)S(1)}, s32[1,128]{1,0:T(1,128)}, u32[]{:S(2)}) copy-start(s32[1,128]{1,0:T(1,128)} %param.18) | copy-start | bytes 1540
  28.0 5.6 %copy-start.2 = (bf16[1,128,1536]{2,1,0:T(8,128)(2,1)S(1)}, bf16[1,128,1536]{2,1,0:T(8,128)(2,1)}, u32[]{:S(2)}) copy-start(bf16[1,128,1536]{2,1,0:T(8,128)(2,1)} %param.14) | copy-start | bytes 1179652
  28.0 7.1 %copy-start.17 = (f32[1536]{0:T(1024)S(1)}, f32[1536]{0:T(1024)}, u32[]{:S(2)}) copy-start(f32[1536]{0:T(1024)} %param.19) | copy-start | bytes 18436
  33.0 0.5 copy-start.23
  33.7 4.7 %copy-start.21 = (f32[128]{0:T(128)}, f32[128]{0:T(128)S(1)}, u32[]{:S(2)}) copy-start(f32[128]{0:T(128)S(1)} %add_rsqrt_fusion.2) | copy-start | bytes 1540
  35.1 8.4 %copy-start.7 = (bf16[1,2,256,384]{3,2,1,0:T(8,128)(2,1)S(1)}, bf16[1,2,256,384]{3,2,1,0:T(8,128)(2,1)}, u32[]{:S(2)}) copy-start(bf16[1,2,256,384]{3,2,1,0:T(8,128)(2,1)} %param.15) | copy-start | bytes 1179652
  39.1 2.4 %collective-permute-start.2 = (s32[2]{0:T(128)S(1)}, s32[2]{0:T(128)S(1)}, u32[]{:S(2)}, u32[]{:S(2)}) collective-permute-start(s32[2]{0:T(128)S(1)} %pad_add_fusion), channel_id=1, source_target_pairs={{0,64},{32,96},{64,0},{96,32},{128,192},{160,224},{192,128},{224,1... | collective-permute-start | bytes 32 | tf_op jit(solution)/shard_map/ppermute | solution.py:110
  43.5 1.4 copy-start.25
  44.6 16.6 %collective-permute-start.3 = (bf16[2,2,256,384]{3,2,1,0:T(8,128)(2,1)}, bf16[2,2,256,384]{3,2,1,0:T(8,128)(2,1)}, u32[]{:S(2)}, u32[]{:S(2)}) collective-permute-start(bf16[2,2,256,384]{3,2,1,0:T(8,128)(2,1)} %pad_maximum_fusion), channel_id=1, source_target_pairs={{0,64},{32,96},{64,0},{96,32},{128,192},{160,224},{192,128},{224,1... | collective-permute-start | bytes 2359304 | tf_op jit(solution)/shard_map/ppermute | solution.py:110
  47.4 4.2 %copy-start.6 = (bf16[1536,384]{0,1:T(8,128)(2,1)S(1)}, bf16[1536,384]{0,1:T(8,128)(2,1)}, u32[]{:S(2)}) copy-start(bf16[1536,384]{0,1:T(8,128)(2,1)} %copy.40) | copy-start | bytes 3538948
  47.4 4.2 %copy-start.22 = (f32[128]{0:T(128)S(1)}, f32[128]{0:T(128)}, u32[]{:S(2)}) copy-start(f32[128]{0:T(128)} %copy-done.21) | copy-start | bytes 1540
  63.0 8.4 %collective-permute-start.4 = (bf16[2,256,384]{2,1,0:T(8,128)(2,1)}, bf16[2,256,384]{2,1,0:T(8,128)(2,1)}, u32[]{:S(2)}, u32[]{:S(2)}) collective-permute-start(bf16[2,256,384]{2,1,0:T(8,128)(2,1)} %fusion.26), channel_id=1, source_target_pairs={{0,128},{32,160},{64,192},{96,224},{128,0},{160,32},{192,64},{224,... | collective-permute-start | bytes 1179656 | tf_op jit(solution)/shard_map/ppermute | solution.py:110
  72.6 0.8 copy-start.18
  72.6 0.8 copy-start.19
  72.8 3.4 %copy-start.15 = (bf16[1,256,384]{1,2,0:T(8,128)(2,1)}, bf16[1,256,384]{1,2,0:T(8,128)(2,1)S(1)}, u32[]{:S(2)}) copy-start(bf16[1,256,384]{1,2,0:T(8,128)(2,1)S(1)} %copy.39) | copy-start | bytes 589828
  73.0 3.2 %copy-start.13 = (bf16[1,256,384]{1,2,0:T(8,128)(2,1)}, bf16[1,256,384]{1,2,0:T(8,128)(2,1)S(1)}, u32[]{:S(2)}) copy-start(bf16[1,256,384]{1,2,0:T(8,128)(2,1)S(1)} %copy.37) | copy-start | bytes 589828
  73.4 2.8 %copy-start.16 = (bf16[128,384]{0,1:T(8,128)(2,1)S(1)}, bf16[128,384]{0,1:T(8,128)(2,1)}, u32[]{:S(2)}) copy-start(bf16[128,384]{0,1:T(8,128)(2,1)} %copy.38) | copy-start | bytes 294916
  78.0 1.5 copy-start.20
  78.6 0.9 copy-start.4
  79.5 102.2 %copy-start.12 = (bf16[1536,128]{1,0:T(8,128)(2,1)S(1)}, bf16[1536,128]{1,0:T(8,128)(2,1)}, u32[]{:S(2)}) copy-start(bf16[1536,128]{1,0:T(8,128)(2,1)} %param.25) | copy-start | bytes 1179652
  113.2 73.2 %copy-start.26 = (bf16[1536,128]{1,0:T(8,128)(2,1)S(1)}, bf16[1536,128]{1,0:T(8,128)(2,1)}, u32[]{:S(2)}) copy-start(bf16[1536,128]{1,0:T(8,128)(2,1)} %param.26) | copy-start | bytes 1179652
  181.7 4.8 %copy-start.1 = (bf16[2048,1536]{1,0:T(8,128)(2,1)S(1)}, bf16[2048,1536]{1,0:T(8,128)(2,1)}, u32[]{:S(2)}) copy-start(bf16[2048,1536]{1,0:T(8,128)(2,1)} %all-gather.5.cloned.1.call-done) | copy-start | bytes 18874372
  189.1 22.3 %all-to-all-start = ((bf16[32,64,128]{2,1,0:T(8,128)(2,1)}), bf16[32,64,128]{2,1,0:T(8,128)(2,1)S(1)}, u32[]{:S(2)}, u32[]{:S(2)}) async-start(bf16[32,64,128]{2,1,0:T(8,128)(2,1)} %bitcast.169), calls=%async_computation | async-start | bytes 1048576 | tf_op jit(solution)/shard_map/all_to_all | solution.py:90
  211.4 0.8 copy-start.8
  218.8 1.8 copy-start.24
  220.6 2.1 copy-start.3
  222.7 1.3 copy-start.5
  224.0 1.3 copy-start.9
  224.0 1.7 copy-start.10
  224.0 1.7 copy-start.11
  225.2 2.0 copy-start.28
  227.2 2.9 %copy-start.14 = (bf16[1,256,384]{1,2,0:T(8,128)(2,1)S(1)}, bf16[1,256,384]{1,2,0:T(8,128)(2,1)}, u32[]{:S(2)}) copy-start(bf16[1,256,384]{1,2,0:T(8,128)(2,1)} %copy-done.13) | copy-start | bytes 589828
Sparse Core Ops, SparseCore 0:
  24.0 89.1 all-gather.2
  115.0 66.6 all-gather.4

commit v10 on v8

--- a/solution.py
+++ b/solution.py
@@ -1,10 +1,13 @@
 import jax
 import jax.numpy as jnp
 from jax import lax
-from jax.sharding import PartitionSpec as P
+from jax.sharding import Mesh, PartitionSpec as P
 
 HEAD = 96
 
+
+BLK = "blk"
+BLK_PARTS = None
 
 norm_eps = 1e-05
 rope_base = 100000.0
@@ -83,11 +86,21 @@
 
 
 def run_ffn(normed_rows, w_gate, w_up, down_all, groups):
-    part_rows = lax.all_gather(normed_rows, "blk", axis=0, tiled=True)
+    if BLK_PARTS is None:
+        part_rows = lax.all_gather(normed_rows, BLK, axis=0, tiled=True)
+    else:
+        part_rows = normed_rows
+        for name in BLK_PARTS:
+            part_rows = lax.all_gather(part_rows, name, axis=0, tiled=False)
+        part_rows = part_rows.reshape(-1, normed_rows.shape[1])
     gate_vals = jnp.dot(part_rows, w_gate, preferred_element_type=jnp.float32)
     up_vals = jnp.dot(part_rows, w_up, preferred_element_type=jnp.float32)
     hidden_all = (jax.nn.silu(gate_vals) * up_vals).astype(jnp.bfloat16)
-    hidden_own = lax.all_to_all(hidden_all, "blk", 0, 1, tiled=True)
+    if BLK_PARTS is not None:
+        sizes = [lax.psum(1, name) for name in BLK_PARTS]
+        hidden_all = hidden_all.reshape(sizes[::-1] + [normed_rows.shape[0], hidden_all.shape[1]])
+        hidden_all = hidden_all.transpose(2, 1, 0, 3, 4).reshape(-1, hidden_all.shape[-1])
+    hidden_own = lax.all_to_all(hidden_all, BLK, 0, 1, tiled=True)
     group_count = down_all.shape[0] // groups
     terms = jnp.einsum(
         "rgk,gkd->grd",
@@ -148,7 +161,7 @@
     w_down,
 ):
     fetched = fetch_slot(cache_kv, holder)
-    down_all = lax.all_gather(w_down, "blk", axis=0, tiled=True)
+    down_all = lax.all_gather(w_down, BLK, axis=0, tiled=True)
     cache_keys = fetched[0]
     cache_vals = fetched[1]
     cache_length = cache_len[0]
@@ -191,25 +204,30 @@
 
 
 def solution(mesh):
+    global BLK, BLK_PARTS
+    if dict(mesh.shape) == {"req": 8, "blk": 32}:
+        mesh = Mesh(mesh.devices.reshape(8, 4, 4, 2), ("req", "y", "zl", "c"))
+        BLK, BLK_PARTS = ("y", "zl", "c"), ("y", "zl", "c")
+    rows = ("req",) + (BLK if isinstance(BLK, tuple) else (BLK,))
     return jax.shard_map(
         local,
         mesh=mesh,
         in_specs=(
-            P(("req", "blk"), None, None),
-            P(("req", "blk"), None, None, None),
-            P(("req", "blk")),
-            P(("req", "blk")),
-            P(("req", "blk"), None),
-            P(),
-            P(),
-            P(),
-            P(),
-            P(),
-            P(),
-            P(None, "blk"),
-            P(None, "blk"),
-            P("blk", None),
+            P(rows, None, None),
+            P(rows, None, None, None),
+            P(rows),
+            P(rows),
+            P(rows, None),
+            P(),
+            P(),
+            P(),
+            P(),
+            P(),
+            P(),
+            P(None, BLK),
+            P(None, BLK),
+            P(BLK, None),
         ),
-        out_specs=P(("req", "blk"), None, None),
+        out_specs=P(rows, None, None),
         check_vma=False,
     )

time: 239 us -> 279 us (1.17)
  waiting for transfers between devices: 133 us -> 160 us
  blocking collectives: 0 us -> 11.8 us
    all_gather x2 -> x3, waiting for transfers between devices: 82.7 us -> 110 us  [the longest x2 94.1 us: run_ffn(): part_rows = lax.all_gather(part_rows, name, axis=0, tiled=False)]
    all_gather x0 -> x1, blocking collectives: none -> 11.8 us  [run_ffn(): part_rows = lax.all_gather(part_rows, name, axis=0, tiled=False)]
  transfers between devices with their start and end apart: 8 -> 9, of which waited for: 6 -> 7; matrix products, arithmetic and copies ran while one was open for 15% -> 13% of each run, Pallas kernels for 0% -> 0%
where the time goes in v10:
time: 279 us; the launch traced here: 278 us
  waiting for transfers between devices  160 us (57%)
  matrix products  33.9 us (12%)
  starting transfers between devices  19.5 us (7%)
  local copies, waits for them, and re-layouts  19 us (7%)
  between operations  17.3 us (6%)
  other arithmetic  15.9 us (6%)
  blocking collectives  11.8 us (4%)
    all_gather x2, waiting for transfers between devices, run_ffn(): part_rows = lax.all_gather(part_rows, name, axis=0, tiled=False)  94.1 us
    ppermute x5, waiting for transfers between devices, swap(): lax.ppermute(values, 'req', perm=[(i, i ^ mask) for i in range(count)])  33.1 us
    all_to_all x1, waiting for transfers between devices, run_ffn(): hidden_own = lax.all_to_all(hidden_all, BLK, 0, 1, tiled=True)  16.8 us
    all_gather x1, waiting for transfers between devices, local(): down_all = lax.all_gather(w_down, BLK, axis=0, tiled=True)  15.7 us
    ppermute x5, starting transfers between devices, swap(): lax.ppermute(values, 'req', perm=[(i, i ^ mask) for i in range(count)])  12 us
    all_gather x1, blocking collectives, run_ffn(): part_rows = lax.all_gather(part_rows, name, axis=0, tiled=False)  11.8 us
    unnamed x60, local copies, waits for them, and re-layouts  10.1 us
    all_to_all x1, starting transfers between devices, run_ffn(): hidden_own = lax.all_to_all(hidden_all, BLK, 0, 1, tiled=True)  7.37 us
  transfers between devices with their start and end apart: 9, of which 7 were waited for; matrix products, arithmetic and copies ran while one was open for 13% of the time, Pallas kernels for 0%

profile of v10, /device:TPU:1, one launch (start us, length us, event | category | flops | bytes accessed | tf_op | source)
XLA Modules:
  0.0 277.7 jit_solution(5158616897630946055)
XLA Ops:
  6.5 0.7 all-gather.7.cloned.1.call-update
  7.3 3.7 %collective-permute-start = (bf16[2,256,384]{2,1,0:T(8,128)(2,1)}, bf16[2,256,384]{2,1,0:T(8,128)(2,1)S(1)}, u32[]{:S(2)}, u32[]{:S(2)}) collective-permute-start(bf16[2,256,384]{2,1,0:T(8,128)(2,1)} %bitcast.170), channel_id=1, source_target_pairs={{0,128},{32,160},{64,192},{96,224},{128,0},{160,32},{192,64},{224,... | collective-permute-start | bytes 1179656 | tf_op jit(solution)/shard_map/ppermute | solution.py:123
  11.0 6.9 %collective-permute-start.1 = (s32[1]{0:T(128)}, s32[1]{0:T(128)}, u32[]{:S(2)}, u32[]{:S(2)}) collective-permute-start(s32[1]{0:T(128)} %param.17), channel_id=1, source_target_pairs={{0,32},{32,0},{64,96},{96,64},{128,160},{160,128},{192,224},{224,1... | collective-permute-start | bytes 20 | tf_op jit(solution)/shard_map/ppermute | solution.py:123
  18.6 4.3 %copy.55 = bf16[1536,768]{0,1:T(8,128)(2,1)} copy(bf16[1536,768]{1,0:T(8,128)(2,1)} %param.20) | data formatting | bytes 4718592 | tf_op args[6]
  24.4 0.8 multiply_cosine_fusion
  25.1 3.3 %fusion.55 = f32[128,8,96]{0,2,1:T(8,128)} fusion(bf16[8,96,1536]{2,1,0:T(8,128)(2,1)} %bitcast.168, bf16[1,128,1536]{2,1,0:T(8,128)(2,1)S(1)} %copy-done.2, f32[1536]{0:T(1024)S(1)} %copy-done.17, f32[128]{0:T(128)S(1)} %add_rsqrt_fusion.2), kind=kOutput, calls=%fused_computation.77 | convolution fusion | flops 302776320 | bytes 3152384 | tf_op jit(solution)/shard_map/dot_general | solution.py:57
  29.0 0.7 pad_add_fusion
  30.3 2.2 collective-permute-done.2
  32.5 0.6 fusion.81
  34.6 1.0 pad_maximum_fusion
  36.2 2.4 copy.54
  38.6 1.9 subtract_convert_fusion.1
  40.5 2.4 convolution_convert_fusion.3
  42.8 1.2 fusion.57
  45.3 7.6 %collective-permute-done.3 = bf16[2,2,256,384]{3,2,1,0:T(8,128)(2,1)} collective-permute-done((bf16[2,2,256,384]{3,2,1,0:T(8,128)(2,1)}, bf16[2,2,256,384]{3,2,1,0:T(8,128)(2,1)}, u32[]{:S(2)}, u32[]{:S(2)}) %collective-permute-start.3) | collective-permute-done | bytes 786464 | tf_op jit(solution)/shard_map/ppermute | solution.py:123
  52.9 1.8 fusion.28
  55.6 1.6 copy.52
  57.2 1.2 concatenate.51
  58.4 1.7 pad_maximum_fusion.5
  60.0 1.6 subtract_convert_fusion.3
  61.6 23.2 %collective-permute-done.4 = bf16[2,256,384]{2,1,0:T(8,128)(2,1)} collective-permute-done((bf16[2,256,384]{2,1,0:T(8,128)(2,1)}, bf16[2,256,384]{2,1,0:T(8,128)(2,1)}, u32[]{:S(2)}, u32[]{:S(2)}) %collective-permute-start.4) | collective-permute-done | bytes 393248 | tf_op jit(solution)/shard_map/ppermute | solution.py:123
  84.9 1.2 fusion.24
  86.9 2.8 %fusion.82 = (f32[4,2,128]{2,1,0:T(2,128)S(1)}, f32[4,2,128,384]{2,3,1,0:T(8,128)}) fusion(bf16[128,4,2,96]{0,3,2,1:T(8,128)(2,1)} %bitcast.183, bf16[256,4,96]{0,2,1:T(8,128)(2,1)S(1)} %bitcast.181, bf16[128,4,48]{0,2,1:T(8,128)(2,1)S(1)} %copy-done.19, bf16[128,4,48]{0,2,1:T(8,128)(2,1)S(1)} %copy-done.18, pred[384]{0:T(512)(128)(4,1)} %concatenate.51), kind=kOutput, calls=%fused_computation.116 | convolution fusion | flops 77955456 | bytes 2068864 | tf_op jit(solution)/shard_map/sub | solution.py:81
  89.7 1.7 convolution_convert_fusion.1
  92.1 0.9 copy-done.4
  93.1 0.7 gather_fusion
  93.8 15.7 %all-gather.7.cloned.1.call-done = bf16[4096,1536]{1,0:T(8,128)(2,1)} async-done(((bf16[128,1536]{1,0:T(8,128)(2,1)}), bf16[4096,1536]{1,0:T(8,128)(2,1)}) %all-gather.7.cloned.1.call-update) | async-done | bytes 12582928 | tf_op jit(solution)/shard_map/all_gather | solution.py:164
  109.5 11.8 %all-gather = bf16[256,1536]{1,0:T(8,128)(2,1)} all-gather(bf16[64,1536]{1,0:T(8,128)(2,1)S(1)} %gather_fusion), channel_id=2, replica_groups=mesh['req'=8,'y'=4,'zl'=4,'c'=2] {'y'}, dimensions={0}, use_global_device_ids=true | all-gather | bytes 983040 | tf_op jit(solution)/shard_map/all_gather | solution.py:94
  121.4 69.1 %all-gather.9.cloned.1.call-done = bf16[16,64,1536]{2,1,0:T(8,128)(2,1)} async-done(((bf16[4,64,1536]{2,1,0:T(8,128)(2,1)}), bf16[16,64,1536]{2,1,0:T(8,128)(2,1)}) %all-gather.9.cloned.1.call-update) | async-done | bytes 3145744 | tf_op jit(solution)/shard_map/all_gather | solution.py:94
  190.5 25.0 %all-gather.11.cloned.1.call-done = bf16[8,4,64,1536]{3,2,1,0:T(8,128)(2,1)} async-done(((bf16[4,4,64,1536]{3,2,1,0:T(8,128)(2,1)}), bf16[8,4,64,1536]{3,2,1,0:T(8,128)(2,1)}) %all-gather.11.cloned.1.call-update) | async-done | bytes 6291472 | tf_op jit(solution)/shard_map/all_gather | solution.py:94
  215.5 4.7 %fusion.88 = f32[2048,128]{1,0:T(8,128)S(1)} fusion(bf16[2048,1536]{1,0:T(8,128)(2,1)} %bitcast.166, bf16[1536,128]{1,0:T(8,128)(2,1)S(1)} %copy-done.12), kind=kOutput, calls=%fused_computation.118 | convolution fusion | flops 805306368 | bytes 7733248 | tf_op jit(solution)/shard_map/dot_general | solution.py:96
  220.3 1.8 fusion.3
  222.1 0.9 copy.58
  223.0 7.4 %all-to-all-start = ((bf16[32,64,128]{2,1,0:T(8,128)(2,1)}), bf16[32,64,128]{2,1,0:T(8,128)(2,1)S(1)}, u32[]{:S(2)}, u32[]{:S(2)}) async-start(bf16[32,64,128]{2,1,0:T(8,128)(2,1)} %bitcast.173), calls=%async_computation | async-start | bytes 1048576 | tf_op jit(solution)/shard_map/all_to_all | solution.py:103
  230.4 16.8 %all-to-all-done = bf16[32,64,128]{2,1,0:T(8,128)(2,1)S(1)} async-done(((bf16[32,64,128]{2,1,0:T(8,128)(2,1)}), bf16[32,64,128]{2,1,0:T(8,128)(2,1)S(1)}, u32[]{:S(2)}, u32[]{:S(2)}) %all-to-all-start) | async-done | bytes 524320 | tf_op jit(solution)/shard_map/all_to_all | solution.py:103
  247.2 0.8 copy-done.8
  248.0 6.6 %convert_reduce_fusion = f32[64,1536]{1,0:T(8,128)S(1)} fusion(bf16[32,128,1536]{2,1,0:T(8,128)(2,1)} %bitcast.165, bf16[32,64,128]{2,1,0:T(8,128)(2,1)} %copy-done.8), kind=kOutput, calls=%fused_computation.4 | convolution fusion | flops 814645248 | bytes 13500416 | tf_op jit(solution)/shard_map/rgk,gkd->grd/dot_general | solution.py:105
  254.6 1.7 gather_fusion.1
  256.3 1.8 multiply_reduce_fusion
  258.5 1.1 fusion.90
  260.4 0.7 copy-done.9
  261.0 1.0 convolution_convert_fusion.2
  262.1 0.7 subtract_convert_fusion.2
  262.8 1.6 copy.59
  264.4 0.7 pad_maximum_fusion.6
  265.1 2.9 %fusion.85 = (f32[4,2,128]{2,1,0:T(2,128)S(1)}, f32[4,2,128,384]{2,3,1,0:T(8,128)}) fusion(bf16[128,4,2,96]{0,3,2,1:T(8,128)(2,1)} %bitcast.184, bf16[256,4,96]{0,2,1:T(8,128)(2,1)} %bitcast.182, bf16[128,4,48]{0,2,1:T(8,128)(2,1)} %get-tuple-element.22, bf16[128,4,48]{0,2,1:T(8,128)(2,1)} %get-tuple-element.21, pred[384]{0:T(512)(128)(4,1)S(1)} %copy-done.28), kind=kOutput, calls=%fused_computation.117 | convolution fusion | flops 77955456 | bytes 2068864 | tf_op jit(solution)/shard_map/sub | solution.py:81
  268.0 1.8 convolution_convert_fusion
  269.8 1.4 fusion.2
  (89 shorter events, 6.3 us)
Async XLA Ops:
  6.5 84.9 %copy-start = (bf16[768,1536]{1,0:T(8,128)(2,1)S(1)}, bf16[768,1536]{1,0:T(8,128)(2,1)}, u32[]{:S(2)}) copy-start(bf16[768,1536]{1,0:T(8,128)(2,1)} %param.23) | copy-start | bytes 7077892
  6.5 103.0 %all-gather.7.cloned.1.call-start = ((), (), s32[]{:S(2)}) async-start(), calls=%async_computation.1 | async-start | bytes 12976128 | tf_op jit(solution)/shard_map/all_gather | solution.py:164
  7.3 183.2 %all-gather.9.cloned.1.call-start = ((), (), s32[]{:S(2)}) async-start(), calls=%async_computation.2 | async-start | bytes 3932160 | tf_op jit(solution)/shard_map/all_gather | solution.py:94
  7.3 27.2 %collective-permute-start = (bf16[2,256,384]{2,1,0:T(8,128)(2,1)}, bf16[2,256,384]{2,1,0:T(8,128)(2,1)S(1)}, u32[]{:S(2)}, u32[]{:S(2)}) collective-permute-start(bf16[2,256,384]{2,1,0:T(8,128)(2,1)} %bitcast.170), channel_id=1, source_target_pairs={{0,128},{32,160},{64,192},{96,224},{128,0},{160,32},{192,64},{224,... | collective-permute-start | bytes 1179656 | tf_op jit(solution)/shard_map/ppermute | solution.py:123
  11.0 18.0 %collective-permute-start.1 = (s32[1]{0:T(128)}, s32[1]{0:T(128)}, u32[]{:S(2)}, u32[]{:S(2)}) collective-permute-start(s32[1]{0:T(128)} %param.17), channel_id=1, source_target_pairs={{0,32},{32,0},{64,96},{96,64},{128,160},{160,128},{192,224},{224,1... | collective-permute-start | bytes 20 | tf_op jit(solution)/shard_map/ppermute | solution.py:123
  18.6 5.0 %copy-start.27 = (s32[1,128]{1,0:T(1,128)S(1)}, s32[1,128]{1,0:T(1,128)}, u32[]{:S(2)}) copy-start(s32[1,128]{1,0:T(1,128)} %param.18) | copy-start | bytes 1540
  18.6 5.6 %copy-start.2 = (bf16[1,128,1536]{2,1,0:T(8,128)(2,1)S(1)}, bf16[1,128,1536]{2,1,0:T(8,128)(2,1)}, u32[]{:S(2)}) copy-start(bf16[1,128,1536]{2,1,0:T(8,128)(2,1)} %param.14) | copy-start | bytes 1179652
  18.6 6.6 %copy-start.17 = (f32[1536]{0:T(1024)S(1)}, f32[1536]{0:T(1024)}, u32[]{:S(2)}) copy-start(f32[1536]{0:T(1024)} %param.19) | copy-start | bytes 18436
  23.6 0.6 copy-start.23
  24.3 4.1 %copy-start.21 = (f32[128]{0:T(128)}, f32[128]{0:T(128)S(1)}, u32[]{:S(2)}) copy-start(f32[128]{0:T(128)S(1)} %add_rsqrt_fusion.2) | copy-start | bytes 1540
  25.1 9.3 %copy-start.7 = (bf16[1,2,256,384]{3,2,1,0:T(8,128)(2,1)S(1)}, bf16[1,2,256,384]{3,2,1,0:T(8,128)(2,1)}, u32[]{:S(2)}) copy-start(bf16[1,2,256,384]{3,2,1,0:T(8,128)(2,1)} %param.15) | copy-start | bytes 1179652
  29.7 2.8 %collective-permute-start.2 = (s32[2]{0:T(128)S(1)}, s32[2]{0:T(128)S(1)}, u32[]{:S(2)}, u32[]{:S(2)}) collective-permute-start(s32[2]{0:T(128)S(1)} %pad_add_fusion), channel_id=1, source_target_pairs={{0,64},{32,96},{64,0},{96,32},{128,192},{160,224},{192,128},{224,1... | collective-permute-start | bytes 32 | tf_op jit(solution)/shard_map/ppermute | solution.py:123
  34.5 1.7 copy-start.25
  35.6 17.4 %collective-permute-start.3 = (bf16[2,2,256,384]{3,2,1,0:T(8,128)(2,1)}, bf16[2,2,256,384]{3,2,1,0:T(8,128)(2,1)}, u32[]{:S(2)}, u32[]{:S(2)}) collective-permute-start(bf16[2,2,256,384]{3,2,1,0:T(8,128)(2,1)} %pad_maximum_fusion), channel_id=1, source_target_pairs={{0,64},{32,96},{64,0},{96,32},{128,192},{160,224},{192,128},{224,1... | collective-permute-start | bytes 2359304 | tf_op jit(solution)/shard_map/ppermute | solution.py:123
  38.6 4.2 %copy-start.6 = (bf16[1536,384]{0,1:T(8,128)(2,1)S(1)}, bf16[1536,384]{0,1:T(8,128)(2,1)}, u32[]{:S(2)}) copy-start(bf16[1536,384]{0,1:T(8,128)(2,1)} %copy.54) | copy-start | bytes 3538948
  38.6 4.2 %copy-start.22 = (f32[128]{0:T(128)S(1)}, f32[128]{0:T(128)}, u32[]{:S(2)}) copy-start(f32[128]{0:T(128)} %copy-done.21) | copy-start | bytes 1540
  54.7 30.1 %collective-permute-start.4 = (bf16[2,256,384]{2,1,0:T(8,128)(2,1)}, bf16[2,256,384]{2,1,0:T(8,128)(2,1)}, u32[]{:S(2)}, u32[]{:S(2)}) collective-permute-start(bf16[2,256,384]{2,1,0:T(8,128)(2,1)} %fusion.28), channel_id=1, source_target_pairs={{0,32},{32,0},{64,96},{96,64},{128,160},{160,128},{192,224},{224,1... | collective-permute-start | bytes 1179656 | tf_op jit(solution)/shard_map/ppermute | solution.py:123
  86.1 0.8 copy-start.18
  86.1 0.8 copy-start.19
  86.3 3.4 %copy-start.15 = (bf16[1,256,384]{1,2,0:T(8,128)(2,1)}, bf16[1,256,384]{1,2,0:T(8,128)(2,1)S(1)}, u32[]{:S(2)}) copy-start(bf16[1,256,384]{1,2,0:T(8,128)(2,1)S(1)} %copy.53) | copy-start | bytes 589828
  86.5 3.2 %copy-start.13 = (bf16[1,256,384]{1,2,0:T(8,128)(2,1)}, bf16[1,256,384]{1,2,0:T(8,128)(2,1)S(1)}, u32[]{:S(2)}) copy-start(bf16[1,256,384]{1,2,0:T(8,128)(2,1)S(1)} %copy.51) | copy-start | bytes 589828
  86.9 2.8 %copy-start.16 = (bf16[128,384]{0,1:T(8,128)(2,1)S(1)}, bf16[128,384]{0,1:T(8,128)(2,1)}, u32[]{:S(2)}) copy-start(bf16[128,384]{0,1:T(8,128)(2,1)} %copy.52) | copy-start | bytes 294916
  91.4 1.5 copy-start.20
  92.0 0.9 copy-start.4
  121.3 94.2 %all-gather.11.cloned.1.call-start = ((), (), s32[]{:S(2)}) async-start(), calls=%async_computation.3 | async-start | bytes 9437184 | tf_op jit(solution)/shard_map/all_gather | solution.py:94
  190.4 25.1 %copy-start.12 = (bf16[1536,128]{1,0:T(8,128)(2,1)S(1)}, bf16[1536,128]{1,0:T(8,128)(2,1)}, u32[]{:S(2)}) copy-start(bf16[1536,128]{1,0:T(8,128)(2,1)} %param.25) | copy-start | bytes 1179652
  215.5 4.7 %copy-start.1 = (bf16[8,4,64,1536]{3,2,1,0:T(8,128)(2,1)S(1)}, bf16[8,4,64,1536]{3,2,1,0:T(8,128)(2,1)}, u32[]{:S(2)}) copy-start(bf16[8,4,64,1536]{3,2,1,0:T(8,128)(2,1)} %all-gather.11.cloned.1.call-done) | copy-start | bytes 18874372
  215.5 4.8 %copy-start.26 = (bf16[1536,128]{1,0:T(8,128)(2,1)S(1)}, bf16[1536,128]{1,0:T(8,128)(2,1)}, u32[]{:S(2)}) copy-start(bf16[1536,128]{1,0:T(8,128)(2,1)} %param.26) | copy-start | bytes 1179652
  223.0 24.2 %all-to-all-start = ((bf16[32,64,128]{2,1,0:T(8,128)(2,1)}), bf16[32,64,128]{2,1,0:T(8,128)(2,1)S(1)}, u32[]{:S(2)}, u32[]{:S(2)}) async-start(bf16[32,64,128]{2,1,0:T(8,128)(2,1)} %bitcast.173), calls=%async_computation | async-start | bytes 1048576 | tf_op jit(solution)/shard_map/all_to_all | solution.py:103
  247.2 0.9 copy-start.8
  254.6 1.8 copy-start.24
  256.3 2.1 copy-start.3
  258.5 1.3 copy-start.5
  259.8 1.3 copy-start.9
  259.8 2.3 copy-start.10
  259.8 2.3 copy-start.11
  261.0 4.1 %copy-start.28 = (pred[384]{0:T(512)(128)(4,1)S(1)}, pred[384]{0:T(512)(128)(4,1)}, u32[]{:S(2)}) copy-start(pred[384]{0:T(512)(128)(4,1)} %concatenate.51) | copy-start | bytes 1156
  265.1 2.9 %copy-start.14 = (bf16[1,256,384]{1,2,0:T(8,128)(2,1)S(1)}, bf16[1,256,384]{1,2,0:T(8,128)(2,1)}, u32[]{:S(2)}) copy-start(bf16[1,256,384]{1,2,0:T(8,128)(2,1)} %copy-done.13) | copy-start | bytes 589828
Sparse Core Ops, SparseCore 0:
  9.2 100.2 all-gather.6
  121.5 68.9 all-gather.8
  192.2 23.2 all-gather.10

commit v11 on v8

--- a/solution.py
+++ b/solution.py
@@ -82,8 +82,11 @@
     return widened + jnp.dot(context, o_weight, preferred_element_type=jnp.float32)
 
 
-def run_ffn(normed_rows, w_gate, w_up, down_all, groups):
-    part_rows = lax.all_gather(normed_rows, "blk", axis=0, tiled=True)
+def run_ffn(normed_rows, w_gate, w_up, w_down):
+    packed = lax.all_gather(jnp.concatenate([normed_rows, w_down], axis=0), "blk", axis=0, tiled=False)
+    part_rows = packed[:, : normed_rows.shape[0]].reshape(-1, normed_rows.shape[1])
+    down_all = packed[:, normed_rows.shape[0] :].reshape(-1, w_down.shape[1])
+    groups = w_down.shape[0]
     gate_vals = jnp.dot(part_rows, w_gate, preferred_element_type=jnp.float32)
     up_vals = jnp.dot(part_rows, w_up, preferred_element_type=jnp.float32)
     hidden_all = (jax.nn.silu(gate_vals) * up_vals).astype(jnp.bfloat16)
@@ -148,7 +151,6 @@
     w_down,
 ):
     fetched = fetch_slot(cache_kv, holder)
-    down_all = lax.all_gather(w_down, "blk", axis=0, tiled=True)
     cache_keys = fetched[0]
     cache_vals = fetched[1]
     cache_length = cache_len[0]
@@ -171,8 +173,7 @@
     hits = chosen_mask[None, :] & (slot_of[None, :] == jnp.arange(kept, dtype=jnp.int32)[:, None])
     kept_rows = jnp.sum(jnp.where(hits, jnp.arange(block_len, dtype=jnp.int32)[None, :], 0), axis=1)
     fnorm = rms_scale(first_pass, ffn_gain).astype(jnp.bfloat16)
-    ffn_rows, down_all = lax.optimization_barrier((fnorm[kept_rows], down_all))
-    ffn_kept = run_ffn(ffn_rows, w_gate, w_up, down_all, w_down.shape[0])
+    ffn_kept = run_ffn(fnorm[kept_rows], w_gate, w_up, w_down)
     ffn_sum = ffn_kept[jnp.clip(slot_of, 0, kept - 1)]
     placed = first_pass + ffn_sum
     second_in = jnp.where(chosen_mask[:, None], placed, block_rows.astype(jnp.float32))

time: 239 us -> 258 us (1.079)
  waiting for transfers between devices: 133 us -> 150 us
  matrix products: 34.7 us -> 31.7 us
  other arithmetic: 16 us -> 18.6 us
    all_gather x2 -> x1, waiting for transfers between devices: 82.7 us -> 117 us  [run_ffn(): lax.all_gather(jnp.concatenate([normed_rows, w_down], axis=0), 'blk', axi...]
    ppermute x5, waiting for transfers between devices: 33 us -> 15.7 us  [swap(): lax.ppermute(values, 'req', perm=[(i, i ^ mask) for i in range(count)])]
    slice x0 -> x1, local copies, waits for them, and re-layouts: none -> 3.52 us  [run_ffn(): packed[:, :normed_rows.shape[0]].reshape(-1, normed_rows.shape[1])]
    dot_general x1, matrix products: 4.73 us -> 1.8 us  [run_ffn(): gate_vals = jnp.dot(part_rows, w_gate, preferred_element_type=jnp.float32)]
    unnamed x60 -> x56, local copies, waits for them, and re-layouts: 10.1 us -> 9.22 us
  transfers between devices with their start and end apart: 8 -> 7, of which waited for: 6 -> 5; matrix products, arithmetic and copies ran while one was open for 15% -> 10% of each run, Pallas kernels for 0% -> 0%
where the time goes in v11:
time: 258 us; the launch traced here: 257 us
  waiting for transfers between devices  150 us (58%)
  matrix products  31.7 us (12%)
  local copies, waits for them, and re-layouts  20.7 us (8%)
  starting transfers between devices  18.8 us (7%)
  other arithmetic  18.6 us (7%)
  between operations  17.4 us (7%)
    all_gather x1, waiting for transfers between devices, run_ffn(): lax.all_gather(jnp.concatenate([normed_rows, w_down], axis=0), 'blk', axi...  117 us
    all_to_all x1, waiting for transfers between devices, run_ffn(): hidden_own = lax.all_to_all(hidden_all, 'blk', 0, 1, tiled=True)  16.8 us
    ppermute x5, waiting for transfers between devices, swap(): lax.ppermute(values, 'req', perm=[(i, i ^ mask) for i in range(count)])  15.7 us
    ppermute x5, starting transfers between devices, swap(): lax.ppermute(values, 'req', perm=[(i, i ^ mask) for i in range(count)])  11.4 us
    unnamed x56, local copies, waits for them, and re-layouts  9.22 us
    all_to_all x1, starting transfers between devices, run_ffn(): hidden_own = lax.all_to_all(hidden_all, 'blk', 0, 1, tiled=True)  7.38 us
    dot_general x1, matrix products, run_ffn(): jnp.einsum('rgk,gkd->grd', hidden_own.reshape(hidden_own.shape[0], group_...  6.58 us
    sub x2, matrix products, attend_block(): expd = jnp.exp(scores - peaks)  5.7 us
  transfers between devices with their start and end apart: 7, of which 5 were waited for; matrix products, arithmetic and copies ran while one was open for 10% of the time, Pallas kernels for 0%

profile of v11, /device:TPU:1, one launch (start us, length us, event | category | flops | bytes accessed | tf_op | source)
XLA Modules:
  0.0 256.7 jit_solution(18137055183974196872)
XLA Ops:
  6.5 7.7 %collective-permute-start.1 = (s32[1]{0:T(128)}, s32[1]{0:T(128)}, u32[]{:S(2)}, u32[]{:S(2)}) collective-permute-start(s32[1]{0:T(128)} %param.17), channel_id=1, source_target_pairs={{0,32},{32,0},{64,96},{96,64},{128,160},{160,128},{192,224},{224,1... | collective-permute-start | bytes 20 | tf_op jit(solution)/shard_map/ppermute | solution.py:113
  14.3 2.7 %collective-permute-start = (bf16[2,256,384]{2,1,0:T(8,128)(2,1)}, bf16[2,256,384]{2,1,0:T(8,128)(2,1)S(1)}, u32[]{:S(2)}, u32[]{:S(2)}) collective-permute-start(bf16[2,256,384]{2,1,0:T(8,128)(2,1)} %bitcast.163), channel_id=1, source_target_pairs={{0,128},{32,160},{64,192},{96,224},{128,0},{160,32},{192,64},{224,... | collective-permute-start | bytes 1179656 | tf_op jit(solution)/shard_map/ppermute | solution.py:113
  18.4 1.2 fusion.21
  19.6 4.3 %copy.41 = bf16[1536,768]{0,1:T(8,128)(2,1)} copy(bf16[1536,768]{1,0:T(8,128)(2,1)} %param.20) | data formatting | bytes 4718592 | tf_op args[6]
  24.3 0.8 multiply_cosine_fusion
  25.3 3.3 %fusion.59 = f32[128,8,96]{0,2,1:T(8,128)} fusion(bf16[8,96,1536]{2,1,0:T(8,128)(2,1)} %bitcast.161, bf16[1,128,1536]{2,1,0:T(8,128)(2,1)S(1)} %copy-done.1, f32[1536]{0:T(1024)S(1)} %copy-done.15, f32[128]{0:T(128)S(1)} %add_rsqrt_fusion.2), kind=kOutput, calls=%fused_computation.80 | convolution fusion | flops 302776320 | bytes 3152384 | tf_op jit(solution)/shard_map/dot_general | solution.py:54
  28.6 0.6 fusion.66
  29.1 0.6 pad_add_fusion
  30.1 2.1 collective-permute-done.2
  32.2 0.6 fusion.85
  34.2 1.0 pad_maximum_fusion
  35.5 2.4 copy.40
  37.9 1.8 subtract_convert_fusion.1
  39.7 2.3 convolution_convert_fusion.3
  42.1 1.2 fusion.61
  44.4 7.7 %collective-permute-done.3 = bf16[2,2,256,384]{3,2,1,0:T(8,128)(2,1)} collective-permute-done((bf16[2,2,256,384]{3,2,1,0:T(8,128)(2,1)}, bf16[2,2,256,384]{3,2,1,0:T(8,128)(2,1)}, u32[]{:S(2)}, u32[]{:S(2)}) %collective-permute-start.3) | collective-permute-done | bytes 786464 | tf_op jit(solution)/shard_map/ppermute | solution.py:113
  52.1 1.8 fusion.32
  54.7 1.6 copy.38
  56.4 1.2 concatenate.54
  57.5 1.6 pad_maximum_fusion.6
  59.2 1.6 subtract_convert_fusion.3
  60.8 5.9 %collective-permute-done.4 = bf16[2,256,384]{2,1,0:T(8,128)(2,1)} collective-permute-done((bf16[2,256,384]{2,1,0:T(8,128)(2,1)}, bf16[2,256,384]{2,1,0:T(8,128)(2,1)}, u32[]{:S(2)}, u32[]{:S(2)}) %collective-permute-start.4) | collective-permute-done | bytes 393248 | tf_op jit(solution)/shard_map/ppermute | solution.py:113
  66.7 1.2 fusion.28
  68.7 2.8 %fusion.86 = (f32[4,2,128]{2,1,0:T(2,128)S(1)}, f32[4,2,128,384]{2,3,1,0:T(8,128)}) fusion(bf16[128,4,2,96]{0,3,2,1:T(8,128)(2,1)} %bitcast.174, bf16[256,4,96]{0,2,1:T(8,128)(2,1)S(1)} %bitcast.172, bf16[128,4,48]{0,2,1:T(8,128)(2,1)S(1)} %copy-done.17, bf16[128,4,48]{0,2,1:T(8,128)(2,1)S(1)} %copy-done.16, pred[384]{0:T(512)(128)(4,1)} %concatenate.54), kind=kOutput, calls=%fused_computation.119 | convolution fusion | flops 77955456 | bytes 2068864 | tf_op jit(solution)/shard_map/sub | solution.py:78
  71.5 1.7 convolution_convert_fusion.1
  73.2 0.6 multiply_reduce_fusion.1
  73.8 0.9 copy-done.3
  74.8 0.7 gather_fusion
  75.6 1.9 pad_maximum_fusion.1
  77.5 117.0 %all-gather.3.cloned.1.call-done = bf16[6144,1536]{1,0:T(8,128)(2,1)} async-done(((bf16[192,1536]{1,0:T(8,128)(2,1)}), bf16[6144,1536]{1,0:T(8,128)(2,1)}) %all-gather.3.cloned.1.call-update) | async-done | bytes 18874384 | tf_op jit(solution)/shard_map/all_gather | solution.py:86
  194.4 3.5 %slice.77 = bf16[32,64,1536]{2,1,0:T(8,128)(2,1)S(1)} slice(bf16[32,192,1536]{2,1,0:T(8,128)(2,1)} %bitcast.164), slice={[0:32], [0:64], [0:1536]} | slice | bytes 12582912 | tf_op jit(solution)/shard_map/slice | solution.py:87
  198.0 1.8 fusion.92
  199.8 2.6 %fusion.7 = bf16[2048,128]{1,0:T(8,128)(2,1)} fusion(bf16[2048,1536]{1,0:T(8,128)(2,1)S(1)} %bitcast.160, bf16[1536,128]{1,0:T(8,128)(2,1)S(1)} %copy-done.24, f32[2048,128]{1,0:T(8,128)S(1)} %fusion.92), kind=kOutput, calls=%fused_computation.11 | convolution fusion | flops 806879232 | bytes 8257536 | tf_op jit(solution)/shard_map/dot_general | solution.py:91
  202.4 7.4 %all-to-all-start = ((bf16[32,64,128]{2,1,0:T(8,128)(2,1)}), bf16[32,64,128]{2,1,0:T(8,128)(2,1)}, u32[]{:S(2)}, u32[]{:S(2)}) async-start(bf16[32,64,128]{2,1,0:T(8,128)(2,1)} %bitcast.34), calls=%async_computation | async-start | bytes 1048576 | tf_op jit(solution)/shard_map/all_to_all | solution.py:93
  209.8 16.8 %all-to-all-done = bf16[32,64,128]{2,1,0:T(8,128)(2,1)} async-done(((bf16[32,64,128]{2,1,0:T(8,128)(2,1)}), bf16[32,64,128]{2,1,0:T(8,128)(2,1)}, u32[]{:S(2)}, u32[]{:S(2)}) %all-to-all-start) | async-done | bytes 524320 | tf_op jit(solution)/shard_map/all_to_all | solution.py:93
  226.7 6.6 %convert_reduce_fusion = f32[64,1536]{1,0:T(8,128)S(1)} fusion(bf16[32,192,1536]{2,1,0:T(8,128)(2,1)} %bitcast.165, bf16[32,64,128]{2,1,0:T(8,128)(2,1)} %all-to-all-done), kind=kOutput, calls=%fused_computation.6 | convolution fusion | flops 814645248 | bytes 13500416 | tf_op jit(solution)/shard_map/rgk,gkd->grd/dot_general | solution.py:95
  233.3 1.8 gather_fusion.1
  235.0 1.8 multiply_reduce_fusion
  237.2 1.1 fusion.94
  238.4 0.6 fusion.93
  239.0 0.7 copy-done.7
  239.7 1.0 convolution_convert_fusion.2
  240.8 0.7 subtract_convert_fusion.2
  241.5 1.6 copy.44
  243.1 0.7 pad_maximum_fusion.7
  243.8 2.9 %fusion.89 = (f32[4,2,128]{2,1,0:T(2,128)S(1)}, f32[4,2,128,384]{2,3,1,0:T(8,128)}) fusion(bf16[128,4,2,96]{0,3,2,1:T(8,128)(2,1)} %bitcast.175, bf16[256,4,96]{0,2,1:T(8,128)(2,1)} %bitcast.173, bf16[128,4,48]{0,2,1:T(8,128)(2,1)} %get-tuple-element.18, bf16[128,4,48]{0,2,1:T(8,128)(2,1)} %get-tuple-element.17, pred[384]{0:T(512)(128)(4,1)S(1)} %copy-done.26), kind=kOutput, calls=%fused_computation.120 | convolution fusion | flops 77955456 | bytes 2068864 | tf_op jit(solution)/shard_map/sub | solution.py:78
  246.7 1.8 convolution_convert_fusion
  248.5 1.4 fusion.6
  (79 shorter events, 3.8 us)
Async XLA Ops:
  6.5 66.7 %copy-start = (bf16[768,1536]{1,0:T(8,128)(2,1)S(1)}, bf16[768,1536]{1,0:T(8,128)(2,1)}, u32[]{:S(2)}) copy-start(bf16[768,1536]{1,0:T(8,128)(2,1)} %param.23) | copy-start | bytes 7077892
  6.5 187.9 %all-gather.3.cloned.1.call-start = ((), (), s32[]{:S(2)}) async-start(), calls=%async_computation.1 | async-start | bytes 19464192 | tf_op jit(solution)/shard_map/all_gather | solution.py:86
  6.5 22.6 %collective-permute-start.1 = (s32[1]{0:T(128)}, s32[1]{0:T(128)}, u32[]{:S(2)}, u32[]{:S(2)}) collective-permute-start(s32[1]{0:T(128)} %param.17), channel_id=1, source_target_pairs={{0,32},{32,0},{64,96},{96,64},{128,160},{160,128},{192,224},{224,1... | collective-permute-start | bytes 20 | tf_op jit(solution)/shard_map/ppermute | solution.py:113
  14.3 19.8 %collective-permute-start = (bf16[2,256,384]{2,1,0:T(8,128)(2,1)}, bf16[2,256,384]{2,1,0:T(8,128)(2,1)S(1)}, u32[]{:S(2)}, u32[]{:S(2)}) collective-permute-start(bf16[2,256,384]{2,1,0:T(8,128)(2,1)} %bitcast.163), channel_id=1, source_target_pairs={{0,128},{32,160},{64,192},{96,224},{128,0},{160,32},{192,64},{224,... | collective-permute-start | bytes 1179656 | tf_op jit(solution)/shard_map/ppermute | solution.py:113
  19.5 5.7 %copy-start.19 = (f32[128]{0:T(128)}, f32[128]{0:T(128)S(1)}, u32[]{:S(2)}) copy-start(f32[128]{0:T(128)S(1)} %add_rsqrt_fusion.2) | copy-start | bytes 1540
  19.5 4.4 %copy-start.25 = (s32[1,128]{1,0:T(1,128)S(1)}, s32[1,128]{1,0:T(1,128)}, u32[]{:S(2)}) copy-start(s32[1,128]{1,0:T(1,128)} %param.18) | copy-start | bytes 1540
  19.5 5.7 %copy-start.1 = (bf16[1,128,1536]{2,1,0:T(8,128)(2,1)S(1)}, bf16[1,128,1536]{2,1,0:T(8,128)(2,1)}, u32[]{:S(2)}) copy-start(bf16[1,128,1536]{2,1,0:T(8,128)(2,1)} %param.14) | copy-start | bytes 1179652
  19.6 5.7 %copy-start.15 = (f32[1536]{0:T(1024)S(1)}, f32[1536]{0:T(1024)}, u32[]{:S(2)}) copy-start(f32[1536]{0:T(1024)} %param.19) | copy-start | bytes 18436
  23.9 1.3 copy-start.21
  25.3 8.8 %copy-start.6 = (bf16[1,2,256,384]{3,2,1,0:T(8,128)(2,1)S(1)}, bf16[1,2,256,384]{3,2,1,0:T(8,128)(2,1)}, u32[]{:S(2)}) copy-start(bf16[1,2,256,384]{3,2,1,0:T(8,128)(2,1)} %param.15) | copy-start | bytes 1179652
  29.8 2.4 collective-permute-start.2
  34.1 1.4 copy-start.23
  35.1 17.0 %collective-permute-start.3 = (bf16[2,2,256,384]{3,2,1,0:T(8,128)(2,1)}, bf16[2,2,256,384]{3,2,1,0:T(8,128)(2,1)}, u32[]{:S(2)}, u32[]{:S(2)}) collective-permute-start(bf16[2,2,256,384]{3,2,1,0:T(8,128)(2,1)} %pad_maximum_fusion), channel_id=1, source_target_pairs={{0,64},{32,96},{64,0},{96,32},{128,192},{160,224},{192,128},{224,1... | collective-permute-start | bytes 2359304 | tf_op jit(solution)/shard_map/ppermute | solution.py:113
  37.9 4.2 %copy-start.5 = (bf16[1536,384]{0,1:T(8,128)(2,1)S(1)}, bf16[1536,384]{0,1:T(8,128)(2,1)}, u32[]{:S(2)}) copy-start(bf16[1536,384]{0,1:T(8,128)(2,1)} %copy.40) | copy-start | bytes 3538948
  37.9 4.2 %copy-start.20 = (f32[128]{0:T(128)S(1)}, f32[128]{0:T(128)}, u32[]{:S(2)}) copy-start(f32[128]{0:T(128)} %copy-done.19) | copy-start | bytes 1540
  53.9 12.8 %collective-permute-start.4 = (bf16[2,256,384]{2,1,0:T(8,128)(2,1)}, bf16[2,256,384]{2,1,0:T(8,128)(2,1)}, u32[]{:S(2)}, u32[]{:S(2)}) collective-permute-start(bf16[2,256,384]{2,1,0:T(8,128)(2,1)} %fusion.32), channel_id=1, source_target_pairs={{0,32},{32,0},{64,96},{96,64},{128,160},{160,128},{192,224},{224,1... | collective-permute-start | bytes 1179656 | tf_op jit(solution)/shard_map/ppermute | solution.py:113
  67.9 0.8 copy-start.16
  67.9 0.8 copy-start.17
  68.1 3.4 %copy-start.13 = (bf16[1,256,384]{1,2,0:T(8,128)(2,1)}, bf16[1,256,384]{1,2,0:T(8,128)(2,1)S(1)}, u32[]{:S(2)}) copy-start(bf16[1,256,384]{1,2,0:T(8,128)(2,1)S(1)} %copy.39) | copy-start | bytes 589828
  68.3 3.2 %copy-start.11 = (bf16[1,256,384]{1,2,0:T(8,128)(2,1)}, bf16[1,256,384]{1,2,0:T(8,128)(2,1)S(1)}, u32[]{:S(2)}) copy-start(bf16[1,256,384]{1,2,0:T(8,128)(2,1)S(1)} %copy.37) | copy-start | bytes 589828
  68.7 2.8 %copy-start.14 = (bf16[128,384]{0,1:T(8,128)(2,1)S(1)}, bf16[128,384]{0,1:T(8,128)(2,1)}, u32[]{:S(2)}) copy-start(bf16[128,384]{0,1:T(8,128)(2,1)} %copy.38) | copy-start | bytes 294916
  73.2 1.5 copy-start.18
  73.8 0.9 copy-start.3
  194.4 3.5 %copy-start.10 = (bf16[1536,128]{1,0:T(8,128)(2,1)S(1)}, bf16[1536,128]{1,0:T(8,128)(2,1)}, u32[]{:S(2)}) copy-start(bf16[1536,128]{1,0:T(8,128)(2,1)} %param.25) | copy-start | bytes 1179652
  198.0 1.8 copy-start.24
  202.4 24.2 %all-to-all-start = ((bf16[32,64,128]{2,1,0:T(8,128)(2,1)}), bf16[32,64,128]{2,1,0:T(8,128)(2,1)}, u32[]{:S(2)}, u32[]{:S(2)}) async-start(bf16[32,64,128]{2,1,0:T(8,128)(2,1)} %bitcast.34), calls=%async_computation | async-start | bytes 1048576 | tf_op jit(solution)/shard_map/all_to_all | solution.py:93
  233.2 1.8 copy-start.22
  235.0 2.1 copy-start.2
  237.2 1.3 copy-start.4
  238.4 1.3 copy-start.7
  238.4 2.3 copy-start.8
  238.4 2.3 copy-start.9
  239.7 4.1 %copy-start.26 = (pred[384]{0:T(512)(128)(4,1)S(1)}, pred[384]{0:T(512)(128)(4,1)}, u32[]{:S(2)}) copy-start(pred[384]{0:T(512)(128)(4,1)} %concatenate.54) | copy-start | bytes 1156
  243.8 2.9 %copy-start.12 = (bf16[1,256,384]{1,2,0:T(8,128)(2,1)S(1)}, bf16[1,256,384]{1,2,0:T(8,128)(2,1)}, u32[]{:S(2)}) copy-start(bf16[1,256,384]{1,2,0:T(8,128)(2,1)} %copy-done.11) | copy-start | bytes 589828
Sparse Core Ops, SparseCore 0:
  77.6 116.7 all-gather.2

commit v12 on v8

--- a/solution.py
+++ b/solution.py
@@ -84,8 +84,8 @@
 
 def run_ffn(normed_rows, w_gate, w_up, down_all, groups):
     part_rows = lax.all_gather(normed_rows, "blk", axis=0, tiled=True)
-    gate_vals = jnp.dot(part_rows, w_gate, preferred_element_type=jnp.float32)
-    up_vals = jnp.dot(part_rows, w_up, preferred_element_type=jnp.float32)
+    both = jnp.dot(part_rows, jnp.concatenate([w_gate, w_up], axis=1), preferred_element_type=jnp.float32)
+    gate_vals, up_vals = both[:, : w_gate.shape[1]], both[:, w_gate.shape[1] :]
     hidden_all = (jax.nn.silu(gate_vals) * up_vals).astype(jnp.bfloat16)
     hidden_own = lax.all_to_all(hidden_all, "blk", 0, 1, tiled=True)
     group_count = down_all.shape[0] // groups

time: 239 us -> 237 us (level)
  matrix products: 34.7 us -> 32 us
    dot_general x2 -> x1, matrix products: 7.39 us -> 4.63 us  [run_ffn(): jnp.dot(part_rows, jnp.concatenate([w_gate, w_up], axis=1), preferred_ele...]
    unnamed x60 -> x56, local copies, waits for them, and re-layouts: 10.1 us -> 10.1 us
where the time goes in v12:
time: 237 us; the launch traced here: 236 us
  waiting for transfers between devices  134 us (57%)
  matrix products  32 us (14%)
  local copies, waits for them, and re-layouts  18.6 us (8%)
  starting transfers between devices  17.5 us (7%)
  between operations  17.5 us (7%)
  other arithmetic  16.8 us (7%)
    all_gather x1, waiting for transfers between devices, run_ffn(): part_rows = lax.all_gather(normed_rows, 'blk', axis=0, tiled=True)  67.8 us
    ppermute x5, waiting for transfers between devices, swap(): lax.ppermute(values, 'req', perm=[(i, i ^ mask) for i in range(count)])  33 us
    all_to_all x1, waiting for transfers between devices, run_ffn(): hidden_own = lax.all_to_all(hidden_all, 'blk', 0, 1, tiled=True)  16.8 us
    all_gather x1, waiting for transfers between devices, local(): down_all = lax.all_gather(w_down, 'blk', axis=0, tiled=True)  15.4 us
    ppermute x5, starting transfers between devices, swap(): lax.ppermute(values, 'req', perm=[(i, i ^ mask) for i in range(count)])  12 us
    unnamed x56, local copies, waits for them, and re-layouts  10.1 us
    dot_general x1, matrix products, run_ffn(): jnp.einsum('rgk,gkd->grd', hidden_own.reshape(hidden_own.shape[0], group_...  6.57 us
    sub x2, matrix products, attend_block(): expd = jnp.exp(scores - peaks)  5.73 us
  transfers between devices with their start and end apart: 8, of which 6 were waited for; matrix products, arithmetic and copies ran while one was open for 15% of the time, Pallas kernels for 0%

profile of v12, /device:TPU:1, one launch (start us, length us, event | category | flops | bytes accessed | tf_op | source)
XLA Modules:
  0.0 236.2 jit_solution(9490013828320855576)
XLA Ops:
  6.5 0.7 all-gather.3.cloned.1.call-update
  7.3 3.7 %collective-permute-start = (bf16[2,256,384]{2,1,0:T(8,128)(2,1)}, bf16[2,256,384]{2,1,0:T(8,128)(2,1)S(1)}, u32[]{:S(2)}, u32[]{:S(2)}) collective-permute-start(bf16[2,256,384]{2,1,0:T(8,128)(2,1)} %bitcast.159), channel_id=1, source_target_pairs={{0,128},{32,160},{64,192},{96,224},{128,0},{160,32},{192,64},{224,... | collective-permute-start | bytes 1179656 | tf_op jit(solution)/shard_map/ppermute | solution.py:110
  11.0 6.9 %collective-permute-start.1 = (s32[1]{0:T(128)}, s32[1]{0:T(128)}, u32[]{:S(2)}, u32[]{:S(2)}) collective-permute-start(s32[1]{0:T(128)} %param.17), channel_id=1, source_target_pairs={{0,32},{32,0},{64,96},{96,64},{128,160},{160,128},{192,224},{224,1... | collective-permute-start | bytes 20 | tf_op jit(solution)/shard_map/ppermute | solution.py:110
  18.6 4.3 %copy.41 = bf16[1536,768]{0,1:T(8,128)(2,1)} copy(bf16[1536,768]{1,0:T(8,128)(2,1)} %param.20) | data formatting | bytes 4718592 | tf_op args[6]
  24.4 0.8 multiply_cosine_fusion
  25.2 3.3 %fusion.59 = f32[128,8,96]{0,2,1:T(8,128)} fusion(bf16[8,96,1536]{2,1,0:T(8,128)(2,1)} %bitcast.157, bf16[1,128,1536]{2,1,0:T(8,128)(2,1)S(1)} %copy-done.1, f32[1536]{0:T(1024)S(1)} %copy-done.15, f32[128]{0:T(128)S(1)} %add_rsqrt_fusion.2), kind=kOutput, calls=%fused_computation.81 | convolution fusion | flops 302776320 | bytes 3152384 | tf_op jit(solution)/shard_map/dot_general | solution.py:54
  29.0 0.7 pad_add_fusion
  29.7 0.6 collective-permute-start.2
  30.3 2.2 collective-permute-done.2
  34.4 1.0 pad_maximum_fusion
  35.4 0.6 collective-permute-start.3
  36.0 2.4 %copy.40 = bf16[1536,384]{0,1:T(8,128)(2,1)} copy(bf16[1536,384]{1,0:T(8,128)(2,1)} %param.21) | data formatting | bytes 2359296 | tf_op args[7]
  38.4 1.9 subtract_convert_fusion.1
  40.3 2.4 %convolution_convert_fusion.3 = bf16[128,384]{1,0:T(8,128)(2,1)} fusion(bf16[1536,384]{1,0:T(8,128)(2,1)} %param.22, bf16[1,128,1536]{2,1,0:T(8,128)(2,1)S(1)} %copy-done.1, f32[1536]{0:T(1024)S(1)} %copy-done.15, f32[128]{0:T(128)} %copy-done.19), kind=kOutput, calls=%fused_computation.23 | convolution fusion | flops 151830528 | bytes 1677824 | tf_op jit(solution)/shard_map/dot_general | solution.py:59
  42.7 1.3 fusion.61
  45.2 7.6 %collective-permute-done.3 = bf16[2,2,256,384]{3,2,1,0:T(8,128)(2,1)} collective-permute-done((bf16[2,2,256,384]{3,2,1,0:T(8,128)(2,1)}, bf16[2,2,256,384]{3,2,1,0:T(8,128)(2,1)}, u32[]{:S(2)}, u32[]{:S(2)}) %collective-permute-start.3) | collective-permute-done | bytes 786464 | tf_op jit(solution)/shard_map/ppermute | solution.py:110
  52.7 1.8 fusion.32
  55.3 1.6 copy.38
  57.0 1.1 concatenate.54
  58.1 1.6 pad_maximum_fusion.5
  59.8 1.6 subtract_convert_fusion.3
  61.4 23.2 %collective-permute-done.4 = bf16[2,256,384]{2,1,0:T(8,128)(2,1)} collective-permute-done((bf16[2,256,384]{2,1,0:T(8,128)(2,1)}, bf16[2,256,384]{2,1,0:T(8,128)(2,1)}, u32[]{:S(2)}, u32[]{:S(2)}) %collective-permute-start.4) | collective-permute-done | bytes 393248 | tf_op jit(solution)/shard_map/ppermute | solution.py:110
  84.5 1.1 fusion.28
  86.5 2.8 %fusion.87 = (f32[4,2,128]{2,1,0:T(2,128)S(1)}, f32[4,2,128,384]{2,3,1,0:T(8,128)}) fusion(bf16[128,4,2,96]{0,3,2,1:T(8,128)(2,1)} %bitcast.169, bf16[256,4,96]{0,2,1:T(8,128)(2,1)S(1)} %bitcast.167, bf16[128,4,48]{0,2,1:T(8,128)(2,1)S(1)} %copy-done.17, bf16[128,4,48]{0,2,1:T(8,128)(2,1)S(1)} %copy-done.16, pred[384]{0:T(512)(128)(4,1)} %concatenate.54), kind=kOutput, calls=%fused_computation.121 | convolution fusion | flops 77955456 | bytes 2068864 | tf_op jit(solution)/shard_map/sub | solution.py:78
  89.3 1.7 convolution_convert_fusion.1
  91.0 0.6 multiply_reduce_fusion.1
  91.7 0.9 copy-done.3
  92.7 1.4 gather_fusion
  94.1 15.4 %all-gather.3.cloned.1.call-done = bf16[4096,1536]{1,0:T(8,128)(2,1)} async-done(((bf16[128,1536]{1,0:T(8,128)(2,1)}), bf16[4096,1536]{1,0:T(8,128)(2,1)}) %all-gather.3.cloned.1.call-update) | async-done | bytes 12582928 | tf_op jit(solution)/shard_map/all_gather | solution.py:151
  109.5 67.8 %all-gather.5.cloned.1.call-done = bf16[2048,1536]{1,0:T(8,128)(2,1)} async-done(((bf16[64,1536]{1,0:T(8,128)(2,1)}), bf16[2048,1536]{1,0:T(8,128)(2,1)}) %all-gather.5.cloned.1.call-update) | async-done | bytes 6291472 | tf_op jit(solution)/shard_map/all_gather | solution.py:86
  177.3 4.6 %fusion.22 = f32[2048,256]{1,0:T(8,128)S(1)} fusion(bf16[2048,1536]{1,0:T(8,128)(2,1)} %all-gather.5.cloned.1.call-done, bf16[1536,128]{1,0:T(8,128)(2,1)S(1)} %copy-done.24, bf16[1536,128]{1,0:T(8,128)(2,1)} %param.25), kind=kOutput, calls=%fused_computation.37 | convolution fusion | flops 1612185600 | bytes 9175040 | tf_op jit(solution)/shard_map/dot_general | solution.py:87
  182.0 1.1 fusion.13
  183.1 5.4 %all-to-all-start = ((bf16[32,64,128]{2,1,0:T(8,128)(2,1)}), bf16[32,64,128]{2,1,0:T(8,128)(2,1)S(1)}, u32[]{:S(2)}, u32[]{:S(2)}) async-start(bf16[32,64,128]{2,1,0:T(8,128)(2,1)} %bitcast.160), calls=%async_computation | async-start | bytes 1048576 | tf_op jit(solution)/shard_map/all_to_all | solution.py:90
  188.5 16.8 %all-to-all-done = bf16[32,64,128]{2,1,0:T(8,128)(2,1)S(1)} async-done(((bf16[32,64,128]{2,1,0:T(8,128)(2,1)}), bf16[32,64,128]{2,1,0:T(8,128)(2,1)S(1)}, u32[]{:S(2)}, u32[]{:S(2)}) %all-to-all-start) | async-done | bytes 524320 | tf_op jit(solution)/shard_map/all_to_all | solution.py:90
  205.3 0.8 copy-done.7
  206.2 6.6 %convert_reduce_fusion = f32[64,1536]{1,0:T(8,128)S(1)} fusion(bf16[32,128,1536]{2,1,0:T(8,128)(2,1)} %bitcast.156, bf16[32,64,128]{2,1,0:T(8,128)(2,1)} %copy-done.7), kind=kOutput, calls=%fused_computation.4 | convolution fusion | flops 814645248 | bytes 13500416 | tf_op jit(solution)/shard_map/rgk,gkd->grd/dot_general | solution.py:92
  212.8 1.8 gather_fusion.1
  214.5 1.8 multiply_reduce_fusion
  216.6 1.1 fusion.94
  217.9 0.6 fusion.93
  218.5 0.7 copy-done.8
  219.2 1.0 convolution_convert_fusion.2
  220.3 0.7 subtract_convert_fusion.2
  221.0 1.6 copy.44
  222.6 0.7 pad_maximum_fusion.6
  223.3 2.9 %fusion.90 = (f32[4,2,128]{2,1,0:T(2,128)S(1)}, f32[4,2,128,384]{2,3,1,0:T(8,128)}) fusion(bf16[128,4,2,96]{0,3,2,1:T(8,128)(2,1)} %bitcast.170, bf16[256,4,96]{0,2,1:T(8,128)(2,1)} %bitcast.168, bf16[128,4,48]{0,2,1:T(8,128)(2,1)} %get-tuple-element.22, bf16[128,4,48]{0,2,1:T(8,128)(2,1)} %get-tuple-element.21, pred[384]{0:T(512)(128)(4,1)S(1)} %copy-done.26), kind=kOutput, calls=%fused_computation.122 | convolution fusion | flops 77955456 | bytes 2068864 | tf_op jit(solution)/shard_map/sub | solution.py:78
  226.2 1.8 convolution_convert_fusion
  228.0 1.4 fusion.2
  (80 shorter events, 4.3 us)
Async XLA Ops:
  6.5 84.5 %copy-start = (bf16[768,1536]{1,0:T(8,128)(2,1)S(1)}, bf16[768,1536]{1,0:T(8,128)(2,1)}, u32[]{:S(2)}) copy-start(bf16[768,1536]{1,0:T(8,128)(2,1)} %param.23) | copy-start | bytes 7077892
  6.5 102.9 %all-gather.3.cloned.1.call-start = ((), (), s32[]{:S(2)}) async-start(), calls=%async_computation.1 | async-start | bytes 12976128 | tf_op jit(solution)/shard_map/all_gather | solution.py:151
  7.3 170.1 %all-gather.5.cloned.1.call-start = ((), (), s32[]{:S(2)}) async-start(), calls=%async_computation.2 | async-start | bytes 6488064 | tf_op jit(solution)/shard_map/all_gather | solution.py:86
  7.3 27.0 %collective-permute-start = (bf16[2,256,384]{2,1,0:T(8,128)(2,1)}, bf16[2,256,384]{2,1,0:T(8,128)(2,1)S(1)}, u32[]{:S(2)}, u32[]{:S(2)}) collective-permute-start(bf16[2,256,384]{2,1,0:T(8,128)(2,1)} %bitcast.159), channel_id=1, source_target_pairs={{0,128},{32,160},{64,192},{96,224},{128,0},{160,32},{192,64},{224,... | collective-permute-start | bytes 1179656 | tf_op jit(solution)/shard_map/ppermute | solution.py:110
  11.0 18.0 %collective-permute-start.1 = (s32[1]{0:T(128)}, s32[1]{0:T(128)}, u32[]{:S(2)}, u32[]{:S(2)}) collective-permute-start(s32[1]{0:T(128)} %param.17), channel_id=1, source_target_pairs={{0,32},{32,0},{64,96},{96,64},{128,160},{160,128},{192,224},{224,1... | collective-permute-start | bytes 20 | tf_op jit(solution)/shard_map/ppermute | solution.py:110
  18.6 5.0 %copy-start.25 = (s32[1,128]{1,0:T(1,128)S(1)}, s32[1,128]{1,0:T(1,128)}, u32[]{:S(2)}) copy-start(s32[1,128]{1,0:T(1,128)} %param.18) | copy-start | bytes 1540
  18.6 5.6 %copy-start.1 = (bf16[1,128,1536]{2,1,0:T(8,128)(2,1)S(1)}, bf16[1,128,1536]{2,1,0:T(8,128)(2,1)}, u32[]{:S(2)}) copy-start(bf16[1,128,1536]{2,1,0:T(8,128)(2,1)} %param.14) | copy-start | bytes 1179652
  18.6 6.6 %copy-start.15 = (f32[1536]{0:T(1024)S(1)}, f32[1536]{0:T(1024)}, u32[]{:S(2)}) copy-start(f32[1536]{0:T(1024)} %param.19) | copy-start | bytes 18436
  23.6 0.5 copy-start.21
  24.4 4.1 %copy-start.19 = (f32[128]{0:T(128)}, f32[128]{0:T(128)S(1)}, u32[]{:S(2)}) copy-start(f32[128]{0:T(128)S(1)} %add_rsqrt_fusion.2) | copy-start | bytes 1540
  25.2 9.1 %copy-start.6 = (bf16[1,2,256,384]{3,2,1,0:T(8,128)(2,1)S(1)}, bf16[1,2,256,384]{3,2,1,0:T(8,128)(2,1)}, u32[]{:S(2)}) copy-start(bf16[1,2,256,384]{3,2,1,0:T(8,128)(2,1)} %param.15) | copy-start | bytes 1179652
  29.7 2.8 %collective-permute-start.2 = (s32[2]{0:T(128)S(1)}, s32[2]{0:T(128)S(1)}, u32[]{:S(2)}, u32[]{:S(2)}) collective-permute-start(s32[2]{0:T(128)S(1)} %pad_add_fusion), channel_id=1, source_target_pairs={{0,64},{32,96},{64,0},{96,32},{128,192},{160,224},{192,128},{224,1... | collective-permute-start | bytes 32 | tf_op jit(solution)/shard_map/ppermute | solution.py:110
  34.3 1.7 copy-start.23
  35.4 17.4 %collective-permute-start.3 = (bf16[2,2,256,384]{3,2,1,0:T(8,128)(2,1)}, bf16[2,2,256,384]{3,2,1,0:T(8,128)(2,1)}, u32[]{:S(2)}, u32[]{:S(2)}) collective-permute-start(bf16[2,2,256,384]{3,2,1,0:T(8,128)(2,1)} %pad_maximum_fusion), channel_id=1, source_target_pairs={{0,64},{32,96},{64,0},{96,32},{128,192},{160,224},{192,128},{224,1... | collective-permute-start | bytes 2359304 | tf_op jit(solution)/shard_map/ppermute | solution.py:110
  38.4 4.3 %copy-start.5 = (bf16[1536,384]{0,1:T(8,128)(2,1)S(1)}, bf16[1536,384]{0,1:T(8,128)(2,1)}, u32[]{:S(2)}) copy-start(bf16[1536,384]{0,1:T(8,128)(2,1)} %copy.40) | copy-start | bytes 3538948
  38.4 4.3 %copy-start.20 = (f32[128]{0:T(128)S(1)}, f32[128]{0:T(128)}, u32[]{:S(2)}) copy-start(f32[128]{0:T(128)} %copy-done.19) | copy-start | bytes 1540
  54.5 30.0 %collective-permute-start.4 = (bf16[2,256,384]{2,1,0:T(8,128)(2,1)}, bf16[2,256,384]{2,1,0:T(8,128)(2,1)}, u32[]{:S(2)}, u32[]{:S(2)}) collective-permute-start(bf16[2,256,384]{2,1,0:T(8,128)(2,1)} %fusion.32), channel_id=1, source_target_pairs={{0,32},{32,0},{64,96},{96,64},{128,160},{160,128},{192,224},{224,1... | collective-permute-start | bytes 1179656 | tf_op jit(solution)/shard_map/ppermute | solution.py:110
  85.6 0.8 copy-start.16
  85.6 0.8 copy-start.17
  85.8 3.4 %copy-start.13 = (bf16[1,256,384]{1,2,0:T(8,128)(2,1)}, bf16[1,256,384]{1,2,0:T(8,128)(2,1)S(1)}, u32[]{:S(2)}) copy-start(bf16[1,256,384]{1,2,0:T(8,128)(2,1)S(1)} %copy.39) | copy-start | bytes 589828
  86.0 3.3 %copy-start.11 = (bf16[1,256,384]{1,2,0:T(8,128)(2,1)}, bf16[1,256,384]{1,2,0:T(8,128)(2,1)S(1)}, u32[]{:S(2)}) copy-start(bf16[1,256,384]{1,2,0:T(8,128)(2,1)S(1)} %copy.37) | copy-start | bytes 589828
  86.5 2.8 %copy-start.14 = (bf16[128,384]{0,1:T(8,128)(2,1)S(1)}, bf16[128,384]{0,1:T(8,128)(2,1)}, u32[]{:S(2)}) copy-start(bf16[128,384]{0,1:T(8,128)(2,1)} %copy.38) | copy-start | bytes 294916
  91.0 1.5 copy-start.18
  91.6 0.9 copy-start.3
  92.7 84.7 %copy-start.24 = (bf16[1536,128]{1,0:T(8,128)(2,1)S(1)}, bf16[1536,128]{1,0:T(8,128)(2,1)}, u32[]{:S(2)}) copy-start(bf16[1536,128]{1,0:T(8,128)(2,1)} %param.26) | copy-start | bytes 1179652
  183.1 22.2 %all-to-all-start = ((bf16[32,64,128]{2,1,0:T(8,128)(2,1)}), bf16[32,64,128]{2,1,0:T(8,128)(2,1)S(1)}, u32[]{:S(2)}, u32[]{:S(2)}) async-start(bf16[32,64,128]{2,1,0:T(8,128)(2,1)} %bitcast.160), calls=%async_computation | async-start | bytes 1048576 | tf_op jit(solution)/shard_map/all_to_all | solution.py:90
  205.3 0.8 copy-start.7
  212.7 1.8 copy-start.22
  214.5 2.1 copy-start.2
  216.6 1.3 copy-start.4
  217.9 1.3 copy-start.8
  217.9 2.3 copy-start.9
  217.9 2.3 copy-start.10
  219.2 4.1 %copy-start.26 = (pred[384]{0:T(512)(128)(4,1)S(1)}, pred[384]{0:T(512)(128)(4,1)}, u32[]{:S(2)}) copy-start(pred[384]{0:T(512)(128)(4,1)} %concatenate.54) | copy-start | bytes 1156
  223.3 2.9 %copy-start.12 = (bf16[1,256,384]{1,2,0:T(8,128)(2,1)S(1)}, bf16[1,256,384]{1,2,0:T(8,128)(2,1)}, u32[]{:S(2)}) copy-start(bf16[1,256,384]{1,2,0:T(8,128)(2,1)} %copy-done.11) | copy-start | bytes 589828
Sparse Core Ops, SparseCore 0:
  9.2 100.2 all-gather.2
  111.3 65.9 all-gather.4

commit v13 on v9

--- a/solution.py
+++ b/solution.py
@@ -84,8 +84,8 @@
 
 def run_ffn(normed_rows, w_gate, w_up, down_all, groups):
     part_rows = lax.all_gather(normed_rows, "blk", axis=0, tiled=True)
-    gate_vals = jnp.dot(part_rows, w_gate, preferred_element_type=jnp.float32)
-    up_vals = jnp.dot(part_rows, w_up, preferred_element_type=jnp.float32)
+    both = jnp.dot(part_rows, jnp.concatenate([w_gate, w_up], axis=1), preferred_element_type=jnp.float32)
+    gate_vals, up_vals = both[:, : w_gate.shape[1]], both[:, w_gate.shape[1] :]
     hidden_all = (jax.nn.silu(gate_vals) * up_vals).astype(jnp.bfloat16)
     hidden_own = lax.all_to_all(hidden_all, "blk", 0, 1, tiled=True)
     group_count = down_all.shape[0] // groups
@@ -148,9 +148,8 @@
     w_up,
     w_down,
 ):
-    fetched, first_stage = fetch_slot(cache_kv, holder)
-    w_down_late, _ = lax.optimization_barrier((w_down, first_stage))
-    down_all = lax.all_gather(w_down_late, "blk", axis=0, tiled=True)
+    fetched, _ = fetch_slot(cache_kv, holder)
+    down_all = lax.all_gather(w_down, "blk", axis=0, tiled=True)
     cache_keys = fetched[0]
     cache_vals = fetched[1]
     cache_length = cache_len[0]

time: 241 us -> 224 us (0.929)
  waiting for transfers between devices: 137 us -> 123 us
  matrix products: 34 us -> 31.3 us
    ppermute x5, waiting for transfers between devices: 19.5 us -> 12.1 us  [swap(): lax.ppermute(values, 'req', perm=[(i, i ^ mask) for i in range(count)])]
    all_gather x1, waiting for transfers between devices: 32.1 us -> 25.5 us  [local(): down_all = lax.all_gather(w_down, 'blk', axis=0, tiled=True)]
    dot_general x2 -> x1, matrix products: 7.39 us -> 4.63 us  [run_ffn(): jnp.dot(part_rows, jnp.concatenate([w_gate, w_up], axis=1), preferred_ele...]
    unnamed x60 -> x56, local copies, waits for them, and re-layouts: 10.1 us -> 10.1 us
  transfers between devices with their start and end apart: 8 -> 8, of which waited for: 7 -> 6; matrix products, arithmetic and copies ran while one was open for 15% -> 16% of each run, Pallas kernels for 0% -> 0%
where the time goes in v13:
time: 224 us; the launch traced here: 223 us
  waiting for transfers between devices  123 us (55%)
  matrix products  31.3 us (14%)
  starting transfers between devices  17.9 us (8%)
  between operations  17.6 us (8%)
  local copies, waits for them, and re-layouts  17.1 us (8%)
  other arithmetic  16.9 us (8%)
    all_gather x1, waiting for transfers between devices, run_ffn(): part_rows = lax.all_gather(normed_rows, 'blk', axis=0, tiled=True)  67.5 us
    all_gather x1, waiting for transfers between devices, local(): down_all = lax.all_gather(w_down, 'blk', axis=0, tiled=True)  25.5 us
    all_to_all x1, waiting for transfers between devices, run_ffn(): hidden_own = lax.all_to_all(hidden_all, 'blk', 0, 1, tiled=True)  16.8 us
    ppermute x5, starting transfers between devices, swap(): lax.ppermute(values, 'req', perm=[(i, i ^ mask) for i in range(count)])  12.4 us
    ppermute x5, waiting for transfers between devices, swap(): lax.ppermute(values, 'req', perm=[(i, i ^ mask) for i in range(count)])  12.1 us
    unnamed x56, local copies, waits for them, and re-layouts  10.1 us
    dot_general x1, matrix products, run_ffn(): jnp.einsum('rgk,gkd->grd', hidden_own.reshape(hidden_own.shape[0], group_...  6.57 us
    sub x2, matrix products, attend_block(): expd = jnp.exp(scores - peaks)  5.76 us
  transfers between devices with their start and end apart: 8, of which 6 were waited for; matrix products, arithmetic and copies ran while one was open for 16% of the time, Pallas kernels for 0%

profile of v13, /device:TPU:1, one launch (start us, length us, event | category | flops | bytes accessed | tf_op | source)
XLA Modules:
  0.0 223.5 jit_solution(17654835415657179143)
XLA Ops:
  6.5 0.7 all-gather.3.cloned.1.call-update
  7.3 7.8 %collective-permute-start = (bf16[2,256,384]{2,1,0:T(8,128)(2,1)}, bf16[2,256,384]{2,1,0:T(8,128)(2,1)S(1)}, u32[]{:S(2)}, u32[]{:S(2)}) collective-permute-start(bf16[2,256,384]{2,1,0:T(8,128)(2,1)} %bitcast.163), channel_id=1, source_target_pairs={{0,32},{32,0},{64,96},{96,64},{128,160},{160,128},{192,224},{224,1... | collective-permute-start | bytes 1179656 | tf_op jit(solution)/shard_map/ppermute | solution.py:110
  15.1 2.7 %collective-permute-start.1 = (s32[1]{0:T(128)}, s32[1]{0:T(128)}, u32[]{:S(2)}, u32[]{:S(2)}) collective-permute-start(s32[1]{0:T(128)} %param.17), channel_id=1, source_target_pairs={{0,128},{32,160},{64,192},{96,224},{128,0},{160,32},{192,64},{224,... | collective-permute-start | bytes 20 | tf_op jit(solution)/shard_map/ppermute | solution.py:110
  18.6 4.3 %copy.41 = bf16[1536,768]{0,1:T(8,128)(2,1)} copy(bf16[1536,768]{1,0:T(8,128)(2,1)} %param.20) | data formatting | bytes 4718592 | tf_op args[6]
  24.4 0.8 multiply_cosine_fusion
  25.2 3.3 %fusion.60 = f32[128,8,96]{0,2,1:T(8,128)} fusion(bf16[8,96,1536]{2,1,0:T(8,128)(2,1)} %bitcast.161, bf16[1,128,1536]{2,1,0:T(8,128)(2,1)S(1)} %copy-done.1, f32[1536]{0:T(1024)S(1)} %copy-done.15, f32[128]{0:T(128)S(1)} %add_rsqrt_fusion.2), kind=kOutput, calls=%fused_computation.81 | convolution fusion | flops 302776320 | bytes 3152384 | tf_op jit(solution)/shard_map/dot_general | solution.py:54
  29.0 0.7 pad_add_fusion
  29.7 0.6 collective-permute-start.2
  30.3 2.2 collective-permute-done.2
  32.5 0.6 fusion.87
  34.4 1.0 pad_maximum_fusion
  35.4 0.6 collective-permute-start.3
  36.0 2.4 %copy.40 = bf16[1536,384]{0,1:T(8,128)(2,1)} copy(bf16[1536,384]{1,0:T(8,128)(2,1)} %param.21) | data formatting | bytes 2359296 | tf_op args[7]
  38.4 1.9 subtract_convert_fusion.1
  40.3 2.3 %convolution_convert_fusion.3 = bf16[128,384]{1,0:T(8,128)(2,1)} fusion(bf16[1536,384]{1,0:T(8,128)(2,1)} %param.22, bf16[1,128,1536]{2,1,0:T(8,128)(2,1)S(1)} %copy-done.1, f32[1536]{0:T(1024)S(1)} %copy-done.15, f32[128]{0:T(128)} %copy-done.19), kind=kOutput, calls=%fused_computation.23 | convolution fusion | flops 151830528 | bytes 1677824 | tf_op jit(solution)/shard_map/dot_general | solution.py:59
  42.6 1.3 fusion.62
  45.1 7.6 %collective-permute-done.3 = bf16[2,2,256,384]{3,2,1,0:T(8,128)(2,1)} collective-permute-done((bf16[2,2,256,384]{3,2,1,0:T(8,128)(2,1)}, bf16[2,2,256,384]{3,2,1,0:T(8,128)(2,1)}, u32[]{:S(2)}, u32[]{:S(2)}) %collective-permute-start.3) | collective-permute-done | bytes 786464 | tf_op jit(solution)/shard_map/ppermute | solution.py:110
  52.7 1.8 fusion.30
  54.5 0.7 collective-permute-start.4
  55.7 1.7 copy.38
  57.4 1.1 concatenate.54
  58.5 1.6 pad_maximum_fusion.5
  60.1 1.6 subtract_convert_fusion.3
  61.8 2.3 %collective-permute-done.4 = bf16[2,256,384]{2,1,0:T(8,128)(2,1)} collective-permute-done((bf16[2,256,384]{2,1,0:T(8,128)(2,1)}, bf16[2,256,384]{2,1,0:T(8,128)(2,1)}, u32[]{:S(2)}, u32[]{:S(2)}) %collective-permute-start.4) | collective-permute-done | bytes 393248 | tf_op jit(solution)/shard_map/ppermute | solution.py:110
  64.1 1.2 fusion.33
  66.1 2.8 %fusion.88 = (f32[4,2,128]{2,1,0:T(2,128)S(1)}, f32[4,2,128,384]{2,3,1,0:T(8,128)}) fusion(bf16[128,4,2,96]{0,3,2,1:T(8,128)(2,1)} %bitcast.173, bf16[256,4,96]{0,2,1:T(8,128)(2,1)S(1)} %bitcast.171, bf16[128,4,48]{0,2,1:T(8,128)(2,1)S(1)} %copy-done.17, bf16[128,4,48]{0,2,1:T(8,128)(2,1)S(1)} %copy-done.16, pred[384]{0:T(512)(128)(4,1)} %concatenate.54), kind=kOutput, calls=%fused_computation.121 | convolution fusion | flops 77955456 | bytes 2068864 | tf_op jit(solution)/shard_map/sub | solution.py:78
  69.0 1.7 convolution_convert_fusion.1
  70.7 0.6 multiply_reduce_fusion.1
  71.4 0.9 copy-done.3
  72.4 1.4 gather_fusion
  73.8 25.5 %all-gather.3.cloned.1.call-done = bf16[4096,1536]{1,0:T(8,128)(2,1)} async-done(((bf16[128,1536]{1,0:T(8,128)(2,1)}), bf16[4096,1536]{1,0:T(8,128)(2,1)}) %all-gather.3.cloned.1.call-update) | async-done | bytes 12582928 | tf_op jit(solution)/shard_map/all_gather | solution.py:152
  99.3 67.5 %all-gather.5.cloned.1.call-done = bf16[2048,1536]{1,0:T(8,128)(2,1)} async-done(((bf16[64,1536]{1,0:T(8,128)(2,1)}), bf16[2048,1536]{1,0:T(8,128)(2,1)}) %all-gather.5.cloned.1.call-update) | async-done | bytes 6291472 | tf_op jit(solution)/shard_map/all_gather | solution.py:86
  166.8 4.6 %fusion.22 = f32[2048,256]{1,0:T(8,128)S(1)} fusion(bf16[2048,1536]{1,0:T(8,128)(2,1)} %all-gather.5.cloned.1.call-done, bf16[1536,128]{1,0:T(8,128)(2,1)S(1)} %copy-done.24, bf16[1536,128]{1,0:T(8,128)(2,1)} %param.25), kind=kOutput, calls=%fused_computation.37 | convolution fusion | flops 1612185600 | bytes 9175040 | tf_op jit(solution)/shard_map/dot_general | solution.py:87
  171.4 1.1 fusion.13
  172.5 5.4 %all-to-all-start = ((bf16[32,64,128]{2,1,0:T(8,128)(2,1)}), bf16[32,64,128]{2,1,0:T(8,128)(2,1)S(1)}, u32[]{:S(2)}, u32[]{:S(2)}) async-start(bf16[32,64,128]{2,1,0:T(8,128)(2,1)} %bitcast.164), calls=%async_computation | async-start | bytes 1048576 | tf_op jit(solution)/shard_map/all_to_all | solution.py:90
  178.0 16.8 %all-to-all-done = bf16[32,64,128]{2,1,0:T(8,128)(2,1)S(1)} async-done(((bf16[32,64,128]{2,1,0:T(8,128)(2,1)}), bf16[32,64,128]{2,1,0:T(8,128)(2,1)S(1)}, u32[]{:S(2)}, u32[]{:S(2)}) %all-to-all-start) | async-done | bytes 524320 | tf_op jit(solution)/shard_map/all_to_all | solution.py:90
  194.8 0.8 copy-done.7
  195.6 6.6 %convert_reduce_fusion = f32[64,1536]{1,0:T(8,128)S(1)} fusion(bf16[32,128,1536]{2,1,0:T(8,128)(2,1)} %bitcast.160, bf16[32,64,128]{2,1,0:T(8,128)(2,1)} %copy-done.7), kind=kOutput, calls=%fused_computation.4 | convolution fusion | flops 814645248 | bytes 13500416 | tf_op jit(solution)/shard_map/rgk,gkd->grd/dot_general | solution.py:92
  202.2 1.8 gather_fusion.1
  203.9 1.8 multiply_reduce_fusion
  206.1 1.1 fusion.95
  207.4 0.6 fusion.94
  208.0 0.7 copy-done.8
  209.1 0.7 subtract_convert_fusion.2
  209.9 0.7 pad_maximum_fusion.6
  210.6 2.9 %fusion.91 = (f32[4,2,128]{2,1,0:T(2,128)S(1)}, f32[4,2,128,384]{2,3,1,0:T(8,128)}) fusion(bf16[128,4,2,96]{0,3,2,1:T(8,128)(2,1)} %bitcast.174, bf16[256,4,96]{0,2,1:T(8,128)(2,1)} %bitcast.172, bf16[128,4,48]{0,2,1:T(8,128)(2,1)} %get-tuple-element.22, bf16[128,4,48]{0,2,1:T(8,128)(2,1)} %get-tuple-element.21, pred[384]{0:T(512)(128)(4,1)S(1)} %copy-done.26), kind=kOutput, calls=%fused_computation.122 | convolution fusion | flops 77955456 | bytes 2068864 | tf_op jit(solution)/shard_map/sub | solution.py:78
  213.5 1.7 convolution_convert_fusion
  215.2 1.4 fusion.2
  (80 shorter events, 4.0 us)
Async XLA Ops:
  6.5 64.2 %copy-start = (bf16[768,1536]{1,0:T(8,128)(2,1)S(1)}, bf16[768,1536]{1,0:T(8,128)(2,1)}, u32[]{:S(2)}) copy-start(bf16[768,1536]{1,0:T(8,128)(2,1)} %param.23) | copy-start | bytes 7077892
  6.5 92.7 %all-gather.3.cloned.1.call-start = ((), (), s32[]{:S(2)}) async-start(), calls=%async_computation.1 | async-start | bytes 12976128 | tf_op jit(solution)/shard_map/all_gather | solution.py:152
  7.3 159.5 %all-gather.5.cloned.1.call-start = ((), (), s32[]{:S(2)}) async-start(), calls=%async_computation.2 | async-start | bytes 6488064 | tf_op jit(solution)/shard_map/all_gather | solution.py:86
  7.3 27.0 %collective-permute-start = (bf16[2,256,384]{2,1,0:T(8,128)(2,1)}, bf16[2,256,384]{2,1,0:T(8,128)(2,1)S(1)}, u32[]{:S(2)}, u32[]{:S(2)}) collective-permute-start(bf16[2,256,384]{2,1,0:T(8,128)(2,1)} %bitcast.163), channel_id=1, source_target_pairs={{0,32},{32,0},{64,96},{96,64},{128,160},{160,128},{192,224},{224,1... | collective-permute-start | bytes 1179656 | tf_op jit(solution)/shard_map/ppermute | solution.py:110
  15.1 13.8 %collective-permute-start.1 = (s32[1]{0:T(128)}, s32[1]{0:T(128)}, u32[]{:S(2)}, u32[]{:S(2)}) collective-permute-start(s32[1]{0:T(128)} %param.17), channel_id=1, source_target_pairs={{0,128},{32,160},{64,192},{96,224},{128,0},{160,32},{192,64},{224,... | collective-permute-start | bytes 20 | tf_op jit(solution)/shard_map/ppermute | solution.py:110
  18.6 5.0 %copy-start.25 = (s32[1,128]{1,0:T(1,128)S(1)}, s32[1,128]{1,0:T(1,128)}, u32[]{:S(2)}) copy-start(s32[1,128]{1,0:T(1,128)} %param.18) | copy-start | bytes 1540
  18.6 5.6 %copy-start.1 = (bf16[1,128,1536]{2,1,0:T(8,128)(2,1)S(1)}, bf16[1,128,1536]{2,1,0:T(8,128)(2,1)}, u32[]{:S(2)}) copy-start(bf16[1,128,1536]{2,1,0:T(8,128)(2,1)} %param.14) | copy-start | bytes 1179652
  18.6 6.6 %copy-start.15 = (f32[1536]{0:T(1024)S(1)}, f32[1536]{0:T(1024)}, u32[]{:S(2)}) copy-start(f32[1536]{0:T(1024)} %param.19) | copy-start | bytes 18436
  23.6 0.5 copy-start.21
  24.4 4.1 %copy-start.19 = (f32[128]{0:T(128)}, f32[128]{0:T(128)S(1)}, u32[]{:S(2)}) copy-start(f32[128]{0:T(128)S(1)} %add_rsqrt_fusion.2) | copy-start | bytes 1540
  25.2 9.1 %copy-start.6 = (bf16[1,2,256,384]{3,2,1,0:T(8,128)(2,1)S(1)}, bf16[1,2,256,384]{3,2,1,0:T(8,128)(2,1)}, u32[]{:S(2)}) copy-start(bf16[1,2,256,384]{3,2,1,0:T(8,128)(2,1)} %param.15) | copy-start | bytes 1179652
  29.7 2.8 %collective-permute-start.2 = (s32[2]{0:T(128)S(1)}, s32[2]{0:T(128)S(1)}, u32[]{:S(2)}, u32[]{:S(2)}) collective-permute-start(s32[2]{0:T(128)S(1)} %pad_add_fusion), channel_id=1, source_target_pairs={{0,64},{32,96},{64,0},{96,32},{128,192},{160,224},{192,128},{224,1... | collective-permute-start | bytes 32 | tf_op jit(solution)/shard_map/ppermute | solution.py:110
  34.3 1.7 copy-start.23
  35.4 17.4 %collective-permute-start.3 = (bf16[2,2,256,384]{3,2,1,0:T(8,128)(2,1)}, bf16[2,2,256,384]{3,2,1,0:T(8,128)(2,1)}, u32[]{:S(2)}, u32[]{:S(2)}) collective-permute-start(bf16[2,2,256,384]{3,2,1,0:T(8,128)(2,1)} %pad_maximum_fusion), channel_id=1, source_target_pairs={{0,64},{32,96},{64,0},{96,32},{128,192},{160,224},{192,128},{224,1... | collective-permute-start | bytes 2359304 | tf_op jit(solution)/shard_map/ppermute | solution.py:110
  38.4 4.2 %copy-start.5 = (bf16[1536,384]{0,1:T(8,128)(2,1)S(1)}, bf16[1536,384]{0,1:T(8,128)(2,1)}, u32[]{:S(2)}) copy-start(bf16[1536,384]{0,1:T(8,128)(2,1)} %copy.40) | copy-start | bytes 3538948
  38.4 4.2 %copy-start.20 = (f32[128]{0:T(128)S(1)}, f32[128]{0:T(128)}, u32[]{:S(2)}) copy-start(f32[128]{0:T(128)} %copy-done.19) | copy-start | bytes 1540
  54.5 9.5 %collective-permute-start.4 = (bf16[2,256,384]{2,1,0:T(8,128)(2,1)}, bf16[2,256,384]{2,1,0:T(8,128)(2,1)}, u32[]{:S(2)}, u32[]{:S(2)}) collective-permute-start(bf16[2,256,384]{2,1,0:T(8,128)(2,1)} %fusion.30), channel_id=1, source_target_pairs={{0,128},{32,160},{64,192},{96,224},{128,0},{160,32},{192,64},{224,... | collective-permute-start | bytes 1179656 | tf_op jit(solution)/shard_map/ppermute | solution.py:110
  65.3 0.8 copy-start.16
  65.3 0.8 copy-start.17
  65.5 3.4 %copy-start.13 = (bf16[1,256,384]{1,2,0:T(8,128)(2,1)}, bf16[1,256,384]{1,2,0:T(8,128)(2,1)S(1)}, u32[]{:S(2)}) copy-start(bf16[1,256,384]{1,2,0:T(8,128)(2,1)S(1)} %copy.39) | copy-start | bytes 589828
  65.7 3.3 %copy-start.11 = (bf16[1,256,384]{1,2,0:T(8,128)(2,1)}, bf16[1,256,384]{1,2,0:T(8,128)(2,1)S(1)}, u32[]{:S(2)}) copy-start(bf16[1,256,384]{1,2,0:T(8,128)(2,1)S(1)} %copy.37) | copy-start | bytes 589828
  66.1 2.8 %copy-start.14 = (bf16[128,384]{0,1:T(8,128)(2,1)S(1)}, bf16[128,384]{0,1:T(8,128)(2,1)}, u32[]{:S(2)}) copy-start(bf16[128,384]{0,1:T(8,128)(2,1)} %copy.38) | copy-start | bytes 294916
  70.7 1.5 copy-start.18
  71.3 0.9 copy-start.3
  72.4 94.4 %copy-start.24 = (bf16[1536,128]{1,0:T(8,128)(2,1)S(1)}, bf16[1536,128]{1,0:T(8,128)(2,1)}, u32[]{:S(2)}) copy-start(bf16[1536,128]{1,0:T(8,128)(2,1)} %param.26) | copy-start | bytes 1179652
  172.5 22.2 %all-to-all-start = ((bf16[32,64,128]{2,1,0:T(8,128)(2,1)}), bf16[32,64,128]{2,1,0:T(8,128)(2,1)S(1)}, u32[]{:S(2)}, u32[]{:S(2)}) async-start(bf16[32,64,128]{2,1,0:T(8,128)(2,1)} %bitcast.164), calls=%async_computation | async-start | bytes 1048576 | tf_op jit(solution)/shard_map/all_to_all | solution.py:90
  194.8 0.8 copy-start.7
  202.2 1.8 copy-start.22
  203.9 2.1 copy-start.2
  206.1 1.3 copy-start.4
  207.4 1.3 copy-start.8
  207.4 1.7 copy-start.9
  207.4 1.7 copy-start.10
  208.6 2.0 copy-start.26
  210.6 2.9 %copy-start.12 = (bf16[1,256,384]{1,2,0:T(8,128)(2,1)S(1)}, bf16[1,256,384]{1,2,0:T(8,128)(2,1)}, u32[]{:S(2)}) copy-start(bf16[1,256,384]{1,2,0:T(8,128)(2,1)} %copy-done.11) | copy-start | bytes 589828
Sparse Core Ops, SparseCore 0:
  9.2 90.0 all-gather.2
  101.1 65.5 all-gather.4

commit v14 on v13

--- a/solution.py
+++ b/solution.py
@@ -88,14 +88,7 @@
     gate_vals, up_vals = both[:, : w_gate.shape[1]], both[:, w_gate.shape[1] :]
     hidden_all = (jax.nn.silu(gate_vals) * up_vals).astype(jnp.bfloat16)
     hidden_own = lax.all_to_all(hidden_all, "blk", 0, 1, tiled=True)
-    group_count = down_all.shape[0] // groups
-    terms = jnp.einsum(
-        "rgk,gkd->grd",
-        hidden_own.reshape(hidden_own.shape[0], group_count, groups),
-        down_all.reshape(group_count, groups, down_all.shape[1]),
-        preferred_element_type=jnp.float32,
-    ).astype(jnp.bfloat16)
-    return jnp.sum(terms.astype(jnp.float32), axis=0)
+    return jnp.dot(hidden_own, down_all, preferred_element_type=jnp.float32)
 
 
 def fetch_slot(cache_kv, holder):

time: 224 us -> 226 us (level)
    unnamed x56 -> x54, local copies, waits for them, and re-layouts: 10.1 us -> 9.22 us
where the time goes in v14:
time: 226 us; the launch traced here: 225 us
  waiting for transfers between devices  122 us (54%)
  matrix products  32.4 us (14%)
  local copies, waits for them, and re-layouts  18 us (8%)
  starting transfers between devices  17.9 us (8%)
  between operations  17.7 us (8%)
  other arithmetic  16.9 us (7%)
    all_gather x1, waiting for transfers between devices, run_ffn(): part_rows = lax.all_gather(normed_rows, 'blk', axis=0, tiled=True)  67.5 us
    all_gather x1, waiting for transfers between devices, local(): down_all = lax.all_gather(w_down, 'blk', axis=0, tiled=True)  25.4 us
    all_to_all x1, waiting for transfers between devices, run_ffn(): hidden_own = lax.all_to_all(hidden_all, 'blk', 0, 1, tiled=True)  16.8 us
    ppermute x5, starting transfers between devices, swap(): lax.ppermute(values, 'req', perm=[(i, i ^ mask) for i in range(count)])  12.4 us
    ppermute x5, waiting for transfers between devices, swap(): lax.ppermute(values, 'req', perm=[(i, i ^ mask) for i in range(count)])  12 us
    unnamed x54, local copies, waits for them, and re-layouts  9.22 us
    dot_general x1, matrix products, run_ffn(): return jnp.dot(hidden_own, down_all, preferred_element_type=jnp.float32)  7.03 us
    sub x2, matrix products, attend_block(): expd = jnp.exp(scores - peaks)  5.74 us
  transfers between devices with their start and end apart: 8, of which 6 were waited for; matrix products, arithmetic and copies ran while one was open for 16% of the time, Pallas kernels for 0%

profile of v14, /device:TPU:1, one launch (start us, length us, event | category | flops | bytes accessed | tf_op | source)
XLA Modules:
  0.0 225.3 jit_solution(1962328207901038145)
XLA Ops:
  6.5 0.7 all-gather.3.cloned.1.call-update
  7.3 7.8 %collective-permute-start = (bf16[2,256,384]{2,1,0:T(8,128)(2,1)}, bf16[2,256,384]{2,1,0:T(8,128)(2,1)S(1)}, u32[]{:S(2)}, u32[]{:S(2)}) collective-permute-start(bf16[2,256,384]{2,1,0:T(8,128)(2,1)} %bitcast.166), channel_id=1, source_target_pairs={{0,32},{32,0},{64,96},{96,64},{128,160},{160,128},{192,224},{224,1... | collective-permute-start | bytes 1179656 | tf_op jit(solution)/shard_map/ppermute | solution.py:103
  15.1 2.7 %collective-permute-start.1 = (s32[1]{0:T(128)}, s32[1]{0:T(128)}, u32[]{:S(2)}, u32[]{:S(2)}) collective-permute-start(s32[1]{0:T(128)} %param.17), channel_id=1, source_target_pairs={{0,128},{32,160},{64,192},{96,224},{128,0},{160,32},{192,64},{224,... | collective-permute-start | bytes 20 | tf_op jit(solution)/shard_map/ppermute | solution.py:103
  18.6 4.3 %copy.54 = bf16[1536,768]{0,1:T(8,128)(2,1)} copy(bf16[1536,768]{1,0:T(8,128)(2,1)} %param.20) | data formatting | bytes 4718592 | tf_op args[6]
  24.3 0.8 multiply_cosine_fusion
  25.1 3.3 %fusion.62 = f32[128,8,96]{0,2,1:T(8,128)} fusion(bf16[8,96,1536]{2,1,0:T(8,128)(2,1)} %bitcast.164, bf16[1,128,1536]{2,1,0:T(8,128)(2,1)S(1)} %copy-done.1, f32[1536]{0:T(1024)S(1)} %copy-done.14, f32[128]{0:T(128)S(1)} %add_rsqrt_fusion.2), kind=kOutput, calls=%fused_computation.82 | convolution fusion | flops 302776320 | bytes 3152384 | tf_op jit(solution)/shard_map/dot_general | solution.py:54
  29.0 0.7 pad_add_fusion
  29.7 0.6 collective-permute-start.2
  30.3 2.2 collective-permute-done.2
  32.6 0.6 fusion.89
  34.6 1.0 pad_maximum_fusion
  36.2 2.4 %copy.53 = bf16[1536,384]{0,1:T(8,128)(2,1)} copy(bf16[1536,384]{1,0:T(8,128)(2,1)} %param.21) | data formatting | bytes 2359296 | tf_op args[7]
  38.6 1.9 subtract_convert_fusion.1
  40.5 2.4 %convolution_convert_fusion.3 = bf16[128,384]{1,0:T(8,128)(2,1)} fusion(bf16[1536,384]{1,0:T(8,128)(2,1)} %param.22, bf16[1,128,1536]{2,1,0:T(8,128)(2,1)S(1)} %copy-done.1, f32[1536]{0:T(1024)S(1)} %copy-done.14, f32[128]{0:T(128)} %copy-done.18), kind=kOutput, calls=%fused_computation.22 | convolution fusion | flops 151830528 | bytes 1677824 | tf_op jit(solution)/shard_map/dot_general | solution.py:59
  42.8 1.2 fusion.64
  45.4 7.6 %collective-permute-done.3 = bf16[2,2,256,384]{3,2,1,0:T(8,128)(2,1)} collective-permute-done((bf16[2,2,256,384]{3,2,1,0:T(8,128)(2,1)}, bf16[2,2,256,384]{3,2,1,0:T(8,128)(2,1)}, u32[]{:S(2)}, u32[]{:S(2)}) %collective-permute-start.3) | collective-permute-done | bytes 786464 | tf_op jit(solution)/shard_map/ppermute | solution.py:103
  53.0 1.8 fusion.32
  54.8 0.6 collective-permute-start.4
  55.4 0.6 iota_compare_fusion.1
  56.0 1.6 copy.51
  57.6 1.2 concatenate.54
  58.9 1.7 pad_maximum_fusion.5
  60.5 1.6 subtract_convert_fusion.3
  62.2 2.2 collective-permute-done.4
  64.3 1.1 fusion.35
  66.2 2.8 %fusion.90 = (f32[4,2,128]{2,1,0:T(2,128)S(1)}, f32[4,2,128,384]{2,3,1,0:T(8,128)}) fusion(bf16[128,4,2,96]{0,3,2,1:T(8,128)(2,1)} %bitcast.175, bf16[256,4,96]{0,2,1:T(8,128)(2,1)S(1)} %bitcast.173, bf16[128,4,48]{0,2,1:T(8,128)(2,1)S(1)} %copy-done.16, bf16[128,4,48]{0,2,1:T(8,128)(2,1)S(1)} %copy-done.15, pred[384]{0:T(512)(128)(4,1)} %concatenate.54), kind=kOutput, calls=%fused_computation.122 | convolution fusion | flops 77955456 | bytes 2068864 | tf_op jit(solution)/shard_map/sub | solution.py:78
  69.0 1.7 convolution_convert_fusion.1
  71.4 0.9 copy-done.3
  72.5 1.4 gather_fusion
  73.9 25.4 %all-gather.3.cloned.1.call-done = bf16[4096,1536]{1,0:T(8,128)(2,1)} async-done(((bf16[128,1536]{1,0:T(8,128)(2,1)}), bf16[4096,1536]{1,0:T(8,128)(2,1)}) %all-gather.3.cloned.1.call-update) | async-done | bytes 12582928 | tf_op jit(solution)/shard_map/all_gather | solution.py:145
  99.3 67.5 %all-gather.5.cloned.1.call-done = bf16[2048,1536]{1,0:T(8,128)(2,1)} async-done(((bf16[64,1536]{1,0:T(8,128)(2,1)}), bf16[2048,1536]{1,0:T(8,128)(2,1)}) %all-gather.5.cloned.1.call-update) | async-done | bytes 6291472 | tf_op jit(solution)/shard_map/all_gather | solution.py:86
  166.8 4.6 %fusion.22 = f32[2048,256]{1,0:T(8,128)S(1)} fusion(bf16[2048,1536]{1,0:T(8,128)(2,1)} %all-gather.5.cloned.1.call-done, bf16[1536,128]{1,0:T(8,128)(2,1)S(1)} %copy-done.23, bf16[1536,128]{1,0:T(8,128)(2,1)} %param.25), kind=kOutput, calls=%fused_computation.36 | convolution fusion | flops 1612185600 | bytes 9175040 | tf_op jit(solution)/shard_map/dot_general | solution.py:87
  171.4 1.1 fusion.13
  172.5 5.5 %all-to-all-start = ((bf16[32,64,128]{2,1,0:T(8,128)(2,1)}), bf16[32,64,128]{2,1,0:T(8,128)(2,1)}, u32[]{:S(2)}, u32[]{:S(2)}) async-start(bf16[32,64,128]{2,1,0:T(8,128)(2,1)} %bitcast.32), calls=%async_computation | async-start | bytes 1048576 | tf_op jit(solution)/shard_map/all_to_all | solution.py:90
  178.0 16.8 %all-to-all-done = bf16[32,64,128]{2,1,0:T(8,128)(2,1)} async-done(((bf16[32,64,128]{2,1,0:T(8,128)(2,1)}), bf16[32,64,128]{2,1,0:T(8,128)(2,1)}, u32[]{:S(2)}, u32[]{:S(2)}) %all-to-all-start) | async-done | bytes 524320 | tf_op jit(solution)/shard_map/all_to_all | solution.py:90
  194.9 7.0 %fusion.26 = f32[64,1536]{1,0:T(8,128)S(1)} fusion(bf16[4096,1536]{1,0:T(8,128)(2,1)} %all-gather.3.cloned.1.call-done, bf16[32,64,128]{2,1,0:T(8,128)(2,1)} %all-to-all-done), kind=kOutput, calls=%fused_computation.44 | convolution fusion | flops 805306368 | bytes 13500416 | tf_op jit(solution)/shard_map/dot_general | solution.py:91
  201.9 1.7 gather_fusion.1
  203.7 1.8 multiply_reduce_fusion
  205.8 1.1 fusion.97
  207.1 0.6 fusion.96
  207.7 0.7 copy-done.7
  208.3 1.0 convolution_convert_fusion.2
  209.4 0.7 subtract_convert_fusion.2
  210.1 1.6 copy.58
  211.7 0.7 pad_maximum_fusion.6
  212.4 2.9 %fusion.93 = (f32[4,2,128]{2,1,0:T(2,128)S(1)}, f32[4,2,128,384]{2,3,1,0:T(8,128)}) fusion(bf16[128,4,2,96]{0,3,2,1:T(8,128)(2,1)} %bitcast.176, bf16[256,4,96]{0,2,1:T(8,128)(2,1)} %bitcast.174, bf16[128,4,48]{0,2,1:T(8,128)(2,1)} %get-tuple-element.22, bf16[128,4,48]{0,2,1:T(8,128)(2,1)} %get-tuple-element.21, pred[384]{0:T(512)(128)(4,1)S(1)} %copy-done.25), kind=kOutput, calls=%fused_computation.123 | convolution fusion | flops 77955456 | bytes 2068864 | tf_op jit(solution)/shard_map/sub | solution.py:78
  215.4 1.8 convolution_convert_fusion
  217.1 1.4 fusion.2
  (78 shorter events, 4.2 us)
Async XLA Ops:
  6.5 64.3 %copy-start = (bf16[768,1536]{1,0:T(8,128)(2,1)S(1)}, bf16[768,1536]{1,0:T(8,128)(2,1)}, u32[]{:S(2)}) copy-start(bf16[768,1536]{1,0:T(8,128)(2,1)} %param.23) | copy-start | bytes 7077892
  6.5 92.7 %all-gather.3.cloned.1.call-start = ((), (), s32[]{:S(2)}) async-start(), calls=%async_computation.1 | async-start | bytes 12976128 | tf_op jit(solution)/shard_map/all_gather | solution.py:145
  7.3 159.5 %all-gather.5.cloned.1.call-start = ((), (), s32[]{:S(2)}) async-start(), calls=%async_computation.2 | async-start | bytes 6488064 | tf_op jit(solution)/shard_map/all_gather | solution.py:86
  7.3 27.2 %collective-permute-start = (bf16[2,256,384]{2,1,0:T(8,128)(2,1)}, bf16[2,256,384]{2,1,0:T(8,128)(2,1)S(1)}, u32[]{:S(2)}, u32[]{:S(2)}) collective-permute-start(bf16[2,256,384]{2,1,0:T(8,128)(2,1)} %bitcast.166), channel_id=1, source_target_pairs={{0,32},{32,0},{64,96},{96,64},{128,160},{160,128},{192,224},{224,1... | collective-permute-start | bytes 1179656 | tf_op jit(solution)/shard_map/ppermute | solution.py:103
  15.1 13.9 %collective-permute-start.1 = (s32[1]{0:T(128)}, s32[1]{0:T(128)}, u32[]{:S(2)}, u32[]{:S(2)}) collective-permute-start(s32[1]{0:T(128)} %param.17), channel_id=1, source_target_pairs={{0,128},{32,160},{64,192},{96,224},{128,0},{160,32},{192,64},{224,... | collective-permute-start | bytes 20 | tf_op jit(solution)/shard_map/ppermute | solution.py:103
  18.6 5.0 %copy-start.24 = (s32[1,128]{1,0:T(1,128)S(1)}, s32[1,128]{1,0:T(1,128)}, u32[]{:S(2)}) copy-start(s32[1,128]{1,0:T(1,128)} %param.18) | copy-start | bytes 1540
  18.6 5.6 %copy-start.1 = (bf16[1,128,1536]{2,1,0:T(8,128)(2,1)S(1)}, bf16[1,128,1536]{2,1,0:T(8,128)(2,1)}, u32[]{:S(2)}) copy-start(bf16[1,128,1536]{2,1,0:T(8,128)(2,1)} %param.14) | copy-start | bytes 1179652
  18.6 6.6 %copy-start.14 = (f32[1536]{0:T(1024)S(1)}, f32[1536]{0:T(1024)}, u32[]{:S(2)}) copy-start(f32[1536]{0:T(1024)} %param.19) | copy-start | bytes 18436
  23.6 0.5 copy-start.20
  24.3 4.1 %copy-start.18 = (f32[128]{0:T(128)}, f32[128]{0:T(128)S(1)}, u32[]{:S(2)}) copy-start(f32[128]{0:T(128)S(1)} %add_rsqrt_fusion.2) | copy-start | bytes 1540
  25.1 9.4 %copy-start.6 = (bf16[1,2,256,384]{3,2,1,0:T(8,128)(2,1)S(1)}, bf16[1,2,256,384]{3,2,1,0:T(8,128)(2,1)}, u32[]{:S(2)}) copy-start(bf16[1,2,256,384]{3,2,1,0:T(8,128)(2,1)} %param.15) | copy-start | bytes 1179652
  29.7 2.8 %collective-permute-start.2 = (s32[2]{0:T(128)S(1)}, s32[2]{0:T(128)S(1)}, u32[]{:S(2)}, u32[]{:S(2)}) collective-permute-start(s32[2]{0:T(128)S(1)} %pad_add_fusion), channel_id=1, source_target_pairs={{0,64},{32,96},{64,0},{96,32},{128,192},{160,224},{192,128},{224,1... | collective-permute-start | bytes 32 | tf_op jit(solution)/shard_map/ppermute | solution.py:103
  34.5 1.7 copy-start.22
  35.6 17.4 %collective-permute-start.3 = (bf16[2,2,256,384]{3,2,1,0:T(8,128)(2,1)}, bf16[2,2,256,384]{3,2,1,0:T(8,128)(2,1)}, u32[]{:S(2)}, u32[]{:S(2)}) collective-permute-start(bf16[2,2,256,384]{3,2,1,0:T(8,128)(2,1)} %pad_maximum_fusion), channel_id=1, source_target_pairs={{0,64},{32,96},{64,0},{96,32},{128,192},{160,224},{192,128},{224,1... | collective-permute-start | bytes 2359304 | tf_op jit(solution)/shard_map/ppermute | solution.py:103
  38.6 4.2 %copy-start.5 = (bf16[1536,384]{0,1:T(8,128)(2,1)S(1)}, bf16[1536,384]{0,1:T(8,128)(2,1)}, u32[]{:S(2)}) copy-start(bf16[1536,384]{0,1:T(8,128)(2,1)} %copy.53) | copy-start | bytes 3538948
  38.6 4.2 %copy-start.19 = (f32[128]{0:T(128)S(1)}, f32[128]{0:T(128)}, u32[]{:S(2)}) copy-start(f32[128]{0:T(128)} %copy-done.18) | copy-start | bytes 1540
  54.8 9.5 %collective-permute-start.4 = (bf16[2,256,384]{2,1,0:T(8,128)(2,1)}, bf16[2,256,384]{2,1,0:T(8,128)(2,1)}, u32[]{:S(2)}, u32[]{:S(2)}) collective-permute-start(bf16[2,256,384]{2,1,0:T(8,128)(2,1)} %fusion.32), channel_id=1, source_target_pairs={{0,128},{32,160},{64,192},{96,224},{128,0},{160,32},{192,64},{224,... | collective-permute-start | bytes 1179656 | tf_op jit(solution)/shard_map/ppermute | solution.py:103
  65.4 0.8 copy-start.15
  65.4 0.8 copy-start.16
  65.6 3.4 %copy-start.12 = (bf16[1,256,384]{1,2,0:T(8,128)(2,1)}, bf16[1,256,384]{1,2,0:T(8,128)(2,1)S(1)}, u32[]{:S(2)}) copy-start(bf16[1,256,384]{1,2,0:T(8,128)(2,1)S(1)} %copy.52) | copy-start | bytes 589828
  65.8 3.3 %copy-start.10 = (bf16[1,256,384]{1,2,0:T(8,128)(2,1)}, bf16[1,256,384]{1,2,0:T(8,128)(2,1)S(1)}, u32[]{:S(2)}) copy-start(bf16[1,256,384]{1,2,0:T(8,128)(2,1)S(1)} %copy.50) | copy-start | bytes 589828
  66.2 2.8 %copy-start.13 = (bf16[128,384]{0,1:T(8,128)(2,1)S(1)}, bf16[128,384]{0,1:T(8,128)(2,1)}, u32[]{:S(2)}) copy-start(bf16[128,384]{0,1:T(8,128)(2,1)} %copy.51) | copy-start | bytes 294916
  70.8 1.5 copy-start.17
  71.4 0.9 copy-start.3
  72.4 94.3 %copy-start.23 = (bf16[1536,128]{1,0:T(8,128)(2,1)S(1)}, bf16[1536,128]{1,0:T(8,128)(2,1)}, u32[]{:S(2)}) copy-start(bf16[1536,128]{1,0:T(8,128)(2,1)} %param.26) | copy-start | bytes 1179652
  172.5 22.4 %all-to-all-start = ((bf16[32,64,128]{2,1,0:T(8,128)(2,1)}), bf16[32,64,128]{2,1,0:T(8,128)(2,1)}, u32[]{:S(2)}, u32[]{:S(2)}) async-start(bf16[32,64,128]{2,1,0:T(8,128)(2,1)} %bitcast.32), calls=%async_computation | async-start | bytes 1048576 | tf_op jit(solution)/shard_map/all_to_all | solution.py:90
  201.9 1.8 copy-start.21
  203.7 2.1 copy-start.2
  205.8 1.3 copy-start.4
  207.1 1.3 copy-start.7
  207.1 2.3 %copy-start.8 = (f32[128,48]{0,1:T(8,128)S(1)}, f32[128,48]{0,1:T(8,128)}, u32[]{:S(2)}) copy-start(f32[128,48]{0,1:T(8,128)} %get-tuple-element.25) | copy-start | bytes 73732
  207.1 2.3 %copy-start.9 = (f32[128,48]{0,1:T(8,128)S(1)}, f32[128,48]{0,1:T(8,128)}, u32[]{:S(2)}) copy-start(f32[128,48]{0,1:T(8,128)} %get-tuple-element.26) | copy-start | bytes 73732
  208.3 4.1 %copy-start.25 = (pred[384]{0:T(512)(128)(4,1)S(1)}, pred[384]{0:T(512)(128)(4,1)}, u32[]{:S(2)}) copy-start(pred[384]{0:T(512)(128)(4,1)} %concatenate.54) | copy-start | bytes 1156
  212.4 2.9 %copy-start.11 = (bf16[1,256,384]{1,2,0:T(8,128)(2,1)S(1)}, bf16[1,256,384]{1,2,0:T(8,128)(2,1)}, u32[]{:S(2)}) copy-start(bf16[1,256,384]{1,2,0:T(8,128)(2,1)} %copy-done.10) | copy-start | bytes 589828
Sparse Core Ops, SparseCore 0:
  9.2 90.0 all-gather.2
  101.1 65.5 all-gather.4

commit v15 on v13

--- a/solution.py
+++ b/solution.py
@@ -98,7 +98,7 @@
     return jnp.sum(terms.astype(jnp.float32), axis=0)
 
 
-def fetch_slot(cache_kv, holder):
+def fetch_slot(cache_kv, holder, anchor):
     count = lax.axis_size("req")
     own = cache_kv[0]
     if count != 8:
@@ -117,6 +117,7 @@
     holders = {0: holder[0], 4: far[0], 2: pair[0], 6: pair[1]}
 
     got1 = swap(own, 1)
+    got1, _ = lax.optimization_barrier((got1, anchor))
     send_a = pick(holders[2] == (me ^ 1), got1, own)
     send_b = pick(holders[6] == (me ^ 1), got1, own)
     got2 = swap(jnp.stack([send_a, send_b]), 2)
@@ -148,7 +149,12 @@
     w_up,
     w_down,
 ):
-    fetched, _ = fetch_slot(cache_kv, holder)
+    anchor = jnp.dot(
+        rms_scale(tokens[0].astype(jnp.float32), attn_gain).astype(jnp.bfloat16),
+        q_weight,
+        preferred_element_type=jnp.float32,
+    )
+    fetched, _ = fetch_slot(cache_kv, holder, anchor)
     down_all = lax.all_gather(w_down, "blk", axis=0, tiled=True)
     cache_keys = fetched[0]
     cache_vals = fetched[1]

time: 224 us -> 224 us (level)
  local copies, waits for them, and re-layouts: 17.1 us -> 14 us
  waiting for transfers between devices: 123 us -> 126 us
    unnamed x56 -> x51, local copies, waits for them, and re-layouts: 10.1 us -> 5.77 us
    all_gather x1, waiting for transfers between devices: 25.5 us -> 29.6 us  [local(): down_all = lax.all_gather(w_down, 'blk', axis=0, tiled=True)]
    dot_general x2 -> x1, matrix products: 4.37 us -> 1.05 us  [attend_block(): jnp.dot(normed, q_weight, preferred_element_type=jnp.float32)]
    dot_general x0 -> x1, matrix products: none -> 2.37 us  [local(): jnp.dot(rms_scale(tokens[0].astype(jnp.float32), attn_gain).astype(jnp.bf...]
  transfers between devices with their start and end apart: 8 -> 8, of which waited for: 6 -> 6; matrix products, arithmetic and copies ran while one was open for 16% -> 15% of each run, Pallas kernels for 0% -> 0%
where the time goes in v15:
time: 224 us; the launch traced here: 223 us
  waiting for transfers between devices  126 us (56%)
  matrix products  30.4 us (14%)
  other arithmetic  18.2 us (8%)
  between operations  17.6 us (8%)
  starting transfers between devices  16.9 us (8%)
  local copies, waits for them, and re-layouts  14 us (6%)
    all_gather x1, waiting for transfers between devices, run_ffn(): part_rows = lax.all_gather(normed_rows, 'blk', axis=0, tiled=True)  67.5 us
    all_gather x1, waiting for transfers between devices, local(): down_all = lax.all_gather(w_down, 'blk', axis=0, tiled=True)  29.6 us
    all_to_all x1, waiting for transfers between devices, run_ffn(): hidden_own = lax.all_to_all(hidden_all, 'blk', 0, 1, tiled=True)  16.8 us
    ppermute x5, waiting for transfers between devices, swap(): lax.ppermute(values, 'req', perm=[(i, i ^ mask) for i in range(count)])  11.8 us
    ppermute x5, starting transfers between devices, swap(): lax.ppermute(values, 'req', perm=[(i, i ^ mask) for i in range(count)])  11.4 us
    dot_general x1, matrix products, run_ffn(): jnp.einsum('rgk,gkd->grd', hidden_own.reshape(hidden_own.shape[0], group_...  6.57 us
    unnamed x51, local copies, waits for them, and re-layouts  5.77 us
    sub x2, matrix products, attend_block(): expd = jnp.exp(scores - peaks)  5.73 us
  transfers between devices with their start and end apart: 8, of which 6 were waited for; matrix products, arithmetic and copies ran while one was open for 15% of the time, Pallas kernels for 0%

profile of v15, /device:TPU:1, one launch (start us, length us, event | category | flops | bytes accessed | tf_op | source)
XLA Modules:
  0.0 223.5 jit_solution(10198474227215998014)
XLA Ops:
  6.5 0.7 all-gather.3.cloned.1.call-update
  7.3 7.8 %collective-permute-start = (bf16[2,256,384]{2,1,0:T(8,128)(2,1)}, bf16[2,256,384]{2,1,0:T(8,128)(2,1)S(1)}, u32[]{:S(2)}, u32[]{:S(2)}) collective-permute-start(bf16[2,256,384]{2,1,0:T(8,128)(2,1)} %bitcast.160), channel_id=1, source_target_pairs={{0,32},{32,0},{64,96},{96,64},{128,160},{160,128},{192,224},{224,1... | collective-permute-start | bytes 1179656 | tf_op jit(solution)/shard_map/ppermute | solution.py:110
  15.1 2.7 %collective-permute-start.1 = (s32[1]{0:T(128)}, s32[1]{0:T(128)}, u32[]{:S(2)}, u32[]{:S(2)}) collective-permute-start(s32[1]{0:T(128)} %param.17), channel_id=1, source_target_pairs={{0,128},{32,160},{64,192},{96,224},{128,0},{160,32},{192,64},{224,... | collective-permute-start | bytes 20 | tf_op jit(solution)/shard_map/ppermute | solution.py:110
  19.2 0.7 compare_bitcast_fusion
  20.4 1.2 fusion.17
  21.6 0.8 multiply_cosine_fusion
  22.4 2.4 %fusion.62 = f32[128,768]{1,0:T(8,128)S(1)} fusion(bf16[1536,768]{1,0:T(8,128)(2,1)} %param.20, bf16[1,128,1536]{2,1,0:T(8,128)(2,1)} %param.14, f32[1536]{0:T(1024)} %param.19, f32[128]{0:T(128)S(1)} %add_rsqrt_fusion.2), kind=kOutput, calls=%fused_computation.82 | convolution fusion | flops 302776320 | bytes 3152384 | tf_op jit(solution)/shard_map/dot_general | solution.py:152
  24.8 0.7 pad_add_fusion
  25.8 2.5 %collective-permute-done.2 = s32[2]{0:T(128)S(1)} collective-permute-done((s32[2]{0:T(128)S(1)}, s32[2]{0:T(128)S(1)}, u32[]{:S(2)}, u32[]{:S(2)}) %collective-permute-start.2) | collective-permute-done | bytes 40 | tf_op jit(solution)/shard_map/ppermute | solution.py:110
  28.3 0.6 fusion.87
  30.4 1.0 pad_maximum_fusion
  31.3 0.9 copy.43
  32.3 2.5 %copy.42 = bf16[1536,384]{0,1:T(8,128)(2,1)} copy(bf16[1536,384]{1,0:T(8,128)(2,1)} %param.21) | data formatting | bytes 2359296 | tf_op args[7]
  34.7 1.9 subtract_convert_fusion.1
  36.6 2.4 %convolution_convert_fusion.3 = bf16[128,384]{1,0:T(8,128)(2,1)} fusion(bf16[1536,384]{1,0:T(8,128)(2,1)} %param.22, bf16[1,128,1536]{2,1,0:T(8,128)(2,1)S(1)} %copy-done.1, f32[1536]{0:T(1024)S(1)} %copy-done.15, f32[128]{0:T(128)} %copy-done.19), kind=kOutput, calls=%fused_computation.23 | convolution fusion | flops 151830528 | bytes 1677824 | tf_op jit(solution)/shard_map/dot_general | solution.py:59
  39.0 1.2 fusion.28
  41.5 7.2 %collective-permute-done.3 = bf16[2,2,256,384]{3,2,1,0:T(8,128)(2,1)} collective-permute-done((bf16[2,2,256,384]{3,2,1,0:T(8,128)(2,1)}, bf16[2,2,256,384]{3,2,1,0:T(8,128)(2,1)}, u32[]{:S(2)}, u32[]{:S(2)}) %collective-permute-start.3) | collective-permute-done | bytes 786464 | tf_op jit(solution)/shard_map/ppermute | solution.py:110
  48.7 1.8 fusion.31
  51.0 0.6 iota_compare_fusion.1
  51.6 1.6 copy.40
  53.3 1.3 concatenate.54
  54.5 1.7 pad_maximum_fusion.5
  56.2 1.6 subtract_convert_fusion.3
  57.8 2.2 collective-permute-done.4
  60.0 1.2 fusion.34
  62.1 2.8 %fusion.88 = (f32[4,2,128]{2,1,0:T(2,128)S(1)}, f32[4,2,128,384]{2,3,1,0:T(8,128)}) fusion(bf16[128,4,2,96]{0,3,2,1:T(8,128)(2,1)} %bitcast.171, bf16[256,4,96]{0,2,1:T(8,128)(2,1)S(1)} %bitcast.169, bf16[128,4,48]{0,2,1:T(8,128)(2,1)S(1)} %copy-done.17, bf16[128,4,48]{0,2,1:T(8,128)(2,1)S(1)} %copy-done.16, pred[384]{0:T(512)(128)(4,1)} %concatenate.54), kind=kOutput, calls=%fused_computation.121 | convolution fusion | flops 77955456 | bytes 2068864 | tf_op jit(solution)/shard_map/sub | solution.py:78
  64.9 1.8 convolution_convert_fusion.1
  66.7 0.6 multiply_reduce_fusion.1
  67.3 0.9 copy-done.3
  68.3 1.4 gather_fusion
  69.7 29.6 %all-gather.3.cloned.1.call-done = bf16[4096,1536]{1,0:T(8,128)(2,1)} async-done(((bf16[128,1536]{1,0:T(8,128)(2,1)}), bf16[4096,1536]{1,0:T(8,128)(2,1)}) %all-gather.3.cloned.1.call-update) | async-done | bytes 12582928 | tf_op jit(solution)/shard_map/all_gather | solution.py:158
  99.3 67.5 %all-gather.5.cloned.1.call-done = bf16[2048,1536]{1,0:T(8,128)(2,1)} async-done(((bf16[64,1536]{1,0:T(8,128)(2,1)}), bf16[2048,1536]{1,0:T(8,128)(2,1)}) %all-gather.5.cloned.1.call-update) | async-done | bytes 6291472 | tf_op jit(solution)/shard_map/all_gather | solution.py:86
  166.8 4.6 %fusion.22 = f32[2048,256]{1,0:T(8,128)S(1)} fusion(bf16[2048,1536]{1,0:T(8,128)(2,1)} %all-gather.5.cloned.1.call-done, bf16[1536,128]{1,0:T(8,128)(2,1)S(1)} %copy-done.23, bf16[1536,128]{1,0:T(8,128)(2,1)} %param.25), kind=kOutput, calls=%fused_computation.37 | convolution fusion | flops 1612185600 | bytes 9175040 | tf_op jit(solution)/shard_map/dot_general | solution.py:87
  171.4 1.1 fusion.13
  172.5 5.4 %all-to-all-start = ((bf16[32,64,128]{2,1,0:T(8,128)(2,1)}), bf16[32,64,128]{2,1,0:T(8,128)(2,1)S(1)}, u32[]{:S(2)}, u32[]{:S(2)}) async-start(bf16[32,64,128]{2,1,0:T(8,128)(2,1)} %bitcast.161), calls=%async_computation | async-start | bytes 1048576 | tf_op jit(solution)/shard_map/all_to_all | solution.py:90
  178.0 16.8 %all-to-all-done = bf16[32,64,128]{2,1,0:T(8,128)(2,1)S(1)} async-done(((bf16[32,64,128]{2,1,0:T(8,128)(2,1)}), bf16[32,64,128]{2,1,0:T(8,128)(2,1)S(1)}, u32[]{:S(2)}, u32[]{:S(2)}) %all-to-all-start) | async-done | bytes 524320 | tf_op jit(solution)/shard_map/all_to_all | solution.py:90
  194.8 0.8 copy-done.7
  195.6 6.6 %convert_reduce_fusion = f32[64,1536]{1,0:T(8,128)S(1)} fusion(bf16[32,128,1536]{2,1,0:T(8,128)(2,1)} %bitcast.158, bf16[32,64,128]{2,1,0:T(8,128)(2,1)} %copy-done.7), kind=kOutput, calls=%fused_computation.4 | convolution fusion | flops 814645248 | bytes 13500416 | tf_op jit(solution)/shard_map/rgk,gkd->grd/dot_general | solution.py:92
  202.2 1.8 gather_fusion.1
  204.0 1.8 multiply_reduce_fusion
  206.1 1.1 fusion.95
  207.4 0.6 fusion.94
  208.0 0.7 copy-done.8
  209.1 0.7 subtract_convert_fusion.2
  209.9 0.7 pad_maximum_fusion.6
  210.6 2.9 %fusion.91 = (f32[4,2,128]{2,1,0:T(2,128)S(1)}, f32[4,2,128,384]{2,3,1,0:T(8,128)}) fusion(bf16[128,4,2,96]{0,3,2,1:T(8,128)(2,1)} %bitcast.172, bf16[256,4,96]{0,2,1:T(8,128)(2,1)} %bitcast.170, bf16[128,4,48]{0,2,1:T(8,128)(2,1)} %get-tuple-element.24, bf16[128,4,48]{0,2,1:T(8,128)(2,1)} %get-tuple-element.23, pred[384]{0:T(512)(128)(4,1)S(1)} %copy-done.24), kind=kOutput, calls=%fused_computation.122 | convolution fusion | flops 77955456 | bytes 2068864 | tf_op jit(solution)/shard_map/sub | solution.py:78
  213.6 1.7 convolution_convert_fusion
  215.3 1.4 fusion.2
  (76 shorter events, 3.7 us)
Async XLA Ops:
  6.5 60.1 %copy-start = (bf16[768,1536]{1,0:T(8,128)(2,1)S(1)}, bf16[768,1536]{1,0:T(8,128)(2,1)}, u32[]{:S(2)}) copy-start(bf16[768,1536]{1,0:T(8,128)(2,1)} %param.23) | copy-start | bytes 7077892
  6.5 92.7 %all-gather.3.cloned.1.call-start = ((), (), s32[]{:S(2)}) async-start(), calls=%async_computation.1 | async-start | bytes 12976128 | tf_op jit(solution)/shard_map/all_gather | solution.py:158
  7.3 159.5 %all-gather.5.cloned.1.call-start = ((), (), s32[]{:S(2)}) async-start(), calls=%async_computation.2 | async-start | bytes 6488064 | tf_op jit(solution)/shard_map/all_gather | solution.py:86
  7.3 22.9 %collective-permute-start = (bf16[2,256,384]{2,1,0:T(8,128)(2,1)}, bf16[2,256,384]{2,1,0:T(8,128)(2,1)S(1)}, u32[]{:S(2)}, u32[]{:S(2)}) collective-permute-start(bf16[2,256,384]{2,1,0:T(8,128)(2,1)} %bitcast.160), channel_id=1, source_target_pairs={{0,32},{32,0},{64,96},{96,64},{128,160},{160,128},{192,224},{224,1... | collective-permute-start | bytes 1179656 | tf_op jit(solution)/shard_map/ppermute | solution.py:110
  15.1 9.6 %collective-permute-start.1 = (s32[1]{0:T(128)}, s32[1]{0:T(128)}, u32[]{:S(2)}, u32[]{:S(2)}) collective-permute-start(s32[1]{0:T(128)} %param.17), channel_id=1, source_target_pairs={{0,128},{32,160},{64,192},{96,224},{128,0},{160,32},{192,64},{224,... | collective-permute-start | bytes 20 | tf_op jit(solution)/shard_map/ppermute | solution.py:110
  19.9 0.5 copy-start.21
  21.6 3.2 %copy-start.19 = (f32[128]{0:T(128)}, f32[128]{0:T(128)S(1)}, u32[]{:S(2)}) copy-start(f32[128]{0:T(128)S(1)} %add_rsqrt_fusion.2) | copy-start | bytes 1540
  22.4 7.9 %copy-start.6 = (bf16[1,2,256,384]{3,2,1,0:T(8,128)(2,1)S(1)}, bf16[1,2,256,384]{3,2,1,0:T(8,128)(2,1)}, u32[]{:S(2)}) copy-start(bf16[1,2,256,384]{3,2,1,0:T(8,128)(2,1)} %param.15) | copy-start | bytes 1179652
  25.5 2.8 %collective-permute-start.2 = (s32[2]{0:T(128)S(1)}, s32[2]{0:T(128)S(1)}, u32[]{:S(2)}, u32[]{:S(2)}) collective-permute-start(s32[2]{0:T(128)S(1)} %pad_add_fusion), channel_id=1, source_target_pairs={{0,64},{32,96},{64,0},{96,32},{128,192},{160,224},{192,128},{224,1... | collective-permute-start | bytes 32 | tf_op jit(solution)/shard_map/ppermute | solution.py:110
  31.3 17.4 %collective-permute-start.3 = (bf16[2,2,256,384]{3,2,1,0:T(8,128)(2,1)}, bf16[2,2,256,384]{3,2,1,0:T(8,128)(2,1)}, u32[]{:S(2)}, u32[]{:S(2)}) collective-permute-start(bf16[2,2,256,384]{3,2,1,0:T(8,128)(2,1)} %pad_maximum_fusion), channel_id=1, source_target_pairs={{0,64},{32,96},{64,0},{96,32},{128,192},{160,224},{192,128},{224,1... | collective-permute-start | bytes 2359304 | tf_op jit(solution)/shard_map/ppermute | solution.py:110
  32.3 4.3 %copy-start.1 = (bf16[1,128,1536]{2,1,0:T(8,128)(2,1)S(1)}, bf16[1,128,1536]{2,1,0:T(8,128)(2,1)}, u32[]{:S(2)}) copy-start(bf16[1,128,1536]{2,1,0:T(8,128)(2,1)} %param.14) | copy-start | bytes 1179652
  32.3 4.3 %copy-start.15 = (f32[1536]{0:T(1024)S(1)}, f32[1536]{0:T(1024)}, u32[]{:S(2)}) copy-start(f32[1536]{0:T(1024)} %param.19) | copy-start | bytes 18436
  34.7 4.3 %copy-start.5 = (bf16[1536,384]{0,1:T(8,128)(2,1)S(1)}, bf16[1536,384]{0,1:T(8,128)(2,1)}, u32[]{:S(2)}) copy-start(bf16[1536,384]{0,1:T(8,128)(2,1)} %copy.42) | copy-start | bytes 3538948
  34.7 4.3 %copy-start.20 = (f32[128]{0:T(128)S(1)}, f32[128]{0:T(128)}, u32[]{:S(2)}) copy-start(f32[128]{0:T(128)} %copy-done.19) | copy-start | bytes 1540
  50.5 9.5 %collective-permute-start.4 = (bf16[2,256,384]{2,1,0:T(8,128)(2,1)}, bf16[2,256,384]{2,1,0:T(8,128)(2,1)}, u32[]{:S(2)}, u32[]{:S(2)}) collective-permute-start(bf16[2,256,384]{2,1,0:T(8,128)(2,1)} %fusion.31), channel_id=1, source_target_pairs={{0,128},{32,160},{64,192},{96,224},{128,0},{160,32},{192,64},{224,... | collective-permute-start | bytes 1179656 | tf_op jit(solution)/shard_map/ppermute | solution.py:110
  61.2 0.8 copy-start.16
  61.2 0.8 copy-start.17
  61.5 3.4 %copy-start.13 = (bf16[1,256,384]{1,2,0:T(8,128)(2,1)}, bf16[1,256,384]{1,2,0:T(8,128)(2,1)S(1)}, u32[]{:S(2)}) copy-start(bf16[1,256,384]{1,2,0:T(8,128)(2,1)S(1)} %copy.41) | copy-start | bytes 589828
  61.6 3.3 %copy-start.11 = (bf16[1,256,384]{1,2,0:T(8,128)(2,1)}, bf16[1,256,384]{1,2,0:T(8,128)(2,1)S(1)}, u32[]{:S(2)}) copy-start(bf16[1,256,384]{1,2,0:T(8,128)(2,1)S(1)} %copy.39) | copy-start | bytes 589828
  62.1 2.8 %copy-start.14 = (bf16[128,384]{0,1:T(8,128)(2,1)S(1)}, bf16[128,384]{0,1:T(8,128)(2,1)}, u32[]{:S(2)}) copy-start(bf16[128,384]{0,1:T(8,128)(2,1)} %copy.40) | copy-start | bytes 294916
  66.6 1.5 copy-start.18
  67.2 0.9 copy-start.3
  68.3 98.5 %copy-start.23 = (bf16[1536,128]{1,0:T(8,128)(2,1)S(1)}, bf16[1536,128]{1,0:T(8,128)(2,1)}, u32[]{:S(2)}) copy-start(bf16[1536,128]{1,0:T(8,128)(2,1)} %param.26) | copy-start | bytes 1179652
  172.5 22.2 %all-to-all-start = ((bf16[32,64,128]{2,1,0:T(8,128)(2,1)}), bf16[32,64,128]{2,1,0:T(8,128)(2,1)S(1)}, u32[]{:S(2)}, u32[]{:S(2)}) async-start(bf16[32,64,128]{2,1,0:T(8,128)(2,1)} %bitcast.161), calls=%async_computation | async-start | bytes 1048576 | tf_op jit(solution)/shard_map/all_to_all | solution.py:90
  194.8 0.8 copy-start.7
  202.2 1.8 copy-start.22
  204.0 2.1 copy-start.2
  206.1 1.3 copy-start.4
  207.4 1.3 copy-start.8
  207.4 1.7 copy-start.9
  207.4 1.7 copy-start.10
  208.7 2.0 copy-start.24
  210.6 2.9 %copy-start.12 = (bf16[1,256,384]{1,2,0:T(8,128)(2,1)S(1)}, bf16[1,256,384]{1,2,0:T(8,128)(2,1)}, u32[]{:S(2)}) copy-start(bf16[1,256,384]{1,2,0:T(8,128)(2,1)} %copy-done.11) | copy-start | bytes 589828
Sparse Core Ops, SparseCore 0:
  9.2 90.0 all-gather.2
  101.1 65.5 all-gather.4

commit v16 on v15

--- a/solution.py
+++ b/solution.py
@@ -82,12 +82,13 @@
     return widened + jnp.dot(context, o_weight, preferred_element_type=jnp.float32)
 
 
-def run_ffn(normed_rows, w_gate, w_up, down_all, groups):
+def run_ffn(normed_rows, w_gate, w_up, down_all, groups, row_slots):
     part_rows = lax.all_gather(normed_rows, "blk", axis=0, tiled=True)
     both = jnp.dot(part_rows, jnp.concatenate([w_gate, w_up], axis=1), preferred_element_type=jnp.float32)
     gate_vals, up_vals = both[:, : w_gate.shape[1]], both[:, w_gate.shape[1] :]
     hidden_all = (jax.nn.silu(gate_vals) * up_vals).astype(jnp.bfloat16)
     hidden_own = lax.all_to_all(hidden_all, "blk", 0, 1, tiled=True)
+    hidden_own = hidden_own[row_slots]
     group_count = down_all.shape[0] // groups
     terms = jnp.einsum(
         "rgk,gkd->grd",
@@ -179,8 +180,7 @@
     kept_rows = jnp.sum(jnp.where(hits, jnp.arange(block_len, dtype=jnp.int32)[None, :], 0), axis=1)
     fnorm = rms_scale(first_pass, ffn_gain).astype(jnp.bfloat16)
     ffn_rows, down_all = lax.optimization_barrier((fnorm[kept_rows], down_all))
-    ffn_kept = run_ffn(ffn_rows, w_gate, w_up, down_all, w_down.shape[0])
-    ffn_sum = ffn_kept[jnp.clip(slot_of, 0, kept - 1)]
+    ffn_sum = run_ffn(ffn_rows, w_gate, w_up, down_all, w_down.shape[0], jnp.clip(slot_of, 0, kept - 1))
     placed = first_pass + ffn_sum
     second_in = jnp.where(chosen_mask[:, None], placed, block_rows.astype(jnp.float32))
     refined = attend_block(

time: 224 us -> 227 us (1.013)
  no operation moved by 1% of the time
where the time goes in v16:
time: 227 us; the launch traced here: 226 us
  waiting for transfers between devices  126 us (56%)
  matrix products  32.2 us (14%)
  between operations  17.6 us (8%)
  starting transfers between devices  17 us (7%)
  other arithmetic  16.7 us (7%)
  local copies, waits for them, and re-layouts  15.7 us (7%)
    all_gather x1, waiting for transfers between devices, run_ffn(): part_rows = lax.all_gather(normed_rows, 'blk', axis=0, tiled=True)  67.5 us
    all_gather x1, waiting for transfers between devices, local(): down_all = lax.all_gather(w_down, 'blk', axis=0, tiled=True)  29.6 us
    all_to_all x1, waiting for transfers between devices, run_ffn(): hidden_own = lax.all_to_all(hidden_all, 'blk', 0, 1, tiled=True)  16.8 us
    ppermute x5, waiting for transfers between devices, swap(): lax.ppermute(values, 'req', perm=[(i, i ^ mask) for i in range(count)])  11.8 us
    ppermute x5, starting transfers between devices, swap(): lax.ppermute(values, 'req', perm=[(i, i ^ mask) for i in range(count)])  11.4 us
    dot_general x1, matrix products, run_ffn(): jnp.einsum('rgk,gkd->grd', hidden_own.reshape(hidden_own.shape[0], group_...  8.39 us
    unnamed x51, local copies, waits for them, and re-layouts  5.92 us
    sub x2, matrix products, attend_block(): expd = jnp.exp(scores - peaks)  5.73 us
  transfers between devices with their start and end apart: 8, of which 6 were waited for; matrix products, arithmetic and copies ran while one was open for 15% of the time, Pallas kernels for 0%

profile of v16, /device:TPU:1, one launch (start us, length us, event | category | flops | bytes accessed | tf_op | source)
XLA Modules:
  0.0 225.7 jit_solution(2790866914379351722)
XLA Ops:
  6.5 0.7 all-gather.3.cloned.1.call-update
  7.3 7.8 %collective-permute-start = (bf16[2,256,384]{2,1,0:T(8,128)(2,1)}, bf16[2,256,384]{2,1,0:T(8,128)(2,1)S(1)}, u32[]{:S(2)}, u32[]{:S(2)}) collective-permute-start(bf16[2,256,384]{2,1,0:T(8,128)(2,1)} %bitcast.170), channel_id=1, source_target_pairs={{0,32},{32,0},{64,96},{96,64},{128,160},{160,128},{192,224},{224,1... | collective-permute-start | bytes 1179656 | tf_op jit(solution)/shard_map/ppermute | solution.py:111
  15.1 2.7 %collective-permute-start.1 = (s32[1]{0:T(128)}, s32[1]{0:T(128)}, u32[]{:S(2)}, u32[]{:S(2)}) collective-permute-start(s32[1]{0:T(128)} %param.17), channel_id=1, source_target_pairs={{0,128},{32,160},{64,192},{96,224},{128,0},{160,32},{192,64},{224,... | collective-permute-start | bytes 20 | tf_op jit(solution)/shard_map/ppermute | solution.py:111
  19.2 0.7 compare_bitcast_fusion
  20.4 1.2 fusion.19
  21.6 0.8 multiply_cosine_fusion
  22.4 2.4 %fusion.63 = f32[128,768]{1,0:T(8,128)S(1)} fusion(bf16[1536,768]{1,0:T(8,128)(2,1)} %param.20, bf16[1,128,1536]{2,1,0:T(8,128)(2,1)} %param.14, f32[1536]{0:T(1024)} %param.19, f32[128]{0:T(128)S(1)} %add_rsqrt_fusion.2), kind=kOutput, calls=%fused_computation.85 | convolution fusion | flops 302776320 | bytes 3152384 | tf_op jit(solution)/shard_map/dot_general | solution.py:153
  24.8 0.7 pad_add_fusion
  25.8 2.5 %collective-permute-done.2 = s32[2]{0:T(128)S(1)} collective-permute-done((s32[2]{0:T(128)S(1)}, s32[2]{0:T(128)S(1)}, u32[]{:S(2)}, u32[]{:S(2)}) %collective-permute-start.2) | collective-permute-done | bytes 40 | tf_op jit(solution)/shard_map/ppermute | solution.py:111
  28.3 0.6 fusion.88
  30.4 1.0 pad_maximum_fusion
  31.3 0.9 copy.47
  32.3 2.5 %copy.46 = bf16[1536,384]{0,1:T(8,128)(2,1)} copy(bf16[1536,384]{1,0:T(8,128)(2,1)} %param.21) | data formatting | bytes 2359296 | tf_op args[7]
  34.7 1.9 subtract_convert_fusion.1
  36.6 2.4 %convolution_convert_fusion.4 = bf16[128,384]{1,0:T(8,128)(2,1)} fusion(bf16[1536,384]{1,0:T(8,128)(2,1)} %param.22, bf16[1,128,1536]{2,1,0:T(8,128)(2,1)S(1)} %copy-done.1, f32[1536]{0:T(1024)S(1)} %copy-done.15, f32[128]{0:T(128)} %copy-done.19), kind=kOutput, calls=%fused_computation.24 | convolution fusion | flops 151830528 | bytes 1677824 | tf_op jit(solution)/shard_map/dot_general | solution.py:59
  39.0 1.2 fusion.29
  41.5 7.2 %collective-permute-done.3 = bf16[2,2,256,384]{3,2,1,0:T(8,128)(2,1)} collective-permute-done((bf16[2,2,256,384]{3,2,1,0:T(8,128)(2,1)}, bf16[2,2,256,384]{3,2,1,0:T(8,128)(2,1)}, u32[]{:S(2)}, u32[]{:S(2)}) %collective-permute-start.3) | collective-permute-done | bytes 786464 | tf_op jit(solution)/shard_map/ppermute | solution.py:111
  48.7 1.8 fusion.32
  51.0 0.6 iota_compare_fusion.1
  51.6 1.6 copy.44
  53.3 1.3 concatenate.54
  54.5 1.7 pad_maximum_fusion.5
  56.2 1.6 subtract_convert_fusion.3
  57.8 2.2 collective-permute-done.4
  60.0 1.2 fusion.35
  62.1 2.8 %fusion.89 = (f32[4,2,128]{2,1,0:T(2,128)S(1)}, f32[4,2,128,384]{2,3,1,0:T(8,128)}) fusion(bf16[128,4,2,96]{0,3,2,1:T(8,128)(2,1)} %bitcast.180, bf16[256,4,96]{0,2,1:T(8,128)(2,1)S(1)} %bitcast.178, bf16[128,4,48]{0,2,1:T(8,128)(2,1)S(1)} %copy-done.17, bf16[128,4,48]{0,2,1:T(8,128)(2,1)S(1)} %copy-done.16, pred[384]{0:T(512)(128)(4,1)} %concatenate.54), kind=kOutput, calls=%fused_computation.124 | convolution fusion | flops 77955456 | bytes 2068864 | tf_op jit(solution)/shard_map/sub | solution.py:78
  64.9 1.8 convolution_convert_fusion.2
  66.7 0.6 multiply_reduce_fusion.1
  67.3 0.9 copy-done.3
  68.3 1.4 gather_fusion
  69.7 29.6 %all-gather.3.cloned.1.call-done = bf16[4096,1536]{1,0:T(8,128)(2,1)} async-done(((bf16[128,1536]{1,0:T(8,128)(2,1)}), bf16[4096,1536]{1,0:T(8,128)(2,1)}) %all-gather.3.cloned.1.call-update) | async-done | bytes 12582928 | tf_op jit(solution)/shard_map/all_gather | solution.py:159
  99.3 67.5 %all-gather.5.cloned.1.call-done = bf16[2048,1536]{1,0:T(8,128)(2,1)} async-done(((bf16[64,1536]{1,0:T(8,128)(2,1)}), bf16[2048,1536]{1,0:T(8,128)(2,1)}) %all-gather.5.cloned.1.call-update) | async-done | bytes 6291472 | tf_op jit(solution)/shard_map/all_gather | solution.py:86
  166.8 4.6 %fusion.24 = f32[2048,256]{1,0:T(8,128)S(1)} fusion(bf16[2048,1536]{1,0:T(8,128)(2,1)} %all-gather.5.cloned.1.call-done, bf16[1536,128]{1,0:T(8,128)(2,1)S(1)} %copy-done.23, bf16[1536,128]{1,0:T(8,128)(2,1)} %param.25), kind=kOutput, calls=%fused_computation.40 | convolution fusion | flops 1612185600 | bytes 9175040 | tf_op jit(solution)/shard_map/dot_general | solution.py:87
  171.4 1.1 fusion.15
  172.5 5.5 %all-to-all-start = ((bf16[32,64,128]{2,1,0:T(8,128)(2,1)}), bf16[32,64,128]{2,1,0:T(8,128)(2,1)}, u32[]{:S(2)}, u32[]{:S(2)}) async-start(bf16[32,64,128]{2,1,0:T(8,128)(2,1)} %bitcast.31), calls=%async_computation | async-start | bytes 1048576 | tf_op jit(solution)/shard_map/all_to_all | solution.py:90
  178.0 16.8 %all-to-all-done = bf16[32,64,128]{2,1,0:T(8,128)(2,1)} async-done(((bf16[32,64,128]{2,1,0:T(8,128)(2,1)}), bf16[32,64,128]{2,1,0:T(8,128)(2,1)}, u32[]{:S(2)}, u32[]{:S(2)}) %all-to-all-start) | async-done | bytes 524320 | tf_op jit(solution)/shard_map/all_to_all | solution.py:90
  194.9 1.1 copy_bitcast_fusion
  196.0 2.2 gather_fusion.1
  198.2 8.4 %convert_reduce_fusion = f32[128,1536]{1,0:T(8,128)S(1)} fusion(bf16[32,128,1536]{2,1,0:T(8,128)(2,1)} %bitcast.168, bf16[128,4096]{1,0:T(8,128)(2,1)} %gather_fusion.1), kind=kOutput, calls=%fused_computation.4 | convolution fusion | flops 1629290496 | bytes 14417920 | tf_op jit(solution)/shard_map/rgk,gkd->grd/dot_general | solution.py:93
  207.1 1.2 copy-done.2
  208.3 1.1 fusion.96
  209.6 0.6 fusion.95
  210.2 0.7 copy-done.8
  211.3 0.7 subtract_convert_fusion.2
  212.1 0.7 pad_maximum_fusion.6
  212.8 2.9 %fusion.92 = (f32[4,2,128]{2,1,0:T(2,128)S(1)}, f32[4,2,128,384]{2,3,1,0:T(8,128)}) fusion(bf16[128,4,2,96]{0,3,2,1:T(8,128)(2,1)} %bitcast.181, bf16[256,4,96]{0,2,1:T(8,128)(2,1)} %bitcast.179, bf16[128,4,48]{0,2,1:T(8,128)(2,1)} %get-tuple-element.24, bf16[128,4,48]{0,2,1:T(8,128)(2,1)} %get-tuple-element.23, pred[384]{0:T(512)(128)(4,1)S(1)} %copy-done.24), kind=kOutput, calls=%fused_computation.125 | convolution fusion | flops 77955456 | bytes 2068864 | tf_op jit(solution)/shard_map/sub | solution.py:78
  215.7 1.7 convolution_convert_fusion.1
  217.4 1.4 fusion.2
  (77 shorter events, 3.8 us)
Async XLA Ops:
  6.5 60.1 %copy-start = (bf16[768,1536]{1,0:T(8,128)(2,1)S(1)}, bf16[768,1536]{1,0:T(8,128)(2,1)}, u32[]{:S(2)}) copy-start(bf16[768,1536]{1,0:T(8,128)(2,1)} %param.23) | copy-start | bytes 7077892
  6.5 92.7 %all-gather.3.cloned.1.call-start = ((), (), s32[]{:S(2)}) async-start(), calls=%async_computation.1 | async-start | bytes 12976128 | tf_op jit(solution)/shard_map/all_gather | solution.py:159
  7.3 159.5 %all-gather.5.cloned.1.call-start = ((), (), s32[]{:S(2)}) async-start(), calls=%async_computation.2 | async-start | bytes 6488064 | tf_op jit(solution)/shard_map/all_gather | solution.py:86
  7.3 22.9 %collective-permute-start = (bf16[2,256,384]{2,1,0:T(8,128)(2,1)}, bf16[2,256,384]{2,1,0:T(8,128)(2,1)S(1)}, u32[]{:S(2)}, u32[]{:S(2)}) collective-permute-start(bf16[2,256,384]{2,1,0:T(8,128)(2,1)} %bitcast.170), channel_id=1, source_target_pairs={{0,32},{32,0},{64,96},{96,64},{128,160},{160,128},{192,224},{224,1... | collective-permute-start | bytes 1179656 | tf_op jit(solution)/shard_map/ppermute | solution.py:111
  15.1 9.6 %collective-permute-start.1 = (s32[1]{0:T(128)}, s32[1]{0:T(128)}, u32[]{:S(2)}, u32[]{:S(2)}) collective-permute-start(s32[1]{0:T(128)} %param.17), channel_id=1, source_target_pairs={{0,128},{32,160},{64,192},{96,224},{128,0},{160,32},{192,64},{224,... | collective-permute-start | bytes 20 | tf_op jit(solution)/shard_map/ppermute | solution.py:111
  19.9 0.5 copy-start.21
  21.6 3.2 %copy-start.19 = (f32[128]{0:T(128)}, f32[128]{0:T(128)S(1)}, u32[]{:S(2)}) copy-start(f32[128]{0:T(128)S(1)} %add_rsqrt_fusion.2) | copy-start | bytes 1540
  22.4 7.9 %copy-start.7 = (bf16[1,2,256,384]{3,2,1,0:T(8,128)(2,1)S(1)}, bf16[1,2,256,384]{3,2,1,0:T(8,128)(2,1)}, u32[]{:S(2)}) copy-start(bf16[1,2,256,384]{3,2,1,0:T(8,128)(2,1)} %param.15) | copy-start | bytes 1179652
  25.5 2.8 %collective-permute-start.2 = (s32[2]{0:T(128)S(1)}, s32[2]{0:T(128)S(1)}, u32[]{:S(2)}, u32[]{:S(2)}) collective-permute-start(s32[2]{0:T(128)S(1)} %pad_add_fusion), channel_id=1, source_target_pairs={{0,64},{32,96},{64,0},{96,32},{128,192},{160,224},{192,128},{224,1... | collective-permute-start | bytes 32 | tf_op jit(solution)/shard_map/ppermute | solution.py:111
  31.3 17.4 %collective-permute-start.3 = (bf16[2,2,256,384]{3,2,1,0:T(8,128)(2,1)}, bf16[2,2,256,384]{3,2,1,0:T(8,128)(2,1)}, u32[]{:S(2)}, u32[]{:S(2)}) collective-permute-start(bf16[2,2,256,384]{3,2,1,0:T(8,128)(2,1)} %pad_maximum_fusion), channel_id=1, source_target_pairs={{0,64},{32,96},{64,0},{96,32},{128,192},{160,224},{192,128},{224,1... | collective-permute-start | bytes 2359304 | tf_op jit(solution)/shard_map/ppermute | solution.py:111
  32.3 4.3 %copy-start.1 = (bf16[1,128,1536]{2,1,0:T(8,128)(2,1)S(1)}, bf16[1,128,1536]{2,1,0:T(8,128)(2,1)}, u32[]{:S(2)}) copy-start(bf16[1,128,1536]{2,1,0:T(8,128)(2,1)} %param.14) | copy-start | bytes 1179652
  32.3 4.3 %copy-start.15 = (f32[1536]{0:T(1024)S(1)}, f32[1536]{0:T(1024)}, u32[]{:S(2)}) copy-start(f32[1536]{0:T(1024)} %param.19) | copy-start | bytes 18436
  34.7 4.3 %copy-start.6 = (bf16[1536,384]{0,1:T(8,128)(2,1)S(1)}, bf16[1536,384]{0,1:T(8,128)(2,1)}, u32[]{:S(2)}) copy-start(bf16[1536,384]{0,1:T(8,128)(2,1)} %copy.46) | copy-start | bytes 3538948
  34.7 4.3 %copy-start.20 = (f32[128]{0:T(128)S(1)}, f32[128]{0:T(128)}, u32[]{:S(2)}) copy-start(f32[128]{0:T(128)} %copy-done.19) | copy-start | bytes 1540
  50.5 9.5 %collective-permute-start.4 = (bf16[2,256,384]{2,1,0:T(8,128)(2,1)}, bf16[2,256,384]{2,1,0:T(8,128)(2,1)}, u32[]{:S(2)}, u32[]{:S(2)}) collective-permute-start(bf16[2,256,384]{2,1,0:T(8,128)(2,1)} %fusion.32), channel_id=1, source_target_pairs={{0,128},{32,160},{64,192},{96,224},{128,0},{160,32},{192,64},{224,... | collective-permute-start | bytes 1179656 | tf_op jit(solution)/shard_map/ppermute | solution.py:111
  61.2 0.8 copy-start.16
  61.2 0.8 copy-start.17
  61.5 3.4 %copy-start.13 = (bf16[1,256,384]{1,2,0:T(8,128)(2,1)}, bf16[1,256,384]{1,2,0:T(8,128)(2,1)S(1)}, u32[]{:S(2)}) copy-start(bf16[1,256,384]{1,2,0:T(8,128)(2,1)S(1)} %copy.45) | copy-start | bytes 589828
  61.6 3.3 %copy-start.11 = (bf16[1,256,384]{1,2,0:T(8,128)(2,1)}, bf16[1,256,384]{1,2,0:T(8,128)(2,1)S(1)}, u32[]{:S(2)}) copy-start(bf16[1,256,384]{1,2,0:T(8,128)(2,1)S(1)} %copy.43) | copy-start | bytes 589828
  62.1 2.8 %copy-start.14 = (bf16[128,384]{0,1:T(8,128)(2,1)S(1)}, bf16[128,384]{0,1:T(8,128)(2,1)}, u32[]{:S(2)}) copy-start(bf16[128,384]{0,1:T(8,128)(2,1)} %copy.44) | copy-start | bytes 294916
  66.6 1.5 copy-start.18
  67.2 0.9 copy-start.3
  68.3 98.5 %copy-start.23 = (bf16[1536,128]{1,0:T(8,128)(2,1)S(1)}, bf16[1536,128]{1,0:T(8,128)(2,1)}, u32[]{:S(2)}) copy-start(bf16[1536,128]{1,0:T(8,128)(2,1)} %param.26) | copy-start | bytes 1179652
  172.5 22.4 %all-to-all-start = ((bf16[32,64,128]{2,1,0:T(8,128)(2,1)}), bf16[32,64,128]{2,1,0:T(8,128)(2,1)}, u32[]{:S(2)}, u32[]{:S(2)}) async-start(bf16[32,64,128]{2,1,0:T(8,128)(2,1)} %bitcast.31), calls=%async_computation | async-start | bytes 1048576 | tf_op jit(solution)/shard_map/all_to_all | solution.py:90
  198.2 8.4 %copy-start.4 = (f32[128,1536]{1,0:T(8,128)S(1)}, f32[128,1536]{1,0:T(8,128)}, u32[]{:S(2)}) copy-start(f32[128,1536]{1,0:T(8,128)} %copy-done.3) | copy-start | bytes 2359300
  198.2 8.4 %copy-start.22 = (pred[128]{0:T(512)(128)(4,1)S(1)}, pred[128]{0:T(512)(128)(4,1)}, u32[]{:S(2)}) copy-start(pred[128]{0:T(512)(128)(4,1)} %copy-done.21) | copy-start | bytes 388
  206.6 1.7 copy-start.2
  208.3 1.3 copy-start.5
  209.6 1.3 copy-start.8
  209.6 1.7 copy-start.9
  209.6 1.7 copy-start.10
  210.8 2.0 copy-start.24
  212.8 2.9 %copy-start.12 = (bf16[1,256,384]{1,2,0:T(8,128)(2,1)S(1)}, bf16[1,256,384]{1,2,0:T(8,128)(2,1)}, u32[]{:S(2)}) copy-start(bf16[1,256,384]{1,2,0:T(8,128)(2,1)} %copy-done.11) | copy-start | bytes 589828
Sparse Core Ops, SparseCore 0:
  9.2 90.0 all-gather.2
  101.1 65.5 all-gather.4

commit v17 on v15

--- a/solution.py
+++ b/solution.py
@@ -50,13 +50,13 @@
     widened = tok_rows.astype(jnp.float32)
     normed = rms_scale(widened, attn_gain).astype(jnp.bfloat16)
     positions = (cache_length + jnp.arange(block_len, dtype=jnp.int32)).astype(jnp.float32)
-    queries = rotate_heads(
-        jnp.dot(normed, q_weight, preferred_element_type=jnp.float32), positions, q_count
-    ).astype(jnp.bfloat16)
-    new_keys = rotate_heads(
-        jnp.dot(normed, k_weight, preferred_element_type=jnp.float32), positions, kv_count
-    ).astype(jnp.bfloat16)
-    new_vals = jnp.dot(normed, v_weight, preferred_element_type=jnp.float32).astype(jnp.bfloat16)
+    qw, kw = q_weight.shape[1], k_weight.shape[1]
+    projected = jnp.dot(
+        normed, jnp.concatenate([q_weight, k_weight, v_weight], axis=1), preferred_element_type=jnp.float32
+    )
+    queries = rotate_heads(projected[:, :qw], positions, q_count).astype(jnp.bfloat16)
+    new_keys = rotate_heads(projected[:, qw : qw + kw], positions, kv_count).astype(jnp.bfloat16)
+    new_vals = projected[:, qw + kw :].astype(jnp.bfloat16)
     all_keys = jnp.concatenate([cache_keys, new_keys], axis=0).reshape(
         slot_len + block_len, kv_count, HEAD
     )

time: 224 us -> 230 us (1.027)
  local copies, waits for them, and re-layouts: 14 us -> 26.2 us
  waiting for transfers between devices: 126 us -> 120 us
  matrix products: 30.4 us -> 26.5 us
  other arithmetic: 18.2 us -> 20.8 us
    slice x0 -> x12, local copies, waits for them, and re-layouts: none -> 14.2 us  [the longest x4 5.49 us: attend_block(): new_vals = projected[:, qw + kw:].astype(jnp.bfloat16)]
    all_gather x1, waiting for transfers between devices: 29.6 us -> 18.9 us  [local(): down_all = lax.all_gather(w_down, 'blk', axis=0, tiled=True)]
    ppermute x5, waiting for transfers between devices: 11.8 us -> 16.4 us  [swap(): lax.ppermute(values, 'req', perm=[(i, i ^ mask) for i in range(count)])]
    dot_general x6 -> x2, matrix products: 8 us -> 4.03 us  [attend_block(): jnp.dot(normed, jnp.concatenate([q_weight, k_weight, v_weight], axis=1),...]
    unnamed x51 -> x46, local copies, waits for them, and re-layouts: 5.77 us -> 6.3 us
  transfers between devices with their start and end apart: 8 -> 8, of which waited for: 6 -> 5; matrix products, arithmetic and copies ran while one was open for 15% -> 16% of each run, Pallas kernels for 0% -> 0%
where the time goes in v17:
time: 230 us; the launch traced here: 229 us
  waiting for transfers between devices  120 us (52%)
  matrix products  26.5 us (12%)
  local copies, waits for them, and re-layouts  26.2 us (11%)
  other arithmetic  20.8 us (9%)
  starting transfers between devices  17.8 us (8%)
  between operations  17.7 us (8%)
    all_gather x1, waiting for transfers between devices, run_ffn(): part_rows = lax.all_gather(normed_rows, 'blk', axis=0, tiled=True)  67.5 us
    all_gather x1, waiting for transfers between devices, local(): down_all = lax.all_gather(w_down, 'blk', axis=0, tiled=True)  18.9 us
    all_to_all x1, waiting for transfers between devices, run_ffn(): hidden_own = lax.all_to_all(hidden_all, 'blk', 0, 1, tiled=True)  16.8 us
    ppermute x5, waiting for transfers between devices, swap(): lax.ppermute(values, 'req', perm=[(i, i ^ mask) for i in range(count)])  16.4 us
    ppermute x5, starting transfers between devices, swap(): lax.ppermute(values, 'req', perm=[(i, i ^ mask) for i in range(count)])  12.3 us
    dot_general x1, matrix products, run_ffn(): jnp.einsum('rgk,gkd->grd', hidden_own.reshape(hidden_own.shape[0], group_...  6.57 us
    unnamed x46, local copies, waits for them, and re-layouts  6.3 us
    sub x2, matrix products, attend_block(): expd = jnp.exp(scores - peaks)  5.65 us
  transfers between devices with their start and end apart: 8, of which 5 were waited for; matrix products, arithmetic and copies ran while one was open for 16% of the time, Pallas kernels for 0%

profile of v17, /device:TPU:1, one launch (start us, length us, event | category | flops | bytes accessed | tf_op | source)
XLA Modules:
  0.0 229.2 jit_solution(1847550815863123746)
XLA Ops:
  7.3 7.8 %collective-permute-start = (bf16[2,256,384]{2,1,0:T(8,128)(2,1)}, bf16[2,256,384]{2,1,0:T(8,128)(2,1)S(1)}, u32[]{:S(2)}, u32[]{:S(2)}) collective-permute-start(bf16[2,256,384]{2,1,0:T(8,128)(2,1)} %bitcast.137), channel_id=1, source_target_pairs={{0,32},{32,0},{64,96},{96,64},{128,160},{160,128},{192,224},{224,1... | collective-permute-start | bytes 1179656 | tf_op jit(solution)/shard_map/ppermute | solution.py:110
  15.1 2.7 %collective-permute-start.1 = (s32[1]{0:T(128)}, s32[1]{0:T(128)}, u32[]{:S(2)}, u32[]{:S(2)}) collective-permute-start(s32[1]{0:T(128)} %param.17), channel_id=1, source_target_pairs={{0,128},{32,160},{64,192},{96,224},{128,0},{160,32},{192,64},{224,... | collective-permute-start | bytes 20 | tf_op jit(solution)/shard_map/ppermute | solution.py:110
  20.7 1.2 fusion.14
  21.9 1.9 constant_dynamic-update-slice_fusion.2
  24.1 1.0 copy-done.9
  25.4 0.9 fusion.23
  26.3 1.3 copy-done.1
  28.9 0.8 slice.102
  29.7 1.9 copy.44
  31.6 1.3 select_reduce_fusion
  33.9 2.5 %collective-permute-done.2 = s32[2]{0:T(128)S(1)} collective-permute-done((s32[2]{0:T(128)S(1)}, s32[2]{0:T(128)S(1)}, u32[]{:S(2)}, u32[]{:S(2)}) %collective-permute-start.2) | collective-permute-done | bytes 40 | tf_op jit(solution)/shard_map/ppermute | solution.py:110
  38.5 1.0 pad_maximum_fusion
  39.8 0.9 multiply_cosine_fusion
  40.7 0.7 subtract_convert_fusion.1
  42.7 13.9 %collective-permute-done.3 = bf16[2,2,256,384]{3,2,1,0:T(8,128)(2,1)} collective-permute-done((bf16[2,2,256,384]{3,2,1,0:T(8,128)(2,1)}, bf16[2,2,256,384]{3,2,1,0:T(8,128)(2,1)}, u32[]{:S(2)}, u32[]{:S(2)}) %collective-permute-start.3) | collective-permute-done | bytes 786464 | tf_op jit(solution)/shard_map/ppermute | solution.py:110
  56.6 1.8 fusion.26
  58.4 1.1 collective-permute-start.4
  60.1 1.6 slice.99
  61.8 1.6 slice.149
  63.3 1.7 copy.43
  65.1 1.6 copy.41
  66.7 1.2 concatenate.59
  67.9 1.6 pad_maximum_fusion.5
  69.5 1.6 subtract_convert_fusion.3
  71.1 1.2 fusion.29
  72.7 2.9 %fusion.82 = (f32[4,2,128]{2,1,0:T(2,128)S(1)}, f32[4,2,128,384]{2,3,1,0:T(8,128)}) fusion(bf16[128,4,2,96]{0,3,2,1:T(8,128)(2,1)} %bitcast.149, bf16[256,4,96]{0,2,1:T(8,128)(2,1)S(1)} %bitcast.147, bf16[128,4,48]{0,2,1:T(8,128)(2,1)} %get-tuple-element.24, bf16[128,4,48]{0,2,1:T(8,128)(2,1)} %get-tuple-element.23, pred[384]{0:T(512)(128)(4,1)} %concatenate.59), kind=kOutput, calls=%fused_computation.122 | convolution fusion | flops 77955456 | bytes 2068864 | tf_op jit(solution)/shard_map/sub | solution.py:78
  75.6 1.8 convolution_convert_fusion.1
  78.0 0.9 copy-done.2
  79.0 1.4 gather_fusion
  80.4 18.9 %all-gather.3.cloned.1.call-done = bf16[4096,1536]{1,0:T(8,128)(2,1)} async-done(((bf16[128,1536]{1,0:T(8,128)(2,1)}), bf16[4096,1536]{1,0:T(8,128)(2,1)}) %all-gather.3.cloned.1.call-update) | async-done | bytes 12582928 | tf_op jit(solution)/shard_map/all_gather | solution.py:158
  99.3 67.5 %all-gather.5.cloned.1.call-done = bf16[2048,1536]{1,0:T(8,128)(2,1)} async-done(((bf16[64,1536]{1,0:T(8,128)(2,1)}), bf16[2048,1536]{1,0:T(8,128)(2,1)}) %all-gather.5.cloned.1.call-update) | async-done | bytes 6291472 | tf_op jit(solution)/shard_map/all_gather | solution.py:86
  166.8 4.8 %fusion.17 = f32[2048,256]{1,0:T(8,128)S(1)} fusion(bf16[2048,1536]{1,0:T(8,128)(2,1)} %all-gather.5.cloned.1.call-done, bf16[1536,128]{1,0:T(8,128)(2,1)} %param.26, bf16[1536,128]{1,0:T(8,128)(2,1)} %param.25), kind=kOutput, calls=%fused_computation.31 | convolution fusion | flops 1612185600 | bytes 9175040 | tf_op jit(solution)/shard_map/dot_general | solution.py:87
  171.5 1.1 fusion.13
  172.6 5.4 %all-to-all-start = ((bf16[32,64,128]{2,1,0:T(8,128)(2,1)}), bf16[32,64,128]{2,1,0:T(8,128)(2,1)S(1)}, u32[]{:S(2)}, u32[]{:S(2)}) async-start(bf16[32,64,128]{2,1,0:T(8,128)(2,1)} %bitcast.138), calls=%async_computation | async-start | bytes 1048576 | tf_op jit(solution)/shard_map/all_to_all | solution.py:90
  178.1 16.8 %all-to-all-done = bf16[32,64,128]{2,1,0:T(8,128)(2,1)S(1)} async-done(((bf16[32,64,128]{2,1,0:T(8,128)(2,1)}), bf16[32,64,128]{2,1,0:T(8,128)(2,1)S(1)}, u32[]{:S(2)}, u32[]{:S(2)}) %all-to-all-start) | async-done | bytes 524320 | tf_op jit(solution)/shard_map/all_to_all | solution.py:90
  194.9 0.8 copy-done.5
  195.7 6.6 %convert_reduce_fusion = f32[64,1536]{1,0:T(8,128)S(1)} fusion(bf16[32,128,1536]{2,1,0:T(8,128)(2,1)} %bitcast.136, bf16[32,64,128]{2,1,0:T(8,128)(2,1)} %copy-done.5), kind=kOutput, calls=%fused_computation.4 | convolution fusion | flops 814645248 | bytes 13500416 | tf_op jit(solution)/shard_map/rgk,gkd->grd/dot_general | solution.py:92
  202.3 1.8 gather_fusion.1
  204.0 1.6 multiply_reduce_fusion
  205.7 3.2 %fusion.22 = f32[128,1536]{1,0:T(8,128)S(1)} fusion(bf16[1536,1536]{1,0:T(8,128)(2,1)} %copy-done.1, f32[128,1536]{1,0:T(8,128)S(1)} %get-tuple-element.12, f32[128]{0:T(128)S(1)} %add_rsqrt_fusion, f32[1536]{0:T(1024)S(1)} %copy-done.16), kind=kOutput, calls=%fused_computation.40 | convolution fusion | flops 604569600 | bytes 6298112 | tf_op jit(solution)/shard_map/dot_general | solution.py:54
  210.3 0.9 copy.49
  211.2 1.1 subtract_convert_fusion
  212.3 1.1 copy.48
  213.3 1.4 subtract_convert_fusion.2
  214.7 1.6 copy.47
  216.4 2.8 %fusion.85 = (f32[4,2,128]{2,1,0:T(2,128)S(1)}, f32[4,2,128,384]{2,3,1,0:T(8,128)}) fusion(bf16[128,4,2,96]{0,3,2,1:T(8,128)(2,1)S(1)} %bitcast.150, bf16[256,4,96]{0,2,1:T(8,128)(2,1)} %bitcast.148, bf16[128,4,48]{0,2,1:T(8,128)(2,1)} %get-tuple-element.22, bf16[128,4,48]{0,2,1:T(8,128)(2,1)} %get-tuple-element.21, pred[384]{0:T(512)(128)(4,1)S(1)} %copy-done.20), kind=kOutput, calls=%fused_computation.123 | convolution fusion | flops 77955456 | bytes 2068864 | tf_op jit(solution)/shard_map/sub | solution.py:78
  219.2 1.8 convolution_convert_fusion
  221.0 1.4 fusion.2
  (76 shorter events, 9.3 us)
Async XLA Ops:
  6.5 70.8 %copy-start = (bf16[768,1536]{1,0:T(8,128)(2,1)S(1)}, bf16[768,1536]{1,0:T(8,128)(2,1)}, u32[]{:S(2)}) copy-start(bf16[768,1536]{1,0:T(8,128)(2,1)} %param.23) | copy-start | bytes 7077892
  6.5 92.7 %all-gather.3.cloned.1.call-start = ((), (), s32[]{:S(2)}) async-start(), calls=%async_computation.1 | async-start | bytes 12976128 | tf_op jit(solution)/shard_map/all_gather | solution.py:158
  7.3 159.5 %all-gather.5.cloned.1.call-start = ((), (), s32[]{:S(2)}) async-start(), calls=%async_computation.2 | async-start | bytes 6488064 | tf_op jit(solution)/shard_map/all_gather | solution.py:86
  7.3 31.1 %collective-permute-start = (bf16[2,256,384]{2,1,0:T(8,128)(2,1)}, bf16[2,256,384]{2,1,0:T(8,128)(2,1)S(1)}, u32[]{:S(2)}, u32[]{:S(2)}) collective-permute-start(bf16[2,256,384]{2,1,0:T(8,128)(2,1)} %bitcast.137), channel_id=1, source_target_pairs={{0,32},{32,0},{64,96},{96,64},{128,160},{160,128},{192,224},{224,1... | collective-permute-start | bytes 1179656 | tf_op jit(solution)/shard_map/ppermute | solution.py:110
  15.1 17.8 %collective-permute-start.1 = (s32[1]{0:T(128)}, s32[1]{0:T(128)}, u32[]{:S(2)}, u32[]{:S(2)}) collective-permute-start(s32[1]{0:T(128)} %param.17), channel_id=1, source_target_pairs={{0,128},{32,160},{64,192},{96,224},{128,0},{160,32},{192,64},{224,... | collective-permute-start | bytes 20 | tf_op jit(solution)/shard_map/ppermute | solution.py:110
  19.2 12.4 %copy-start.18 = (pred[128]{0:T(512)(128)(4,1)}, pred[128]{0:T(512)(128)(4,1)S(1)}, u32[]{:S(2)}) copy-start(pred[128]{0:T(512)(128)(4,1)S(1)} %get-tuple-element.27) | copy-start | bytes 388
  21.9 2.0 copy-start.8
  23.9 1.3 copy-start.9
  23.9 1.5 copy-start.3
  23.9 1.5 copy-start.16
  25.4 2.2 copy-start.1
  25.4 13.0 %copy-start.4 = (bf16[1,2,256,384]{3,2,1,0:T(8,128)(2,1)S(1)}, bf16[1,2,256,384]{3,2,1,0:T(8,128)(2,1)}, u32[]{:S(2)}) copy-start(bf16[1,2,256,384]{3,2,1,0:T(8,128)(2,1)} %param.15) | copy-start | bytes 1179652
  27.6 1.3 copy-start.6
  33.6 2.8 %collective-permute-start.2 = (s32[2]{0:T(128)S(1)}, s32[2]{0:T(128)S(1)}, u32[]{:S(2)}, u32[]{:S(2)}) collective-permute-start(s32[2]{0:T(128)S(1)} %pad_add_fusion), channel_id=1, source_target_pairs={{0,64},{32,96},{64,0},{96,32},{128,192},{160,224},{192,128},{224,1... | collective-permute-start | bytes 32 | tf_op jit(solution)/shard_map/ppermute | solution.py:110
  37.1 2.8 %copy-start.21 = (s32[64]{0:T(128)S(1)}, s32[64]{0:T(128)}, u32[]{:S(2)}) copy-start(s32[64]{0:T(128)} %select_reduce_fusion) | copy-start | bytes 772
  38.4 2.3 %copy-start.7 = (f32[128,768]{0,1:T(8,128)S(1)}, f32[128,768]{0,1:T(8,128)}, u32[]{:S(2)}) copy-start(f32[128,768]{0,1:T(8,128)} %copy.44) | copy-start | bytes 1179652
  39.5 17.1 %collective-permute-start.3 = (bf16[2,2,256,384]{3,2,1,0:T(8,128)(2,1)}, bf16[2,2,256,384]{3,2,1,0:T(8,128)(2,1)}, u32[]{:S(2)}, u32[]{:S(2)}) collective-permute-start(bf16[2,2,256,384]{3,2,1,0:T(8,128)(2,1)} %pad_maximum_fusion), channel_id=1, source_target_pairs={{0,64},{32,96},{64,0},{96,32},{128,192},{160,224},{192,128},{224,1... | collective-permute-start | bytes 2359304 | tf_op jit(solution)/shard_map/ppermute | solution.py:110
  40.7 0.8 copy-start.10
  40.7 0.8 copy-start.11
  58.4 12.7 %collective-permute-start.4 = (bf16[2,256,384]{2,1,0:T(8,128)(2,1)}, bf16[2,256,384]{2,1,0:T(8,128)(2,1)}, u32[]{:S(2)}, u32[]{:S(2)}) collective-permute-start(bf16[2,256,384]{2,1,0:T(8,128)(2,1)} %fusion.26), channel_id=1, source_target_pairs={{0,128},{32,160},{64,192},{96,224},{128,0},{160,32},{192,64},{224,... | collective-permute-start | bytes 1179656 | tf_op jit(solution)/shard_map/ppermute | solution.py:110
  72.4 3.2 %copy-start.14 = (bf16[128,384]{0,1:T(8,128)(2,1)S(1)}, bf16[128,384]{0,1:T(8,128)(2,1)}, u32[]{:S(2)}) copy-start(bf16[128,384]{0,1:T(8,128)(2,1)} %copy.41) | copy-start | bytes 294916
  72.5 4.8 %copy-start.13 = (bf16[1,256,384]{1,2,0:T(8,128)(2,1)}, bf16[1,256,384]{1,2,0:T(8,128)(2,1)S(1)}, u32[]{:S(2)}) copy-start(bf16[1,256,384]{1,2,0:T(8,128)(2,1)S(1)} %copy.42) | copy-start | bytes 589828
  72.7 4.7 %copy-start.12 = (bf16[1,256,384]{1,2,0:T(8,128)(2,1)}, bf16[1,256,384]{1,2,0:T(8,128)(2,1)S(1)}, u32[]{:S(2)}) copy-start(bf16[1,256,384]{1,2,0:T(8,128)(2,1)S(1)} %copy.40) | copy-start | bytes 589828
  77.4 1.5 copy-start.17
  78.0 0.9 copy-start.2
  172.6 22.2 %all-to-all-start = ((bf16[32,64,128]{2,1,0:T(8,128)(2,1)}), bf16[32,64,128]{2,1,0:T(8,128)(2,1)S(1)}, u32[]{:S(2)}, u32[]{:S(2)}) async-start(bf16[32,64,128]{2,1,0:T(8,128)(2,1)} %bitcast.138), calls=%async_computation | async-start | bytes 1048576 | tf_op jit(solution)/shard_map/all_to_all | solution.py:90
  194.9 0.8 copy-start.5
  202.3 1.8 copy-start.19
  208.9 7.5 %copy-start.20 = (pred[384]{0:T(512)(128)(4,1)S(1)}, pred[384]{0:T(512)(128)(4,1)}, u32[]{:S(2)}) copy-start(pred[384]{0:T(512)(128)(4,1)} %concatenate.59) | copy-start | bytes 1156
  216.4 2.8 %copy-start.15 = (bf16[128,384]{0,1:T(8,128)(2,1)S(1)}, bf16[128,384]{0,1:T(8,128)(2,1)}, u32[]{:S(2)}) copy-start(bf16[128,384]{0,1:T(8,128)(2,1)} %copy.47) | copy-start | bytes 294916
Sparse Core Ops, SparseCore 0:
  9.2 90.0 all-gather.2
  101.1 65.5 all-gather.4
